TPU v7x, 128 devices: a whole 4x4x4 slice. The times are simulated.
128 devices in a mesh: row: 4 (over z), col: 32 (over x, y, core).
Axes of the slice: x: 4, y: 4, z: 4, core: 2. Of those that a mesh axis runs over, the one named last changes fastest.
Arguments:
- matrix_real: bfloat16 [512, 16384], P('col', 'row'), may hold values from -0.25 to 0.25
- matrix_imag: bfloat16 [512, 16384], P('col', 'row'), may hold values from -0.25 to 0.25
- valence_index: int32 [512], P('col'), may hold values from 0 to 15
- conduction_index: int32 [512], P('col'), may hold values from 0 to 31
- valence_energy: float32 [16], replicated, may hold values from -1.5 to -0.1
- conduction_energy: float32 [32], replicated, may hold values from 0.1 to 2
- frequency: float32 [2], replicated, may hold values from 0.2 to 2
Outputs:
- chi_real: bfloat16 [2, 16384, 16384], P(None, 'row', 'col')
- chi_imag: bfloat16 [2, 16384, 16384], P(None, 'row', 'col')
All inputs are finite; a program needn't handle non-finite values.
Results may differ from a plain program's by a relative error of at most 0.005.
Values may be sent and summed in bfloat16 or wider, within the bound.
No kernel may reach another device: no remote copies, remote signals or barrier semaphores. Data moves between devices by JAX's collectives and lax.ppermute only.
A program may use at most 192 MiB of HBM per device.

v0:
```python
import jax
import jax.numpy as jnp
from jax import lax
from jax.sharding import PartitionSpec as P


def lookup(indices, table):
    count = table.shape[0]
    picks = indices[:, None] == lax.broadcasted_iota(jnp.int32, (1, count), 1)
    return jnp.sum(jnp.where(picks, table[None, :], 0.0), axis=1)


def contract(left_side, right_side):
    return lax.dot_general(
        left_side, right_side, (((0,), (0,)), ((), ())), preferred_element_type=jnp.float32
    )


def on_device(
    matrix_real,
    matrix_imag,
    valence_index,
    conduction_index,
    valence_energy,
    conduction_energy,
    frequency,
):
    all_valence, all_conduction = (
        lax.all_gather(valence_index, "col", axis=0, tiled=True),
        lax.all_gather(conduction_index, "col", axis=0, tiled=True),
    )
    gap = lookup(all_conduction, conduction_energy) - lookup(all_valence, valence_energy)
    spread_real, spread_imag = (
        lax.all_gather(matrix_real, "row", axis=1, tiled=True),
        lax.all_gather(matrix_imag, "row", axis=1, tiled=True),
    )
    column_real, column_imag = (
        lax.all_to_all(spread_real, "col", split_axis=1, concat_axis=0, tiled=True),
        lax.all_to_all(spread_imag, "col", split_axis=1, concat_axis=0, tiled=True),
    )
    width = column_real.shape[1]
    wide_real = column_real.astype(jnp.float32)
    wide_imag = column_imag.astype(jnp.float32)
    upper_parts = []
    lower_parts = []
    for index in range(frequency.shape[0]):
        omega = frequency[index]
        weight = 4.0 * gap / (gap * gap + omega * omega)
        scaled_real = (weight[:, None] * wide_real).astype(jnp.bfloat16)
        scaled_imag = (weight[:, None] * wide_imag).astype(jnp.bfloat16)
        upper_parts.extend([scaled_real, scaled_imag])
        lower_parts.extend([scaled_imag, -scaled_real])
    upper_side = jnp.concatenate(upper_parts, axis=1)
    lower_side = jnp.concatenate(lower_parts, axis=1)
    right_side = jnp.concatenate([upper_side, lower_side], axis=0)
    block_real, block_imag = (
        lax.all_to_all(matrix_real, "col", split_axis=1, concat_axis=0, tiled=True),
        lax.all_to_all(matrix_imag, "col", split_axis=1, concat_axis=0, tiled=True),
    )
    stacked = jnp.concatenate([block_real, block_imag], axis=0)
    joined = contract(lax.all_gather(stacked, "col", axis=1, tiled=True), right_side)
    real_out = []
    imag_out = []
    for index in range(frequency.shape[0]):
        start = 2 * width * index
        real_out.append((-joined[:, start : start + width]).astype(jnp.bfloat16))
        imag_out.append((-joined[:, start + width : start + 2 * width]).astype(jnp.bfloat16))
    return (jnp.stack(real_out, axis=0), jnp.stack(imag_out, axis=0))


def solution(mesh):
    placed = (P("col", "row"), P("col", "row"), P("col"), P("col"), P(), P(), P())
    return jax.shard_map(
        on_device,
        mesh=mesh,
        in_specs=placed,
        out_specs=(P(None, "row", "col"), P(None, "row", "col")),
        check_vma=False,
    )
```

profile of v0, /device:TPU:1, one launch (start us, length us, event | category | flops | bytes accessed | tf_op | source)
XLA Modules:
  0.0 199.1 jit_solution(13468990475961677798)
XLA Ops:
  7.2 1.6 copy_bitcast_fusion.3
  8.7 8.6 %all-to-all-start = ((bf16[16,32,128]{2,0,1:T(8,128)(2,1)}), bf16[16,32,128]{2,0,1:T(8,128)(2,1)S(1)}, u32[]{:S(2)}, u32[]{:S(2)}) async-start(bf16[16,32,128]{2,0,1:T(8,128)(2,1)} %copy_bitcast_fusion.3), calls=%async_computation | async-start | bytes 262144 | tf_op jit(solution)/shard_map/all_to_all | solution.py:57
  17.3 0.0 all-gather.2.cloned.1.call-start
  17.4 0.9 copy_bitcast_fusion.2
  18.3 6.7 %all-to-all-done = bf16[16,32,128]{2,0,1:T(8,128)(2,1)S(1)} async-done(((bf16[16,32,128]{2,0,1:T(8,128)(2,1)}), bf16[16,32,128]{2,0,1:T(8,128)(2,1)S(1)}, u32[]{:S(2)}, u32[]{:S(2)}) %all-to-all-start) | async-done | bytes 131104 | tf_op jit(solution)/shard_map/all_to_all | solution.py:57
  25.0 11.3 %all_to_all.64 = bf16[16,32,128]{2,0,1:T(8,128)(2,1)S(1)} all-to-all(bf16[16,32,128]{2,0,1:T(8,128)(2,1)S(1)} %copy_bitcast_fusion.2), channel_id=1, replica_groups=mesh['row'=4,'col'=32] {'col'}, dimensions={1} | all-to-all | bytes 262144 | tf_op jit(solution)/shard_map/all_to_all | solution.py:58
  36.3 0.7 pad_maximum_fusion.2
  37.0 0.0 all-gather.2.cloned.1.call-update
  37.1 12.7 %all_gather.19 = bf16[16,16384]{1,0:T(8,128)(2,1)S(1)} all-gather(bf16[16,4096]{1,0:T(8,128)(2,1)} %param.8), channel_id=1, replica_groups=mesh['row'=4,'col'=32] {'row'}, dimensions={1}, use_global_device_ids=true | all-gather | bytes 655360 | tf_op jit(solution)/shard_map/all_gather | solution.py:35
  49.7 0.9 copy.29
  50.6 5.5 %all-to-all-start.3 = ((bf16[16,32,512]{2,0,1:T(8,128)(2,1)}), bf16[16,32,512]{2,0,1:T(8,128)(2,1)S(1)}, u32[]{:S(2)}, u32[]{:S(2)}) async-start(bf16[16,32,512]{2,0,1:T(8,128)(2,1)} %bitcast.54), calls=%async_computation.3 | async-start | bytes 1048576 | tf_op jit(solution)/shard_map/all_to_all | solution.py:39
  56.1 12.0 %all_gather.18 = bf16[16,16384]{1,0:T(8,128)(2,1)S(1)} all-gather(bf16[16,4096]{1,0:T(8,128)(2,1)} %param.7), channel_id=1, replica_groups=mesh['row'=4,'col'=32] {'row'}, dimensions={1}, use_global_device_ids=true | all-gather | bytes 655360 | tf_op jit(solution)/shard_map/all_gather | solution.py:34
  68.1 0.9 copy.30
  68.9 1.3 dynamic-slice
  70.8 0.9 dynamic-update-slice
  71.7 0.9 dynamic-update-slice.1
  72.5 15.7 %all-reduce.2 = (s32[512]{0:T(512)S(1)}, s32[512]{0:T(512)S(1)}) all-reduce(s32[512]{0:T(512)S(1)} %dynamic-update-slice, s32[512]{0:T(512)S(1)} %dynamic-update-slice.1), channel_id=1, replica_groups=mesh['row'=4,'col'=32] {'col'}, use_global_device_ids=true, to_apply=%add | all-reduce | flops 1024 | bytes 8192
  88.3 0.7 select_reduce_fusion.1
  89.0 0.7 select_reduce_fusion
  89.8 0.0 all-to-all-done.3
  89.8 6.8 %all-to-all-start.2 = ((bf16[16,32,512]{2,0,1:T(8,128)(2,1)}), bf16[16,32,512]{2,0,1:T(8,128)(2,1)S(1)}, u32[]{:S(2)}, u32[]{:S(2)}) async-start(bf16[16,32,512]{2,0,1:T(8,128)(2,1)} %bitcast.55), calls=%async_computation.2 | async-start | bytes 1048576 | tf_op jit(solution)/shard_map/all_to_all | solution.py:38
  96.6 1.3 fusion.33
  100.5 0.2 fusion.24
  100.7 7.6 %all-to-all-done.2 = bf16[16,32,512]{2,0,1:T(8,128)(2,1)S(1)} async-done(((bf16[16,32,512]{2,0,1:T(8,128)(2,1)}), bf16[16,32,512]{2,0,1:T(8,128)(2,1)S(1)}, u32[]{:S(2)}, u32[]{:S(2)}) %all-to-all-start.2) | async-done | bytes 524320 | tf_op jit(solution)/shard_map/all_to_all | solution.py:38
  108.3 1.1 fusion.29
  109.4 0.0 all-gather.2.cloned.1.call-done
  109.4 52.4 %fusion.8 = f32[4096,2048]{1,0:T(8,128)} fusion(bf16[1024,4096]{1,0:T(8,128)(2,1)} %all-gather.2.cloned.1.call-done, bf16[512,512]{1,0:T(8,128)(2,1)S(1)} %get-tuple-element.14, bf16[512,512]{1,0:T(8,128)(2,1)S(1)} %get-tuple-element.13, bf16[512,512]{1,0:T(8,128)(2,1)S(1)} %get-tuple-element.4, bf16[512,512]{1,0:T(8,128)(2,1)S(1)} %get-tuple-element.12, ...), kind=kOutput, calls=%fused_computation.14 | convolution fusion | flops 17213423616 | bytes 45088768 | tf_op jit(solution)/shard_map/dot_general | solution.py:14
  161.8 18.9 %fusion.6 = (bf16[1,4096,512]{2,1,0:T(8,128)(2,1)}, bf16[1,4096,512]{2,1,0:T(8,128)(2,1)}, bf16[1,4096,512]{2,1,0:T(8,128)(2,1)}, bf16[1,4096,512]{2,1,0:T(8,128)(2,1)}) fusion(f32[4096,2048]{1,0:T(8,128)} %fusion.8), kind=kLoop, calls=%fused_computation.12 | loop fusion | flops 16777216 | bytes 50331648 | tf_op jit(solution)/shard_map/stack | solution.py:68
  180.7 11.5 %pad_maximum_fusion = (bf16[2,4096,512]{2,1,0:T(8,128)(2,1)}, bf16[2,4096,512]{2,1,0:T(8,128)(2,1)}) fusion(bf16[1,4096,512]{2,1,0:T(8,128)(2,1)} %get-tuple-element.10, bf16[1,4096,512]{2,1,0:T(8,128)(2,1)} %get-tuple-element.11, bf16[1,4096,512]{2,1,0:T(8,128)(2,1)} %get-tuple-element.9, bf16[1,4096,512]{2,1,0:T(8,128)(2,1)} %get-tuple-element.8), kind=kLoop, calls=%fused_computation.8 | loop fusion | flops 8388608 | bytes 33554432 | tf_op jit(solution)/shard_map/stack | solution.py:68
  (3 shorter events, 0.0 us)
Async XLA Ops:
  8.7 16.3 %all-to-all-start = ((bf16[16,32,128]{2,0,1:T(8,128)(2,1)}), bf16[16,32,128]{2,0,1:T(8,128)(2,1)S(1)}, u32[]{:S(2)}, u32[]{:S(2)}) async-start(bf16[16,32,128]{2,0,1:T(8,128)(2,1)} %copy_bitcast_fusion.3), calls=%async_computation | async-start | bytes 262144 | tf_op jit(solution)/shard_map/all_to_all | solution.py:57
  17.3 92.1 %all-gather.2.cloned.1.call-start = ((), (), s32[]{:S(2)}) async-start(), calls=%async_computation.4 | async-start | bytes 8650752 | tf_op jit(solution)/shard_map/all_gather | solution.py:61
  50.6 39.2 %all-to-all-start.3 = ((bf16[16,32,512]{2,0,1:T(8,128)(2,1)}), bf16[16,32,512]{2,0,1:T(8,128)(2,1)S(1)}, u32[]{:S(2)}, u32[]{:S(2)}) async-start(bf16[16,32,512]{2,0,1:T(8,128)(2,1)} %bitcast.54), calls=%async_computation.3 | async-start | bytes 1048576 | tf_op jit(solution)/shard_map/all_to_all | solution.py:39
  89.8 18.5 %all-to-all-start.2 = ((bf16[16,32,512]{2,0,1:T(8,128)(2,1)}), bf16[16,32,512]{2,0,1:T(8,128)(2,1)S(1)}, u32[]{:S(2)}, u32[]{:S(2)}) async-start(bf16[16,32,512]{2,0,1:T(8,128)(2,1)} %bitcast.55), calls=%async_computation.2 | async-start | bytes 1048576 | tf_op jit(solution)/shard_map/all_to_all | solution.py:38
Sparse Core Ops, SparseCore 0:
  37.2 62.9 all-gather.1
where the time goes:
time: 200 us; the launch traced here: 199 us
  matrix products  52.4 us (26%)
  blocking collectives  51.7 us (26%)
  other arithmetic  34 us (17%)
  starting transfers between devices  20.9 us (10%)
  between operations  17.3 us (9%)
  waiting for transfers between devices  14.3 us (7%)
  local copies, waits for them, and re-layouts  8.55 us (4%)
    dot_general x1, matrix products, contract(): lax.dot_general(left_side, right_side, (((0,), (0,)), ((), ())), preferre...  52.4 us
    another operation x2, other arithmetic, on_device(): return (jnp.stack(real_out, axis=0), jnp.stack(imag_out, axis=0))  30.5 us
    unnamed x1, blocking collectives  15.7 us
    all_gather x1, blocking collectives, on_device(): lax.all_gather(matrix_imag, 'row', axis=1, tiled=True)  12.7 us
    all_gather x1, blocking collectives, on_device(): lax.all_gather(matrix_real, 'row', axis=1, tiled=True)  12 us
    all_to_all x1, blocking collectives, on_device(): lax.all_to_all(matrix_imag, 'col', split_axis=1, concat_axis=0, tiled=True)  11.3 us
    all_to_all x1, starting transfers between devices, on_device(): lax.all_to_all(matrix_real, 'col', split_axis=1, concat_axis=0, tiled=True)  8.59 us
    all_to_all x1, waiting for transfers between devices, on_device(): lax.all_to_all(spread_real, 'col', split_axis=1, concat_axis=0, tiled=True)  7.6 us
  transfers between devices with their start and end apart: 4, of which 2 were waited for; matrix products, arithmetic and copies ran while one was open for 5% of the time, Pallas kernels for 0%

commit v1 on v0

v1 whole, which is shorter than its diff:
```python
import jax
import jax.numpy as jnp
from jax import lax
from jax.sharding import PartitionSpec as P


def lookup(indices, table):
    count = table.shape[0]
    picks = indices[:, None] == lax.broadcasted_iota(jnp.int32, (1, count), 1)
    return jnp.sum(jnp.where(picks, table[None, :], 0.0), axis=1)


def contract(left_side, right_side):
    return lax.dot_general(
        left_side, right_side, (((0,), (0,)), ((), ())), preferred_element_type=jnp.float32
    )


CHUNKS = 4


def on_device(
    matrix_real,
    matrix_imag,
    valence_index,
    conduction_index,
    valence_energy,
    conduction_energy,
    frequency,
):
    ncol = lax.psum(1, "col")
    local_pairs, local_g = matrix_real.shape
    pairs = local_pairs * ncol
    both = jnp.stack([matrix_real, matrix_imag])
    bands = jnp.stack([valence_index, conduction_index]).astype(jnp.float32)
    all_bands = lax.all_gather(bands, "col", axis=1, tiled=True).astype(jnp.int32)
    gap = lookup(all_bands[1], conduction_energy) - lookup(all_bands[0], valence_energy)
    spread = lax.all_gather(both, "row", axis=2, tiled=True)
    spread = spread.reshape(2, local_pairs, ncol, -1)
    column = lax.all_to_all(spread, "col", split_axis=2, concat_axis=1, tiled=True)
    width = column.shape[-1]
    wide = column.reshape(2, pairs, width).astype(jnp.float32)
    right_real = []
    right_imag = []
    for index in range(frequency.shape[0]):
        omega = frequency[index]
        weight = 4.0 * gap / (gap * gap + omega * omega)
        scaled_real = (weight[:, None] * wide[0]).astype(jnp.bfloat16)
        scaled_imag = (weight[:, None] * wide[1]).astype(jnp.bfloat16)
        right_real.append(jnp.concatenate([-scaled_real, -scaled_imag], axis=0))
        right_imag.append(jnp.concatenate([-scaled_imag, scaled_real], axis=0))
    step = local_g // CHUNKS
    real_parts = [[] for _ in right_real]
    imag_parts = [[] for _ in right_real]
    for chunk in range(CHUNKS):
        piece = both[:, :, chunk * step : (chunk + 1) * step]
        left = lax.all_gather(piece, "col", axis=1, tiled=True).reshape(2 * pairs, step)
        for index in range(len(right_real)):
            real_parts[index].append(contract(left, right_real[index]).astype(jnp.bfloat16))
            imag_parts[index].append(contract(left, right_imag[index]).astype(jnp.bfloat16))
    chi_real = jnp.stack([jnp.concatenate(p, axis=0) for p in real_parts])
    chi_imag = jnp.stack([jnp.concatenate(p, axis=0) for p in imag_parts])
    return chi_real, chi_imag


def solution(mesh):
    placed = (P("col", "row"), P("col", "row"), P("col"), P("col"), P(), P(), P())
    return jax.shard_map(
        on_device,
        mesh=mesh,
        in_specs=placed,
        out_specs=(P(None, "row", "col"), P(None, "row", "col")),
        check_vma=False,
    )
```

time: 200 us -> 272 us (1.36)
  waiting for transfers between devices: 14.3 us -> 150 us
  blocking collectives: 51.7 us -> 29 us
  matrix products: 52.4 us -> 38.2 us
  starting transfers between devices: 20.9 us -> 8.64 us
  other arithmetic: 34 us -> 25.1 us
  local copies, waits for them, and re-layouts: 8.55 us -> 4.61 us
    all_gather x1 -> x5, waiting for transfers between devices: 0.01 us -> 148 us  [the longest x4 123 us: on_device(): lax.all_gather(piece, 'col', axis=1, tiled=True).reshape(2 * pairs, step)]
    unnamed x1 -> x0, blocking collectives: 15.7 us -> none
    all_to_all x3 -> x1, waiting for transfers between devices: 14.3 us -> 0.01 us  [on_device(): lax.all_to_all(spread, 'col', split_axis=2, concat_axis=1, tiled=True)]
    dot_general x1 -> x16, matrix products: 52.4 us -> 38.2 us  [contract(): lax.dot_general(left_side, right_side, (((0,), (0,)), ((), ())), preferre...]
    all_to_all x3 -> x1, starting transfers between devices: 20.8 us -> 8.44 us  [on_device(): lax.all_to_all(spread, 'col', split_axis=2, concat_axis=1, tiled=True)]
    all_to_all x1 -> x0, blocking collectives: 11.3 us -> none  [on_device(): lax.all_to_all(matrix_imag, 'col', split_axis=1, concat_axis=0, tiled=True)]
    another operation x2 -> x6, other arithmetic: 30.5 us -> 23.2 us  [the longest x2 10.8 us: on_device(): chi_imag = jnp.stack([jnp.concatenate(p, axis=0) for p in imag_parts])]
    all_gather x2 -> x1, blocking collectives: 24.7 us -> 29 us  [on_device(): lax.all_gather(bands, 'col', axis=1, tiled=True).astype(jnp.int32)]
  transfers between devices with their start and end apart: 4 -> 6, of which waited for: 2 -> 5; matrix products, arithmetic and copies ran while one was open for 5% -> 9% of each run, Pallas kernels for 0% -> 0%
where the time goes in v1:
time: 272 us
  waiting for transfers between devices  150 us (55%)
  matrix products  38.2 us (14%)
  blocking collectives  29 us (11%)
  other arithmetic  25.1 us (9%)
  between operations  16.5 us (6%)
  starting transfers between devices  8.64 us (3%)
  local copies, waits for them, and re-layouts  4.61 us (2%)
    all_gather x4, waiting for transfers between devices, on_device(): lax.all_gather(piece, 'col', axis=1, tiled=True).reshape(2 * pairs, step)  123 us
    dot_general x16, matrix products, contract(): lax.dot_general(left_side, right_side, (((0,), (0,)), ((), ())), preferre...  38.2 us
    all_gather x1, blocking collectives, on_device(): lax.all_gather(bands, 'col', axis=1, tiled=True).astype(jnp.int32)  29 us
    all_gather x1, waiting for transfers between devices, on_device(): spread = lax.all_gather(both, 'row', axis=2, tiled=True)  24.9 us
    another operation x2, other arithmetic, on_device(): chi_imag = jnp.stack([jnp.concatenate(p, axis=0) for p in imag_parts])  10.8 us
    another operation x2, other arithmetic, on_device(): chi_real = jnp.stack([jnp.concatenate(p, axis=0) for p in real_parts])  9.18 us
    all_to_all x1, starting transfers between devices, on_device(): lax.all_to_all(spread, 'col', split_axis=2, concat_axis=1, tiled=True)  8.44 us
  transfers between devices with their start and end apart: 6, of which 5 were waited for; matrix products, arithmetic and copies ran while one was open for 9% of the time, Pallas kernels for 0%

profile of v1, /device:TPU:1, one launch (start us, length us, event | category | flops | bytes accessed | tf_op | source)
XLA Modules:
  0.0 271.8 jit_solution(17406845412309366294)
XLA Ops:
  7.2 1.7 pad_maximum_fusion.6
  9.0 1.6 fusion.6
  10.6 0.7 all-gather.7.cloned.1.call-update
  11.9 24.9 %all-gather.9.cloned.1.call-done = bf16[2,16,16384]{2,1,0:T(8,128)(2,1)} async-done(((bf16[2,16,4096]{2,1,0:T(8,128)(2,1)}), bf16[2,16,16384]{2,1,0:T(8,128)(2,1)}) %all-gather.9.cloned.1.call-update) | async-done | bytes 1048592 | tf_op jit(solution)/shard_map/all_gather | solution.py:38
  36.8 2.4 copy.26
  39.2 8.4 %all-to-all-start = ((bf16[2,16,32,512]{3,1,0,2:T(8,128)(2,1)}), bf16[2,16,32,512]{3,1,0,2:T(8,128)(2,1)S(1)}, u32[]{:S(2)}, u32[]{:S(2)}) async-start(bf16[2,16,32,512]{3,1,0,2:T(8,128)(2,1)} %bitcast.71), calls=%async_computation | async-start | bytes 2097152 | tf_op jit(solution)/shard_map/all_to_all | solution.py:40
  51.3 29.0 %all-gather = f32[32,16,2]{1,2,0:T(2,128)S(1)} all-gather(f32[1,16,2]{1,2,0:T(2,128)S(1)} %fusion.10), channel_id=1, replica_groups=mesh['row'=4,'col'=32] {'col'}, dimensions={0}, use_global_device_ids=true | all-gather | bytes 4224 | tf_op jit(solution)/shard_map/all_gather | solution.py:36
  81.3 1.4 fusion.5
  82.7 5.7 %all-gather.11.cloned.1.call-done = bf16[2,512,1024]{2,1,0:T(8,128)(2,1)} async-done(((bf16[2,16,1024]{2,1,0:T(8,128)(2,1)}), bf16[2,512,1024]{2,1,0:T(8,128)(2,1)}) %all-gather.11.cloned.1.call-update) | async-done | bytes 2097168 | tf_op jit(solution)/shard_map/all_gather | solution.py:57
  88.4 3.8 %convolution_convert_fusion.10 = bf16[1024,512]{1,0:T(8,128)(2,1)} fusion(bf16[1024,1024]{1,0:T(8,128)(2,1)} %bitcast.82, bf16[512,512]{1,0:T(8,128)(2,1)S(1)} %get-tuple-element.11, bf16[512,512]{1,0:T(8,128)(2,1)S(1)} %get-tuple-element.16), kind=kOutput, calls=%fused_computation.17 | convolution fusion | flops 1076363264 | bytes 4194304 | tf_op jit(solution)/shard_map/dot_general | solution.py:14
  92.3 41.5 %all-gather.7.cloned.1.call-done = bf16[2,512,1024]{2,1,0:T(8,128)(2,1)} async-done(((bf16[2,16,1024]{2,1,0:T(8,128)(2,1)}), bf16[2,512,1024]{2,1,0:T(8,128)(2,1)}) %all-gather.7.cloned.1.call-update) | async-done | bytes 2097168 | tf_op jit(solution)/shard_map/all_gather | solution.py:57
  133.8 4.0 %convolution_convert_fusion.11 = bf16[1024,512]{1,0:T(8,128)(2,1)} fusion(bf16[1024,1024]{1,0:T(8,128)(2,1)} %bitcast.86, bf16[512,512]{1,0:T(8,128)(2,1)S(1)} %get-tuple-element.11, bf16[512,512]{1,0:T(8,128)(2,1)S(1)} %get-tuple-element.16), kind=kOutput, calls=%fused_computation.18 | convolution fusion | flops 1076363264 | bytes 4194304 | tf_op jit(solution)/shard_map/dot_general | solution.py:14
  137.8 1.3 convolution_convert_fusion.3
  139.3 2.5 convolution_convert_fusion.2
  141.9 37.1 %all-gather.13.cloned.1.call-done = bf16[2,512,1024]{2,1,0:T(8,128)(2,1)} async-done(((bf16[2,16,1024]{2,1,0:T(8,128)(2,1)}), bf16[2,512,1024]{2,1,0:T(8,128)(2,1)}) %all-gather.13.cloned.1.call-update) | async-done | bytes 2097168 | tf_op jit(solution)/shard_map/all_gather | solution.py:57
  179.0 4.2 %convolution_convert_fusion.9 = bf16[1024,512]{1,0:T(8,128)(2,1)} fusion(bf16[1024,1024]{1,0:T(8,128)(2,1)} %bitcast.90, bf16[512,512]{1,0:T(8,128)(2,1)} %copy-done.5, bf16[512,512]{1,0:T(8,128)(2,1)} %copy-done.11), kind=kOutput, calls=%fused_computation.16 | convolution fusion | flops 1076363264 | bytes 4194304 | tf_op jit(solution)/shard_map/dot_general | solution.py:14
  183.2 2.3 convolution_convert_fusion.1
  185.5 38.7 %all-gather.15.cloned.1.call-done = bf16[2,512,1024]{2,1,0:T(8,128)(2,1)} async-done(((bf16[2,16,1024]{2,1,0:T(8,128)(2,1)}), bf16[2,512,1024]{2,1,0:T(8,128)(2,1)}) %all-gather.15.cloned.1.call-update) | async-done | bytes 2097168 | tf_op jit(solution)/shard_map/all_gather | solution.py:57
  224.2 3.3 %convolution_convert_fusion.8 = bf16[1024,512]{1,0:T(8,128)(2,1)S(1)} fusion(bf16[1024,1024]{1,0:T(8,128)(2,1)} %bitcast.94, bf16[512,512]{1,0:T(8,128)(2,1)} %copy-done.5, bf16[512,512]{1,0:T(8,128)(2,1)} %copy-done.11), kind=kOutput, calls=%fused_computation.15 | convolution fusion | flops 1076363264 | bytes 4194304 | tf_op jit(solution)/shard_map/dot_general | solution.py:14
  227.5 2.3 convolution_convert_fusion
  229.8 1.3 convolution_convert_fusion.14
  231.4 1.3 convolution_convert_fusion.13
  232.7 2.5 convolution_convert_fusion.6
  235.2 2.3 convolution_convert_fusion.5
  237.5 1.3 convolution_convert_fusion.12
  238.8 2.4 convolution_convert_fusion.4
  241.2 2.3 convolution_convert_fusion.7
  243.4 1.3 convolution_convert_fusion.15
  245.3 2.8 %maximum_bitcast_fusion = (bf16[1,4096,512]{2,1,0:T(8,128)(2,1)S(1)}, bf16[1,4096,512]{2,1,0:T(8,128)(2,1)}) fusion(bf16[1024,512]{1,0:T(8,128)(2,1)S(1)} %convolution_convert_fusion.12, bf16[1024,512]{1,0:T(8,128)(2,1)S(1)} %convolution_convert_fusion.13, bf16[1024,512]{1,0:T(8,128)(2,1)S(1)} %convolution_convert_fusion.14, ...), kind=kLoop, calls=%fused_computation.2 | loop fusion | flops 33554432 | bytes 16777216 | tf_op jit(solution)/shard_map/stack | solution.py:61
  248.1 6.3 %pad_maximum_fusion = bf16[2,4096,512]{2,1,0:T(8,128)(2,1)} fusion(bf16[1,4096,512]{2,1,0:T(8,128)(2,1)} %get-tuple-element.27, bf16[1,4096,512]{2,1,0:T(8,128)(2,1)S(1)} %get-tuple-element.26), kind=kLoop, calls=%fused_computation | loop fusion | flops 4194304 | bytes 16777216 | tf_op jit(solution)/shard_map/stack | solution.py:61
  254.5 4.4 %maximum_bitcast_fusion.2 = (bf16[1,4096,512]{2,1,0:T(8,128)(2,1)S(1)}, bf16[1,4096,512]{2,1,0:T(8,128)(2,1)}) fusion(bf16[1024,512]{1,0:T(8,128)(2,1)} %convolution_convert_fusion.4, bf16[1024,512]{1,0:T(8,128)(2,1)} %convolution_convert_fusion.5, bf16[1024,512]{1,0:T(8,128)(2,1)} %convolution_convert_fusion.6, ...), kind=kLoop, calls=%fused_computation.4 | loop fusion | flops 33554432 | bytes 16777216 | tf_op jit(solution)/shard_map/stack | solution.py:62
  258.9 6.3 %pad_maximum_fusion.1 = bf16[2,4096,512]{2,1,0:T(8,128)(2,1)} fusion(bf16[1,4096,512]{2,1,0:T(8,128)(2,1)} %get-tuple-element.29, bf16[1,4096,512]{2,1,0:T(8,128)(2,1)S(1)} %get-tuple-element.28), kind=kLoop, calls=%fused_computation.1 | loop fusion | flops 4194304 | bytes 16777216 | tf_op jit(solution)/shard_map/stack | solution.py:62
  (70 shorter events, 4.0 us)
Async XLA Ops:
  7.2 29.6 %all-gather.9.cloned.1.call-start = ((), (), s32[]{:S(2)}) async-start(), calls=%async_computation.2 | async-start | bytes 1310720 | tf_op jit(solution)/shard_map/all_gather | solution.py:38
  8.9 79.5 %all-gather.11.cloned.1.call-start = ((), (), s32[]{:S(2)}) async-start(), calls=%async_computation.3 | async-start | bytes 2162688 | tf_op jit(solution)/shard_map/all_gather | solution.py:57
  10.6 123.2 %all-gather.7.cloned.1.call-start = ((), (), s32[]{:S(2)}) async-start(), calls=%async_computation.1 | async-start | bytes 2162688 | tf_op jit(solution)/shard_map/all_gather | solution.py:57
  11.3 167.7 %all-gather.13.cloned.1.call-start = ((), (), s32[]{:S(2)}) async-start(), calls=%async_computation.4 | async-start | bytes 2162688 | tf_op jit(solution)/shard_map/all_gather | solution.py:57
  36.8 11.5 %copy-start.12 = (f32[2]{0:T(128)S(1)}, f32[2]{0:T(128)}, u32[]{:S(2)}) copy-start(f32[2]{0:T(128)} %param.13) | copy-start | bytes 28
  36.8 14.5 %copy-start.15 = (s32[16]{0:T(128)S(1)}, s32[16]{0:T(128)}, u32[]{:S(2)}) copy-start(s32[16]{0:T(128)} %param.10) | copy-start | bytes 196
  36.8 14.5 %copy-start.16 = (s32[16]{0:T(128)S(1)}, s32[16]{0:T(128)}, u32[]{:S(2)}) copy-start(s32[16]{0:T(128)} %param.9) | copy-start | bytes 196
  36.8 43.8 %copy-start.13 = (f32[16]{0:T(128)S(1)}, f32[16]{0:T(128)}, u32[]{:S(2)}) copy-start(f32[16]{0:T(128)} %param.11) | copy-start | bytes 196
  36.8 43.9 %copy-start.14 = (f32[32]{0:T(128)S(1)}, f32[32]{0:T(128)}, u32[]{:S(2)}) copy-start(f32[32]{0:T(128)} %param.12) | copy-start | bytes 388
  39.2 41.6 %all-to-all-start = ((bf16[2,16,32,512]{3,1,0,2:T(8,128)(2,1)}), bf16[2,16,32,512]{3,1,0,2:T(8,128)(2,1)S(1)}, u32[]{:S(2)}, u32[]{:S(2)}) async-start(bf16[2,16,32,512]{3,1,0,2:T(8,128)(2,1)} %bitcast.71), calls=%async_computation | async-start | bytes 2097152 | tf_op jit(solution)/shard_map/all_to_all | solution.py:40
  47.6 176.6 %all-gather.15.cloned.1.call-start = ((), (), s32[]{:S(2)}) async-start(), calls=%async_computation.5 | async-start | bytes 2162688 | tf_op jit(solution)/shard_map/all_gather | solution.py:57
  82.7 51.0 %copy-start.11 = (bf16[512,512]{1,0:T(8,128)(2,1)}, bf16[512,512]{1,0:T(8,128)(2,1)S(1)}, u32[]{:S(2)}) copy-start(bf16[512,512]{1,0:T(8,128)(2,1)S(1)} %get-tuple-element.16) | copy-start | bytes 1572868
  82.7 55.0 %copy-start.5 = (bf16[512,512]{1,0:T(8,128)(2,1)}, bf16[512,512]{1,0:T(8,128)(2,1)S(1)}, u32[]{:S(2)}) copy-start(bf16[512,512]{1,0:T(8,128)(2,1)S(1)} %get-tuple-element.11) | copy-start | bytes 1572868
  82.7 55.0 %copy-start.8 = (bf16[512,512]{1,0:T(8,128)(2,1)}, bf16[512,512]{1,0:T(8,128)(2,1)S(1)}, u32[]{:S(2)}) copy-start(bf16[512,512]{1,0:T(8,128)(2,1)S(1)} %get-tuple-element.17) | copy-start | bytes 1572868
  133.7 4.0 %copy-start.19 = (bf16[2,512,1024]{2,1,0:T(8,128)(2,1)S(1)}, bf16[2,512,1024]{2,1,0:T(8,128)(2,1)}, u32[]{:S(2)}) copy-start(bf16[2,512,1024]{2,1,0:T(8,128)(2,1)} %all-gather.7.cloned.1.call-done) | copy-start | bytes 6291460
  137.8 1.6 copy-start.17
  179.0 4.2 %copy-start.6 = (bf16[512,512]{1,0:T(8,128)(2,1)S(1)}, bf16[512,512]{1,0:T(8,128)(2,1)}, u32[]{:S(2)}) copy-start(bf16[512,512]{1,0:T(8,128)(2,1)} %copy-done.5) | copy-start | bytes 1572868
  179.0 4.2 %copy-start.9 = (bf16[512,512]{1,0:T(8,128)(2,1)S(1)}, bf16[512,512]{1,0:T(8,128)(2,1)}, u32[]{:S(2)}) copy-start(bf16[512,512]{1,0:T(8,128)(2,1)} %copy-done.8) | copy-start | bytes 1572868
  179.0 4.2 %copy-start.21 = (bf16[2,512,1024]{2,1,0:T(8,128)(2,1)S(1)}, bf16[2,512,1024]{2,1,0:T(8,128)(2,1)}, u32[]{:S(2)}) copy-start(bf16[2,512,1024]{2,1,0:T(8,128)(2,1)} %all-gather.13.cloned.1.call-done) | copy-start | bytes 6291460
  224.2 3.3 %copy-start.7 = (bf16[512,512]{1,0:T(8,128)(2,1)S(1)}, bf16[512,512]{1,0:T(8,128)(2,1)}, u32[]{:S(2)}) copy-start(bf16[512,512]{1,0:T(8,128)(2,1)} %copy-done.5) | copy-start | bytes 1572868
  224.2 3.3 %copy-start.10 = (bf16[512,512]{1,0:T(8,128)(2,1)S(1)}, bf16[512,512]{1,0:T(8,128)(2,1)}, u32[]{:S(2)}) copy-start(bf16[512,512]{1,0:T(8,128)(2,1)} %copy-done.8) | copy-start | bytes 1572868
  224.2 3.3 %copy-start.23 = (bf16[2,512,1024]{2,1,0:T(8,128)(2,1)S(1)}, bf16[2,512,1024]{2,1,0:T(8,128)(2,1)}, u32[]{:S(2)}) copy-start(bf16[2,512,1024]{2,1,0:T(8,128)(2,1)} %all-gather.15.cloned.1.call-done) | copy-start | bytes 6291460
  227.5 2.3 copy-start.3
  227.5 2.3 copy-start.18
  229.8 1.6 copy-start.22
  231.4 1.3 copy-start.4
  238.8 2.4 copy-start.20
  243.4 1.3 copy-start
  243.4 1.5 copy-start.1
  243.4 1.9 copy-start.2
Sparse Core Ops, SparseCore 0:
  10.2 26.4 all-gather.8
  39.7 48.6 all-gather.10
  90.8 42.9 all-gather.6
  136.0 42.9 all-gather.12
  181.2 42.9 all-gather.14

commit v2 on v1

v2 whole, which is shorter than its diff:
```python
import jax
import jax.numpy as jnp
from jax import lax
from jax.sharding import PartitionSpec as P


def lookup(indices, table):
    count = table.shape[0]
    picks = indices[:, None] == lax.broadcasted_iota(jnp.int32, (1, count), 1)
    return jnp.sum(jnp.where(picks, table[None, :], 0.0), axis=1)


def on_device(
    matrix_real,
    matrix_imag,
    valence_index,
    conduction_index,
    valence_energy,
    conduction_energy,
    frequency,
):
    nrow = lax.psum(1, "row")
    ncol = lax.psum(1, "col")
    local_pairs, local_g = matrix_real.shape
    pairs = local_pairs * ncol
    width = local_g * nrow // ncol
    both = jnp.stack([matrix_real, matrix_imag])
    left = lax.all_gather(both, "col", axis=1, tiled=True).reshape(2 * pairs, local_g)
    copies = jnp.broadcast_to(both[None], (nrow,) + both.shape)
    spread = lax.all_to_all(copies, "row", 0, 0, tiled=True)
    spread = spread.reshape(nrow, 2, local_pairs, local_g // width, width)
    payload = spread.transpose(1, 2, 0, 3, 4).reshape(2, local_pairs, ncol, width)
    bands = jnp.stack([valence_index, conduction_index]).astype(jnp.bfloat16)
    tags = jnp.broadcast_to(bands[:, :, None, None], (2, local_pairs, ncol, 128))
    payload = jnp.concatenate([payload, tags], axis=3)
    column = lax.all_to_all(payload, "col", split_axis=2, concat_axis=1, tiled=True)
    column = column.reshape(2, pairs, width + 128)
    all_bands = column[:, :, width].astype(jnp.int32)
    gap = lookup(all_bands[1], conduction_energy) - lookup(all_bands[0], valence_energy)
    wide = column[:, :, :width].astype(jnp.float32)
    right_real = []
    right_imag = []
    for index in range(frequency.shape[0]):
        omega = frequency[index]
        weight = 4.0 * gap / (gap * gap + omega * omega)
        scaled_real = (weight[:, None] * wide[0]).astype(jnp.bfloat16)
        scaled_imag = (weight[:, None] * wide[1]).astype(jnp.bfloat16)
        right_real.append(jnp.concatenate([-scaled_real, -scaled_imag], axis=0))
        right_imag.append(jnp.concatenate([-scaled_imag, scaled_real], axis=0))
    nf = len(right_real)
    lefts = jnp.broadcast_to(left[None], (nf,) + left.shape)
    dims = (((1,), (1,)), ((0,), (0,)))
    chi_real = lax.dot_general(lefts, jnp.stack(right_real), dims, preferred_element_type=jnp.float32)
    chi_imag = lax.dot_general(lefts, jnp.stack(right_imag), dims, preferred_element_type=jnp.float32)
    return chi_real.astype(jnp.bfloat16), chi_imag.astype(jnp.bfloat16)


def solution(mesh):
    placed = (P("col", "row"), P("col", "row"), P("col"), P("col"), P(), P(), P())
    return jax.shard_map(
        on_device,
        mesh=mesh,
        in_specs=placed,
        out_specs=(P(None, "row", "col"), P(None, "row", "col")),
        check_vma=False,
    )
```

time: 272 us -> 123 us (0.45)
  waiting for transfers between devices: 150 us -> 45.1 us
  blocking collectives: 29 us -> 0 us
  other arithmetic: 25.1 us -> 4.22 us
  matrix products: 38.2 us -> 24 us
  local copies, waits for them, and re-layouts: 4.61 us -> 17 us
  starting transfers between devices: 8.64 us -> 14.8 us
    all_gather x5 -> x1, waiting for transfers between devices: 148 us -> 4.56 us  [on_device(): lax.all_gather(both, 'col', axis=1, tiled=True).reshape(2 * pairs, local_g)]
    all_to_all x1 -> x2, waiting for transfers between devices: 0.01 us -> 40.5 us  [the longest x1 26.4 us: on_device(): lax.all_to_all(payload, 'col', split_axis=2, concat_axis=1, tiled=True)]
    all_gather x1 -> x0, blocking collectives: 29 us -> none  [on_device(): lax.all_gather(bands, 'col', axis=1, tiled=True).astype(jnp.int32)]
    another operation x4, other arithmetic: 20 us -> 1.43 us  [the longest x2 1.41 us: on_device(): jnp.stack(right_imag)]
    dot_general x16 -> x2, matrix products: 38.2 us -> 24 us  [the longest x1 13.1 us: on_device(): lax.dot_general(lefts, jnp.stack(right_imag), dims, preferred_element_typ...]
    broadcast_in_dim x0 -> x3, local copies, waits for them, and re-layouts: none -> 14.1 us  [the longest x1 11.9 us: on_device(): lefts = jnp.broadcast_to(left[None], (nf,) + left.shape)]
    all_to_all x1 -> x2, starting transfers between devices: 8.44 us -> 14.8 us  [the longest x1 8.95 us: on_device(): lax.all_to_all(payload, 'col', split_axis=2, concat_axis=1, tiled=True)]
  transfers between devices with their start and end apart: 6 -> 3, of which waited for: 5 -> 3; matrix products, arithmetic and copies ran while one was open for 9% -> 6% of each run, Pallas kernels for 0% -> 0%
where the time goes in v2:
time: 123 us; the launch traced here: 122 us
  waiting for transfers between devices  45.1 us (37%)
  matrix products  24 us (20%)
  local copies, waits for them, and re-layouts  17 us (14%)
  between operations  16.7 us (14%)
  starting transfers between devices  14.8 us (12%)
  other arithmetic  4.22 us (3%)
    all_to_all x1, waiting for transfers between devices, on_device(): lax.all_to_all(payload, 'col', split_axis=2, concat_axis=1, tiled=True)  26.4 us
    all_to_all x1, waiting for transfers between devices, on_device(): spread = lax.all_to_all(copies, 'row', 0, 0, tiled=True)  14.2 us
    dot_general x1, matrix products, on_device(): lax.dot_general(lefts, jnp.stack(right_imag), dims, preferred_element_typ...  13.1 us
    broadcast_in_dim x1, local copies, waits for them, and re-layouts, on_device(): lefts = jnp.broadcast_to(left[None], (nf,) + left.shape)  11.9 us
    dot_general x1, matrix products, on_device(): lax.dot_general(lefts, jnp.stack(right_real), dims, preferred_element_typ...  10.9 us
    all_to_all x1, starting transfers between devices, on_device(): lax.all_to_all(payload, 'col', split_axis=2, concat_axis=1, tiled=True)  8.95 us
    all_to_all x1, starting transfers between devices, on_device(): spread = lax.all_to_all(copies, 'row', 0, 0, tiled=True)  5.86 us
    all_gather x1, waiting for transfers between devices, on_device(): lax.all_gather(both, 'col', axis=1, tiled=True).reshape(2 * pairs, local_g)  4.56 us
  transfers between devices with their start and end apart: 3, of which 3 were waited for; matrix products, arithmetic and copies ran while one was open for 6% of the time, Pallas kernels for 0%

profile of v2, /device:TPU:1, one launch (start us, length us, event | category | flops | bytes accessed | tf_op | source)
XLA Modules:
  0.0 121.9 jit_solution(815024570781896858)
XLA Ops:
  7.2 0.0 all-gather.2.cloned.1.call-start
  7.2 0.0 copy-start.4
  7.2 0.0 copy-start.5
  7.2 1.7 %pad_maximum_fusion.1 = bf16[2,16,4096]{2,1,0:T(8,128)(2,1)} fusion(bf16[1,16,4096]{2,1,0:T(8,128)(2,1)} %bitcast.56, bf16[1,16,4096]{2,1,0:T(8,128)(2,1)} %bitcast.57), kind=kLoop, calls=%fused_computation.30 | loop fusion | flops 131072 | bytes 524288 | tf_op jit(solution)/shard_map/stack | solution.py:27
  8.9 0.0 all-gather.2.cloned.1.call-update
  9.0 2.0 %broadcast_in_dim.51 = bf16[4,2,16,4096]{3,2,1,0:T(8,128)(2,1)} broadcast(bf16[2,16,4096]{2,1,0:T(8,128)(2,1)} %pad_maximum_fusion.1), dimensions={1,2,3} | broadcast | bytes 1310720 | tf_op jit(solution)/shard_map/broadcast_in_dim | solution.py:29
  11.0 5.9 %all-to-all-start = ((bf16[4,2,16,4096]{3,2,1,0:T(8,128)(2,1)}), bf16[4,2,16,4096]{3,2,1,0:T(8,128)(2,1)S(1)}, u32[]{:S(2)}, u32[]{:S(2)}) async-start(bf16[4,2,16,4096]{3,2,1,0:T(8,128)(2,1)} %broadcast_in_dim.51), calls=%async_computation | async-start | bytes 2097152 | tf_op jit(solution)/shard_map/all_to_all | solution.py:30
  16.9 14.2 %all-to-all-done = bf16[4,2,16,4096]{3,2,1,0:T(8,128)(2,1)S(1)} async-done(((bf16[4,2,16,4096]{3,2,1,0:T(8,128)(2,1)}), bf16[4,2,16,4096]{3,2,1,0:T(8,128)(2,1)S(1)}, u32[]{:S(2)}, u32[]{:S(2)}) %all-to-all-start) | async-done | bytes 1048608 | tf_op jit(solution)/shard_map/all_to_all | solution.py:30
  31.0 0.4 copy.22
  31.4 0.1 copy.24
  31.5 0.1 broadcast_in_dim.52
  31.7 0.1 pad_maximum_fusion
  31.8 0.0 copy-start.1
  31.8 1.5 %copy.20 = bf16[2,16,32,640]{3,1,0,2:T(8,128)(2,1)} copy(bf16[2,16,32,640]{3,2,1,0:T(8,128)(2,1)S(1)} %pad_maximum_fusion) | data formatting | bytes 2621440 | tf_op jit(solution)/shard_map/concatenate | solution.py:35
  33.3 8.9 %all-to-all-start.1 = ((bf16[2,16,32,640]{3,1,0,2:T(8,128)(2,1)}), bf16[2,16,32,640]{3,1,0,2:T(8,128)(2,1)S(1)}, u32[]{:S(2)}, u32[]{:S(2)}) async-start(bf16[2,16,32,640]{3,1,0,2:T(8,128)(2,1)} %copy.20), calls=%async_computation.1 | async-start | bytes 2621440 | tf_op jit(solution)/shard_map/all_to_all | solution.py:36
  42.2 0.0 copy-start.2
  42.3 0.0 copy-start.3
  42.3 0.6 fusion.22
  45.4 26.4 %all-to-all-done.1 = bf16[2,16,32,640]{3,1,0,2:T(8,128)(2,1)S(1)} async-done(((bf16[2,16,32,640]{3,1,0,2:T(8,128)(2,1)}), bf16[2,16,32,640]{3,1,0,2:T(8,128)(2,1)S(1)}, u32[]{:S(2)}, u32[]{:S(2)}) %all-to-all-start.1) | async-done | bytes 1310752 | tf_op jit(solution)/shard_map/all_to_all | solution.py:36
  71.8 0.1 copy.21
  71.9 0.1 slice_convert_fusion.1
  72.0 0.2 slice_reduce_fusion
  72.2 0.1 select_reduce_fusion.1
  72.3 0.1 select_reduce_fusion
  72.4 0.3 slice_convert_fusion
  72.7 0.4 fusion.20
  73.1 0.2 maximum_bitcast_fusion.2
  73.3 1.2 %maximum_bitcast_fusion.3 = (bf16[1,1024,512]{2,1,0:T(8,128)(2,1)}, bf16[1,1024,512]{2,1,0:T(8,128)(2,1)S(1)}) fusion(bf16[512,512]{1,0:T(8,128)(2,1)S(1)} %get-tuple-element.12, bf16[512,512]{1,0:T(8,128)(2,1)S(1)} %get-tuple-element.10, bf16[512,512]{1,0:T(8,128)(2,1)S(1)} %get-tuple-element.11), kind=kLoop, calls=%fused_computation.19 | loop fusion | flops 4194304 | bytes 3670016 | tf_op jit(solution)/shard_map/stack | solution.py:54
  74.5 4.6 %all-gather.2.cloned.1.call-done = bf16[2,512,4096]{2,1,0:T(8,128)(2,1)} async-done(((bf16[2,16,4096]{2,1,0:T(8,128)(2,1)}), bf16[2,512,4096]{2,1,0:T(8,128)(2,1)}) %all-gather.2.cloned.1.call-update) | async-done | bytes 8388624 | tf_op jit(solution)/shard_map/all_gather | solution.py:28
  79.1 11.9 %copy.18 = bf16[1024,4096]{0,1:T(8,128)(2,1)} copy(bf16[1024,4096]{1,0:T(8,128)(2,1)} %bitcast.49) | data formatting | bytes 16777216 | tf_op jit(solution)/shard_map/broadcast_in_dim | solution.py:51
  91.0 13.1 %fusion.7 = bf16[2,4096,512]{2,1,0:T(8,128)(2,1)} fusion(bf16[1024,4096]{0,1:T(8,128)(2,1)} %copy.18, bf16[1,1024,512]{2,1,0:T(8,128)(2,1)} %get-tuple-element.15, bf16[1,1024,512]{2,1,0:T(8,128)(2,1)S(1)} %get-tuple-element.13), kind=kOutput, calls=%fused_computation.5 | convolution fusion | flops 8595177472 | bytes 18874368 | tf_op jit(solution)/shard_map/dot_general | solution.py:54
  104.1 10.9 %fusion.4 = bf16[2,4096,512]{2,1,0:T(8,128)(2,1)} fusion(bf16[1024,4096]{0,1:T(8,128)(2,1)S(1)} %copy-done, bf16[1,1024,512]{2,1,0:T(8,128)(2,1)S(1)} %get-tuple-element.16, bf16[1,1024,512]{2,1,0:T(8,128)(2,1)S(1)} %get-tuple-element.14), kind=kOutput, calls=%fused_computation.4 | convolution fusion | flops 8595177472 | bytes 18874368 | tf_op jit(solution)/shard_map/dot_general | solution.py:53
  (10 shorter events, 0.0 us)
Async XLA Ops:
  7.2 71.9 %all-gather.2.cloned.1.call-start = ((), (), s32[]{:S(2)}) async-start(), calls=%async_computation.2 | async-start | bytes 8650752 | tf_op jit(solution)/shard_map/all_gather | solution.py:28
  7.2 9.6 %copy-start.4 = (s32[16]{0:T(128)S(1)}, s32[16]{0:T(128)}, u32[]{:S(2)}) copy-start(s32[16]{0:T(128)} %param.10) | copy-start | bytes 196
  7.2 9.6 %copy-start.5 = (s32[16]{0:T(128)S(1)}, s32[16]{0:T(128)}, u32[]{:S(2)}) copy-start(s32[16]{0:T(128)} %param.9) | copy-start | bytes 196
  11.0 20.0 %all-to-all-start = ((bf16[4,2,16,4096]{3,2,1,0:T(8,128)(2,1)}), bf16[4,2,16,4096]{3,2,1,0:T(8,128)(2,1)S(1)}, u32[]{:S(2)}, u32[]{:S(2)}) async-start(bf16[4,2,16,4096]{3,2,1,0:T(8,128)(2,1)} %broadcast_in_dim.51), calls=%async_computation | async-start | bytes 2097152 | tf_op jit(solution)/shard_map/all_to_all | solution.py:30
  31.8 10.4 %copy-start.1 = (f32[2]{0:T(128)S(1)}, f32[2]{0:T(128)}, u32[]{:S(2)}) copy-start(f32[2]{0:T(128)} %param.13) | copy-start | bytes 28
  33.3 38.5 %all-to-all-start.1 = ((bf16[2,16,32,640]{3,1,0,2:T(8,128)(2,1)}), bf16[2,16,32,640]{3,1,0,2:T(8,128)(2,1)S(1)}, u32[]{:S(2)}, u32[]{:S(2)}) async-start(bf16[2,16,32,640]{3,1,0,2:T(8,128)(2,1)} %copy.20), calls=%async_computation.1 | async-start | bytes 2621440 | tf_op jit(solution)/shard_map/all_to_all | solution.py:36
  42.2 29.9 %copy-start.2 = (f32[16]{0:T(128)S(1)}, f32[16]{0:T(128)}, u32[]{:S(2)}) copy-start(f32[16]{0:T(128)} %param.11) | copy-start | bytes 196
  42.3 30.0 %copy-start.3 = (f32[32]{0:T(128)S(1)}, f32[32]{0:T(128)}, u32[]{:S(2)}) copy-start(f32[32]{0:T(128)} %param.12) | copy-start | bytes 388
  91.0 13.1 %copy-start = (bf16[1024,4096]{0,1:T(8,128)(2,1)S(1)}, bf16[1024,4096]{0,1:T(8,128)(2,1)}, u32[]{:S(2)}) copy-start(bf16[1024,4096]{0,1:T(8,128)(2,1)} %copy.18) | copy-start | bytes 25165828
Sparse Core Ops, SparseCore 0:
  10.9 68.1 all-gather.1

commit v3 on v2

--- a/solution.py
+++ b/solution.py
@@ -47,11 +47,11 @@
         scaled_imag = (weight[:, None] * wide[1]).astype(jnp.bfloat16)
         right_real.append(jnp.concatenate([-scaled_real, -scaled_imag], axis=0))
         right_imag.append(jnp.concatenate([-scaled_imag, scaled_real], axis=0))
-    nf = len(right_real)
-    lefts = jnp.broadcast_to(left[None], (nf,) + left.shape)
-    dims = (((1,), (1,)), ((0,), (0,)))
-    chi_real = lax.dot_general(lefts, jnp.stack(right_real), dims, preferred_element_type=jnp.float32)
-    chi_imag = lax.dot_general(lefts, jnp.stack(right_imag), dims, preferred_element_type=jnp.float32)
+    dims = (((0,), (0,)), ((), ()))
+    chi_real = lax.dot_general(left, jnp.stack(right_real, axis=1), dims, preferred_element_type=jnp.float32)
+    chi_imag = lax.dot_general(left, jnp.stack(right_imag, axis=1), dims, preferred_element_type=jnp.float32)
+    chi_real = chi_real.transpose(1, 0, 2)
+    chi_imag = chi_imag.transpose(1, 0, 2)
     return chi_real.astype(jnp.bfloat16), chi_imag.astype(jnp.bfloat16)
 
 

time: 123 us -> 112 us (0.911)
  local copies, waits for them, and re-layouts: 17 us -> 5.04 us
  matrix products: 24 us -> 26.2 us
    broadcast_in_dim x1 -> x0, local copies, waits for them, and re-layouts: 11.9 us -> none  [on_device(): lefts = jnp.broadcast_to(left[None], (nf,) + left.shape)]
    dot_general x2, matrix products: 24 us -> 26.2 us  [the longest x1 14.9 us: on_device(): lax.dot_general(left, jnp.stack(right_imag, axis=1), dims, preferred_elem...]
  transfers between devices with their start and end apart: 3 -> 3, of which waited for: 3 -> 3; matrix products, arithmetic and copies ran while one was open for 6% -> 7% of each run, Pallas kernels for 0% -> 0%
where the time goes in v3:
time: 112 us
  waiting for transfers between devices  45.3 us (40%)
  matrix products  26.2 us (23%)
  between operations  16.6 us (15%)
  starting transfers between devices  14.8 us (13%)
  local copies, waits for them, and re-layouts  5.04 us (4%)
  other arithmetic  4.16 us (4%)
    all_to_all x1, waiting for transfers between devices, on_device(): lax.all_to_all(payload, 'col', split_axis=2, concat_axis=1, tiled=True)  27.2 us
    dot_general x1, matrix products, on_device(): lax.dot_general(left, jnp.stack(right_imag, axis=1), dims, preferred_elem...  14.9 us
    all_to_all x1, waiting for transfers between devices, on_device(): spread = lax.all_to_all(copies, 'row', 0, 0, tiled=True)  14.2 us
    dot_general x1, matrix products, on_device(): lax.dot_general(left, jnp.stack(right_real, axis=1), dims, preferred_elem...  11.3 us
    all_to_all x1, starting transfers between devices, on_device(): lax.all_to_all(payload, 'col', split_axis=2, concat_axis=1, tiled=True)  8.95 us
    all_to_all x1, starting transfers between devices, on_device(): spread = lax.all_to_all(copies, 'row', 0, 0, tiled=True)  5.86 us
    all_gather x1, waiting for transfers between devices, on_device(): lax.all_gather(both, 'col', axis=1, tiled=True).reshape(2 * pairs, local_g)  3.99 us
  transfers between devices with their start and end apart: 3, of which 3 were waited for; matrix products, arithmetic and copies ran while one was open for 7% of the time, Pallas kernels for 0%

profile of v3, /device:TPU:1, one launch (start us, length us, event | category | flops | bytes accessed | tf_op | source)
XLA Modules:
  0.0 112.1 jit_solution(10852796124410890849)
XLA Ops:
  7.2 0.0 all-gather.2.cloned.1.call-start
  7.2 0.0 copy-start.3
  7.2 1.7 %pad_maximum_fusion.1 = bf16[2,16,4096]{2,1,0:T(8,128)(2,1)} fusion(bf16[1,16,4096]{2,1,0:T(8,128)(2,1)} %bitcast.65, bf16[1,16,4096]{2,1,0:T(8,128)(2,1)} %bitcast.66), kind=kLoop, calls=%fused_computation.26 | loop fusion | flops 131072 | bytes 524288 | tf_op jit(solution)/shard_map/stack | solution.py:27
  9.0 0.0 all-gather.2.cloned.1.call-update
  9.0 2.0 %broadcast_in_dim.28 = bf16[4,2,16,4096]{3,2,1,0:T(8,128)(2,1)} broadcast(bf16[2,16,4096]{2,1,0:T(8,128)(2,1)} %pad_maximum_fusion.1), dimensions={1,2,3} | broadcast | bytes 1310720 | tf_op jit(solution)/shard_map/broadcast_in_dim | solution.py:29
  11.0 5.9 %all-to-all-start = ((bf16[4,2,16,4096]{3,2,1,0:T(8,128)(2,1)}), bf16[4,2,16,4096]{3,2,1,0:T(8,128)(2,1)S(1)}, u32[]{:S(2)}, u32[]{:S(2)}) async-start(bf16[4,2,16,4096]{3,2,1,0:T(8,128)(2,1)} %broadcast_in_dim.28), calls=%async_computation | async-start | bytes 2097152 | tf_op jit(solution)/shard_map/all_to_all | solution.py:30
  16.9 14.2 %all-to-all-done = bf16[4,2,16,4096]{3,2,1,0:T(8,128)(2,1)S(1)} async-done(((bf16[4,2,16,4096]{3,2,1,0:T(8,128)(2,1)}), bf16[4,2,16,4096]{3,2,1,0:T(8,128)(2,1)S(1)}, u32[]{:S(2)}, u32[]{:S(2)}) %all-to-all-start) | async-done | bytes 1048608 | tf_op jit(solution)/shard_map/all_to_all | solution.py:30
  31.0 0.4 copy.23
  31.4 0.1 copy.25
  31.6 0.1 broadcast_in_dim.29
  31.7 0.1 pad_maximum_fusion
  31.8 0.0 copy-start
  31.8 1.5 %copy.20 = bf16[2,16,32,640]{3,1,0,2:T(8,128)(2,1)} copy(bf16[2,16,32,640]{3,2,1,0:T(8,128)(2,1)S(1)} %pad_maximum_fusion) | data formatting | bytes 2621440 | tf_op jit(solution)/shard_map/concatenate | solution.py:35
  33.3 8.9 %all-to-all-start.1 = ((bf16[2,16,32,640]{3,1,0,2:T(8,128)(2,1)}), bf16[2,16,32,640]{3,1,0,2:T(8,128)(2,1)S(1)}, u32[]{:S(2)}, u32[]{:S(2)}) async-start(bf16[2,16,32,640]{3,1,0,2:T(8,128)(2,1)} %copy.20), calls=%async_computation.1 | async-start | bytes 2621440 | tf_op jit(solution)/shard_map/all_to_all | solution.py:36
  42.3 0.0 copy-start.1
  42.3 0.0 copy-start.2
  42.3 0.6 fusion.12
  45.3 27.2 %all-to-all-done.1 = bf16[2,16,32,640]{3,1,0,2:T(8,128)(2,1)S(1)} async-done(((bf16[2,16,32,640]{3,1,0,2:T(8,128)(2,1)}), bf16[2,16,32,640]{3,1,0,2:T(8,128)(2,1)S(1)}, u32[]{:S(2)}, u32[]{:S(2)}) %all-to-all-start.1) | async-done | bytes 1310752 | tf_op jit(solution)/shard_map/all_to_all | solution.py:36
  72.5 0.1 copy.21
  72.6 0.1 slice_convert_fusion.1
  72.7 0.2 slice_reduce_fusion
  72.9 0.1 select_reduce_fusion.1
  73.0 0.0 copy-done.2
  73.0 0.1 select_reduce_fusion
  73.1 0.3 slice_convert_fusion
  73.3 0.4 fusion.10
  73.8 0.2 maximum_bitcast_fusion.2
  74.0 1.2 %maximum_bitcast_fusion.3 = (bf16[1024,1,512]{2,0,1:T(8,128)(2,1)}, bf16[1024,1,512]{2,0,1:T(8,128)(2,1)S(1)}) fusion(bf16[512,512]{1,0:T(8,128)(2,1)S(1)} %get-tuple-element.12, bf16[512,512]{1,0:T(8,128)(2,1)S(1)} %get-tuple-element.10, bf16[512,512]{1,0:T(8,128)(2,1)S(1)} %get-tuple-element.11), kind=kLoop, calls=%fused_computation.15 | loop fusion | flops 4194304 | bytes 3670016 | tf_op jit(solution)/shard_map/stack | solution.py:52
  75.1 4.0 %all-gather.2.cloned.1.call-done = bf16[2,512,4096]{2,1,0:T(8,128)(2,1)} async-done(((bf16[2,16,4096]{2,1,0:T(8,128)(2,1)}), bf16[2,512,4096]{2,1,0:T(8,128)(2,1)}) %all-gather.2.cloned.1.call-update) | async-done | bytes 8388624 | tf_op jit(solution)/shard_map/all_gather | solution.py:28
  79.1 14.9 %convert_bitcast_fusion = bf16[2,4096,512]{2,1,0:T(8,128)(2,1)} fusion(bf16[1024,4096,1]{1,0,2:T(8,128)(2,1)} %bitcast.67, bf16[1024,1,512]{2,0,1:T(8,128)(2,1)} %get-tuple-element.15, bf16[1024,1,512]{2,0,1:T(8,128)(2,1)S(1)} %get-tuple-element.13), kind=kOutput, calls=%fused_computation | convolution fusion | flops 8598323200 | bytes 18874368 | tf_op jit(solution)/shard_map/dot_general | solution.py:52
  94.0 0.0 copy-done.5
  94.0 11.3 %convert_bitcast_fusion.1 = bf16[2,4096,512]{2,1,0:T(8,128)(2,1)} fusion(bf16[1024,4096,1]{1,0,2:T(8,128)(2,1)S(1)} %bitcast.68, bf16[1024,1,512]{2,0,1:T(8,128)(2,1)S(1)} %get-tuple-element.16, bf16[1024,1,512]{2,0,1:T(8,128)(2,1)S(1)} %get-tuple-element.14), kind=kOutput, calls=%fused_computation.1 | convolution fusion | flops 8598323200 | bytes 18874368 | tf_op jit(solution)/shard_map/dot_general | solution.py:51
  (9 shorter events, 0.0 us)
Async XLA Ops:
  7.2 72.0 %all-gather.2.cloned.1.call-start = ((), (), s32[]{:S(2)}) async-start(), calls=%async_computation.2 | async-start | bytes 8650752 | tf_op jit(solution)/shard_map/all_gather | solution.py:28
  7.2 9.7 %copy-start.3 = (s32[16]{0:T(128)S(1)}, s32[16]{0:T(128)}, u32[]{:S(2)}) copy-start(s32[16]{0:T(128)} %param.10) | copy-start | bytes 196
  7.2 9.6 %copy-start.4 = (s32[16]{0:T(128)S(1)}, s32[16]{0:T(128)}, u32[]{:S(2)}) copy-start(s32[16]{0:T(128)} %param.9) | copy-start | bytes 196
  11.0 20.0 %all-to-all-start = ((bf16[4,2,16,4096]{3,2,1,0:T(8,128)(2,1)}), bf16[4,2,16,4096]{3,2,1,0:T(8,128)(2,1)S(1)}, u32[]{:S(2)}, u32[]{:S(2)}) async-start(bf16[4,2,16,4096]{3,2,1,0:T(8,128)(2,1)} %broadcast_in_dim.28), calls=%async_computation | async-start | bytes 2097152 | tf_op jit(solution)/shard_map/all_to_all | solution.py:30
  31.8 10.4 %copy-start = (f32[2]{0:T(128)S(1)}, f32[2]{0:T(128)}, u32[]{:S(2)}) copy-start(f32[2]{0:T(128)} %param.13) | copy-start | bytes 28
  33.3 39.2 %all-to-all-start.1 = ((bf16[2,16,32,640]{3,1,0,2:T(8,128)(2,1)}), bf16[2,16,32,640]{3,1,0,2:T(8,128)(2,1)S(1)}, u32[]{:S(2)}, u32[]{:S(2)}) async-start(bf16[2,16,32,640]{3,1,0,2:T(8,128)(2,1)} %copy.20), calls=%async_computation.1 | async-start | bytes 2621440 | tf_op jit(solution)/shard_map/all_to_all | solution.py:36
  42.3 30.6 %copy-start.1 = (f32[16]{0:T(128)S(1)}, f32[16]{0:T(128)}, u32[]{:S(2)}) copy-start(f32[16]{0:T(128)} %param.11) | copy-start | bytes 196
  42.3 30.7 %copy-start.2 = (f32[32]{0:T(128)S(1)}, f32[32]{0:T(128)}, u32[]{:S(2)}) copy-start(f32[32]{0:T(128)} %param.12) | copy-start | bytes 388
  79.1 14.9 %copy-start.5 = (bf16[2,512,4096]{2,1,0:T(8,128)(2,1)S(1)}, bf16[2,512,4096]{2,1,0:T(8,128)(2,1)}, u32[]{:S(2)}) copy-start(bf16[2,512,4096]{2,1,0:T(8,128)(2,1)} %all-gather.2.cloned.1.call-done) | copy-start | bytes 25165828
Sparse Core Ops, SparseCore 0:
  10.4 68.7 all-gather.1

commit v4 on v3

v4 whole, which is shorter than its diff:
```python
import jax
import jax.numpy as jnp
from jax import lax
from jax.sharding import Mesh, PartitionSpec as P

CORE_PAIRS = [(0, 1), (1, 0)]


def lookup(indices, table):
    count = table.shape[0]
    picks = indices[:, None] == lax.broadcasted_iota(jnp.int32, (1, count), 1)
    return jnp.sum(jnp.where(picks, table[None, :], 0.0), axis=1)


def shift(value, axis, step):
    size = lax.psum(1, axis)
    return lax.ppermute(value, axis, [(i, (i + step) % size) for i in range(size)])


def ring_gather(block, axis):
    half = block.shape[-1] // 2
    from_minus = shift(block, axis, 1)
    from_plus = shift(block, axis, -1)
    far_first = shift(from_minus[..., :half], axis, 1)
    far_second = shift(from_plus[..., half:], axis, -1)
    far = jnp.concatenate([far_first, far_second], axis=-1)
    return jnp.stack([block, from_plus, far, from_minus])


def on_device(
    matrix_real,
    matrix_imag,
    valence_index,
    conduction_index,
    valence_energy,
    conduction_energy,
    frequency,
):
    cols = ("x", "y", "core")
    nrow = lax.psum(1, "row")
    nx, ny, ncore = lax.psum(1, "x"), lax.psum(1, "y"), lax.psum(1, "core")
    ncol = nx * ny * ncore
    local_pairs, local_g = matrix_real.shape
    pairs = local_pairs * ncol
    width = local_g * nrow // ncol
    both = jnp.stack([matrix_real, matrix_imag])

    row_real = ring_gather(matrix_real, "x")
    col_imag = ring_gather(matrix_imag, "y")
    all_real = ring_gather(row_real, "y")
    all_imag = ring_gather(col_imag, "x")
    mine = jnp.stack([all_real, all_imag.transpose(1, 0, 2, 3)])
    other = lax.ppermute(mine, "core", CORE_PAIRS)
    left = jnp.stack([mine, other], axis=3)
    left = left.transpose(0, 2, 1, 3, 4, 5).reshape(2 * pairs, local_g)

    copies = jnp.broadcast_to(both[None], (nrow,) + both.shape)
    spread = lax.all_to_all(copies, "row", 0, 0, tiled=True)
    spread = spread.reshape(nrow, 2, local_pairs, local_g // width, width)
    payload = spread.transpose(1, 2, 0, 3, 4).reshape(2, local_pairs, ncol, width)
    bands = jnp.stack([valence_index, conduction_index]).astype(jnp.bfloat16)
    tags = jnp.broadcast_to(bands[:, :, None, None], (2, local_pairs, ncol, 128))
    payload = jnp.concatenate([payload, tags], axis=3)
    column = lax.all_to_all(payload, cols, split_axis=2, concat_axis=1, tiled=True)
    column = column.reshape(2, pairs, width + 128)
    all_bands = column[:, :, width].astype(jnp.int32)
    gap = lookup(all_bands[1], conduction_energy) - lookup(all_bands[0], valence_energy)
    wide = column[:, :, :width].astype(jnp.float32)
    here = (lax.axis_index("x"), lax.axis_index("y"), lax.axis_index("core"))

    def relative(scaled):
        grid = scaled.reshape(nx, ny, ncore, local_pairs, width)
        for axis, start in enumerate(here):
            size = grid.shape[axis]
            doubled = jnp.concatenate([grid, grid], axis=axis)
            grid = lax.dynamic_slice_in_dim(doubled, start, size, axis=axis)
        return grid.reshape(pairs, width)

    right_real = []
    right_imag = []
    for index in range(frequency.shape[0]):
        omega = frequency[index]
        weight = 4.0 * gap / (gap * gap + omega * omega)
        scaled_real = relative((weight[:, None] * wide[0]).astype(jnp.bfloat16))
        scaled_imag = relative((weight[:, None] * wide[1]).astype(jnp.bfloat16))
        right_real.append(jnp.concatenate([-scaled_real, -scaled_imag], axis=0))
        right_imag.append(jnp.concatenate([-scaled_imag, scaled_real], axis=0))
    dims = (((0,), (0,)), ((), ()))
    chi_real = lax.dot_general(left, jnp.stack(right_real, axis=1), dims, preferred_element_type=jnp.float32)
    chi_imag = lax.dot_general(left, jnp.stack(right_imag, axis=1), dims, preferred_element_type=jnp.float32)
    chi_real = chi_real.transpose(1, 0, 2)
    chi_imag = chi_imag.transpose(1, 0, 2)
    return chi_real.astype(jnp.bfloat16), chi_imag.astype(jnp.bfloat16)


def solution(mesh):
    rows, cols = mesh.devices.shape
    grid = Mesh(mesh.devices.reshape(rows, 4, cols // 8, 2), ("row", "x", "y", "core"))
    cols = ("x", "y", "core")
    placed = (P(cols, "row"), P(cols, "row"), P(cols), P(cols), P(), P(), P())
    return jax.shard_map(
        on_device,
        mesh=grid,
        in_specs=placed,
        out_specs=(P(None, "row", cols), P(None, "row", cols)),
        check_vma=False,
    )
```

time: 112 us -> 112 us (level)
  waiting for transfers between devices: 45.3 us -> 18.6 us
  starting transfers between devices: 14.8 us -> 34.1 us
  other arithmetic: 4.16 us -> 21 us
  between operations: 16.6 us -> 3.34 us
  local copies, waits for them, and re-layouts: 5.04 us -> 8.22 us
    ppermute x0 -> x17, starting transfers between devices: none -> 19.2 us  [the longest x16 18.9 us: shift(): lax.ppermute(value, axis, [(i, (i + step) % size) for i in range(size)])]
    all_to_all x1, waiting for transfers between devices: 27.2 us -> 9.21 us  [on_device(): lax.all_to_all(payload, cols, split_axis=2, concat_axis=1, tiled=True)]
    another operation x0 -> x9, other arithmetic: none -> 14.8 us  [the longest x2 10.2 us: on_device(): left = jnp.stack([mine, other], axis=3)]
    all_to_all x1, waiting for transfers between devices: 14.2 us -> 0.01 us  [on_device(): spread = lax.all_to_all(copies, 'row', 0, 0, tiled=True)]
    ppermute x0 -> x17, waiting for transfers between devices: none -> 9.37 us  [the longest x16 9.37 us: shift(): lax.ppermute(value, axis, [(i, (i + step) % size) for i in range(size)])]
    all_gather x1 -> x0, waiting for transfers between devices: 3.99 us -> none  [on_device(): lax.all_gather(both, 'col', axis=1, tiled=True).reshape(2 * pairs, local_g)]
    slice x0 -> x9, local copies, waits for them, and re-layouts: none -> 2.5 us  [the longest x4 1.52 us: ring_gather(): far_first = shift(from_minus[..., :half], axis, 1)]
    concatenate x0 -> x8, other arithmetic: none -> 1.65 us  [relative(): doubled = jnp.concatenate([grid, grid], axis=axis)]
  transfers between devices with their start and end apart: 3 -> 19, of which waited for: 3 -> 3; matrix products, arithmetic and copies ran while one was open for 7% -> 19% of each run, Pallas kernels for 0% -> 0%
where the time goes in v4:
time: 112 us; the launch traced here: 111 us
  starting transfers between devices  34.1 us (30%)
  matrix products  26.2 us (23%)
  other arithmetic  21 us (19%)
  waiting for transfers between devices  18.6 us (17%)
  local copies, waits for them, and re-layouts  8.22 us (7%)
  between operations  3.34 us (3%)
    ppermute x16, starting transfers between devices, shift(): lax.ppermute(value, axis, [(i, (i + step) % size) for i in range(size)])  18.9 us
    dot_general x1, matrix products, on_device(): lax.dot_general(left, jnp.stack(right_imag, axis=1), dims, preferred_elem...  14.9 us
    dot_general x1, matrix products, on_device(): lax.dot_general(left, jnp.stack(right_real, axis=1), dims, preferred_elem...  11.3 us
    another operation x2, other arithmetic, on_device(): left = jnp.stack([mine, other], axis=3)  10.2 us
    all_to_all x1, starting transfers between devices, on_device(): lax.all_to_all(payload, cols, split_axis=2, concat_axis=1, tiled=True)  9.82 us
    ppermute x16, waiting for transfers between devices, shift(): lax.ppermute(value, axis, [(i, (i + step) % size) for i in range(size)])  9.37 us
    all_to_all x1, waiting for transfers between devices, on_device(): lax.all_to_all(payload, cols, split_axis=2, concat_axis=1, tiled=True)  9.21 us
    all_to_all x1, starting transfers between devices, on_device(): spread = lax.all_to_all(copies, 'row', 0, 0, tiled=True)  5.06 us
  transfers between devices with their start and end apart: 19, of which 3 were waited for; matrix products, arithmetic and copies ran while one was open for 19% of the time, Pallas kernels for 0%

profile of v4, /device:TPU:1, one launch (start us, length us, event | category | flops | bytes accessed | tf_op | source)
XLA Modules:
  0.0 111.4 jit_solution(6573407689960076563)
XLA Ops:
  0.6 2.2 %collective-permute-start.9 = (bf16[16,4096]{1,0:T(8,128)(2,1)}, bf16[16,4096]{1,0:T(8,128)(2,1)S(1)}, u32[]{:S(2)}, u32[]{:S(2)}) collective-permute-start(bf16[16,4096]{1,0:T(8,128)(2,1)} %param.8), channel_id=1, source_target_pairs={{0,2},{2,4},{4,6},{6,0},{1,3},{3,5},{5,7},{7,1},{8,10},{10,12},{12... | collective-permute-start | bytes 393224 | tf_op jit(solution)/shard_map/ppermute | solution.py:17
  2.8 1.5 %collective-permute-start.8 = (bf16[16,4096]{1,0:T(8,128)(2,1)}, bf16[16,4096]{1,0:T(8,128)(2,1)S(1)}, u32[]{:S(2)}, u32[]{:S(2)}) collective-permute-start(bf16[16,4096]{1,0:T(8,128)(2,1)} %param.8), channel_id=1, source_target_pairs={{0,6},{2,0},{4,2},{6,4},{1,7},{3,1},{5,3},{7,5},{8,14},{10,8},{12,... | collective-permute-start | bytes 393224 | tf_op jit(solution)/shard_map/ppermute | solution.py:17
  4.3 1.2 %collective-permute-start.1 = (bf16[16,4096]{1,0:T(8,128)(2,1)}, bf16[16,4096]{1,0:T(8,128)(2,1)S(1)}, u32[]{:S(2)}, u32[]{:S(2)}) collective-permute-start(bf16[16,4096]{1,0:T(8,128)(2,1)} %param.7), channel_id=1, source_target_pairs={{0,8},{8,16},{16,24},{24,0},{1,9},{9,17},{17,25},{25,1},{2,10},{10... | collective-permute-start | bytes 393224 | tf_op jit(solution)/shard_map/ppermute | solution.py:17
  5.6 1.5 %collective-permute-start = (bf16[16,4096]{1,0:T(8,128)(2,1)}, bf16[16,4096]{1,0:T(8,128)(2,1)S(1)}, u32[]{:S(2)}, u32[]{:S(2)}) collective-permute-start(bf16[16,4096]{1,0:T(8,128)(2,1)} %param.7), channel_id=1, source_target_pairs={{0,24},{8,0},{16,8},{24,16},{1,25},{9,1},{17,9},{25,17},{2,26},{10... | collective-permute-start | bytes 393224 | tf_op jit(solution)/shard_map/ppermute | solution.py:17
  7.6 2.7 %collective-permute-start.11 = (bf16[16,2048]{1,0:T(8,128)(2,1)S(1)}, bf16[16,2048]{1,0:T(8,128)(2,1)S(1)}, u32[]{:S(2)}, u32[]{:S(2)}) collective-permute-start(bf16[16,2048]{1,0:T(8,128)(2,1)S(1)} %slice.73), channel_id=1, source_target_pairs={{0,6},{2,0},{4,2},{6,4},{1,7},{3,1},{5,3},{7,5},{8,14},{10,8},{12,... | collective-permute-start | bytes 196616 | tf_op jit(solution)/shard_map/ppermute | solution.py:17
  10.3 1.0 pad_maximum_fusion.5
  11.3 1.1 broadcast_in_dim.28
  12.4 5.1 %all-to-all-start = ((bf16[4,2,16,4096]{3,2,1,0:T(8,128)(2,1)}), bf16[4,2,16,4096]{3,2,1,0:T(8,128)(2,1)S(1)}, u32[]{:S(2)}, u32[]{:S(2)}) async-start(bf16[4,2,16,4096]{3,2,1,0:T(8,128)(2,1)} %broadcast_in_dim.28), calls=%async_computation | async-start | bytes 2097152 | tf_op jit(solution)/shard_map/all_to_all | solution.py:58
  17.5 1.3 %collective-permute-start.2 = (bf16[16,2048]{1,0:T(8,128)(2,1)S(1)}, bf16[16,2048]{1,0:T(8,128)(2,1)S(1)}, u32[]{:S(2)}, u32[]{:S(2)}) collective-permute-start(bf16[16,2048]{1,0:T(8,128)(2,1)S(1)} %slice.68), channel_id=1, source_target_pairs={{0,8},{8,16},{16,24},{24,0},{1,9},{9,17},{17,25},{25,1},{2,10},{10... | collective-permute-start | bytes 196616 | tf_op jit(solution)/shard_map/ppermute | solution.py:17
  18.8 1.5 %collective-permute-start.3 = (bf16[16,2048]{1,0:T(8,128)(2,1)S(1)}, bf16[16,2048]{1,0:T(8,128)(2,1)S(1)}, u32[]{:S(2)}, u32[]{:S(2)}) collective-permute-start(bf16[16,2048]{1,0:T(8,128)(2,1)S(1)} %slice.69), channel_id=1, source_target_pairs={{0,24},{8,0},{16,8},{24,16},{1,25},{9,1},{17,9},{25,17},{2,26},{10... | collective-permute-start | bytes 196616 | tf_op jit(solution)/shard_map/ppermute | solution.py:17
  20.3 0.9 fusion.22
  21.2 1.3 %collective-permute-start.12 = (bf16[4,16,4096]{2,1,0:T(8,128)(2,1)S(1)}, bf16[4,16,4096]{2,1,0:T(8,128)(2,1)S(1)}, u32[]{:S(2)}, u32[]{:S(2)}) collective-permute-start(bf16[4,16,4096]{2,1,0:T(8,128)(2,1)S(1)} %get-tuple-element.19), channel_id=1, source_target_pairs={{0,24},{8,0},{16,8},{24,16},{1,25},{9,1},{17,9},{25,17},{2,26},{10... | collective-permute-start | bytes 1572872 | tf_op jit(solution)/shard_map/ppermute | solution.py:17
  23.1 1.3 %collective-permute-start.5 = (bf16[4,16,4096]{2,1,0:T(8,128)(2,1)S(1)}, bf16[4,16,4096]{2,1,0:T(8,128)(2,1)S(1)}, u32[]{:S(2)}, u32[]{:S(2)}) collective-permute-start(bf16[4,16,4096]{2,1,0:T(8,128)(2,1)S(1)} %get-tuple-element.17), channel_id=1, source_target_pairs={{0,2},{2,4},{4,6},{6,0},{1,3},{3,5},{5,7},{7,1},{8,10},{10,12},{12... | collective-permute-start | bytes 1572872 | tf_op jit(solution)/shard_map/ppermute | solution.py:17
  24.4 8.8 %collective-permute-done.12 = bf16[4,16,4096]{2,1,0:T(8,128)(2,1)S(1)} collective-permute-done((bf16[4,16,4096]{2,1,0:T(8,128)(2,1)S(1)}, bf16[4,16,4096]{2,1,0:T(8,128)(2,1)S(1)}, u32[]{:S(2)}, u32[]{:S(2)}) %collective-permute-start.12) | collective-permute-done | bytes 524320 | tf_op jit(solution)/shard_map/ppermute | solution.py:17
  33.2 2.5 %collective-permute-start.15 = (bf16[4,16,2048]{2,1,0:T(8,128)(2,1)S(1)}, bf16[4,16,2048]{2,1,0:T(8,128)(2,1)}, u32[]{:S(2)}, u32[]{:S(2)}) collective-permute-start(bf16[4,16,2048]{2,1,0:T(8,128)(2,1)S(1)} %slice.75), channel_id=1, source_target_pairs={{0,24},{8,0},{16,8},{24,16},{1,25},{9,1},{17,9},{25,17},{2,26},{10... | collective-permute-start | bytes 786440 | tf_op jit(solution)/shard_map/ppermute | solution.py:17
  35.7 0.7 slice.74
  36.5 0.8 slice.71
  37.4 0.8 slice.70
  38.2 1.4 %collective-permute-start.6 = (bf16[4,16,2048]{2,1,0:T(8,128)(2,1)}, bf16[4,16,2048]{2,1,0:T(8,128)(2,1)}, u32[]{:S(2)}, u32[]{:S(2)}) collective-permute-start(bf16[4,16,2048]{2,1,0:T(8,128)(2,1)} %slice.70), channel_id=1, source_target_pairs={{0,2},{2,4},{4,6},{6,0},{1,3},{3,5},{5,7},{7,1},{8,10},{10,12},{12... | collective-permute-start | bytes 786440 | tf_op jit(solution)/shard_map/ppermute | solution.py:17
  40.4 1.5 %copy.37 = bf16[2,16,32,640]{3,1,0,2:T(8,128)(2,1)} copy(bf16[2,16,32,640]{3,2,1,0:T(8,128)(2,1)S(1)} %pad_maximum_fusion.2) | data formatting | bytes 2621440 | tf_op jit(solution)/shard_map/concatenate | solution.py:63
  41.9 9.8 %all-to-all-start.1 = ((bf16[2,16,32,640]{3,1,0,2:T(8,128)(2,1)}), bf16[2,16,32,640]{3,1,0,2:T(8,128)(2,1)S(1)}, u32[]{:S(2)}, u32[]{:S(2)}) async-start(bf16[2,16,32,640]{3,1,0,2:T(8,128)(2,1)} %copy.37), calls=%async_computation.1 | async-start | bytes 2621440 | tf_op jit(solution)/shard_map/all_to_all | solution.py:64
  51.7 1.1 maximum_bitcast_fusion.7
  52.8 1.4 %maximum_bitcast_fusion.1 = bf16[1,4,4,16,4096]{4,3,1,2,0:T(8,128)(2,1)S(1)} fusion(bf16[1,4,16,4096]{3,2,1,0:T(8,128)(2,1)} %bitcast.100, bf16[1,4,16,4096]{3,2,1,0:T(8,128)(2,1)S(1)} %maximum_bitcast_fusion.7, bf16[1,4,16,4096]{3,2,1,0:T(8,128)(2,1)S(1)} %bitcast.99, bf16[1,4,16,4096]{3,2,1,0:T(8,128)(2,1)S(1)} %copy-done.2), kind=kLoop, calls=%fused_computation.5 | loop fusion | flops 3145728 | bytes 4194304 | tf_op jit(solution)/shard_map/stack | solution.py:52
  54.3 1.1 maximum_bitcast_fusion.6
  55.4 3.9 %fusion.24 = (bf16[2,4,4,1,16,4096]{5,4,3,1,2,0:T(8,128)(2,1)}, bf16[2,4,4,16,4096]{4,3,1,2,0:T(8,128)(2,1)}) fusion(bf16[1,4,4,16,4096]{4,3,1,2,0:T(8,128)(2,1)S(1)} %maximum_bitcast_fusion.1, bf16[1,4,16,4096]{3,2,1,0:T(8,128)(2,1)S(1)} %bitcast.98, bf16[1,4,16,4096]{3,2,1,0:T(8,128)(2,1)S(1)} %maximum_bitcast_fusion.6, ...), kind=kLoop, calls=%fused_computation.86 | loop fusion | flops 11534336 | bytes 12582912 | tf_op jit(solution)/shard_map/stack | solution.py:54
  59.5 0.6 fusion.26
  62.3 9.2 %all-to-all-done.1 = bf16[2,16,32,640]{3,1,0,2:T(8,128)(2,1)S(1)} async-done(((bf16[2,16,32,640]{3,1,0,2:T(8,128)(2,1)}), bf16[2,16,32,640]{3,1,0,2:T(8,128)(2,1)S(1)}, u32[]{:S(2)}, u32[]{:S(2)}) %all-to-all-start.1) | async-done | bytes 1310752 | tf_op jit(solution)/shard_map/all_to_all | solution.py:64
  76.0 1.5 %maximum_bitcast_fusion.5 = (bf16[1024,1,512]{2,0,1:T(8,128)(2,1)}, bf16[1024,1,512]{2,0,1:T(8,128)(2,1)}) fusion(bf16[512,512]{1,0:T(8,128)(2,1)S(1)} %bitcast.88, bf16[512,512]{1,0:T(8,128)(2,1)S(1)} %bitcast.95, bf16[512,512]{1,0:T(8,128)(2,1)S(1)} %bitcast_negate_fusion), kind=kLoop, calls=%fused_computation.41 | loop fusion | flops 4194304 | bytes 3670016 | tf_op jit(solution)/shard_map/stack | solution.py:90
  77.5 1.3 %copy-done = bf16[2,4,4,1,16,4096]{5,4,3,1,2,0:T(8,128)(2,1)S(1)} copy-done((bf16[2,4,4,1,16,4096]{5,4,3,1,2,0:T(8,128)(2,1)S(1)}, bf16[2,4,4,1,16,4096]{5,4,3,1,2,0:T(8,128)(2,1)}, u32[]{:S(2)}) %copy-start) | copy-done | bytes 4194328
  78.8 6.4 %pad_maximum_fusion = bf16[2,4,4,2,16,4096]{5,4,3,1,2,0:T(8,128)(2,1)} fusion(bf16[2,4,4,1,16,4096]{5,4,3,1,2,0:T(8,128)(2,1)} %bitcast.21, bf16[2,4,4,1,16,4096]{5,4,3,1,2,0:T(8,128)(2,1)S(1)} %copy-done), kind=kLoop, calls=%fused_computation | loop fusion | flops 4194304 | bytes 16777216 | tf_op jit(solution)/shard_map/stack | solution.py:54
  85.2 14.9 %convert_bitcast_fusion = bf16[2,4096,512]{2,1,0:T(8,128)(2,1)} fusion(bf16[1024,4096,1]{1,0,2:T(8,128)(2,1)} %bitcast.84, bf16[1024,1,512]{2,0,1:T(8,128)(2,1)} %get-tuple-element.14, bf16[1024,1,512]{2,0,1:T(8,128)(2,1)S(1)} %get-tuple-element.12), kind=kOutput, calls=%fused_computation.1 | convolution fusion | flops 8598323200 | bytes 18874368 | tf_op jit(solution)/shard_map/dot_general | solution.py:90
  100.1 11.3 %convert_bitcast_fusion.1 = bf16[2,4096,512]{2,1,0:T(8,128)(2,1)} fusion(bf16[1024,4096,1]{1,0,2:T(8,128)(2,1)S(1)} %bitcast.85, bf16[1024,1,512]{2,0,1:T(8,128)(2,1)S(1)} %copy-done.8, bf16[1024,1,512]{2,0,1:T(8,128)(2,1)S(1)} %get-tuple-element.13), kind=kOutput, calls=%fused_computation.2 | convolution fusion | flops 8598323200 | bytes 18874368 | tf_op jit(solution)/shard_map/dot_general | solution.py:89
  (93 shorter events, 6.6 us)
Async XLA Ops:
  0.6 6.9 %collective-permute-start.9 = (bf16[16,4096]{1,0:T(8,128)(2,1)}, bf16[16,4096]{1,0:T(8,128)(2,1)S(1)}, u32[]{:S(2)}, u32[]{:S(2)}) collective-permute-start(bf16[16,4096]{1,0:T(8,128)(2,1)} %param.8), channel_id=1, source_target_pairs={{0,2},{2,4},{4,6},{6,0},{1,3},{3,5},{5,7},{7,1},{8,10},{10,12},{12... | collective-permute-start | bytes 393224 | tf_op jit(solution)/shard_map/ppermute | solution.py:17
  2.8 4.7 %collective-permute-start.8 = (bf16[16,4096]{1,0:T(8,128)(2,1)}, bf16[16,4096]{1,0:T(8,128)(2,1)S(1)}, u32[]{:S(2)}, u32[]{:S(2)}) collective-permute-start(bf16[16,4096]{1,0:T(8,128)(2,1)} %param.8), channel_id=1, source_target_pairs={{0,6},{2,0},{4,2},{6,4},{1,7},{3,1},{5,3},{7,5},{8,14},{10,8},{12,... | collective-permute-start | bytes 393224 | tf_op jit(solution)/shard_map/ppermute | solution.py:17
  4.3 13.1 %collective-permute-start.1 = (bf16[16,4096]{1,0:T(8,128)(2,1)}, bf16[16,4096]{1,0:T(8,128)(2,1)S(1)}, u32[]{:S(2)}, u32[]{:S(2)}) collective-permute-start(bf16[16,4096]{1,0:T(8,128)(2,1)} %param.7), channel_id=1, source_target_pairs={{0,8},{8,16},{16,24},{24,0},{1,9},{9,17},{17,25},{25,1},{2,10},{10... | collective-permute-start | bytes 393224 | tf_op jit(solution)/shard_map/ppermute | solution.py:17
  5.6 13.2 %collective-permute-start = (bf16[16,4096]{1,0:T(8,128)(2,1)}, bf16[16,4096]{1,0:T(8,128)(2,1)S(1)}, u32[]{:S(2)}, u32[]{:S(2)}) collective-permute-start(bf16[16,4096]{1,0:T(8,128)(2,1)} %param.7), channel_id=1, source_target_pairs={{0,24},{8,0},{16,8},{24,16},{1,25},{9,1},{17,9},{25,17},{2,26},{10... | collective-permute-start | bytes 393224 | tf_op jit(solution)/shard_map/ppermute | solution.py:17
  7.6 12.7 %collective-permute-start.10 = (bf16[16,2048]{1,0:T(8,128)(2,1)S(1)}, bf16[16,2048]{1,0:T(8,128)(2,1)S(1)}, u32[]{:S(2)}, u32[]{:S(2)}) collective-permute-start(bf16[16,2048]{1,0:T(8,128)(2,1)S(1)} %slice.72), channel_id=1, source_target_pairs={{0,2},{2,4},{4,6},{6,0},{1,3},{3,5},{5,7},{7,1},{8,10},{10,12},{12... | collective-permute-start | bytes 196616 | tf_op jit(solution)/shard_map/ppermute | solution.py:17
  7.6 12.7 %collective-permute-start.11 = (bf16[16,2048]{1,0:T(8,128)(2,1)S(1)}, bf16[16,2048]{1,0:T(8,128)(2,1)S(1)}, u32[]{:S(2)}, u32[]{:S(2)}) collective-permute-start(bf16[16,2048]{1,0:T(8,128)(2,1)S(1)} %slice.73), channel_id=1, source_target_pairs={{0,6},{2,0},{4,2},{6,4},{1,7},{3,1},{5,3},{7,5},{8,14},{10,8},{12,... | collective-permute-start | bytes 196616 | tf_op jit(solution)/shard_map/ppermute | solution.py:17
  11.3 9.0 %copy-start.9 = (bf16[16,4096]{1,0:T(8,128)(2,1)S(1)}, bf16[16,4096]{1,0:T(8,128)(2,1)}, u32[]{:S(2)}) copy-start(bf16[16,4096]{1,0:T(8,128)(2,1)} %param.8) | copy-start | bytes 393220
  12.4 10.3 %copy-start.10 = (bf16[16,4096]{1,0:T(8,128)(2,1)S(1)}, bf16[16,4096]{1,0:T(8,128)(2,1)}, u32[]{:S(2)}) copy-start(bf16[16,4096]{1,0:T(8,128)(2,1)} %param.7) | copy-start | bytes 393220
  12.4 27.2 %all-to-all-start = ((bf16[4,2,16,4096]{3,2,1,0:T(8,128)(2,1)}), bf16[4,2,16,4096]{3,2,1,0:T(8,128)(2,1)S(1)}, u32[]{:S(2)}, u32[]{:S(2)}) async-start(bf16[4,2,16,4096]{3,2,1,0:T(8,128)(2,1)} %broadcast_in_dim.28), calls=%async_computation | async-start | bytes 2097152 | tf_op jit(solution)/shard_map/all_to_all | solution.py:58
  17.5 6.9 %copy-start.14 = (s32[16]{0:T(128)S(1)}, s32[16]{0:T(128)}, u32[]{:S(2)}) copy-start(s32[16]{0:T(128)} %param.9) | copy-start | bytes 196
  17.5 5.2 %collective-permute-start.2 = (bf16[16,2048]{1,0:T(8,128)(2,1)S(1)}, bf16[16,2048]{1,0:T(8,128)(2,1)S(1)}, u32[]{:S(2)}, u32[]{:S(2)}) collective-permute-start(bf16[16,2048]{1,0:T(8,128)(2,1)S(1)} %slice.68), channel_id=1, source_target_pairs={{0,8},{8,16},{16,24},{24,0},{1,9},{9,17},{17,25},{25,1},{2,10},{10... | collective-permute-start | bytes 196616 | tf_op jit(solution)/shard_map/ppermute | solution.py:17
  18.8 3.9 %collective-permute-start.3 = (bf16[16,2048]{1,0:T(8,128)(2,1)S(1)}, bf16[16,2048]{1,0:T(8,128)(2,1)S(1)}, u32[]{:S(2)}, u32[]{:S(2)}) collective-permute-start(bf16[16,2048]{1,0:T(8,128)(2,1)S(1)} %slice.69), channel_id=1, source_target_pairs={{0,24},{8,0},{16,8},{24,16},{1,25},{9,1},{17,9},{25,17},{2,26},{10... | collective-permute-start | bytes 196616 | tf_op jit(solution)/shard_map/ppermute | solution.py:17
  20.3 16.2 %copy-start.15 = (s32[16]{0:T(128)S(1)}, s32[16]{0:T(128)}, u32[]{:S(2)}) copy-start(s32[16]{0:T(128)} %param.10) | copy-start | bytes 196
  21.2 11.9 %collective-permute-start.12 = (bf16[4,16,4096]{2,1,0:T(8,128)(2,1)S(1)}, bf16[4,16,4096]{2,1,0:T(8,128)(2,1)S(1)}, u32[]{:S(2)}, u32[]{:S(2)}) collective-permute-start(bf16[4,16,4096]{2,1,0:T(8,128)(2,1)S(1)} %get-tuple-element.19), channel_id=1, source_target_pairs={{0,24},{8,0},{16,8},{24,16},{1,25},{9,1},{17,9},{25,17},{2,26},{10... | collective-permute-start | bytes 1572872 | tf_op jit(solution)/shard_map/ppermute | solution.py:17
  22.5 13.3 %collective-permute-start.13 = (bf16[4,16,4096]{2,1,0:T(8,128)(2,1)S(1)}, bf16[4,16,4096]{2,1,0:T(8,128)(2,1)S(1)}, u32[]{:S(2)}, u32[]{:S(2)}) collective-permute-start(bf16[4,16,4096]{2,1,0:T(8,128)(2,1)S(1)} %get-tuple-element.19), channel_id=1, source_target_pairs={{0,8},{8,16},{16,24},{24,0},{1,9},{9,17},{17,25},{25,1},{2,10},{10... | collective-permute-start | bytes 1572872 | tf_op jit(solution)/shard_map/ppermute | solution.py:17
  22.8 13.7 %collective-permute-start.4 = (bf16[4,16,4096]{2,1,0:T(8,128)(2,1)S(1)}, bf16[4,16,4096]{2,1,0:T(8,128)(2,1)S(1)}, u32[]{:S(2)}, u32[]{:S(2)}) collective-permute-start(bf16[4,16,4096]{2,1,0:T(8,128)(2,1)S(1)} %get-tuple-element.17), channel_id=1, source_target_pairs={{0,6},{2,0},{4,2},{6,4},{1,7},{3,1},{5,3},{7,5},{8,14},{10,8},{12,... | collective-permute-start | bytes 1572872 | tf_op jit(solution)/shard_map/ppermute | solution.py:17
  23.1 14.4 %collective-permute-start.5 = (bf16[4,16,4096]{2,1,0:T(8,128)(2,1)S(1)}, bf16[4,16,4096]{2,1,0:T(8,128)(2,1)S(1)}, u32[]{:S(2)}, u32[]{:S(2)}) collective-permute-start(bf16[4,16,4096]{2,1,0:T(8,128)(2,1)S(1)} %get-tuple-element.17), channel_id=1, source_target_pairs={{0,2},{2,4},{4,6},{6,0},{1,3},{3,5},{5,7},{7,1},{8,10},{10,12},{12... | collective-permute-start | bytes 1572872 | tf_op jit(solution)/shard_map/ppermute | solution.py:17
  33.2 18.5 %collective-permute-start.15 = (bf16[4,16,2048]{2,1,0:T(8,128)(2,1)S(1)}, bf16[4,16,2048]{2,1,0:T(8,128)(2,1)}, u32[]{:S(2)}, u32[]{:S(2)}) collective-permute-start(bf16[4,16,2048]{2,1,0:T(8,128)(2,1)S(1)} %slice.75), channel_id=1, source_target_pairs={{0,24},{8,0},{16,8},{24,16},{1,25},{9,1},{17,9},{25,17},{2,26},{10... | collective-permute-start | bytes 786440 | tf_op jit(solution)/shard_map/ppermute | solution.py:17
  36.5 15.2 %collective-permute-start.14 = (bf16[4,16,2048]{2,1,0:T(8,128)(2,1)}, bf16[4,16,2048]{2,1,0:T(8,128)(2,1)}, u32[]{:S(2)}, u32[]{:S(2)}) collective-permute-start(bf16[4,16,2048]{2,1,0:T(8,128)(2,1)} %slice.74), channel_id=1, source_target_pairs={{0,8},{8,16},{16,24},{24,0},{1,9},{9,17},{17,25},{25,1},{2,10},{10... | collective-permute-start | bytes 786440 | tf_op jit(solution)/shard_map/ppermute | solution.py:17
  36.5 3.6 %copy-start.3 = (bf16[4,16,4096]{2,1,0:T(8,128)(2,1)}, bf16[4,16,4096]{2,1,0:T(8,128)(2,1)S(1)}, u32[]{:S(2)}) copy-start(bf16[4,16,4096]{2,1,0:T(8,128)(2,1)S(1)} %collective-permute-done.4) | copy-start | bytes 1572868
  37.3 16.9 %collective-permute-start.7 = (bf16[4,16,2048]{2,1,0:T(8,128)(2,1)}, bf16[4,16,2048]{2,1,0:T(8,128)(2,1)}, u32[]{:S(2)}, u32[]{:S(2)}) collective-permute-start(bf16[4,16,2048]{2,1,0:T(8,128)(2,1)} %slice.71), channel_id=1, source_target_pairs={{0,6},{2,0},{4,2},{6,4},{1,7},{3,1},{5,3},{7,5},{8,14},{10,8},{12,... | collective-permute-start | bytes 786440 | tf_op jit(solution)/shard_map/ppermute | solution.py:17
  37.4 2.7 %copy-start.5 = (bf16[4,16,4096]{2,1,0:T(8,128)(2,1)}, bf16[4,16,4096]{2,1,0:T(8,128)(2,1)S(1)}, u32[]{:S(2)}) copy-start(bf16[4,16,4096]{2,1,0:T(8,128)(2,1)S(1)} %collective-permute-done.5) | copy-start | bytes 1572868
  38.2 16.1 %collective-permute-start.6 = (bf16[4,16,2048]{2,1,0:T(8,128)(2,1)}, bf16[4,16,2048]{2,1,0:T(8,128)(2,1)}, u32[]{:S(2)}, u32[]{:S(2)}) collective-permute-start(bf16[4,16,2048]{2,1,0:T(8,128)(2,1)} %slice.70), channel_id=1, source_target_pairs={{0,2},{2,4},{4,6},{6,0},{1,3},{3,5},{5,7},{7,1},{8,10},{10,12},{12... | collective-permute-start | bytes 786440 | tf_op jit(solution)/shard_map/ppermute | solution.py:17
  41.9 10.9 %copy-start.2 = (bf16[1,4,16,4096]{3,2,1,0:T(8,128)(2,1)S(1)}, bf16[1,4,16,4096]{3,2,1,0:T(8,128)(2,1)}, u32[]{:S(2)}) copy-start(bf16[1,4,16,4096]{3,2,1,0:T(8,128)(2,1)} %get-tuple-element.18) | copy-start | bytes 1572868
  41.9 29.6 %all-to-all-start.1 = ((bf16[2,16,32,640]{3,1,0,2:T(8,128)(2,1)}), bf16[2,16,32,640]{3,1,0,2:T(8,128)(2,1)S(1)}, u32[]{:S(2)}, u32[]{:S(2)}) async-start(bf16[2,16,32,640]{3,1,0,2:T(8,128)(2,1)} %copy.37), calls=%async_computation.1 | async-start | bytes 2621440 | tf_op jit(solution)/shard_map/all_to_all | solution.py:64
  55.3 4.1 %copy-start.11 = (f32[2]{0:T(128)S(1)}, f32[2]{0:T(128)}, u32[]{:S(2)}) copy-start(f32[2]{0:T(128)} %param.13) | copy-start | bytes 28
  59.2 12.7 %copy-start.12 = (f32[16]{0:T(128)S(1)}, f32[16]{0:T(128)}, u32[]{:S(2)}) copy-start(f32[16]{0:T(128)} %param.11) | copy-start | bytes 196
  59.2 12.8 %copy-start.13 = (f32[32]{0:T(128)S(1)}, f32[32]{0:T(128)}, u32[]{:S(2)}) copy-start(f32[32]{0:T(128)} %param.12) | copy-start | bytes 388
  59.2 18.2 %collective-permute-start.16 = (bf16[2,4,4,16,4096]{4,3,1,2,0:T(8,128)(2,1)}, bf16[2,4,4,16,4096]{4,3,1,2,0:T(8,128)(2,1)}, u32[]{:S(2)}, u32[]{:S(2)}) collective-permute-start(bf16[2,4,4,16,4096]{4,3,1,2,0:T(8,128)(2,1)} %get-tuple-element.5), channel_id=1, source_target_pairs={{0,1},{1,0},{2,3},{3,2},{4,5},{5,4},{6,7},{7,6},{8,9},{9,8},{10,11... | collective-permute-start | bytes 12582920 | tf_op jit(solution)/shard_map/ppermute | solution.py:53
  75.9 2.9 %copy-start = (bf16[2,4,4,1,16,4096]{5,4,3,1,2,0:T(8,128)(2,1)S(1)}, bf16[2,4,4,1,16,4096]{5,4,3,1,2,0:T(8,128)(2,1)}, u32[]{:S(2)}) copy-start(bf16[2,4,4,1,16,4096]{5,4,3,1,2,0:T(8,128)(2,1)} %get-tuple-element.4) | copy-start | bytes 12582916
  85.2 14.9 %copy-start.1 = (bf16[2,4,4,2,16,4096]{5,4,3,1,2,0:T(8,128)(2,1)S(1)}, bf16[2,4,4,2,16,4096]{5,4,3,1,2,0:T(8,128)(2,1)}, u32[]{:S(2)}) copy-start(bf16[2,4,4,2,16,4096]{5,4,3,1,2,0:T(8,128)(2,1)} %pad_maximum_fusion) | copy-start | bytes 25165828
  85.2 14.9 %copy-start.8 = (bf16[1024,1,512]{2,0,1:T(8,128)(2,1)S(1)}, bf16[1024,1,512]{2,0,1:T(8,128)(2,1)}, u32[]{:S(2)}) copy-start(bf16[1024,1,512]{2,0,1:T(8,128)(2,1)} %get-tuple-element.15) | copy-start | bytes 3145732
  (3 other events, 7.5 us)

commit v5 on v4

--- a/solution.py
+++ b/solution.py
@@ -24,7 +24,7 @@
     far_first = shift(from_minus[..., :half], axis, 1)
     far_second = shift(from_plus[..., half:], axis, -1)
     far = jnp.concatenate([far_first, far_second], axis=-1)
-    return jnp.stack([block, from_plus, far, from_minus])
+    return from_plus, far, from_minus
 
 
 def on_device(
@@ -45,14 +45,23 @@
     width = local_g * nrow // ncol
     both = jnp.stack([matrix_real, matrix_imag])
 
-    row_real = ring_gather(matrix_real, "x")
-    col_imag = ring_gather(matrix_imag, "y")
-    all_real = ring_gather(row_real, "y")
-    all_imag = ring_gather(col_imag, "x")
-    mine = jnp.stack([all_real, all_imag.transpose(1, 0, 2, 3)])
-    other = lax.ppermute(mine, "core", CORE_PAIRS)
-    left = jnp.stack([mine, other], axis=3)
-    left = left.transpose(0, 2, 1, 3, 4, 5).reshape(2 * pairs, local_g)
+    row_real = jnp.stack((matrix_real,) + ring_gather(matrix_real, "x"))
+    col_imag = jnp.stack((matrix_imag,) + ring_gather(matrix_imag, "y"))
+    first = jnp.stack([row_real, col_imag])
+    first_other = lax.ppermute(first, "core", CORE_PAIRS)
+    real_plus, real_far, real_minus = ring_gather(row_real, "y")
+    imag_plus, imag_far, imag_minus = ring_gather(col_imag, "x")
+    near = jnp.stack([real_plus, real_minus, imag_plus, imag_minus])
+    near_other = lax.ppermute(near, "core", CORE_PAIRS)
+    far = jnp.stack([real_far, imag_far])
+    far_other = lax.ppermute(far, "core", CORE_PAIRS)
+    parts = []
+    for part in range(2):
+        for src_first, src_near, src_far in ((first, near, far), (first_other, near_other, far_other)):
+            parts.append(
+                jnp.stack([src_first[part], src_near[2 * part], src_far[part], src_near[2 * part + 1]])
+            )
+    left = jnp.stack(parts).reshape(2 * pairs, local_g)
 
     copies = jnp.broadcast_to(both[None], (nrow,) + both.shape)
     spread = lax.all_to_all(copies, "row", 0, 0, tiled=True)
@@ -68,23 +77,29 @@
     wide = column[:, :, :width].astype(jnp.float32)
     here = (lax.axis_index("x"), lax.axis_index("y"), lax.axis_index("core"))
 
-    def relative(scaled):
+    def relative(scaled, order):
         grid = scaled.reshape(nx, ny, ncore, local_pairs, width)
         for axis, start in enumerate(here):
             size = grid.shape[axis]
             doubled = jnp.concatenate([grid, grid], axis=axis)
             grid = lax.dynamic_slice_in_dim(doubled, start, size, axis=axis)
-        return grid.reshape(pairs, width)
+        return grid.transpose(order + (3, 4)).reshape(pairs, width)
 
+    real_order = (2, 1, 0)
+    imag_order = (2, 0, 1)
     right_real = []
     right_imag = []
     for index in range(frequency.shape[0]):
         omega = frequency[index]
         weight = 4.0 * gap / (gap * gap + omega * omega)
-        scaled_real = relative((weight[:, None] * wide[0]).astype(jnp.bfloat16))
-        scaled_imag = relative((weight[:, None] * wide[1]).astype(jnp.bfloat16))
-        right_real.append(jnp.concatenate([-scaled_real, -scaled_imag], axis=0))
-        right_imag.append(jnp.concatenate([-scaled_imag, scaled_real], axis=0))
+        scaled_real = (weight[:, None] * wide[0]).astype(jnp.bfloat16)
+        scaled_imag = (weight[:, None] * wide[1]).astype(jnp.bfloat16)
+        real_a = relative(scaled_real, real_order)
+        imag_b = relative(scaled_imag, imag_order)
+        real_b = relative(scaled_real, imag_order)
+        imag_a = relative(scaled_imag, real_order)
+        right_real.append(jnp.concatenate([-real_a, -imag_b], axis=0))
+        right_imag.append(jnp.concatenate([-imag_a, real_b], axis=0))
     dims = (((0,), (0,)), ((), ()))
     chi_real = lax.dot_general(left, jnp.stack(right_real, axis=1), dims, preferred_element_type=jnp.float32)
     chi_imag = lax.dot_general(left, jnp.stack(right_imag, axis=1), dims, preferred_element_type=jnp.float32)

time: 112 us -> 109 us (0.973)
  local copies, waits for them, and re-layouts: 8.22 us -> 15.5 us
  waiting for transfers between devices: 18.6 us -> 13.7 us
  other arithmetic: 21 us -> 17 us
  matrix products: 26.2 us -> 22.6 us
  starting transfers between devices: 34.1 us -> 36.1 us
    ppermute x16, waiting for transfers between devices: 9.37 us -> 3.6 us  [shift(): lax.ppermute(value, axis, [(i, (i + step) % size) for i in range(size)])]
    slice x1 -> x4, local copies, waits for them, and re-layouts: 0.17 us -> 4.25 us  [the longest x1 1.74 us: on_device(): src_near[2 * part]]
    ppermute x1 -> x3, starting transfers between devices: 0.24 us -> 4.17 us  [the longest x1 3.58 us: on_device(): first_other = lax.ppermute(first, 'core', CORE_PAIRS)]
    dot_general x1, matrix products: 14.9 us -> 11.3 us  [on_device(): lax.dot_general(left, jnp.stack(right_imag, axis=1), dims, preferred_elem...]
    another operation x9 -> x13, other arithmetic: 14.8 us -> 12.4 us  [the longest x3 6.14 us: on_device(): left = jnp.stack(parts).reshape(2 * pairs, local_g)]
    all_to_all x1, starting transfers between devices: 9.82 us -> 7.62 us  [on_device(): lax.all_to_all(payload, cols, split_axis=2, concat_axis=1, tiled=True)]
    slice x4, local copies, waits for them, and re-layouts: 0.8 us -> 2.39 us  [ring_gather(): far_second = shift(from_plus[..., half:], axis, -1)]
    another operation x2, other arithmetic: 1.67 us -> 0.14 us  [on_device(): jnp.stack(right_imag, axis=1)]
  transfers between devices with their start and end apart: 19 -> 21, of which waited for: 3 -> 2; matrix products, arithmetic and copies ran while one was open for 19% -> 25% of each run, Pallas kernels for 0% -> 0%
where the time goes in v5:
time: 109 us
  starting transfers between devices  36.1 us (33%)
  matrix products  22.6 us (21%)
  other arithmetic  17 us (16%)
  local copies, waits for them, and re-layouts  15.5 us (14%)
  waiting for transfers between devices  13.7 us (13%)
  between operations  3.79 us (3%)
    ppermute x16, starting transfers between devices, shift(): lax.ppermute(value, axis, [(i, (i + step) % size) for i in range(size)])  19.2 us
    dot_general x1, matrix products, on_device(): lax.dot_general(left, jnp.stack(right_imag, axis=1), dims, preferred_elem...  11.3 us
    dot_general x1, matrix products, on_device(): lax.dot_general(left, jnp.stack(right_real, axis=1), dims, preferred_elem...  11.3 us
    all_to_all x1, waiting for transfers between devices, on_device(): lax.all_to_all(payload, cols, split_axis=2, concat_axis=1, tiled=True)  10.1 us
    all_to_all x1, starting transfers between devices, on_device(): lax.all_to_all(payload, cols, split_axis=2, concat_axis=1, tiled=True)  7.62 us
    another operation x3, other arithmetic, on_device(): left = jnp.stack(parts).reshape(2 * pairs, local_g)  6.14 us
    all_to_all x1, starting transfers between devices, on_device(): spread = lax.all_to_all(copies, 'row', 0, 0, tiled=True)  5.16 us
    another operation x3, other arithmetic, on_device(): first = jnp.stack([row_real, col_imag])  3.83 us
  transfers between devices with their start and end apart: 21, of which 2 were waited for; matrix products, arithmetic and copies ran while one was open for 25% of the time, Pallas kernels for 0%

profile of v5, /device:TPU:1, one launch (start us, length us, event | category | flops | bytes accessed | tf_op | source)
XLA Modules:
  0.0 108.7 jit_solution(13922724313202195130)
XLA Ops:
  0.7 2.1 %collective-permute-start.1 = (bf16[16,4096]{1,0:T(8,128)(2,1)}, bf16[16,4096]{1,0:T(8,128)(2,1)S(1)}, u32[]{:S(2)}, u32[]{:S(2)}) collective-permute-start(bf16[16,4096]{1,0:T(8,128)(2,1)} %param.7), channel_id=1, source_target_pairs={{0,8},{8,16},{16,24},{24,0},{1,9},{9,17},{17,25},{25,1},{2,10},{10... | collective-permute-start | bytes 393224 | tf_op jit(solution)/shard_map/ppermute | solution.py:17
  2.8 1.4 %collective-permute-start = (bf16[16,4096]{1,0:T(8,128)(2,1)}, bf16[16,4096]{1,0:T(8,128)(2,1)S(1)}, u32[]{:S(2)}, u32[]{:S(2)}) collective-permute-start(bf16[16,4096]{1,0:T(8,128)(2,1)} %param.7), channel_id=1, source_target_pairs={{0,24},{8,0},{16,8},{24,16},{1,25},{9,1},{17,9},{25,17},{2,26},{10... | collective-permute-start | bytes 393224 | tf_op jit(solution)/shard_map/ppermute | solution.py:17
  4.1 1.4 %collective-permute-start.9 = (bf16[16,4096]{1,0:T(8,128)(2,1)}, bf16[16,4096]{1,0:T(8,128)(2,1)S(1)}, u32[]{:S(2)}, u32[]{:S(2)}) collective-permute-start(bf16[16,4096]{1,0:T(8,128)(2,1)} %param.8), channel_id=1, source_target_pairs={{0,2},{2,4},{4,6},{6,0},{1,3},{3,5},{5,7},{7,1},{8,10},{10,12},{12... | collective-permute-start | bytes 393224 | tf_op jit(solution)/shard_map/ppermute | solution.py:17
  5.5 1.4 %collective-permute-start.8 = (bf16[16,4096]{1,0:T(8,128)(2,1)}, bf16[16,4096]{1,0:T(8,128)(2,1)S(1)}, u32[]{:S(2)}, u32[]{:S(2)}) collective-permute-start(bf16[16,4096]{1,0:T(8,128)(2,1)} %param.8), channel_id=1, source_target_pairs={{0,6},{2,0},{4,2},{6,4},{1,7},{3,1},{5,3},{7,5},{8,14},{10,8},{12,... | collective-permute-start | bytes 393224 | tf_op jit(solution)/shard_map/ppermute | solution.py:17
  7.0 1.0 pad_maximum_fusion.8
  8.0 1.1 broadcast_in_dim.28
  9.1 5.2 %all-to-all-start = ((bf16[4,2,16,4096]{3,2,1,0:T(8,128)(2,1)}), bf16[4,2,16,4096]{3,2,1,0:T(8,128)(2,1)S(1)}, u32[]{:S(2)}, u32[]{:S(2)}) async-start(bf16[4,2,16,4096]{3,2,1,0:T(8,128)(2,1)} %broadcast_in_dim.28), calls=%async_computation | async-start | bytes 2097152 | tf_op jit(solution)/shard_map/all_to_all | solution.py:67
  14.4 2.7 %collective-permute-start.11 = (bf16[16,2048]{1,0:T(8,128)(2,1)S(1)}, bf16[16,2048]{1,0:T(8,128)(2,1)S(1)}, u32[]{:S(2)}, u32[]{:S(2)}) collective-permute-start(bf16[16,2048]{1,0:T(8,128)(2,1)S(1)} %slice.105), channel_id=1, source_target_pairs={{0,6},{2,0},{4,2},{6,4},{1,7},{3,1},{5,3},{7,5},{8,14},{10,8},{12,... | collective-permute-start | bytes 196616 | tf_op jit(solution)/shard_map/ppermute | solution.py:17
  17.8 2.7 %collective-permute-start.3 = (bf16[16,2048]{1,0:T(8,128)(2,1)S(1)}, bf16[16,2048]{1,0:T(8,128)(2,1)S(1)}, u32[]{:S(2)}, u32[]{:S(2)}) collective-permute-start(bf16[16,2048]{1,0:T(8,128)(2,1)S(1)} %slice.101), channel_id=1, source_target_pairs={{0,24},{8,0},{16,8},{24,16},{1,25},{9,1},{17,9},{25,17},{2,26},{10... | collective-permute-start | bytes 196616 | tf_op jit(solution)/shard_map/ppermute | solution.py:17
  20.6 0.9 fusion.29
  21.5 1.4 %collective-permute-start.14 = (bf16[4,16,4096]{2,1,0:T(8,128)(2,1)}, bf16[4,16,4096]{2,1,0:T(8,128)(2,1)S(1)}, u32[]{:S(2)}, u32[]{:S(2)}) collective-permute-start(bf16[4,16,4096]{2,1,0:T(8,128)(2,1)} %get-tuple-element.32), channel_id=1, source_target_pairs={{0,8},{8,16},{16,24},{24,0},{1,9},{9,17},{17,25},{25,1},{2,10},{10... | collective-permute-start | bytes 1572872 | tf_op jit(solution)/shard_map/ppermute | solution.py:17
  23.0 1.8 %fusion.30 = (bf16[1,4,16,4096]{3,2,1,0:T(8,128)(2,1)S(1)}, bf16[4,16,4096]{2,1,0:T(8,128)(2,1)}) fusion(bf16[1,16,4096]{2,1,0:T(8,128)(2,1)} %bitcast.118, bf16[1,16,4096]{2,1,0:T(8,128)(2,1)S(1)} %maximum_bitcast_fusion.9, bf16[1,16,4096]{2,1,0:T(8,128)(2,1)} %bitcast.119, bf16[1,16,4096]{2,1,0:T(8,128)(2,1)S(1)} %bitcast.117), kind=kLoop, calls=%fused_computation.96 | loop fusion | flops 786432 | bytes 1572864 | tf_op jit(solution)/shard_map/stack | solution.py:50
  28.9 3.6 %collective-permute-done.13 = bf16[4,16,4096]{2,1,0:T(8,128)(2,1)S(1)} collective-permute-done((bf16[4,16,4096]{2,1,0:T(8,128)(2,1)}, bf16[4,16,4096]{2,1,0:T(8,128)(2,1)S(1)}, u32[]{:S(2)}, u32[]{:S(2)}) %collective-permute-start.13) | collective-permute-done | bytes 524320 | tf_op jit(solution)/shard_map/ppermute | solution.py:17
  33.2 2.2 %collective-permute-start.17 = (bf16[4,16,2048]{2,1,0:T(8,128)(2,1)}, bf16[4,16,2048]{2,1,0:T(8,128)(2,1)}, u32[]{:S(2)}, u32[]{:S(2)}) collective-permute-start(bf16[4,16,2048]{2,1,0:T(8,128)(2,1)} %slice.109), channel_id=1, source_target_pairs={{0,24},{8,0},{16,8},{24,16},{1,25},{9,1},{17,9},{25,17},{2,26},{10... | collective-permute-start | bytes 786440 | tf_op jit(solution)/shard_map/ppermute | solution.py:17
  36.2 1.1 %pad_maximum_fusion.4 = bf16[2,4,16,4096]{3,2,1,0:T(8,128)(2,1)} fusion(bf16[1,4,16,4096]{3,2,1,0:T(8,128)(2,1)S(1)} %get-tuple-element.31, bf16[1,4,16,4096]{3,2,1,0:T(8,128)(2,1)S(1)} %get-tuple-element.29), kind=kLoop, calls=%fused_computation.17 | loop fusion | flops 524288 | bytes 2097152 | tf_op jit(solution)/shard_map/stack | solution.py:50
  37.2 3.6 %collective-permute-start.12 = (bf16[2,4,16,4096]{3,2,1,0:T(8,128)(2,1)}, bf16[2,4,16,4096]{3,2,1,0:T(8,128)(2,1)}, u32[]{:S(2)}, u32[]{:S(2)}) collective-permute-start(bf16[2,4,16,4096]{3,2,1,0:T(8,128)(2,1)} %pad_maximum_fusion.4), channel_id=1, source_target_pairs={{0,1},{1,0},{2,3},{3,2},{4,5},{5,4},{6,7},{7,6},{8,9},{9,8},{10,11... | collective-permute-start | bytes 3145736 | tf_op jit(solution)/shard_map/ppermute | solution.py:51
  40.8 1.7 %slice.103 = bf16[4,16,2048]{2,1,0:T(8,128)(2,1)} slice(bf16[4,16,4096]{2,1,0:T(8,128)(2,1)} %collective-permute-done.4), slice={[0:4], [0:16], [2048:4096]} | slice | bytes 524288 | tf_op jit(solution)/shard_map/slice | solution.py:25
  42.5 2.1 %collective-permute-start.7 = (bf16[4,16,2048]{2,1,0:T(8,128)(2,1)}, bf16[4,16,2048]{2,1,0:T(8,128)(2,1)}, u32[]{:S(2)}, u32[]{:S(2)}) collective-permute-start(bf16[4,16,2048]{2,1,0:T(8,128)(2,1)} %slice.103), channel_id=1, source_target_pairs={{0,6},{2,0},{4,2},{6,4},{1,7},{3,1},{5,3},{7,5},{8,14},{10,8},{12,... | collective-permute-start | bytes 786440 | tf_op jit(solution)/shard_map/ppermute | solution.py:17
  44.6 1.7 %slice.102 = bf16[4,16,2048]{2,1,0:T(8,128)(2,1)} slice(bf16[4,16,4096]{2,1,0:T(8,128)(2,1)} %collective-permute-done.5), slice={[0:4], [0:16], [0:2048]} | slice | bytes 524288 | tf_op jit(solution)/shard_map/slice | solution.py:24
  47.1 1.5 %copy.39 = bf16[2,16,32,640]{3,1,0,2:T(8,128)(2,1)} copy(bf16[2,16,32,640]{3,2,1,0:T(8,128)(2,1)S(1)} %pad_maximum_fusion.3) | data formatting | bytes 2621440 | tf_op jit(solution)/shard_map/concatenate | solution.py:72
  48.6 7.6 %all-to-all-start.1 = ((bf16[2,16,32,640]{3,1,0,2:T(8,128)(2,1)}), bf16[2,16,32,640]{3,1,0,2:T(8,128)(2,1)S(1)}, u32[]{:S(2)}, u32[]{:S(2)}) async-start(bf16[2,16,32,640]{3,1,0,2:T(8,128)(2,1)} %copy.39), calls=%async_computation.1 | async-start | bytes 2621440 | tf_op jit(solution)/shard_map/all_to_all | solution.py:73
  56.2 1.1 maximum_bitcast_fusion.8
  57.3 1.1 maximum_bitcast_fusion.7
  58.8 4.5 %maximum_bitcast_fusion = (bf16[1,4,4,16,4096]{4,3,2,1,0:T(8,128)(2,1)}, bf16[4,4,16,4096]{3,2,1,0:T(8,128)(2,1)}, bf16[1,4,4,16,4096]{4,3,2,1,0:T(8,128)(2,1)}) fusion(bf16[1,4,16,4096]{3,2,1,0:T(8,128)(2,1)} %bitcast.7, bf16[1,4,16,4096]{3,2,1,0:T(8,128)(2,1)S(1)} %maximum_bitcast_fusion.7, bf16[1,4,16,4096]{3,2,1,0:T(8,128)(2,1)} %bitcast.5, ...), kind=kLoop, calls=%fused_computation.6 | loop fusion | flops 9437184 | bytes 10485760 | tf_op jit(solution)/shard_map/stack | solution.py:64
  63.6 1.3 %fusion.33 = (bf16[1,4,16,4096]{3,2,1,0:T(8,128)(2,1)S(1)}, bf16[1,4,16,4096]{3,2,1,0:T(8,128)(2,1)S(1)}) fusion(bf16[2,4,16,4096]{3,2,1,0:T(8,128)(2,1)} %collective-permute-done.12), kind=kLoop, calls=%fused_computation.99 | loop fusion | bytes 2097152 | tf_op jit(solution)/shard_map/slice | solution.py:62
  64.9 1.1 fusion.34
  65.9 10.1 %all-to-all-done.1 = bf16[2,16,32,640]{3,1,0,2:T(8,128)(2,1)S(1)} async-done(((bf16[2,16,32,640]{3,1,0,2:T(8,128)(2,1)}), bf16[2,16,32,640]{3,1,0,2:T(8,128)(2,1)S(1)}, u32[]{:S(2)}, u32[]{:S(2)}) %all-to-all-start.1) | async-done | bytes 1310752 | tf_op jit(solution)/shard_map/all_to_all | solution.py:73
  80.9 1.7 %fusion.32 = (bf16[1,4,16,4096]{3,2,1,0:T(8,128)(2,1)S(1)}, bf16[1,4,16,4096]{3,2,1,0:T(8,128)(2,1)S(1)}, bf16[1,4,16,4096]{3,2,1,0:T(8,128)(2,1)S(1)}, bf16[1,4,16,4096]{3,2,1,0:T(8,128)(2,1)S(1)}) fusion(bf16[4,4,16,4096]{3,2,1,0:T(8,128)(2,1)} %collective-permute-done.15), kind=kLoop, calls=%fused_computation.98 | loop fusion | bytes 4194304 | tf_op jit(solution)/shard_map/slice | solution.py:62
  83.3 1.0 copy-done
  85.0 1.1 %pad_maximum_fusion = bf16[4,4,4,16,4096]{4,3,2,1,0:T(8,128)(2,1)S(1)} fusion(bf16[1,4,4,16,4096]{4,3,2,1,0:T(8,128)(2,1)S(1)} %get-tuple-element.40, bf16[1,4,4,16,4096]{4,3,2,1,0:T(8,128)(2,1)S(1)} %copy-done.1, bf16[1,4,4,16,4096]{4,3,2,1,0:T(8,128)(2,1)S(1)} %get-tuple-element.39, bf16[1,4,4,16,4096]{4,3,2,1,0:T(8,128)(2,1)S(1)} %copy-done), kind=kLoop, calls=%fused_computation | loop fusion | flops 12582912 | bytes 16777216 | tf_op jit(solution)/shard_map/stack | solution.py:64
  86.1 11.3 %convert_bitcast_fusion = bf16[2,4096,512]{2,1,0:T(8,128)(2,1)} fusion(bf16[1024,4096,1]{1,0,2:T(8,128)(2,1)S(1)} %bitcast.95, bf16[1024,1,512]{2,0,1:T(8,128)(2,1)S(1)} %maximum_bitcast_fusion.6, bf16[1024,1,512]{2,0,1:T(8,128)(2,1)S(1)} %maximum_bitcast_fusion.5), kind=kOutput, calls=%fused_computation.1 | convolution fusion | flops 8598323200 | bytes 18874368 | tf_op jit(solution)/shard_map/dot_general | solution.py:105
  97.4 11.3 %convert_bitcast_fusion.1 = bf16[2,4096,512]{2,1,0:T(8,128)(2,1)} fusion(bf16[1024,4096,1]{1,0,2:T(8,128)(2,1)S(1)} %bitcast.96, bf16[1024,1,512]{2,0,1:T(8,128)(2,1)S(1)} %maximum_bitcast_fusion.4, bf16[1024,1,512]{2,0,1:T(8,128)(2,1)S(1)} %maximum_bitcast_fusion.3), kind=kOutput, calls=%fused_computation.2 | convolution fusion | flops 8598323200 | bytes 18874368 | tf_op jit(solution)/shard_map/dot_general | solution.py:104
  (104 shorter events, 11.2 us)
Async XLA Ops:
  0.6 13.6 %copy-start.11 = (s32[16]{0:T(128)S(1)}, s32[16]{0:T(128)}, u32[]{:S(2)}) copy-start(s32[16]{0:T(128)} %param.9) | copy-start | bytes 196
  0.6 13.6 %copy-start.12 = (s32[16]{0:T(128)S(1)}, s32[16]{0:T(128)}, u32[]{:S(2)}) copy-start(s32[16]{0:T(128)} %param.10) | copy-start | bytes 196
  0.7 17.1 %collective-permute-start.1 = (bf16[16,4096]{1,0:T(8,128)(2,1)}, bf16[16,4096]{1,0:T(8,128)(2,1)S(1)}, u32[]{:S(2)}, u32[]{:S(2)}) collective-permute-start(bf16[16,4096]{1,0:T(8,128)(2,1)} %param.7), channel_id=1, source_target_pairs={{0,8},{8,16},{16,24},{24,0},{1,9},{9,17},{17,25},{25,1},{2,10},{10... | collective-permute-start | bytes 393224 | tf_op jit(solution)/shard_map/ppermute | solution.py:17
  2.8 15.1 %collective-permute-start = (bf16[16,4096]{1,0:T(8,128)(2,1)}, bf16[16,4096]{1,0:T(8,128)(2,1)S(1)}, u32[]{:S(2)}, u32[]{:S(2)}) collective-permute-start(bf16[16,4096]{1,0:T(8,128)(2,1)} %param.7), channel_id=1, source_target_pairs={{0,24},{8,0},{16,8},{24,16},{1,25},{9,1},{17,9},{25,17},{2,26},{10... | collective-permute-start | bytes 393224 | tf_op jit(solution)/shard_map/ppermute | solution.py:17
  4.1 10.1 %collective-permute-start.9 = (bf16[16,4096]{1,0:T(8,128)(2,1)}, bf16[16,4096]{1,0:T(8,128)(2,1)S(1)}, u32[]{:S(2)}, u32[]{:S(2)}) collective-permute-start(bf16[16,4096]{1,0:T(8,128)(2,1)} %param.8), channel_id=1, source_target_pairs={{0,2},{2,4},{4,6},{6,0},{1,3},{3,5},{5,7},{7,1},{8,10},{10,12},{12... | collective-permute-start | bytes 393224 | tf_op jit(solution)/shard_map/ppermute | solution.py:17
  5.5 8.9 %collective-permute-start.8 = (bf16[16,4096]{1,0:T(8,128)(2,1)}, bf16[16,4096]{1,0:T(8,128)(2,1)S(1)}, u32[]{:S(2)}, u32[]{:S(2)}) collective-permute-start(bf16[16,4096]{1,0:T(8,128)(2,1)} %param.8), channel_id=1, source_target_pairs={{0,6},{2,0},{4,2},{6,4},{1,7},{3,1},{5,3},{7,5},{8,14},{10,8},{12,... | collective-permute-start | bytes 393224 | tf_op jit(solution)/shard_map/ppermute | solution.py:17
  7.0 10.1 %copy-start.8 = (f32[2]{0:T(128)S(1)}, f32[2]{0:T(128)}, u32[]{:S(2)}) copy-start(f32[2]{0:T(128)} %param.13) | copy-start | bytes 28
  8.0 12.6 %copy-start.4 = (bf16[16,4096]{1,0:T(8,128)(2,1)S(1)}, bf16[16,4096]{1,0:T(8,128)(2,1)}, u32[]{:S(2)}) copy-start(bf16[16,4096]{1,0:T(8,128)(2,1)} %param.8) | copy-start | bytes 393220
  9.1 13.9 %copy-start.5 = (bf16[16,4096]{1,0:T(8,128)(2,1)S(1)}, bf16[16,4096]{1,0:T(8,128)(2,1)}, u32[]{:S(2)}) copy-start(bf16[16,4096]{1,0:T(8,128)(2,1)} %param.7) | copy-start | bytes 393220
  9.1 37.2 %all-to-all-start = ((bf16[4,2,16,4096]{3,2,1,0:T(8,128)(2,1)}), bf16[4,2,16,4096]{3,2,1,0:T(8,128)(2,1)S(1)}, u32[]{:S(2)}, u32[]{:S(2)}) async-start(bf16[4,2,16,4096]{3,2,1,0:T(8,128)(2,1)} %broadcast_in_dim.28), calls=%async_computation | async-start | bytes 2097152 | tf_op jit(solution)/shard_map/all_to_all | solution.py:67
  14.3 6.3 %collective-permute-start.10 = (bf16[16,2048]{1,0:T(8,128)(2,1)S(1)}, bf16[16,2048]{1,0:T(8,128)(2,1)S(1)}, u32[]{:S(2)}, u32[]{:S(2)}) collective-permute-start(bf16[16,2048]{1,0:T(8,128)(2,1)S(1)} %slice.104), channel_id=1, source_target_pairs={{0,2},{2,4},{4,6},{6,0},{1,3},{3,5},{5,7},{7,1},{8,10},{10,12},{12... | collective-permute-start | bytes 196616 | tf_op jit(solution)/shard_map/ppermute | solution.py:17
  14.4 6.2 %collective-permute-start.11 = (bf16[16,2048]{1,0:T(8,128)(2,1)S(1)}, bf16[16,2048]{1,0:T(8,128)(2,1)S(1)}, u32[]{:S(2)}, u32[]{:S(2)}) collective-permute-start(bf16[16,2048]{1,0:T(8,128)(2,1)S(1)} %slice.105), channel_id=1, source_target_pairs={{0,6},{2,0},{4,2},{6,4},{1,7},{3,1},{5,3},{7,5},{8,14},{10,8},{12,... | collective-permute-start | bytes 196616 | tf_op jit(solution)/shard_map/ppermute | solution.py:17
  17.7 5.2 %copy-start.6 = (bf16[16,4096]{1,0:T(8,128)(2,1)}, bf16[16,4096]{1,0:T(8,128)(2,1)S(1)}, u32[]{:S(2)}) copy-start(bf16[16,4096]{1,0:T(8,128)(2,1)S(1)} %collective-permute-done.1) | copy-start | bytes 393220
  17.7 5.2 %collective-permute-start.2 = (bf16[16,2048]{1,0:T(8,128)(2,1)S(1)}, bf16[16,2048]{1,0:T(8,128)(2,1)S(1)}, u32[]{:S(2)}, u32[]{:S(2)}) collective-permute-start(bf16[16,2048]{1,0:T(8,128)(2,1)S(1)} %slice.100), channel_id=1, source_target_pairs={{0,8},{8,16},{16,24},{24,0},{1,9},{9,17},{17,25},{25,1},{2,10},{10... | collective-permute-start | bytes 196616 | tf_op jit(solution)/shard_map/ppermute | solution.py:17
  17.8 5.2 %copy-start.7 = (bf16[16,4096]{1,0:T(8,128)(2,1)}, bf16[16,4096]{1,0:T(8,128)(2,1)S(1)}, u32[]{:S(2)}) copy-start(bf16[16,4096]{1,0:T(8,128)(2,1)S(1)} %collective-permute-done) | copy-start | bytes 393220
  17.8 5.1 %collective-permute-start.3 = (bf16[16,2048]{1,0:T(8,128)(2,1)S(1)}, bf16[16,2048]{1,0:T(8,128)(2,1)S(1)}, u32[]{:S(2)}, u32[]{:S(2)}) collective-permute-start(bf16[16,2048]{1,0:T(8,128)(2,1)S(1)} %slice.101), channel_id=1, source_target_pairs={{0,24},{8,0},{16,8},{24,16},{1,25},{9,1},{17,9},{25,17},{2,26},{10... | collective-permute-start | bytes 196616 | tf_op jit(solution)/shard_map/ppermute | solution.py:17
  21.5 11.0 %collective-permute-start.13 = (bf16[4,16,4096]{2,1,0:T(8,128)(2,1)}, bf16[4,16,4096]{2,1,0:T(8,128)(2,1)S(1)}, u32[]{:S(2)}, u32[]{:S(2)}) collective-permute-start(bf16[4,16,4096]{2,1,0:T(8,128)(2,1)} %get-tuple-element.32), channel_id=1, source_target_pairs={{0,24},{8,0},{16,8},{24,16},{1,25},{9,1},{17,9},{25,17},{2,26},{10... | collective-permute-start | bytes 1572872 | tf_op jit(solution)/shard_map/ppermute | solution.py:17
  21.5 13.9 %collective-permute-start.14 = (bf16[4,16,4096]{2,1,0:T(8,128)(2,1)}, bf16[4,16,4096]{2,1,0:T(8,128)(2,1)S(1)}, u32[]{:S(2)}, u32[]{:S(2)}) collective-permute-start(bf16[4,16,4096]{2,1,0:T(8,128)(2,1)} %get-tuple-element.32), channel_id=1, source_target_pairs={{0,8},{8,16},{16,24},{24,0},{1,9},{9,17},{17,25},{25,1},{2,10},{10... | collective-permute-start | bytes 1572872 | tf_op jit(solution)/shard_map/ppermute | solution.py:17
  24.8 16.0 %collective-permute-start.4 = (bf16[4,16,4096]{2,1,0:T(8,128)(2,1)}, bf16[4,16,4096]{2,1,0:T(8,128)(2,1)}, u32[]{:S(2)}, u32[]{:S(2)}) collective-permute-start(bf16[4,16,4096]{2,1,0:T(8,128)(2,1)} %get-tuple-element.30), channel_id=1, source_target_pairs={{0,6},{2,0},{4,2},{6,4},{1,7},{3,1},{5,3},{7,5},{8,14},{10,8},{12,... | collective-permute-start | bytes 1572872 | tf_op jit(solution)/shard_map/ppermute | solution.py:17
  25.7 18.9 %collective-permute-start.5 = (bf16[4,16,4096]{2,1,0:T(8,128)(2,1)}, bf16[4,16,4096]{2,1,0:T(8,128)(2,1)}, u32[]{:S(2)}, u32[]{:S(2)}) collective-permute-start(bf16[4,16,4096]{2,1,0:T(8,128)(2,1)} %get-tuple-element.30), channel_id=1, source_target_pairs={{0,2},{2,4},{4,6},{6,0},{1,3},{3,5},{5,7},{7,1},{8,10},{10,12},{12... | collective-permute-start | bytes 1572872 | tf_op jit(solution)/shard_map/ppermute | solution.py:17
  33.2 23.0 %collective-permute-start.17 = (bf16[4,16,2048]{2,1,0:T(8,128)(2,1)}, bf16[4,16,2048]{2,1,0:T(8,128)(2,1)}, u32[]{:S(2)}, u32[]{:S(2)}) collective-permute-start(bf16[4,16,2048]{2,1,0:T(8,128)(2,1)} %slice.109), channel_id=1, source_target_pairs={{0,24},{8,0},{16,8},{24,16},{1,25},{9,1},{17,9},{25,17},{2,26},{10... | collective-permute-start | bytes 786440 | tf_op jit(solution)/shard_map/ppermute | solution.py:17
  36.1 20.1 %collective-permute-start.16 = (bf16[4,16,2048]{2,1,0:T(8,128)(2,1)}, bf16[4,16,2048]{2,1,0:T(8,128)(2,1)}, u32[]{:S(2)}, u32[]{:S(2)}) collective-permute-start(bf16[4,16,2048]{2,1,0:T(8,128)(2,1)} %slice.108), channel_id=1, source_target_pairs={{0,8},{8,16},{16,24},{24,0},{1,9},{9,17},{17,25},{25,1},{2,10},{10... | collective-permute-start | bytes 786440 | tf_op jit(solution)/shard_map/ppermute | solution.py:17
  37.2 26.3 %collective-permute-start.12 = (bf16[2,4,16,4096]{3,2,1,0:T(8,128)(2,1)}, bf16[2,4,16,4096]{3,2,1,0:T(8,128)(2,1)}, u32[]{:S(2)}, u32[]{:S(2)}) collective-permute-start(bf16[2,4,16,4096]{3,2,1,0:T(8,128)(2,1)} %pad_maximum_fusion.4), channel_id=1, source_target_pairs={{0,1},{1,0},{2,3},{3,2},{4,5},{5,4},{6,7},{7,6},{8,9},{9,8},{10,11... | collective-permute-start | bytes 3145736 | tf_op jit(solution)/shard_map/ppermute | solution.py:51
  42.5 14.8 %collective-permute-start.7 = (bf16[4,16,2048]{2,1,0:T(8,128)(2,1)}, bf16[4,16,2048]{2,1,0:T(8,128)(2,1)}, u32[]{:S(2)}, u32[]{:S(2)}) collective-permute-start(bf16[4,16,2048]{2,1,0:T(8,128)(2,1)} %slice.103), channel_id=1, source_target_pairs={{0,6},{2,0},{4,2},{6,4},{1,7},{3,1},{5,3},{7,5},{8,14},{10,8},{12,... | collective-permute-start | bytes 786440 | tf_op jit(solution)/shard_map/ppermute | solution.py:17
  46.3 11.0 %collective-permute-start.6 = (bf16[4,16,2048]{2,1,0:T(8,128)(2,1)}, bf16[4,16,2048]{2,1,0:T(8,128)(2,1)}, u32[]{:S(2)}, u32[]{:S(2)}) collective-permute-start(bf16[4,16,2048]{2,1,0:T(8,128)(2,1)} %slice.102), channel_id=1, source_target_pairs={{0,2},{2,4},{4,6},{6,0},{1,3},{3,5},{5,7},{7,1},{8,10},{10,12},{12... | collective-permute-start | bytes 786440 | tf_op jit(solution)/shard_map/ppermute | solution.py:17
  48.6 27.4 %all-to-all-start.1 = ((bf16[2,16,32,640]{3,1,0,2:T(8,128)(2,1)}), bf16[2,16,32,640]{3,1,0,2:T(8,128)(2,1)S(1)}, u32[]{:S(2)}, u32[]{:S(2)}) async-start(bf16[2,16,32,640]{3,1,0,2:T(8,128)(2,1)} %copy.39), calls=%async_computation.1 | async-start | bytes 2621440 | tf_op jit(solution)/shard_map/all_to_all | solution.py:73
  58.5 6.4 %collective-permute-start.18 = (bf16[2,4,16,4096]{3,2,1,0:T(8,128)(2,1)S(1)}, bf16[2,4,16,4096]{3,2,1,0:T(8,128)(2,1)S(1)}, u32[]{:S(2)}, u32[]{:S(2)}) collective-permute-start(bf16[2,4,16,4096]{3,2,1,0:T(8,128)(2,1)S(1)} %pad_maximum_fusion.5), channel_id=1, source_target_pairs={{0,1},{1,0},{2,3},{3,2},{4,5},{5,4},{6,7},{7,6},{8,9},{9,8},{10,11... | collective-permute-start | bytes 3145736 | tf_op jit(solution)/shard_map/ppermute | solution.py:57
  63.3 17.6 %collective-permute-start.15 = (bf16[4,4,16,4096]{3,2,1,0:T(8,128)(2,1)}, bf16[4,4,16,4096]{3,2,1,0:T(8,128)(2,1)}, u32[]{:S(2)}, u32[]{:S(2)}) collective-permute-start(bf16[4,4,16,4096]{3,2,1,0:T(8,128)(2,1)} %get-tuple-element.15), channel_id=1, source_target_pairs={{0,1},{1,0},{2,3},{3,2},{4,5},{5,4},{6,7},{7,6},{8,9},{9,8},{10,11... | collective-permute-start | bytes 6291464 | tf_op jit(solution)/shard_map/ppermute | solution.py:55
  80.9 1.8 %copy-start.2 = (bf16[1,4,16,4096]{3,2,1,0:T(8,128)(2,1)S(1)}, bf16[1,4,16,4096]{3,2,1,0:T(8,128)(2,1)}, u32[]{:S(2)}) copy-start(bf16[1,4,16,4096]{3,2,1,0:T(8,128)(2,1)} %get-tuple-element.19) | copy-start | bytes 1572868
  80.9 1.8 %copy-start.3 = (bf16[1,4,16,4096]{3,2,1,0:T(8,128)(2,1)S(1)}, bf16[1,4,16,4096]{3,2,1,0:T(8,128)(2,1)}, u32[]{:S(2)}) copy-start(bf16[1,4,16,4096]{3,2,1,0:T(8,128)(2,1)} %get-tuple-element.20) | copy-start | bytes 1572868
  82.7 1.6 %copy-start = (bf16[1,4,4,16,4096]{4,3,2,1,0:T(8,128)(2,1)S(1)}, bf16[1,4,4,16,4096]{4,3,2,1,0:T(8,128)(2,1)}, u32[]{:S(2)}) copy-start(bf16[1,4,4,16,4096]{4,3,2,1,0:T(8,128)(2,1)} %get-tuple-element.14) | copy-start | bytes 6291460
  82.7 2.2 %copy-start.1 = (bf16[1,4,4,16,4096]{4,3,2,1,0:T(8,128)(2,1)S(1)}, bf16[1,4,4,16,4096]{4,3,2,1,0:T(8,128)(2,1)}, u32[]{:S(2)}) copy-start(bf16[1,4,4,16,4096]{4,3,2,1,0:T(8,128)(2,1)} %get-tuple-element.16) | copy-start | bytes 6291460
  (2 other events, 1.4 us)

commit v6 on v5

--- a/solution.py
+++ b/solution.py
@@ -45,10 +45,20 @@
     width = local_g * nrow // ncol
     both = jnp.stack([matrix_real, matrix_imag])
 
+    copies = jnp.broadcast_to(both[None], (nrow,) + both.shape)
+    spread = lax.all_to_all(copies, "row", 0, 0, tiled=True)
+    spread = spread.reshape(nrow, 2, local_pairs, local_g // width, width)
     row_real = jnp.stack((matrix_real,) + ring_gather(matrix_real, "x"))
     col_imag = jnp.stack((matrix_imag,) + ring_gather(matrix_imag, "y"))
     first = jnp.stack([row_real, col_imag])
     first_other = lax.ppermute(first, "core", CORE_PAIRS)
+    spread, row_real, col_imag, first = lax.optimization_barrier((spread, row_real, col_imag, first))
+    payload = spread.transpose(1, 2, 0, 3, 4).reshape(2, local_pairs, ncol, width)
+    bands = jnp.stack([valence_index, conduction_index]).astype(jnp.bfloat16)
+    tags = jnp.broadcast_to(bands[:, :, None, None], (2, local_pairs, ncol, 128))
+    payload = jnp.concatenate([payload, tags], axis=3)
+    column = lax.all_to_all(payload, cols, split_axis=2, concat_axis=1, tiled=True)
+    column = column.reshape(2, pairs, width + 128)
     real_plus, real_far, real_minus = ring_gather(row_real, "y")
     imag_plus, imag_far, imag_minus = ring_gather(col_imag, "x")
     near = jnp.stack([real_plus, real_minus, imag_plus, imag_minus])
@@ -63,15 +73,6 @@
             )
     left = jnp.stack(parts).reshape(2 * pairs, local_g)
 
-    copies = jnp.broadcast_to(both[None], (nrow,) + both.shape)
-    spread = lax.all_to_all(copies, "row", 0, 0, tiled=True)
-    spread = spread.reshape(nrow, 2, local_pairs, local_g // width, width)
-    payload = spread.transpose(1, 2, 0, 3, 4).reshape(2, local_pairs, ncol, width)
-    bands = jnp.stack([valence_index, conduction_index]).astype(jnp.bfloat16)
-    tags = jnp.broadcast_to(bands[:, :, None, None], (2, local_pairs, ncol, 128))
-    payload = jnp.concatenate([payload, tags], axis=3)
-    column = lax.all_to_all(payload, cols, split_axis=2, concat_axis=1, tiled=True)
-    column = column.reshape(2, pairs, width + 128)
     all_bands = column[:, :, width].astype(jnp.int32)
     gap = lookup(all_bands[1], conduction_energy) - lookup(all_bands[0], valence_energy)
     wide = column[:, :, :width].astype(jnp.float32)

time: 109 us -> 109 us (level)
  starting transfers between devices: 36.1 us -> 40.2 us
  other arithmetic: 17 us -> 13.8 us
  local copies, waits for them, and re-layouts: 15.5 us -> 12.8 us
    ppermute x16, waiting for transfers between devices: 3.6 us -> 14.6 us  [shift(): lax.ppermute(value, axis, [(i, (i + step) % size) for i in range(size)])]
    all_to_all x1, waiting for transfers between devices: 10.1 us -> 0.01 us  [on_device(): lax.all_to_all(payload, cols, split_axis=2, concat_axis=1, tiled=True)]
    ppermute x16, starting transfers between devices: 19.2 us -> 24.5 us  [shift(): lax.ppermute(value, axis, [(i, (i + step) % size) for i in range(size)])]
    all_to_all x1, starting transfers between devices: 7.62 us -> 5.14 us  [on_device(): lax.all_to_all(payload, cols, split_axis=2, concat_axis=1, tiled=True)]
    another operation x3, other arithmetic: 3.83 us -> 1.87 us  [on_device(): first = jnp.stack([row_real, col_imag])]
    ppermute x1, starting transfers between devices: 0.32 us -> 1.89 us  [on_device(): far_other = lax.ppermute(far, 'core', CORE_PAIRS)]
    slice x4, local copies, waits for them, and re-layouts: 2.42 us -> 1 us  [ring_gather(): far_first = shift(from_minus[..., :half], axis, 1)]
    slice x4, local copies, waits for them, and re-layouts: 2.39 us -> 1 us  [ring_gather(): far_second = shift(from_plus[..., half:], axis, -1)]
  transfers between devices with their start and end apart: 21 -> 21, of which waited for: 2 -> 4; matrix products, arithmetic and copies ran while one was open for 25% -> 20% of each run, Pallas kernels for 0% -> 0%
where the time goes in v6:
time: 109 us; the launch traced here: 108 us
  starting transfers between devices  40.2 us (37%)
  matrix products  22.6 us (21%)
  waiting for transfers between devices  14.6 us (13%)
  other arithmetic  13.8 us (13%)
  local copies, waits for them, and re-layouts  12.8 us (12%)
  between operations  3.77 us (3%)
    ppermute x16, starting transfers between devices, shift(): lax.ppermute(value, axis, [(i, (i + step) % size) for i in range(size)])  24.5 us
    ppermute x16, waiting for transfers between devices, shift(): lax.ppermute(value, axis, [(i, (i + step) % size) for i in range(size)])  14.6 us
    dot_general x1, matrix products, on_device(): lax.dot_general(left, jnp.stack(right_imag, axis=1), dims, preferred_elem...  11.3 us
    dot_general x1, matrix products, on_device(): lax.dot_general(left, jnp.stack(right_real, axis=1), dims, preferred_elem...  11.3 us
    another operation x3, other arithmetic, on_device(): left = jnp.stack(parts).reshape(2 * pairs, local_g)  6.04 us
    all_to_all x1, starting transfers between devices, on_device(): spread = lax.all_to_all(copies, 'row', 0, 0, tiled=True)  5.16 us
    all_to_all x1, starting transfers between devices, on_device(): lax.all_to_all(payload, cols, split_axis=2, concat_axis=1, tiled=True)  5.14 us
    ppermute x1, starting transfers between devices, on_device(): first_other = lax.ppermute(first, 'core', CORE_PAIRS)  3.51 us
  transfers between devices with their start and end apart: 21, of which 4 were waited for; matrix products, arithmetic and copies ran while one was open for 20% of the time, Pallas kernels for 0%

profile of v6, /device:TPU:1, one launch (start us, length us, event | category | flops | bytes accessed | tf_op | source)
XLA Modules:
  0.0 107.8 jit_solution(7268171062171858421)
XLA Ops:
  0.7 2.1 %collective-permute-start.1 = (bf16[16,4096]{1,0:T(8,128)(2,1)}, bf16[16,4096]{1,0:T(8,128)(2,1)S(1)}, u32[]{:S(2)}, u32[]{:S(2)}) collective-permute-start(bf16[16,4096]{1,0:T(8,128)(2,1)} %param.7), channel_id=1, source_target_pairs={{0,8},{8,16},{16,24},{24,0},{1,9},{9,17},{17,25},{25,1},{2,10},{10... | collective-permute-start | bytes 393224 | tf_op jit(solution)/shard_map/ppermute | solution.py:17
  2.8 1.4 %collective-permute-start = (bf16[16,4096]{1,0:T(8,128)(2,1)}, bf16[16,4096]{1,0:T(8,128)(2,1)S(1)}, u32[]{:S(2)}, u32[]{:S(2)}) collective-permute-start(bf16[16,4096]{1,0:T(8,128)(2,1)} %param.7), channel_id=1, source_target_pairs={{0,24},{8,0},{16,8},{24,16},{1,25},{9,1},{17,9},{25,17},{2,26},{10... | collective-permute-start | bytes 393224 | tf_op jit(solution)/shard_map/ppermute | solution.py:17
  4.1 1.4 %collective-permute-start.5 = (bf16[16,4096]{1,0:T(8,128)(2,1)}, bf16[16,4096]{1,0:T(8,128)(2,1)S(1)}, u32[]{:S(2)}, u32[]{:S(2)}) collective-permute-start(bf16[16,4096]{1,0:T(8,128)(2,1)} %param.8), channel_id=1, source_target_pairs={{0,2},{2,4},{4,6},{6,0},{1,3},{3,5},{5,7},{7,1},{8,10},{10,12},{12... | collective-permute-start | bytes 393224 | tf_op jit(solution)/shard_map/ppermute | solution.py:17
  5.5 1.4 %collective-permute-start.4 = (bf16[16,4096]{1,0:T(8,128)(2,1)}, bf16[16,4096]{1,0:T(8,128)(2,1)S(1)}, u32[]{:S(2)}, u32[]{:S(2)}) collective-permute-start(bf16[16,4096]{1,0:T(8,128)(2,1)} %param.8), channel_id=1, source_target_pairs={{0,6},{2,0},{4,2},{6,4},{1,7},{3,1},{5,3},{7,5},{8,14},{10,8},{12,... | collective-permute-start | bytes 393224 | tf_op jit(solution)/shard_map/ppermute | solution.py:17
  7.0 1.0 pad_maximum_fusion.8
  8.0 1.1 broadcast_in_dim.28
  9.1 5.2 %all-to-all-start = ((bf16[4,2,16,4096]{3,2,1,0:T(8,128)(2,1)}), bf16[4,2,16,4096]{3,2,1,0:T(8,128)(2,1)S(1)}, u32[]{:S(2)}, u32[]{:S(2)}) async-start(bf16[4,2,16,4096]{3,2,1,0:T(8,128)(2,1)} %broadcast_in_dim.28), calls=%async_computation | async-start | bytes 2097152 | tf_op jit(solution)/shard_map/all_to_all | solution.py:49
  17.5 2.7 %collective-permute-start.7 = (bf16[16,2048]{1,0:T(8,128)(2,1)S(1)}, bf16[16,2048]{1,0:T(8,128)(2,1)S(1)}, u32[]{:S(2)}, u32[]{:S(2)}) collective-permute-start(bf16[16,2048]{1,0:T(8,128)(2,1)S(1)} %slice.111), channel_id=1, source_target_pairs={{0,6},{2,0},{4,2},{6,4},{1,7},{3,1},{5,3},{7,5},{8,14},{10,8},{12,... | collective-permute-start | bytes 196616 | tf_op jit(solution)/shard_map/ppermute | solution.py:17
  20.4 2.7 %collective-permute-start.3 = (bf16[16,2048]{1,0:T(8,128)(2,1)S(1)}, bf16[16,2048]{1,0:T(8,128)(2,1)S(1)}, u32[]{:S(2)}, u32[]{:S(2)}) collective-permute-start(bf16[16,2048]{1,0:T(8,128)(2,1)S(1)} %slice.109), channel_id=1, source_target_pairs={{0,24},{8,0},{16,8},{24,16},{1,25},{9,1},{17,9},{25,17},{2,26},{10... | collective-permute-start | bytes 196616 | tf_op jit(solution)/shard_map/ppermute | solution.py:17
  23.1 0.9 fusion.29
  24.0 0.9 collective-permute-done.2
  26.0 3.5 %collective-permute-start.12 = (bf16[2,4,16,4096]{3,2,1,0:T(8,128)(2,1)S(1)}, bf16[2,4,16,4096]{3,2,1,0:T(8,128)(2,1)}, u32[]{:S(2)}, u32[]{:S(2)}) collective-permute-start(bf16[2,4,16,4096]{3,2,1,0:T(8,128)(2,1)S(1)} %pad_maximum_fusion.4), channel_id=1, source_target_pairs={{0,1},{1,0},{2,3},{3,2},{4,5},{5,4},{6,7},{7,6},{8,9},{9,8},{10,11... | collective-permute-start | bytes 3145736 | tf_op jit(solution)/shard_map/ppermute | solution.py:54
  30.1 2.7 %collective-permute-start.8 = (bf16[4,16,4096]{2,1,0:T(8,128)(2,1)}, bf16[4,16,4096]{2,1,0:T(8,128)(2,1)S(1)}, u32[]{:S(2)}, u32[]{:S(2)}) collective-permute-start(bf16[4,16,4096]{2,1,0:T(8,128)(2,1)} %get-tuple-element.7), channel_id=1, source_target_pairs={{0,6},{2,0},{4,2},{6,4},{1,7},{3,1},{5,3},{7,5},{8,14},{10,8},{12,... | collective-permute-start | bytes 1572872 | tf_op jit(solution)/shard_map/ppermute | solution.py:17
  33.1 2.7 %collective-permute-start.13 = (bf16[4,16,4096]{2,1,0:T(8,128)(2,1)}, bf16[4,16,4096]{2,1,0:T(8,128)(2,1)}, u32[]{:S(2)}, u32[]{:S(2)}) collective-permute-start(bf16[4,16,4096]{2,1,0:T(8,128)(2,1)} %get-tuple-element.8), channel_id=1, source_target_pairs={{0,24},{8,0},{16,8},{24,16},{1,25},{9,1},{17,9},{25,17},{2,26},{10... | collective-permute-start | bytes 1572872 | tf_op jit(solution)/shard_map/ppermute | solution.py:17
  36.0 1.5 %copy.39 = bf16[2,16,32,640]{3,1,0,2:T(8,128)(2,1)} copy(bf16[2,16,32,640]{3,2,1,0:T(8,128)(2,1)S(1)} %pad_maximum_fusion.3) | data formatting | bytes 2621440 | tf_op jit(solution)/shard_map/concatenate | solution.py:59
  37.6 5.1 %all-to-all-start.1 = ((bf16[2,16,32,640]{3,1,0,2:T(8,128)(2,1)}), bf16[2,16,32,640]{3,1,0,2:T(8,128)(2,1)S(1)}, u32[]{:S(2)}, u32[]{:S(2)}) async-start(bf16[2,16,32,640]{3,1,0,2:T(8,128)(2,1)} %copy.39), calls=%async_computation.1 | async-start | bytes 2621440 | tf_op jit(solution)/shard_map/all_to_all | solution.py:60
  42.8 1.5 %collective-permute-done.9 = bf16[4,16,4096]{2,1,0:T(8,128)(2,1)S(1)} collective-permute-done((bf16[4,16,4096]{2,1,0:T(8,128)(2,1)}, bf16[4,16,4096]{2,1,0:T(8,128)(2,1)S(1)}, u32[]{:S(2)}, u32[]{:S(2)}) %collective-permute-start.9) | collective-permute-done | bytes 524320 | tf_op jit(solution)/shard_map/ppermute | solution.py:17
  44.4 2.7 %collective-permute-start.11 = (bf16[4,16,2048]{2,1,0:T(8,128)(2,1)S(1)}, bf16[4,16,2048]{2,1,0:T(8,128)(2,1)S(1)}, u32[]{:S(2)}, u32[]{:S(2)}) collective-permute-start(bf16[4,16,2048]{2,1,0:T(8,128)(2,1)S(1)} %slice.113), channel_id=1, source_target_pairs={{0,6},{2,0},{4,2},{6,4},{1,7},{3,1},{5,3},{7,5},{8,14},{10,8},{12,... | collective-permute-start | bytes 786440 | tf_op jit(solution)/shard_map/ppermute | solution.py:17
  47.2 1.3 %fusion.34 = (bf16[1,4,16,4096]{3,2,1,0:T(8,128)(2,1)S(1)}, bf16[1,4,16,4096]{3,2,1,0:T(8,128)(2,1)S(1)}) fusion(bf16[2,4,16,4096]{3,2,1,0:T(8,128)(2,1)} %collective-permute-done.12), kind=kLoop, calls=%fused_computation.99 | loop fusion | bytes 2097152 | tf_op jit(solution)/shard_map/slice | solution.py:72
  48.4 1.0 slice.116
  50.2 1.0 slice.117
  51.1 3.3 %collective-permute-start.17 = (bf16[4,16,2048]{2,1,0:T(8,128)(2,1)S(1)}, bf16[4,16,2048]{2,1,0:T(8,128)(2,1)S(1)}, u32[]{:S(2)}, u32[]{:S(2)}) collective-permute-start(bf16[4,16,2048]{2,1,0:T(8,128)(2,1)S(1)} %slice.117), channel_id=1, source_target_pairs={{0,24},{8,0},{16,8},{24,16},{1,25},{9,1},{17,9},{25,17},{2,26},{10... | collective-permute-start | bytes 786440 | tf_op jit(solution)/shard_map/ppermute | solution.py:17
  54.5 11.4 %collective-permute-done.10 = bf16[4,16,2048]{2,1,0:T(8,128)(2,1)S(1)} collective-permute-done((bf16[4,16,2048]{2,1,0:T(8,128)(2,1)S(1)}, bf16[4,16,2048]{2,1,0:T(8,128)(2,1)S(1)}, u32[]{:S(2)}, u32[]{:S(2)}) %collective-permute-start.10) | collective-permute-done | bytes 262176 | tf_op jit(solution)/shard_map/ppermute | solution.py:17
  66.7 1.1 pad_maximum_fusion.5
  67.8 1.9 %collective-permute-start.18 = (bf16[2,4,16,4096]{3,2,1,0:T(8,128)(2,1)}, bf16[2,4,16,4096]{3,2,1,0:T(8,128)(2,1)}, u32[]{:S(2)}, u32[]{:S(2)}) collective-permute-start(bf16[2,4,16,4096]{3,2,1,0:T(8,128)(2,1)} %pad_maximum_fusion.5), channel_id=1, source_target_pairs={{0,1},{1,0},{2,3},{3,2},{4,5},{5,4},{6,7},{7,6},{8,9},{9,8},{10,11... | collective-permute-start | bytes 3145736 | tf_op jit(solution)/shard_map/ppermute | solution.py:67
  69.7 4.4 %maximum_bitcast_fusion = (bf16[1,4,4,16,4096]{4,3,2,1,0:T(8,128)(2,1)}, bf16[4,4,16,4096]{3,2,1,0:T(8,128)(2,1)}, bf16[1,4,4,16,4096]{4,3,2,1,0:T(8,128)(2,1)}) fusion(bf16[1,4,16,4096]{3,2,1,0:T(8,128)(2,1)S(1)} %bitcast.110, bf16[1,4,16,4096]{3,2,1,0:T(8,128)(2,1)S(1)} %maximum_bitcast_fusion.7, bf16[1,4,16,4096]{3,2,1,0:T(8,128)(2,1)S(1)} %bitcast.111, ...), kind=kLoop, calls=%fused_computation.6 | loop fusion | flops 9437184 | bytes 10485760 | tf_op jit(solution)/shard_map/stack | solution.py:74
  79.0 1.3 %fusion.35 = (bf16[1,4,16,4096]{3,2,1,0:T(8,128)(2,1)S(1)}, bf16[1,4,16,4096]{3,2,1,0:T(8,128)(2,1)S(1)}) fusion(bf16[2,4,16,4096]{3,2,1,0:T(8,128)(2,1)} %collective-permute-done.18), kind=kLoop, calls=%fused_computation.100 | loop fusion | bytes 2097152 | tf_op jit(solution)/shard_map/slice | solution.py:72
  80.2 1.7 %fusion.32 = (bf16[1,4,16,4096]{3,2,1,0:T(8,128)(2,1)S(1)}, bf16[1,4,16,4096]{3,2,1,0:T(8,128)(2,1)S(1)}, bf16[1,4,16,4096]{3,2,1,0:T(8,128)(2,1)S(1)}, bf16[1,4,16,4096]{3,2,1,0:T(8,128)(2,1)S(1)}) fusion(bf16[4,4,16,4096]{3,2,1,0:T(8,128)(2,1)} %collective-permute-done.15), kind=kLoop, calls=%fused_computation.97 | loop fusion | bytes 4194304 | tf_op jit(solution)/shard_map/slice | solution.py:72
  82.5 1.0 copy-done
  84.1 1.1 %pad_maximum_fusion = bf16[4,4,4,16,4096]{4,3,2,1,0:T(8,128)(2,1)S(1)} fusion(bf16[1,4,4,16,4096]{4,3,2,1,0:T(8,128)(2,1)S(1)} %get-tuple-element.50, bf16[1,4,4,16,4096]{4,3,2,1,0:T(8,128)(2,1)S(1)} %copy-done.1, bf16[1,4,4,16,4096]{4,3,2,1,0:T(8,128)(2,1)S(1)} %get-tuple-element.49, bf16[1,4,4,16,4096]{4,3,2,1,0:T(8,128)(2,1)S(1)} %copy-done), kind=kLoop, calls=%fused_computation | loop fusion | flops 12582912 | bytes 16777216 | tf_op jit(solution)/shard_map/stack | solution.py:74
  85.2 11.3 %convert_bitcast_fusion = bf16[2,4096,512]{2,1,0:T(8,128)(2,1)} fusion(bf16[1024,4096,1]{1,0,2:T(8,128)(2,1)S(1)} %bitcast.93, bf16[1024,1,512]{2,0,1:T(8,128)(2,1)S(1)} %maximum_bitcast_fusion.6, bf16[1024,1,512]{2,0,1:T(8,128)(2,1)S(1)} %maximum_bitcast_fusion.5), kind=kOutput, calls=%fused_computation.1 | convolution fusion | flops 8598323200 | bytes 18874368 | tf_op jit(solution)/shard_map/dot_general | solution.py:106
  96.5 11.3 %convert_bitcast_fusion.1 = bf16[2,4096,512]{2,1,0:T(8,128)(2,1)} fusion(bf16[1024,4096,1]{1,0,2:T(8,128)(2,1)S(1)} %bitcast.94, bf16[1024,1,512]{2,0,1:T(8,128)(2,1)S(1)} %maximum_bitcast_fusion.4, bf16[1024,1,512]{2,0,1:T(8,128)(2,1)S(1)} %maximum_bitcast_fusion.3), kind=kOutput, calls=%fused_computation.2 | convolution fusion | flops 8598323200 | bytes 18874368 | tf_op jit(solution)/shard_map/dot_general | solution.py:105
  (105 shorter events, 10.7 us)
Async XLA Ops:
  0.6 13.6 %copy-start.11 = (s32[16]{0:T(128)S(1)}, s32[16]{0:T(128)}, u32[]{:S(2)}) copy-start(s32[16]{0:T(128)} %param.9) | copy-start | bytes 196
  0.6 13.6 %copy-start.12 = (s32[16]{0:T(128)S(1)}, s32[16]{0:T(128)}, u32[]{:S(2)}) copy-start(s32[16]{0:T(128)} %param.10) | copy-start | bytes 196
  0.7 13.6 %copy-start.8 = (f32[2]{0:T(128)S(1)}, f32[2]{0:T(128)}, u32[]{:S(2)}) copy-start(f32[2]{0:T(128)} %param.13) | copy-start | bytes 28
  0.7 19.6 %collective-permute-start.1 = (bf16[16,4096]{1,0:T(8,128)(2,1)}, bf16[16,4096]{1,0:T(8,128)(2,1)S(1)}, u32[]{:S(2)}, u32[]{:S(2)}) collective-permute-start(bf16[16,4096]{1,0:T(8,128)(2,1)} %param.7), channel_id=1, source_target_pairs={{0,8},{8,16},{16,24},{24,0},{1,9},{9,17},{17,25},{25,1},{2,10},{10... | collective-permute-start | bytes 393224 | tf_op jit(solution)/shard_map/ppermute | solution.py:17
  2.8 17.6 %collective-permute-start = (bf16[16,4096]{1,0:T(8,128)(2,1)}, bf16[16,4096]{1,0:T(8,128)(2,1)S(1)}, u32[]{:S(2)}, u32[]{:S(2)}) collective-permute-start(bf16[16,4096]{1,0:T(8,128)(2,1)} %param.7), channel_id=1, source_target_pairs={{0,24},{8,0},{16,8},{24,16},{1,25},{9,1},{17,9},{25,17},{2,26},{10... | collective-permute-start | bytes 393224 | tf_op jit(solution)/shard_map/ppermute | solution.py:17
  4.1 13.3 %collective-permute-start.5 = (bf16[16,4096]{1,0:T(8,128)(2,1)}, bf16[16,4096]{1,0:T(8,128)(2,1)S(1)}, u32[]{:S(2)}, u32[]{:S(2)}) collective-permute-start(bf16[16,4096]{1,0:T(8,128)(2,1)} %param.8), channel_id=1, source_target_pairs={{0,2},{2,4},{4,6},{6,0},{1,3},{3,5},{5,7},{7,1},{8,10},{10,12},{12... | collective-permute-start | bytes 393224 | tf_op jit(solution)/shard_map/ppermute | solution.py:17
  5.5 12.0 %collective-permute-start.4 = (bf16[16,4096]{1,0:T(8,128)(2,1)}, bf16[16,4096]{1,0:T(8,128)(2,1)S(1)}, u32[]{:S(2)}, u32[]{:S(2)}) collective-permute-start(bf16[16,4096]{1,0:T(8,128)(2,1)} %param.8), channel_id=1, source_target_pairs={{0,6},{2,0},{4,2},{6,4},{1,7},{3,1},{5,3},{7,5},{8,14},{10,8},{12,... | collective-permute-start | bytes 393224 | tf_op jit(solution)/shard_map/ppermute | solution.py:17
  8.0 15.2 %copy-start.6 = (bf16[16,4096]{1,0:T(8,128)(2,1)S(1)}, bf16[16,4096]{1,0:T(8,128)(2,1)}, u32[]{:S(2)}) copy-start(bf16[16,4096]{1,0:T(8,128)(2,1)} %param.8) | copy-start | bytes 393220
  9.1 15.9 %copy-start.7 = (bf16[16,4096]{1,0:T(8,128)(2,1)S(1)}, bf16[16,4096]{1,0:T(8,128)(2,1)}, u32[]{:S(2)}) copy-start(bf16[16,4096]{1,0:T(8,128)(2,1)} %param.7) | copy-start | bytes 393220
  9.1 20.4 %all-to-all-start = ((bf16[4,2,16,4096]{3,2,1,0:T(8,128)(2,1)}), bf16[4,2,16,4096]{3,2,1,0:T(8,128)(2,1)S(1)}, u32[]{:S(2)}, u32[]{:S(2)}) async-start(bf16[4,2,16,4096]{3,2,1,0:T(8,128)(2,1)} %broadcast_in_dim.28), calls=%async_computation | async-start | bytes 2097152 | tf_op jit(solution)/shard_map/all_to_all | solution.py:49
  17.4 5.7 %collective-permute-start.6 = (bf16[16,2048]{1,0:T(8,128)(2,1)S(1)}, bf16[16,2048]{1,0:T(8,128)(2,1)S(1)}, u32[]{:S(2)}, u32[]{:S(2)}) collective-permute-start(bf16[16,2048]{1,0:T(8,128)(2,1)S(1)} %slice.110), channel_id=1, source_target_pairs={{0,2},{2,4},{4,6},{6,0},{1,3},{3,5},{5,7},{7,1},{8,10},{10,12},{12... | collective-permute-start | bytes 196616 | tf_op jit(solution)/shard_map/ppermute | solution.py:17
  17.5 5.6 %collective-permute-start.7 = (bf16[16,2048]{1,0:T(8,128)(2,1)S(1)}, bf16[16,2048]{1,0:T(8,128)(2,1)S(1)}, u32[]{:S(2)}, u32[]{:S(2)}) collective-permute-start(bf16[16,2048]{1,0:T(8,128)(2,1)S(1)} %slice.111), channel_id=1, source_target_pairs={{0,6},{2,0},{4,2},{6,4},{1,7},{3,1},{5,3},{7,5},{8,14},{10,8},{12,... | collective-permute-start | bytes 196616 | tf_op jit(solution)/shard_map/ppermute | solution.py:17
  20.3 4.7 %collective-permute-start.2 = (bf16[16,2048]{1,0:T(8,128)(2,1)S(1)}, bf16[16,2048]{1,0:T(8,128)(2,1)S(1)}, u32[]{:S(2)}, u32[]{:S(2)}) collective-permute-start(bf16[16,2048]{1,0:T(8,128)(2,1)S(1)} %slice.108), channel_id=1, source_target_pairs={{0,8},{8,16},{16,24},{24,0},{1,9},{9,17},{17,25},{25,1},{2,10},{10... | collective-permute-start | bytes 196616 | tf_op jit(solution)/shard_map/ppermute | solution.py:17
  20.4 4.6 %collective-permute-start.3 = (bf16[16,2048]{1,0:T(8,128)(2,1)S(1)}, bf16[16,2048]{1,0:T(8,128)(2,1)S(1)}, u32[]{:S(2)}, u32[]{:S(2)}) collective-permute-start(bf16[16,2048]{1,0:T(8,128)(2,1)S(1)} %slice.109), channel_id=1, source_target_pairs={{0,24},{8,0},{16,8},{24,16},{1,25},{9,1},{17,9},{25,17},{2,26},{10... | collective-permute-start | bytes 196616 | tf_op jit(solution)/shard_map/ppermute | solution.py:17
  26.0 21.2 %collective-permute-start.12 = (bf16[2,4,16,4096]{3,2,1,0:T(8,128)(2,1)S(1)}, bf16[2,4,16,4096]{3,2,1,0:T(8,128)(2,1)}, u32[]{:S(2)}, u32[]{:S(2)}) collective-permute-start(bf16[2,4,16,4096]{3,2,1,0:T(8,128)(2,1)S(1)} %pad_maximum_fusion.4), channel_id=1, source_target_pairs={{0,1},{1,0},{2,3},{3,2},{4,5},{5,4},{6,7},{7,6},{8,9},{9,8},{10,11... | collective-permute-start | bytes 3145736 | tf_op jit(solution)/shard_map/ppermute | solution.py:54
  30.0 14.3 %collective-permute-start.9 = (bf16[4,16,4096]{2,1,0:T(8,128)(2,1)}, bf16[4,16,4096]{2,1,0:T(8,128)(2,1)S(1)}, u32[]{:S(2)}, u32[]{:S(2)}) collective-permute-start(bf16[4,16,4096]{2,1,0:T(8,128)(2,1)} %get-tuple-element.7), channel_id=1, source_target_pairs={{0,2},{2,4},{4,6},{6,0},{1,3},{3,5},{5,7},{7,1},{8,10},{10,12},{12... | collective-permute-start | bytes 1572872 | tf_op jit(solution)/shard_map/ppermute | solution.py:17
  30.1 14.3 %collective-permute-start.8 = (bf16[4,16,4096]{2,1,0:T(8,128)(2,1)}, bf16[4,16,4096]{2,1,0:T(8,128)(2,1)S(1)}, u32[]{:S(2)}, u32[]{:S(2)}) collective-permute-start(bf16[4,16,4096]{2,1,0:T(8,128)(2,1)} %get-tuple-element.7), channel_id=1, source_target_pairs={{0,6},{2,0},{4,2},{6,4},{1,7},{3,1},{5,3},{7,5},{8,14},{10,8},{12,... | collective-permute-start | bytes 1572872 | tf_op jit(solution)/shard_map/ppermute | solution.py:17
  32.8 15.7 %collective-permute-start.14 = (bf16[4,16,4096]{2,1,0:T(8,128)(2,1)}, bf16[4,16,4096]{2,1,0:T(8,128)(2,1)}, u32[]{:S(2)}, u32[]{:S(2)}) collective-permute-start(bf16[4,16,4096]{2,1,0:T(8,128)(2,1)} %get-tuple-element.8), channel_id=1, source_target_pairs={{0,8},{8,16},{16,24},{24,0},{1,9},{9,17},{17,25},{25,1},{2,10},{10... | collective-permute-start | bytes 1572872 | tf_op jit(solution)/shard_map/ppermute | solution.py:17
  33.1 17.0 %collective-permute-start.13 = (bf16[4,16,4096]{2,1,0:T(8,128)(2,1)}, bf16[4,16,4096]{2,1,0:T(8,128)(2,1)}, u32[]{:S(2)}, u32[]{:S(2)}) collective-permute-start(bf16[4,16,4096]{2,1,0:T(8,128)(2,1)} %get-tuple-element.8), channel_id=1, source_target_pairs={{0,24},{8,0},{16,8},{24,16},{1,25},{9,1},{17,9},{25,17},{2,26},{10... | collective-permute-start | bytes 1572872 | tf_op jit(solution)/shard_map/ppermute | solution.py:17
  37.6 36.5 %all-to-all-start.1 = ((bf16[2,16,32,640]{3,1,0,2:T(8,128)(2,1)}), bf16[2,16,32,640]{3,1,0,2:T(8,128)(2,1)S(1)}, u32[]{:S(2)}, u32[]{:S(2)}) async-start(bf16[2,16,32,640]{3,1,0,2:T(8,128)(2,1)} %copy.39), calls=%async_computation.1 | async-start | bytes 2621440 | tf_op jit(solution)/shard_map/all_to_all | solution.py:60
  44.3 2.9 %copy-start.2 = (bf16[4,16,4096]{2,1,0:T(8,128)(2,1)}, bf16[4,16,4096]{2,1,0:T(8,128)(2,1)S(1)}, u32[]{:S(2)}) copy-start(bf16[4,16,4096]{2,1,0:T(8,128)(2,1)S(1)} %collective-permute-done.9) | copy-start | bytes 1572868
  44.3 21.6 %collective-permute-start.10 = (bf16[4,16,2048]{2,1,0:T(8,128)(2,1)S(1)}, bf16[4,16,2048]{2,1,0:T(8,128)(2,1)S(1)}, u32[]{:S(2)}, u32[]{:S(2)}) collective-permute-start(bf16[4,16,2048]{2,1,0:T(8,128)(2,1)S(1)} %slice.112), channel_id=1, source_target_pairs={{0,2},{2,4},{4,6},{6,0},{1,3},{3,5},{5,7},{7,1},{8,10},{10,12},{12... | collective-permute-start | bytes 786440 | tf_op jit(solution)/shard_map/ppermute | solution.py:17
  44.4 2.8 %copy-start.4 = (bf16[4,16,4096]{2,1,0:T(8,128)(2,1)}, bf16[4,16,4096]{2,1,0:T(8,128)(2,1)S(1)}, u32[]{:S(2)}) copy-start(bf16[4,16,4096]{2,1,0:T(8,128)(2,1)S(1)} %collective-permute-done.8) | copy-start | bytes 1572868
  44.4 21.4 %collective-permute-start.11 = (bf16[4,16,2048]{2,1,0:T(8,128)(2,1)S(1)}, bf16[4,16,2048]{2,1,0:T(8,128)(2,1)S(1)}, u32[]{:S(2)}, u32[]{:S(2)}) collective-permute-start(bf16[4,16,2048]{2,1,0:T(8,128)(2,1)S(1)} %slice.113), channel_id=1, source_target_pairs={{0,6},{2,0},{4,2},{6,4},{1,7},{3,1},{5,3},{7,5},{8,14},{10,8},{12,... | collective-permute-start | bytes 786440 | tf_op jit(solution)/shard_map/ppermute | solution.py:17
  49.4 17.2 %collective-permute-start.16 = (bf16[4,16,2048]{2,1,0:T(8,128)(2,1)S(1)}, bf16[4,16,2048]{2,1,0:T(8,128)(2,1)S(1)}, u32[]{:S(2)}, u32[]{:S(2)}) collective-permute-start(bf16[4,16,2048]{2,1,0:T(8,128)(2,1)S(1)} %slice.116), channel_id=1, source_target_pairs={{0,8},{8,16},{16,24},{24,0},{1,9},{9,17},{17,25},{25,1},{2,10},{10... | collective-permute-start | bytes 786440 | tf_op jit(solution)/shard_map/ppermute | solution.py:17
  51.1 18.5 %copy-start.3 = (bf16[4,16,4096]{2,1,0:T(8,128)(2,1)S(1)}, bf16[4,16,4096]{2,1,0:T(8,128)(2,1)}, u32[]{:S(2)}) copy-start(bf16[4,16,4096]{2,1,0:T(8,128)(2,1)} %copy-done.2) | copy-start | bytes 1572868
  51.1 18.5 %copy-start.5 = (bf16[4,16,4096]{2,1,0:T(8,128)(2,1)S(1)}, bf16[4,16,4096]{2,1,0:T(8,128)(2,1)}, u32[]{:S(2)}) copy-start(bf16[4,16,4096]{2,1,0:T(8,128)(2,1)} %copy-done.4) | copy-start | bytes 1572868
  51.1 15.5 %collective-permute-start.17 = (bf16[4,16,2048]{2,1,0:T(8,128)(2,1)S(1)}, bf16[4,16,2048]{2,1,0:T(8,128)(2,1)S(1)}, u32[]{:S(2)}, u32[]{:S(2)}) collective-permute-start(bf16[4,16,2048]{2,1,0:T(8,128)(2,1)S(1)} %slice.117), channel_id=1, source_target_pairs={{0,24},{8,0},{16,8},{24,16},{1,25},{9,1},{17,9},{25,17},{2,26},{10... | collective-permute-start | bytes 786440 | tf_op jit(solution)/shard_map/ppermute | solution.py:17
  67.8 11.2 %collective-permute-start.18 = (bf16[2,4,16,4096]{3,2,1,0:T(8,128)(2,1)}, bf16[2,4,16,4096]{3,2,1,0:T(8,128)(2,1)}, u32[]{:S(2)}, u32[]{:S(2)}) collective-permute-start(bf16[2,4,16,4096]{3,2,1,0:T(8,128)(2,1)} %pad_maximum_fusion.5), channel_id=1, source_target_pairs={{0,1},{1,0},{2,3},{3,2},{4,5},{5,4},{6,7},{7,6},{8,9},{9,8},{10,11... | collective-permute-start | bytes 3145736 | tf_op jit(solution)/shard_map/ppermute | solution.py:67
  74.0 6.2 %collective-permute-start.15 = (bf16[4,4,16,4096]{3,2,1,0:T(8,128)(2,1)}, bf16[4,4,16,4096]{3,2,1,0:T(8,128)(2,1)}, u32[]{:S(2)}, u32[]{:S(2)}) collective-permute-start(bf16[4,4,16,4096]{3,2,1,0:T(8,128)(2,1)} %get-tuple-element.23), channel_id=1, source_target_pairs={{0,1},{1,0},{2,3},{3,2},{4,5},{5,4},{6,7},{7,6},{8,9},{9,8},{10,11... | collective-permute-start | bytes 6291464 | tf_op jit(solution)/shard_map/ppermute | solution.py:65
  81.9 1.6 %copy-start = (bf16[1,4,4,16,4096]{4,3,2,1,0:T(8,128)(2,1)S(1)}, bf16[1,4,4,16,4096]{4,3,2,1,0:T(8,128)(2,1)}, u32[]{:S(2)}) copy-start(bf16[1,4,4,16,4096]{4,3,2,1,0:T(8,128)(2,1)} %get-tuple-element.22) | copy-start | bytes 6291460
  81.9 2.2 %copy-start.1 = (bf16[1,4,4,16,4096]{4,3,2,1,0:T(8,128)(2,1)S(1)}, bf16[1,4,4,16,4096]{4,3,2,1,0:T(8,128)(2,1)}, u32[]{:S(2)}) copy-start(bf16[1,4,4,16,4096]{4,3,2,1,0:T(8,128)(2,1)} %get-tuple-element.24) | copy-start | bytes 6291460
  (2 other events, 1.4 us)

commit v7 on v6

--- a/solution.py
+++ b/solution.py
@@ -65,13 +65,14 @@
     near_other = lax.ppermute(near, "core", CORE_PAIRS)
     far = jnp.stack([real_far, imag_far])
     far_other = lax.ppermute(far, "core", CORE_PAIRS)
-    parts = []
-    for part in range(2):
-        for src_first, src_near, src_far in ((first, near, far), (first_other, near_other, far_other)):
+    halves = []
+    for src_first, src_near, src_far in ((first, near, far), (first_other, near_other, far_other)):
+        parts = []
+        for part in range(2):
             parts.append(
                 jnp.stack([src_first[part], src_near[2 * part], src_far[part], src_near[2 * part + 1]])
             )
-    left = jnp.stack(parts).reshape(2 * pairs, local_g)
+        halves.append(jnp.stack(parts).reshape(pairs, local_g))
 
     all_bands = column[:, :, width].astype(jnp.int32)
     gap = lookup(all_bands[1], conduction_energy) - lookup(all_bands[0], valence_energy)
@@ -99,14 +100,20 @@
         imag_b = relative(scaled_imag, imag_order)
         real_b = relative(scaled_real, imag_order)
         imag_a = relative(scaled_imag, real_order)
-        right_real.append(jnp.concatenate([-real_a, -imag_b], axis=0))
-        right_imag.append(jnp.concatenate([-imag_a, real_b], axis=0))
+        right_real.append(jnp.stack([-real_a, -imag_b]))
+        right_imag.append(jnp.stack([-imag_a, real_b]))
     dims = (((0,), (0,)), ((), ()))
-    chi_real = lax.dot_general(left, jnp.stack(right_real, axis=1), dims, preferred_element_type=jnp.float32)
-    chi_imag = lax.dot_general(left, jnp.stack(right_imag, axis=1), dims, preferred_element_type=jnp.float32)
-    chi_real = chi_real.transpose(1, 0, 2)
-    chi_imag = chi_imag.transpose(1, 0, 2)
-    return chi_real.astype(jnp.bfloat16), chi_imag.astype(jnp.bfloat16)
+    span = pairs // ncore
+    outputs = []
+    for right in (right_real, right_imag):
+        right = jnp.stack(right, axis=2)
+        total = None
+        for core, half in enumerate(halves):
+            piece = right[:, core * span : (core + 1) * span].reshape(pairs, frequency.shape[0], width)
+            term = lax.dot_general(half, piece, dims, preferred_element_type=jnp.float32)
+            total = term if total is None else total + term
+        outputs.append(total.transpose(1, 0, 2).astype(jnp.bfloat16))
+    return tuple(outputs)
 
 
 def solution(mesh):

time: 109 us -> 124 us (1.14)
  matrix products: 22.6 us -> 36.9 us
    dot_general x2 -> x4, matrix products: 22.6 us -> 36.9 us  [on_device(): lax.dot_general(half, piece, dims, preferred_element_type=jnp.float32)]
    another operation x7 -> x10, other arithmetic: 6.32 us -> 7.08 us  [the longest x3 3.33 us: on_device(): halves.append(jnp.stack(parts).reshape(pairs, local_g))]
    unnamed x27 -> x25, local copies, waits for them, and re-layouts: 2.16 us -> 2.48 us
  transfers between devices with their start and end apart: 21 -> 21, of which waited for: 4 -> 4; matrix products, arithmetic and copies ran while one was open for 20% -> 32% of each run, Pallas kernels for 0% -> 0%
where the time goes in v7:
time: 124 us; the launch traced here: 123 us
  starting transfers between devices  40.3 us (32%)
  matrix products  36.9 us (30%)
  waiting for transfers between devices  14.6 us (12%)
  other arithmetic  14.5 us (12%)
  local copies, waits for them, and re-layouts  13.1 us (11%)
  between operations  3.76 us (3%)
    dot_general x4, matrix products, on_device(): lax.dot_general(half, piece, dims, preferred_element_type=jnp.float32)  36.9 us
    ppermute x16, starting transfers between devices, shift(): lax.ppermute(value, axis, [(i, (i + step) % size) for i in range(size)])  24.5 us
    ppermute x16, waiting for transfers between devices, shift(): lax.ppermute(value, axis, [(i, (i + step) % size) for i in range(size)])  14.6 us
    all_to_all x1, starting transfers between devices, on_device(): spread = lax.all_to_all(copies, 'row', 0, 0, tiled=True)  5.16 us
    all_to_all x1, starting transfers between devices, on_device(): lax.all_to_all(payload, cols, split_axis=2, concat_axis=1, tiled=True)  5.15 us
    ppermute x1, starting transfers between devices, on_device(): first_other = lax.ppermute(first, 'core', CORE_PAIRS)  3.51 us
    another operation x3, other arithmetic, on_device(): halves.append(jnp.stack(parts).reshape(pairs, local_g))  3.33 us
    another operation x1, other arithmetic, on_device(): near = jnp.stack([real_plus, real_minus, imag_plus, imag_minus])  3 us
  transfers between devices with their start and end apart: 21, of which 4 were waited for; matrix products, arithmetic and copies ran while one was open for 32% of the time, Pallas kernels for 0%

profile of v7, /device:TPU:1, one launch (start us, length us, event | category | flops | bytes accessed | tf_op | source)
XLA Modules:
  0.0 123.2 jit_solution(3305382764794819901)
XLA Ops:
  0.7 2.1 %collective-permute-start.1 = (bf16[16,4096]{1,0:T(8,128)(2,1)}, bf16[16,4096]{1,0:T(8,128)(2,1)S(1)}, u32[]{:S(2)}, u32[]{:S(2)}) collective-permute-start(bf16[16,4096]{1,0:T(8,128)(2,1)} %param.7), channel_id=1, source_target_pairs={{0,8},{8,16},{16,24},{24,0},{1,9},{9,17},{17,25},{25,1},{2,10},{10... | collective-permute-start | bytes 393224 | tf_op jit(solution)/shard_map/ppermute | solution.py:17
  2.8 1.4 %collective-permute-start = (bf16[16,4096]{1,0:T(8,128)(2,1)}, bf16[16,4096]{1,0:T(8,128)(2,1)S(1)}, u32[]{:S(2)}, u32[]{:S(2)}) collective-permute-start(bf16[16,4096]{1,0:T(8,128)(2,1)} %param.7), channel_id=1, source_target_pairs={{0,24},{8,0},{16,8},{24,16},{1,25},{9,1},{17,9},{25,17},{2,26},{10... | collective-permute-start | bytes 393224 | tf_op jit(solution)/shard_map/ppermute | solution.py:17
  4.1 1.4 %collective-permute-start.5 = (bf16[16,4096]{1,0:T(8,128)(2,1)}, bf16[16,4096]{1,0:T(8,128)(2,1)S(1)}, u32[]{:S(2)}, u32[]{:S(2)}) collective-permute-start(bf16[16,4096]{1,0:T(8,128)(2,1)} %param.8), channel_id=1, source_target_pairs={{0,2},{2,4},{4,6},{6,0},{1,3},{3,5},{5,7},{7,1},{8,10},{10,12},{12... | collective-permute-start | bytes 393224 | tf_op jit(solution)/shard_map/ppermute | solution.py:17
  5.5 1.4 %collective-permute-start.4 = (bf16[16,4096]{1,0:T(8,128)(2,1)}, bf16[16,4096]{1,0:T(8,128)(2,1)S(1)}, u32[]{:S(2)}, u32[]{:S(2)}) collective-permute-start(bf16[16,4096]{1,0:T(8,128)(2,1)} %param.8), channel_id=1, source_target_pairs={{0,6},{2,0},{4,2},{6,4},{1,7},{3,1},{5,3},{7,5},{8,14},{10,8},{12,... | collective-permute-start | bytes 393224 | tf_op jit(solution)/shard_map/ppermute | solution.py:17
  7.0 1.0 pad_maximum_fusion.11
  8.0 1.1 broadcast_in_dim.28
  9.1 5.2 %all-to-all-start = ((bf16[4,2,16,4096]{3,2,1,0:T(8,128)(2,1)}), bf16[4,2,16,4096]{3,2,1,0:T(8,128)(2,1)S(1)}, u32[]{:S(2)}, u32[]{:S(2)}) async-start(bf16[4,2,16,4096]{3,2,1,0:T(8,128)(2,1)} %broadcast_in_dim.28), calls=%async_computation | async-start | bytes 2097152 | tf_op jit(solution)/shard_map/all_to_all | solution.py:49
  17.5 2.7 %collective-permute-start.7 = (bf16[16,2048]{1,0:T(8,128)(2,1)S(1)}, bf16[16,2048]{1,0:T(8,128)(2,1)S(1)}, u32[]{:S(2)}, u32[]{:S(2)}) collective-permute-start(bf16[16,2048]{1,0:T(8,128)(2,1)S(1)} %slice.127), channel_id=1, source_target_pairs={{0,6},{2,0},{4,2},{6,4},{1,7},{3,1},{5,3},{7,5},{8,14},{10,8},{12,... | collective-permute-start | bytes 196616 | tf_op jit(solution)/shard_map/ppermute | solution.py:17
  20.4 2.7 %collective-permute-start.3 = (bf16[16,2048]{1,0:T(8,128)(2,1)S(1)}, bf16[16,2048]{1,0:T(8,128)(2,1)S(1)}, u32[]{:S(2)}, u32[]{:S(2)}) collective-permute-start(bf16[16,2048]{1,0:T(8,128)(2,1)S(1)} %slice.125), channel_id=1, source_target_pairs={{0,24},{8,0},{16,8},{24,16},{1,25},{9,1},{17,9},{25,17},{2,26},{10... | collective-permute-start | bytes 196616 | tf_op jit(solution)/shard_map/ppermute | solution.py:17
  26.0 3.5 %collective-permute-start.16 = (bf16[2,4,16,4096]{3,2,1,0:T(8,128)(2,1)S(1)}, bf16[2,4,16,4096]{3,2,1,0:T(8,128)(2,1)}, u32[]{:S(2)}, u32[]{:S(2)}) collective-permute-start(bf16[2,4,16,4096]{3,2,1,0:T(8,128)(2,1)S(1)} %pad_maximum_fusion.7), channel_id=1, source_target_pairs={{0,1},{1,0},{2,3},{3,2},{4,5},{5,4},{6,7},{7,6},{8,9},{9,8},{10,11... | collective-permute-start | bytes 3145736 | tf_op jit(solution)/shard_map/ppermute | solution.py:54
  30.1 2.7 %collective-permute-start.8 = (bf16[4,16,4096]{2,1,0:T(8,128)(2,1)}, bf16[4,16,4096]{2,1,0:T(8,128)(2,1)S(1)}, u32[]{:S(2)}, u32[]{:S(2)}) collective-permute-start(bf16[4,16,4096]{2,1,0:T(8,128)(2,1)} %get-tuple-element.7), channel_id=1, source_target_pairs={{0,6},{2,0},{4,2},{6,4},{1,7},{3,1},{5,3},{7,5},{8,14},{10,8},{12,... | collective-permute-start | bytes 1572872 | tf_op jit(solution)/shard_map/ppermute | solution.py:17
  33.1 2.7 %collective-permute-start.12 = (bf16[4,16,4096]{2,1,0:T(8,128)(2,1)}, bf16[4,16,4096]{2,1,0:T(8,128)(2,1)}, u32[]{:S(2)}, u32[]{:S(2)}) collective-permute-start(bf16[4,16,4096]{2,1,0:T(8,128)(2,1)} %get-tuple-element.8), channel_id=1, source_target_pairs={{0,24},{8,0},{16,8},{24,16},{1,25},{9,1},{17,9},{25,17},{2,26},{10... | collective-permute-start | bytes 1572872 | tf_op jit(solution)/shard_map/ppermute | solution.py:17
  36.0 1.5 %copy.49 = bf16[2,16,32,640]{3,1,0,2:T(8,128)(2,1)} copy(bf16[2,16,32,640]{3,2,1,0:T(8,128)(2,1)S(1)} %pad_maximum_fusion.4) | data formatting | bytes 2621440 | tf_op jit(solution)/shard_map/concatenate | solution.py:59
  37.5 5.2 %all-to-all-start.1 = ((bf16[2,16,32,640]{3,1,0,2:T(8,128)(2,1)}), bf16[2,16,32,640]{3,1,0,2:T(8,128)(2,1)S(1)}, u32[]{:S(2)}, u32[]{:S(2)}) async-start(bf16[2,16,32,640]{3,1,0,2:T(8,128)(2,1)} %copy.49), calls=%async_computation.1 | async-start | bytes 2621440 | tf_op jit(solution)/shard_map/all_to_all | solution.py:60
  42.8 1.5 %collective-permute-done.9 = bf16[4,16,4096]{2,1,0:T(8,128)(2,1)S(1)} collective-permute-done((bf16[4,16,4096]{2,1,0:T(8,128)(2,1)}, bf16[4,16,4096]{2,1,0:T(8,128)(2,1)S(1)}, u32[]{:S(2)}, u32[]{:S(2)}) %collective-permute-start.9) | collective-permute-done | bytes 524320 | tf_op jit(solution)/shard_map/ppermute | solution.py:17
  44.4 2.7 %collective-permute-start.11 = (bf16[4,16,2048]{2,1,0:T(8,128)(2,1)S(1)}, bf16[4,16,2048]{2,1,0:T(8,128)(2,1)S(1)}, u32[]{:S(2)}, u32[]{:S(2)}) collective-permute-start(bf16[4,16,2048]{2,1,0:T(8,128)(2,1)S(1)} %slice.129), channel_id=1, source_target_pairs={{0,6},{2,0},{4,2},{6,4},{1,7},{3,1},{5,3},{7,5},{8,14},{10,8},{12,... | collective-permute-start | bytes 786440 | tf_op jit(solution)/shard_map/ppermute | solution.py:17
  47.1 1.3 %fusion.29 = (bf16[1,4,16,4096]{3,2,1,0:T(8,128)(2,1)S(1)}, bf16[1,4,16,4096]{3,2,1,0:T(8,128)(2,1)S(1)}) fusion(bf16[2,4,16,4096]{3,2,1,0:T(8,128)(2,1)} %collective-permute-done.16), kind=kLoop, calls=%fused_computation.101 | loop fusion | bytes 2097152 | tf_op jit(solution)/shard_map/slice | solution.py:73
  48.4 1.0 slice.130
  50.1 1.0 slice.131
  51.1 3.3 %collective-permute-start.15 = (bf16[4,16,2048]{2,1,0:T(8,128)(2,1)S(1)}, bf16[4,16,2048]{2,1,0:T(8,128)(2,1)S(1)}, u32[]{:S(2)}, u32[]{:S(2)}) collective-permute-start(bf16[4,16,2048]{2,1,0:T(8,128)(2,1)S(1)} %slice.131), channel_id=1, source_target_pairs={{0,24},{8,0},{16,8},{24,16},{1,25},{9,1},{17,9},{25,17},{2,26},{10... | collective-permute-start | bytes 786440 | tf_op jit(solution)/shard_map/ppermute | solution.py:17
  54.4 11.4 %collective-permute-done.10 = bf16[4,16,2048]{2,1,0:T(8,128)(2,1)S(1)} collective-permute-done((bf16[4,16,2048]{2,1,0:T(8,128)(2,1)S(1)}, bf16[4,16,2048]{2,1,0:T(8,128)(2,1)S(1)}, u32[]{:S(2)}, u32[]{:S(2)}) %collective-permute-start.10) | collective-permute-done | bytes 262176 | tf_op jit(solution)/shard_map/ppermute | solution.py:17
  66.7 1.0 pad_maximum_fusion.8
  67.7 1.9 %collective-permute-start.18 = (bf16[2,4,16,4096]{3,2,1,0:T(8,128)(2,1)}, bf16[2,4,16,4096]{3,2,1,0:T(8,128)(2,1)}, u32[]{:S(2)}, u32[]{:S(2)}) collective-permute-start(bf16[2,4,16,4096]{3,2,1,0:T(8,128)(2,1)} %pad_maximum_fusion.8), channel_id=1, source_target_pairs={{0,1},{1,0},{2,3},{3,2},{4,5},{5,4},{6,7},{7,6},{8,9},{9,8},{10,11... | collective-permute-start | bytes 3145736 | tf_op jit(solution)/shard_map/ppermute | solution.py:67
  69.6 3.0 %pad_maximum_fusion.2 = (bf16[4,4,16,4096]{3,2,1,0:T(8,128)(2,1)}, bf16[1,4,4,16,4096]{4,3,2,1,0:T(8,128)(2,1)S(1)}, bf16[1,4,4,16,4096]{4,3,2,1,0:T(8,128)(2,1)S(1)}) fusion(bf16[1,4,16,4096]{3,2,1,0:T(8,128)(2,1)} %bitcast.16, bf16[1,4,16,4096]{3,2,1,0:T(8,128)(2,1)} %bitcast.14, bf16[1,4,16,4096]{3,2,1,0:T(8,128)(2,1)S(1)} %bitcast.126, ...), kind=kLoop, calls=%fused_computation.6 | loop fusion | flops 9437184 | bytes 10485760 | tf_op jit(solution)/shard_map/stack | solution.py:64
  72.6 2.4 %pad_maximum_fusion = bf16[2,4,4,16,4096]{4,3,2,1,0:T(8,128)(2,1)} fusion(bf16[1,4,4,16,4096]{4,3,2,1,0:T(8,128)(2,1)S(1)} %get-tuple-element.28, bf16[1,4,4,16,4096]{4,3,2,1,0:T(8,128)(2,1)S(1)} %get-tuple-element.27), kind=kLoop, calls=%fused_computation.4 | loop fusion | flops 2097152 | bytes 8388608 | tf_op jit(solution)/shard_map/stack | solution.py:75
  80.2 1.9 %copy-done = bf16[2,4,4,16,4096]{4,3,2,1,0:T(8,128)(2,1)S(1)} copy-done((bf16[2,4,4,16,4096]{4,3,2,1,0:T(8,128)(2,1)S(1)}, bf16[2,4,4,16,4096]{4,3,2,1,0:T(8,128)(2,1)}, u32[]{:S(2)}) %copy-start) | copy-done | bytes 4194328
  82.2 8.1 %fusion.34 = f32[4096,2,512]{2,0,1:T(8,128)} fusion(bf16[512,4096,1]{1,0,2:T(8,128)(2,1)S(1)} %bitcast.109, bf16[512,2,512]{2,0,1:T(8,128)(2,1)S(1)} %bitcast.131), kind=kOutput, calls=%fused_computation.106 | convolution fusion | flops 4294967296 | bytes 22020096 | tf_op jit(solution)/shard_map/dot_general | solution.py:113
  90.5 8.1 %fusion.33 = f32[4096,2,512]{2,0,1:T(8,128)} fusion(bf16[512,4096,1]{1,0,2:T(8,128)(2,1)S(1)} %bitcast.110, bf16[512,2,512]{2,0,1:T(8,128)(2,1)S(1)} %bitcast.130), kind=kOutput, calls=%fused_computation.105 | convolution fusion | flops 4294967296 | bytes 22020096 | tf_op jit(solution)/shard_map/dot_general | solution.py:113
  98.6 1.3 %fusion.30 = (bf16[1,4,16,4096]{3,2,1,0:T(8,128)(2,1)S(1)}, bf16[1,4,16,4096]{3,2,1,0:T(8,128)(2,1)S(1)}) fusion(bf16[2,4,16,4096]{3,2,1,0:T(8,128)(2,1)} %collective-permute-done.18), kind=kLoop, calls=%fused_computation.102 | loop fusion | bytes 2097152 | tf_op jit(solution)/shard_map/slice | solution.py:73
  99.9 1.7 %fusion.27 = (bf16[1,4,16,4096]{3,2,1,0:T(8,128)(2,1)S(1)}, bf16[1,4,16,4096]{3,2,1,0:T(8,128)(2,1)S(1)}, bf16[1,4,16,4096]{3,2,1,0:T(8,128)(2,1)S(1)}, bf16[1,4,16,4096]{3,2,1,0:T(8,128)(2,1)S(1)}) fusion(bf16[4,4,16,4096]{3,2,1,0:T(8,128)(2,1)} %collective-permute-done.17), kind=kLoop, calls=%fused_computation.99 | loop fusion | bytes 4194304 | tf_op jit(solution)/shard_map/slice | solution.py:73
  102.5 10.3 %fusion.1 = bf16[2,4096,512]{2,1,0:T(8,128)(2,1)} fusion(f32[4096,2,512]{2,0,1:T(8,128)} %fusion.34, bf16[512,4096,1]{1,0,2:T(8,128)(2,1)S(1)} %bitcast.111, bf16[512,2,512]{2,0,1:T(8,128)(2,1)S(1)} %bitcast.128), kind=kOutput, calls=%fused_computation.3 | convolution fusion | flops 4303355904 | bytes 30408704 | tf_op jit(solution)/shard_map/dot_general | solution.py:113
  112.8 10.3 %fusion = bf16[2,4096,512]{2,1,0:T(8,128)(2,1)} fusion(f32[4096,2,512]{2,0,1:T(8,128)} %fusion.33, bf16[512,4096,1]{1,0,2:T(8,128)(2,1)S(1)} %bitcast.112, bf16[512,2,512]{2,0,1:T(8,128)(2,1)S(1)} %bitcast.129), kind=kOutput, calls=%fused_computation.2 | convolution fusion | flops 4303355904 | bytes 30408704 | tf_op jit(solution)/shard_map/dot_general | solution.py:113
  (108 shorter events, 12.7 us)
Async XLA Ops:
  0.6 13.6 %copy-start.10 = (s32[16]{0:T(128)S(1)}, s32[16]{0:T(128)}, u32[]{:S(2)}) copy-start(s32[16]{0:T(128)} %param.9) | copy-start | bytes 196
  0.6 13.6 %copy-start.11 = (s32[16]{0:T(128)S(1)}, s32[16]{0:T(128)}, u32[]{:S(2)}) copy-start(s32[16]{0:T(128)} %param.10) | copy-start | bytes 196
  0.7 13.6 %copy-start.7 = (f32[2]{0:T(128)S(1)}, f32[2]{0:T(128)}, u32[]{:S(2)}) copy-start(f32[2]{0:T(128)} %param.13) | copy-start | bytes 28
  0.7 19.6 %collective-permute-start.1 = (bf16[16,4096]{1,0:T(8,128)(2,1)}, bf16[16,4096]{1,0:T(8,128)(2,1)S(1)}, u32[]{:S(2)}, u32[]{:S(2)}) collective-permute-start(bf16[16,4096]{1,0:T(8,128)(2,1)} %param.7), channel_id=1, source_target_pairs={{0,8},{8,16},{16,24},{24,0},{1,9},{9,17},{17,25},{25,1},{2,10},{10... | collective-permute-start | bytes 393224 | tf_op jit(solution)/shard_map/ppermute | solution.py:17
  2.8 17.6 %collective-permute-start = (bf16[16,4096]{1,0:T(8,128)(2,1)}, bf16[16,4096]{1,0:T(8,128)(2,1)S(1)}, u32[]{:S(2)}, u32[]{:S(2)}) collective-permute-start(bf16[16,4096]{1,0:T(8,128)(2,1)} %param.7), channel_id=1, source_target_pairs={{0,24},{8,0},{16,8},{24,16},{1,25},{9,1},{17,9},{25,17},{2,26},{10... | collective-permute-start | bytes 393224 | tf_op jit(solution)/shard_map/ppermute | solution.py:17
  4.1 13.3 %collective-permute-start.5 = (bf16[16,4096]{1,0:T(8,128)(2,1)}, bf16[16,4096]{1,0:T(8,128)(2,1)S(1)}, u32[]{:S(2)}, u32[]{:S(2)}) collective-permute-start(bf16[16,4096]{1,0:T(8,128)(2,1)} %param.8), channel_id=1, source_target_pairs={{0,2},{2,4},{4,6},{6,0},{1,3},{3,5},{5,7},{7,1},{8,10},{10,12},{12... | collective-permute-start | bytes 393224 | tf_op jit(solution)/shard_map/ppermute | solution.py:17
  5.5 12.0 %collective-permute-start.4 = (bf16[16,4096]{1,0:T(8,128)(2,1)}, bf16[16,4096]{1,0:T(8,128)(2,1)S(1)}, u32[]{:S(2)}, u32[]{:S(2)}) collective-permute-start(bf16[16,4096]{1,0:T(8,128)(2,1)} %param.8), channel_id=1, source_target_pairs={{0,6},{2,0},{4,2},{6,4},{1,7},{3,1},{5,3},{7,5},{8,14},{10,8},{12,... | collective-permute-start | bytes 393224 | tf_op jit(solution)/shard_map/ppermute | solution.py:17
  8.0 15.1 %copy-start.5 = (bf16[16,4096]{1,0:T(8,128)(2,1)S(1)}, bf16[16,4096]{1,0:T(8,128)(2,1)}, u32[]{:S(2)}) copy-start(bf16[16,4096]{1,0:T(8,128)(2,1)} %param.8) | copy-start | bytes 393220
  9.1 15.9 %copy-start.6 = (bf16[16,4096]{1,0:T(8,128)(2,1)S(1)}, bf16[16,4096]{1,0:T(8,128)(2,1)}, u32[]{:S(2)}) copy-start(bf16[16,4096]{1,0:T(8,128)(2,1)} %param.7) | copy-start | bytes 393220
  9.1 20.4 %all-to-all-start = ((bf16[4,2,16,4096]{3,2,1,0:T(8,128)(2,1)}), bf16[4,2,16,4096]{3,2,1,0:T(8,128)(2,1)S(1)}, u32[]{:S(2)}, u32[]{:S(2)}) async-start(bf16[4,2,16,4096]{3,2,1,0:T(8,128)(2,1)} %broadcast_in_dim.28), calls=%async_computation | async-start | bytes 2097152 | tf_op jit(solution)/shard_map/all_to_all | solution.py:49
  17.4 5.7 %collective-permute-start.6 = (bf16[16,2048]{1,0:T(8,128)(2,1)S(1)}, bf16[16,2048]{1,0:T(8,128)(2,1)S(1)}, u32[]{:S(2)}, u32[]{:S(2)}) collective-permute-start(bf16[16,2048]{1,0:T(8,128)(2,1)S(1)} %slice.126), channel_id=1, source_target_pairs={{0,2},{2,4},{4,6},{6,0},{1,3},{3,5},{5,7},{7,1},{8,10},{10,12},{12... | collective-permute-start | bytes 196616 | tf_op jit(solution)/shard_map/ppermute | solution.py:17
  17.5 5.6 %collective-permute-start.7 = (bf16[16,2048]{1,0:T(8,128)(2,1)S(1)}, bf16[16,2048]{1,0:T(8,128)(2,1)S(1)}, u32[]{:S(2)}, u32[]{:S(2)}) collective-permute-start(bf16[16,2048]{1,0:T(8,128)(2,1)S(1)} %slice.127), channel_id=1, source_target_pairs={{0,6},{2,0},{4,2},{6,4},{1,7},{3,1},{5,3},{7,5},{8,14},{10,8},{12,... | collective-permute-start | bytes 196616 | tf_op jit(solution)/shard_map/ppermute | solution.py:17
  20.3 4.7 %collective-permute-start.2 = (bf16[16,2048]{1,0:T(8,128)(2,1)S(1)}, bf16[16,2048]{1,0:T(8,128)(2,1)S(1)}, u32[]{:S(2)}, u32[]{:S(2)}) collective-permute-start(bf16[16,2048]{1,0:T(8,128)(2,1)S(1)} %slice.124), channel_id=1, source_target_pairs={{0,8},{8,16},{16,24},{24,0},{1,9},{9,17},{17,25},{25,1},{2,10},{10... | collective-permute-start | bytes 196616 | tf_op jit(solution)/shard_map/ppermute | solution.py:17
  20.4 4.6 %collective-permute-start.3 = (bf16[16,2048]{1,0:T(8,128)(2,1)S(1)}, bf16[16,2048]{1,0:T(8,128)(2,1)S(1)}, u32[]{:S(2)}, u32[]{:S(2)}) collective-permute-start(bf16[16,2048]{1,0:T(8,128)(2,1)S(1)} %slice.125), channel_id=1, source_target_pairs={{0,24},{8,0},{16,8},{24,16},{1,25},{9,1},{17,9},{25,17},{2,26},{10... | collective-permute-start | bytes 196616 | tf_op jit(solution)/shard_map/ppermute | solution.py:17
  26.0 21.2 %collective-permute-start.16 = (bf16[2,4,16,4096]{3,2,1,0:T(8,128)(2,1)S(1)}, bf16[2,4,16,4096]{3,2,1,0:T(8,128)(2,1)}, u32[]{:S(2)}, u32[]{:S(2)}) collective-permute-start(bf16[2,4,16,4096]{3,2,1,0:T(8,128)(2,1)S(1)} %pad_maximum_fusion.7), channel_id=1, source_target_pairs={{0,1},{1,0},{2,3},{3,2},{4,5},{5,4},{6,7},{7,6},{8,9},{9,8},{10,11... | collective-permute-start | bytes 3145736 | tf_op jit(solution)/shard_map/ppermute | solution.py:54
  30.0 14.3 %collective-permute-start.9 = (bf16[4,16,4096]{2,1,0:T(8,128)(2,1)}, bf16[4,16,4096]{2,1,0:T(8,128)(2,1)S(1)}, u32[]{:S(2)}, u32[]{:S(2)}) collective-permute-start(bf16[4,16,4096]{2,1,0:T(8,128)(2,1)} %get-tuple-element.7), channel_id=1, source_target_pairs={{0,2},{2,4},{4,6},{6,0},{1,3},{3,5},{5,7},{7,1},{8,10},{10,12},{12... | collective-permute-start | bytes 1572872 | tf_op jit(solution)/shard_map/ppermute | solution.py:17
  30.1 14.3 %collective-permute-start.8 = (bf16[4,16,4096]{2,1,0:T(8,128)(2,1)}, bf16[4,16,4096]{2,1,0:T(8,128)(2,1)S(1)}, u32[]{:S(2)}, u32[]{:S(2)}) collective-permute-start(bf16[4,16,4096]{2,1,0:T(8,128)(2,1)} %get-tuple-element.7), channel_id=1, source_target_pairs={{0,6},{2,0},{4,2},{6,4},{1,7},{3,1},{5,3},{7,5},{8,14},{10,8},{12,... | collective-permute-start | bytes 1572872 | tf_op jit(solution)/shard_map/ppermute | solution.py:17
  32.7 15.7 %collective-permute-start.13 = (bf16[4,16,4096]{2,1,0:T(8,128)(2,1)}, bf16[4,16,4096]{2,1,0:T(8,128)(2,1)}, u32[]{:S(2)}, u32[]{:S(2)}) collective-permute-start(bf16[4,16,4096]{2,1,0:T(8,128)(2,1)} %get-tuple-element.8), channel_id=1, source_target_pairs={{0,8},{8,16},{16,24},{24,0},{1,9},{9,17},{17,25},{25,1},{2,10},{10... | collective-permute-start | bytes 1572872 | tf_op jit(solution)/shard_map/ppermute | solution.py:17
  33.1 17.0 %collective-permute-start.12 = (bf16[4,16,4096]{2,1,0:T(8,128)(2,1)}, bf16[4,16,4096]{2,1,0:T(8,128)(2,1)}, u32[]{:S(2)}, u32[]{:S(2)}) collective-permute-start(bf16[4,16,4096]{2,1,0:T(8,128)(2,1)} %get-tuple-element.8), channel_id=1, source_target_pairs={{0,24},{8,0},{16,8},{24,16},{1,25},{9,1},{17,9},{25,17},{2,26},{10... | collective-permute-start | bytes 1572872 | tf_op jit(solution)/shard_map/ppermute | solution.py:17
  37.5 37.5 %all-to-all-start.1 = ((bf16[2,16,32,640]{3,1,0,2:T(8,128)(2,1)}), bf16[2,16,32,640]{3,1,0,2:T(8,128)(2,1)S(1)}, u32[]{:S(2)}, u32[]{:S(2)}) async-start(bf16[2,16,32,640]{3,1,0,2:T(8,128)(2,1)} %copy.49), calls=%async_computation.1 | async-start | bytes 2621440 | tf_op jit(solution)/shard_map/all_to_all | solution.py:60
  44.3 2.9 %copy-start.1 = (bf16[4,16,4096]{2,1,0:T(8,128)(2,1)}, bf16[4,16,4096]{2,1,0:T(8,128)(2,1)S(1)}, u32[]{:S(2)}) copy-start(bf16[4,16,4096]{2,1,0:T(8,128)(2,1)S(1)} %collective-permute-done.9) | copy-start | bytes 1572868
  44.3 21.6 %collective-permute-start.10 = (bf16[4,16,2048]{2,1,0:T(8,128)(2,1)S(1)}, bf16[4,16,2048]{2,1,0:T(8,128)(2,1)S(1)}, u32[]{:S(2)}, u32[]{:S(2)}) collective-permute-start(bf16[4,16,2048]{2,1,0:T(8,128)(2,1)S(1)} %slice.128), channel_id=1, source_target_pairs={{0,2},{2,4},{4,6},{6,0},{1,3},{3,5},{5,7},{7,1},{8,10},{10,12},{12... | collective-permute-start | bytes 786440 | tf_op jit(solution)/shard_map/ppermute | solution.py:17
  44.4 2.8 %copy-start.3 = (bf16[4,16,4096]{2,1,0:T(8,128)(2,1)}, bf16[4,16,4096]{2,1,0:T(8,128)(2,1)S(1)}, u32[]{:S(2)}) copy-start(bf16[4,16,4096]{2,1,0:T(8,128)(2,1)S(1)} %collective-permute-done.8) | copy-start | bytes 1572868
  44.4 21.4 %collective-permute-start.11 = (bf16[4,16,2048]{2,1,0:T(8,128)(2,1)S(1)}, bf16[4,16,2048]{2,1,0:T(8,128)(2,1)S(1)}, u32[]{:S(2)}, u32[]{:S(2)}) collective-permute-start(bf16[4,16,2048]{2,1,0:T(8,128)(2,1)S(1)} %slice.129), channel_id=1, source_target_pairs={{0,6},{2,0},{4,2},{6,4},{1,7},{3,1},{5,3},{7,5},{8,14},{10,8},{12,... | collective-permute-start | bytes 786440 | tf_op jit(solution)/shard_map/ppermute | solution.py:17
  49.4 17.2 %collective-permute-start.14 = (bf16[4,16,2048]{2,1,0:T(8,128)(2,1)S(1)}, bf16[4,16,2048]{2,1,0:T(8,128)(2,1)S(1)}, u32[]{:S(2)}, u32[]{:S(2)}) collective-permute-start(bf16[4,16,2048]{2,1,0:T(8,128)(2,1)S(1)} %slice.130), channel_id=1, source_target_pairs={{0,8},{8,16},{16,24},{24,0},{1,9},{9,17},{17,25},{25,1},{2,10},{10... | collective-permute-start | bytes 786440 | tf_op jit(solution)/shard_map/ppermute | solution.py:17
  51.1 18.5 %copy-start.2 = (bf16[4,16,4096]{2,1,0:T(8,128)(2,1)S(1)}, bf16[4,16,4096]{2,1,0:T(8,128)(2,1)}, u32[]{:S(2)}) copy-start(bf16[4,16,4096]{2,1,0:T(8,128)(2,1)} %copy-done.1) | copy-start | bytes 1572868
  51.1 18.5 %copy-start.4 = (bf16[4,16,4096]{2,1,0:T(8,128)(2,1)S(1)}, bf16[4,16,4096]{2,1,0:T(8,128)(2,1)}, u32[]{:S(2)}) copy-start(bf16[4,16,4096]{2,1,0:T(8,128)(2,1)} %copy-done.3) | copy-start | bytes 1572868
  51.1 15.5 %collective-permute-start.15 = (bf16[4,16,2048]{2,1,0:T(8,128)(2,1)S(1)}, bf16[4,16,2048]{2,1,0:T(8,128)(2,1)S(1)}, u32[]{:S(2)}, u32[]{:S(2)}) collective-permute-start(bf16[4,16,2048]{2,1,0:T(8,128)(2,1)S(1)} %slice.131), channel_id=1, source_target_pairs={{0,24},{8,0},{16,8},{24,16},{1,25},{9,1},{17,9},{25,17},{2,26},{10... | collective-permute-start | bytes 786440 | tf_op jit(solution)/shard_map/ppermute | solution.py:17
  67.7 30.9 %collective-permute-start.18 = (bf16[2,4,16,4096]{3,2,1,0:T(8,128)(2,1)}, bf16[2,4,16,4096]{3,2,1,0:T(8,128)(2,1)}, u32[]{:S(2)}, u32[]{:S(2)}) collective-permute-start(bf16[2,4,16,4096]{3,2,1,0:T(8,128)(2,1)} %pad_maximum_fusion.8), channel_id=1, source_target_pairs={{0,1},{1,0},{2,3},{3,2},{4,5},{5,4},{6,7},{7,6},{8,9},{9,8},{10,11... | collective-permute-start | bytes 3145736 | tf_op jit(solution)/shard_map/ppermute | solution.py:67
  72.6 27.3 %collective-permute-start.17 = (bf16[4,4,16,4096]{3,2,1,0:T(8,128)(2,1)}, bf16[4,4,16,4096]{3,2,1,0:T(8,128)(2,1)}, u32[]{:S(2)}, u32[]{:S(2)}) collective-permute-start(bf16[4,4,16,4096]{3,2,1,0:T(8,128)(2,1)} %get-tuple-element.26), channel_id=1, source_target_pairs={{0,1},{1,0},{2,3},{3,2},{4,5},{5,4},{6,7},{7,6},{8,9},{9,8},{10,11... | collective-permute-start | bytes 6291464 | tf_op jit(solution)/shard_map/ppermute | solution.py:65
  75.1 0.7 copy-start.9
  80.0 2.2 %copy-start = (bf16[2,4,4,16,4096]{4,3,2,1,0:T(8,128)(2,1)S(1)}, bf16[2,4,4,16,4096]{4,3,2,1,0:T(8,128)(2,1)}, u32[]{:S(2)}) copy-start(bf16[2,4,4,16,4096]{4,3,2,1,0:T(8,128)(2,1)} %pad_maximum_fusion) | copy-start | bytes 12582916
  (1 other events, 0.7 us)

commit v8 on v6

--- a/solution.py
+++ b/solution.py
@@ -18,13 +18,7 @@
 
 
 def ring_gather(block, axis):
-    half = block.shape[-1] // 2
-    from_minus = shift(block, axis, 1)
-    from_plus = shift(block, axis, -1)
-    far_first = shift(from_minus[..., :half], axis, 1)
-    far_second = shift(from_plus[..., half:], axis, -1)
-    far = jnp.concatenate([far_first, far_second], axis=-1)
-    return from_plus, far, from_minus
+    return shift(block, axis, -1), shift(block, axis, 2), shift(block, axis, 1)
 
 
 def on_device(

time: 109 us -> 124 us (1.14)
  waiting for transfers between devices: 14.6 us -> 31.2 us
    ppermute x16 -> x12, waiting for transfers between devices: 14.6 us -> 31.1 us  [shift(): lax.ppermute(value, axis, [(i, (i + step) % size) for i in range(size)])]
    ppermute x16 -> x12, starting transfers between devices: 24.5 us -> 20.7 us  [shift(): lax.ppermute(value, axis, [(i, (i + step) % size) for i in range(size)])]
    all_to_all x1, starting transfers between devices: 5.14 us -> 8.88 us  [on_device(): lax.all_to_all(payload, cols, split_axis=2, concat_axis=1, tiled=True)]
    slice x8 -> x0, local copies, waits for them, and re-layouts: 2 us -> none  [the longest x4 1 us: ring_gather(): far_first = shift(from_minus[..., :half], axis, 1)]
    unnamed x27 -> x23, local copies, waits for them, and re-layouts: 2.16 us -> 2.93 us
  transfers between devices with their start and end apart: 21 -> 17, of which waited for: 4 -> 5; matrix products, arithmetic and copies ran while one was open for 20% -> 16% of each run, Pallas kernels for 0% -> 0%
where the time goes in v8:
time: 124 us; the launch traced here: 123 us
  starting transfers between devices  40.1 us (32%)
  waiting for transfers between devices  31.2 us (25%)
  matrix products  22.6 us (18%)
  other arithmetic  14 us (11%)
  local copies, waits for them, and re-layouts  11.7 us (9%)
  between operations  3.66 us (3%)
    ppermute x12, waiting for transfers between devices, shift(): lax.ppermute(value, axis, [(i, (i + step) % size) for i in range(size)])  31.1 us
    ppermute x12, starting transfers between devices, shift(): lax.ppermute(value, axis, [(i, (i + step) % size) for i in range(size)])  20.7 us
    dot_general x1, matrix products, on_device(): lax.dot_general(left, jnp.stack(right_imag, axis=1), dims, preferred_elem...  11.3 us
    dot_general x1, matrix products, on_device(): lax.dot_general(left, jnp.stack(right_real, axis=1), dims, preferred_elem...  11.3 us
    all_to_all x1, starting transfers between devices, on_device(): lax.all_to_all(payload, cols, split_axis=2, concat_axis=1, tiled=True)  8.88 us
    another operation x3, other arithmetic, on_device(): left = jnp.stack(parts).reshape(2 * pairs, local_g)  6.29 us
    all_to_all x1, starting transfers between devices, on_device(): spread = lax.all_to_all(copies, 'row', 0, 0, tiled=True)  5.03 us
    ppermute x1, starting transfers between devices, on_device(): first_other = lax.ppermute(first, 'core', CORE_PAIRS)  3.3 us
  transfers between devices with their start and end apart: 17, of which 5 were waited for; matrix products, arithmetic and copies ran while one was open for 16% of the time, Pallas kernels for 0%

profile of v8, /device:TPU:1, one launch (start us, length us, event | category | flops | bytes accessed | tf_op | source)
XLA Modules:
  0.0 123.2 jit_solution(3373084487393192124)
XLA Ops:
  0.7 3.4 %collective-permute-start = (bf16[16,4096]{1,0:T(8,128)(2,1)}, bf16[16,4096]{1,0:T(8,128)(2,1)S(1)}, u32[]{:S(2)}, u32[]{:S(2)}) collective-permute-start(bf16[16,4096]{1,0:T(8,128)(2,1)} %param.7), channel_id=1, source_target_pairs={{0,24},{8,0},{16,8},{24,16},{1,25},{9,1},{17,9},{25,17},{2,26},{10... | collective-permute-start | bytes 393224 | tf_op jit(solution)/shard_map/ppermute | solution.py:17
  4.1 2.7 %collective-permute-start.3 = (bf16[16,4096]{1,0:T(8,128)(2,1)}, bf16[16,4096]{1,0:T(8,128)(2,1)S(1)}, u32[]{:S(2)}, u32[]{:S(2)}) collective-permute-start(bf16[16,4096]{1,0:T(8,128)(2,1)} %param.8), channel_id=1, source_target_pairs={{0,6},{2,0},{4,2},{6,4},{1,7},{3,1},{5,3},{7,5},{8,14},{10,8},{12,... | collective-permute-start | bytes 393224 | tf_op jit(solution)/shard_map/ppermute | solution.py:17
  6.8 1.6 %collective-permute-start.4 = (bf16[16,4096]{1,0:T(8,128)(2,1)}, bf16[16,4096]{1,0:T(8,128)(2,1)S(1)}, u32[]{:S(2)}, u32[]{:S(2)}) collective-permute-start(bf16[16,4096]{1,0:T(8,128)(2,1)} %param.8), channel_id=1, source_target_pairs={{0,4},{2,6},{4,0},{6,2},{1,5},{3,7},{5,1},{7,3},{8,12},{10,14},{12... | collective-permute-start | bytes 393224 | tf_op jit(solution)/shard_map/ppermute | solution.py:17
  8.4 1.0 pad_maximum_fusion.8
  9.4 1.1 broadcast_in_dim.28
  10.5 5.0 %all-to-all-start = ((bf16[4,2,16,4096]{3,2,1,0:T(8,128)(2,1)}), bf16[4,2,16,4096]{3,2,1,0:T(8,128)(2,1)S(1)}, u32[]{:S(2)}, u32[]{:S(2)}) async-start(bf16[4,2,16,4096]{3,2,1,0:T(8,128)(2,1)} %broadcast_in_dim.28), calls=%async_computation | async-start | bytes 2097152 | tf_op jit(solution)/shard_map/all_to_all | solution.py:43
  18.8 1.8 %collective-permute-start.1 = (bf16[16,4096]{1,0:T(8,128)(2,1)S(1)}, bf16[16,4096]{1,0:T(8,128)(2,1)S(1)}, u32[]{:S(2)}, u32[]{:S(2)}) collective-permute-start(bf16[16,4096]{1,0:T(8,128)(2,1)S(1)} %copy-done.5), channel_id=1, source_target_pairs={{0,16},{8,24},{16,0},{24,8},{1,17},{9,25},{17,1},{25,9},{2,18},{10... | collective-permute-start | bytes 393224 | tf_op jit(solution)/shard_map/ppermute | solution.py:17
  20.7 0.9 fusion.29
  21.6 2.7 %collective-permute-done.1 = bf16[16,4096]{1,0:T(8,128)(2,1)S(1)} collective-permute-done((bf16[16,4096]{1,0:T(8,128)(2,1)S(1)}, bf16[16,4096]{1,0:T(8,128)(2,1)S(1)}, u32[]{:S(2)}, u32[]{:S(2)}) %collective-permute-start.1) | collective-permute-done | bytes 131104 | tf_op jit(solution)/shard_map/ppermute | solution.py:17
  24.2 0.9 fusion.30
  25.2 3.3 %collective-permute-start.9 = (bf16[2,4,16,4096]{3,2,1,0:T(8,128)(2,1)S(1)}, bf16[2,4,16,4096]{3,2,1,0:T(8,128)(2,1)}, u32[]{:S(2)}, u32[]{:S(2)}) collective-permute-start(bf16[2,4,16,4096]{3,2,1,0:T(8,128)(2,1)S(1)} %pad_maximum_fusion.4), channel_id=1, source_target_pairs={{0,1},{1,0},{2,3},{3,2},{4,5},{5,4},{6,7},{7,6},{8,9},{9,8},{10,11... | collective-permute-start | bytes 3145736 | tf_op jit(solution)/shard_map/ppermute | solution.py:48
  29.1 1.7 %collective-permute-start.8 = (bf16[4,16,4096]{2,1,0:T(8,128)(2,1)}, bf16[4,16,4096]{2,1,0:T(8,128)(2,1)}, u32[]{:S(2)}, u32[]{:S(2)}) collective-permute-start(bf16[4,16,4096]{2,1,0:T(8,128)(2,1)} %get-tuple-element.7), channel_id=1, source_target_pairs={{0,2},{2,4},{4,6},{6,0},{1,3},{3,5},{5,7},{7,1},{8,10},{10,12},{12... | collective-permute-start | bytes 1572872 | tf_op jit(solution)/shard_map/ppermute | solution.py:17
  30.8 0.9 collective-permute-start.7
  31.7 1.6 %collective-permute-start.6 = (bf16[4,16,4096]{2,1,0:T(8,128)(2,1)}, bf16[4,16,4096]{2,1,0:T(8,128)(2,1)}, u32[]{:S(2)}, u32[]{:S(2)}) collective-permute-start(bf16[4,16,4096]{2,1,0:T(8,128)(2,1)} %get-tuple-element.7), channel_id=1, source_target_pairs={{0,6},{2,0},{4,2},{6,4},{1,7},{3,1},{5,3},{7,5},{8,14},{10,8},{12,... | collective-permute-start | bytes 1572872 | tf_op jit(solution)/shard_map/ppermute | solution.py:17
  33.5 1.5 %copy.39 = bf16[2,16,32,640]{3,1,0,2:T(8,128)(2,1)} copy(bf16[2,16,32,640]{3,2,1,0:T(8,128)(2,1)S(1)} %pad_maximum_fusion.3) | data formatting | bytes 2621440 | tf_op jit(solution)/shard_map/concatenate | solution.py:53
  35.1 8.9 %all-to-all-start.1 = ((bf16[2,16,32,640]{3,1,0,2:T(8,128)(2,1)}), bf16[2,16,32,640]{3,1,0,2:T(8,128)(2,1)S(1)}, u32[]{:S(2)}, u32[]{:S(2)}) async-start(bf16[2,16,32,640]{3,1,0,2:T(8,128)(2,1)} %copy.39), calls=%async_computation.1 | async-start | bytes 2621440 | tf_op jit(solution)/shard_map/all_to_all | solution.py:54
  44.0 3.0 %collective-permute-start.13 = (bf16[4,16,4096]{2,1,0:T(8,128)(2,1)}, bf16[4,16,4096]{2,1,0:T(8,128)(2,1)S(1)}, u32[]{:S(2)}, u32[]{:S(2)}) collective-permute-start(bf16[4,16,4096]{2,1,0:T(8,128)(2,1)} %get-tuple-element.8), channel_id=1, source_target_pairs={{0,16},{8,24},{16,0},{24,8},{1,17},{9,25},{17,1},{25,9},{2,18},{10... | collective-permute-start | bytes 1572872 | tf_op jit(solution)/shard_map/ppermute | solution.py:17
  47.4 14.4 %collective-permute-done.7 = bf16[4,16,4096]{2,1,0:T(8,128)(2,1)S(1)} collective-permute-done((bf16[4,16,4096]{2,1,0:T(8,128)(2,1)}, bf16[4,16,4096]{2,1,0:T(8,128)(2,1)S(1)}, u32[]{:S(2)}, u32[]{:S(2)}) %collective-permute-start.7) | collective-permute-done | bytes 524320 | tf_op jit(solution)/shard_map/ppermute | solution.py:17
  62.6 3.6 %collective-permute-start.10 = (bf16[4,16,4096]{2,1,0:T(8,128)(2,1)}, bf16[4,16,4096]{2,1,0:T(8,128)(2,1)S(1)}, u32[]{:S(2)}, u32[]{:S(2)}) collective-permute-start(bf16[4,16,4096]{2,1,0:T(8,128)(2,1)} %get-tuple-element.8), channel_id=1, source_target_pairs={{0,24},{8,0},{16,8},{24,16},{1,25},{9,1},{17,9},{25,17},{2,26},{10... | collective-permute-start | bytes 1572872 | tf_op jit(solution)/shard_map/ppermute | solution.py:17
  66.2 1.3 %fusion.34 = (bf16[1,4,16,4096]{3,2,1,0:T(8,128)(2,1)S(1)}, bf16[1,4,16,4096]{3,2,1,0:T(8,128)(2,1)S(1)}) fusion(bf16[2,4,16,4096]{3,2,1,0:T(8,128)(2,1)} %collective-permute-done.9), kind=kLoop, calls=%fused_computation.95 | loop fusion | bytes 2097152 | tf_op jit(solution)/shard_map/slice | solution.py:66
  67.5 5.4 %collective-permute-done.13 = bf16[4,16,4096]{2,1,0:T(8,128)(2,1)S(1)} collective-permute-done((bf16[4,16,4096]{2,1,0:T(8,128)(2,1)}, bf16[4,16,4096]{2,1,0:T(8,128)(2,1)S(1)}, u32[]{:S(2)}, u32[]{:S(2)}) %collective-permute-start.13) | collective-permute-done | bytes 524320 | tf_op jit(solution)/shard_map/ppermute | solution.py:17
  73.0 1.1 pad_maximum_fusion.5
  74.1 1.3 %collective-permute-start.14 = (bf16[2,4,16,4096]{3,2,1,0:T(8,128)(2,1)}, bf16[2,4,16,4096]{3,2,1,0:T(8,128)(2,1)}, u32[]{:S(2)}, u32[]{:S(2)}) collective-permute-start(bf16[2,4,16,4096]{3,2,1,0:T(8,128)(2,1)} %pad_maximum_fusion.5), channel_id=1, source_target_pairs={{0,1},{1,0},{2,3},{3,2},{4,5},{5,4},{6,7},{7,6},{8,9},{9,8},{10,11... | collective-permute-start | bytes 3145736 | tf_op jit(solution)/shard_map/ppermute | solution.py:61
  75.4 8.6 %collective-permute-done.11 = bf16[4,16,4096]{2,1,0:T(8,128)(2,1)S(1)} collective-permute-done((bf16[4,16,4096]{2,1,0:T(8,128)(2,1)}, bf16[4,16,4096]{2,1,0:T(8,128)(2,1)S(1)}, u32[]{:S(2)}, u32[]{:S(2)}) %collective-permute-start.11) | collective-permute-done | bytes 524320 | tf_op jit(solution)/shard_map/ppermute | solution.py:17
  84.0 4.6 %maximum_bitcast_fusion = (bf16[1,4,4,16,4096]{4,3,2,1,0:T(8,128)(2,1)}, bf16[4,4,16,4096]{3,2,1,0:T(8,128)(2,1)}, bf16[1,4,4,16,4096]{4,3,2,1,0:T(8,128)(2,1)}) fusion(bf16[1,4,16,4096]{3,2,1,0:T(8,128)(2,1)} %bitcast.12, bf16[1,4,16,4096]{3,2,1,0:T(8,128)(2,1)S(1)} %bitcast.99, bf16[1,4,16,4096]{3,2,1,0:T(8,128)(2,1)} %bitcast.10, ...), kind=kLoop, calls=%fused_computation.6 | loop fusion | flops 9437184 | bytes 10485760 | tf_op jit(solution)/shard_map/stack | solution.py:68
  88.6 0.9 collective-permute-start.12
  94.4 1.3 %fusion.35 = (bf16[1,4,16,4096]{3,2,1,0:T(8,128)(2,1)S(1)}, bf16[1,4,16,4096]{3,2,1,0:T(8,128)(2,1)S(1)}) fusion(bf16[2,4,16,4096]{3,2,1,0:T(8,128)(2,1)} %collective-permute-done.14), kind=kLoop, calls=%fused_computation.96 | loop fusion | bytes 2097152 | tf_op jit(solution)/shard_map/slice | solution.py:66
  95.7 1.7 %fusion.32 = (bf16[1,4,16,4096]{3,2,1,0:T(8,128)(2,1)S(1)}, bf16[1,4,16,4096]{3,2,1,0:T(8,128)(2,1)S(1)}, bf16[1,4,16,4096]{3,2,1,0:T(8,128)(2,1)S(1)}, bf16[1,4,16,4096]{3,2,1,0:T(8,128)(2,1)S(1)}) fusion(bf16[4,4,16,4096]{3,2,1,0:T(8,128)(2,1)} %collective-permute-done.12), kind=kLoop, calls=%fused_computation.93 | loop fusion | bytes 4194304 | tf_op jit(solution)/shard_map/slice | solution.py:66
  97.9 1.0 copy-done
  99.5 1.1 pad_maximum_fusion
  100.6 11.3 %convert_bitcast_fusion = bf16[2,4096,512]{2,1,0:T(8,128)(2,1)} fusion(bf16[1024,4096,1]{1,0,2:T(8,128)(2,1)S(1)} %bitcast.89, bf16[1024,1,512]{2,0,1:T(8,128)(2,1)S(1)} %maximum_bitcast_fusion.6, bf16[1024,1,512]{2,0,1:T(8,128)(2,1)S(1)} %maximum_bitcast_fusion.5), kind=kOutput, calls=%fused_computation.1 | convolution fusion | flops 8598323200 | bytes 18874368 | tf_op jit(solution)/shard_map/dot_general | solution.py:100
  112.0 11.3 %convert_bitcast_fusion.1 = bf16[2,4096,512]{2,1,0:T(8,128)(2,1)} fusion(bf16[1024,4096,1]{1,0,2:T(8,128)(2,1)S(1)} %bitcast.90, bf16[1024,1,512]{2,0,1:T(8,128)(2,1)S(1)} %maximum_bitcast_fusion.4, bf16[1024,1,512]{2,0,1:T(8,128)(2,1)S(1)} %maximum_bitcast_fusion.3), kind=kOutput, calls=%fused_computation.2 | convolution fusion | flops 8598323200 | bytes 18874368 | tf_op jit(solution)/shard_map/dot_general | solution.py:99
  (81 shorter events, 8.8 us)
Async XLA Ops:
  0.6 18.2 %copy-start.5 = (bf16[16,4096]{1,0:T(8,128)(2,1)S(1)}, bf16[16,4096]{1,0:T(8,128)(2,1)}, u32[]{:S(2)}) copy-start(bf16[16,4096]{1,0:T(8,128)(2,1)} %param.7) | copy-start | bytes 393220
  0.6 20.0 %copy-start.4 = (bf16[16,4096]{1,0:T(8,128)(2,1)S(1)}, bf16[16,4096]{1,0:T(8,128)(2,1)}, u32[]{:S(2)}) copy-start(bf16[16,4096]{1,0:T(8,128)(2,1)} %param.8) | copy-start | bytes 393220
  0.7 14.9 %copy-start.9 = (s32[16]{0:T(128)S(1)}, s32[16]{0:T(128)}, u32[]{:S(2)}) copy-start(s32[16]{0:T(128)} %param.9) | copy-start | bytes 196
  0.7 14.9 %copy-start.10 = (s32[16]{0:T(128)S(1)}, s32[16]{0:T(128)}, u32[]{:S(2)}) copy-start(s32[16]{0:T(128)} %param.10) | copy-start | bytes 196
  0.7 14.9 %copy-start.6 = (f32[2]{0:T(128)S(1)}, f32[2]{0:T(128)}, u32[]{:S(2)}) copy-start(f32[2]{0:T(128)} %param.13) | copy-start | bytes 28
  0.7 20.9 %collective-permute-start = (bf16[16,4096]{1,0:T(8,128)(2,1)}, bf16[16,4096]{1,0:T(8,128)(2,1)S(1)}, u32[]{:S(2)}, u32[]{:S(2)}) collective-permute-start(bf16[16,4096]{1,0:T(8,128)(2,1)} %param.7), channel_id=1, source_target_pairs={{0,24},{8,0},{16,8},{24,16},{1,25},{9,1},{17,9},{25,17},{2,26},{10... | collective-permute-start | bytes 393224 | tf_op jit(solution)/shard_map/ppermute | solution.py:17
  4.1 17.5 %collective-permute-start.2 = (bf16[16,4096]{1,0:T(8,128)(2,1)}, bf16[16,4096]{1,0:T(8,128)(2,1)S(1)}, u32[]{:S(2)}, u32[]{:S(2)}) collective-permute-start(bf16[16,4096]{1,0:T(8,128)(2,1)} %param.7), channel_id=1, source_target_pairs={{0,8},{8,16},{16,24},{24,0},{1,9},{9,17},{17,25},{25,1},{2,10},{10... | collective-permute-start | bytes 393224 | tf_op jit(solution)/shard_map/ppermute | solution.py:17
  4.1 14.8 %collective-permute-start.3 = (bf16[16,4096]{1,0:T(8,128)(2,1)}, bf16[16,4096]{1,0:T(8,128)(2,1)S(1)}, u32[]{:S(2)}, u32[]{:S(2)}) collective-permute-start(bf16[16,4096]{1,0:T(8,128)(2,1)} %param.8), channel_id=1, source_target_pairs={{0,6},{2,0},{4,2},{6,4},{1,7},{3,1},{5,3},{7,5},{8,14},{10,8},{12,... | collective-permute-start | bytes 393224 | tf_op jit(solution)/shard_map/ppermute | solution.py:17
  6.8 13.9 %collective-permute-start.5 = (bf16[16,4096]{1,0:T(8,128)(2,1)}, bf16[16,4096]{1,0:T(8,128)(2,1)S(1)}, u32[]{:S(2)}, u32[]{:S(2)}) collective-permute-start(bf16[16,4096]{1,0:T(8,128)(2,1)} %param.8), channel_id=1, source_target_pairs={{0,2},{2,4},{4,6},{6,0},{1,3},{3,5},{5,7},{7,1},{8,10},{10,12},{12... | collective-permute-start | bytes 393224 | tf_op jit(solution)/shard_map/ppermute | solution.py:17
  6.8 13.9 %collective-permute-start.4 = (bf16[16,4096]{1,0:T(8,128)(2,1)}, bf16[16,4096]{1,0:T(8,128)(2,1)S(1)}, u32[]{:S(2)}, u32[]{:S(2)}) collective-permute-start(bf16[16,4096]{1,0:T(8,128)(2,1)} %param.8), channel_id=1, source_target_pairs={{0,4},{2,6},{4,0},{6,2},{1,5},{3,7},{5,1},{7,3},{8,12},{10,14},{12... | collective-permute-start | bytes 393224 | tf_op jit(solution)/shard_map/ppermute | solution.py:17
  10.5 18.1 %all-to-all-start = ((bf16[4,2,16,4096]{3,2,1,0:T(8,128)(2,1)}), bf16[4,2,16,4096]{3,2,1,0:T(8,128)(2,1)S(1)}, u32[]{:S(2)}, u32[]{:S(2)}) async-start(bf16[4,2,16,4096]{3,2,1,0:T(8,128)(2,1)} %broadcast_in_dim.28), calls=%async_computation | async-start | bytes 2097152 | tf_op jit(solution)/shard_map/all_to_all | solution.py:43
  18.8 5.4 %collective-permute-start.1 = (bf16[16,4096]{1,0:T(8,128)(2,1)S(1)}, bf16[16,4096]{1,0:T(8,128)(2,1)S(1)}, u32[]{:S(2)}, u32[]{:S(2)}) collective-permute-start(bf16[16,4096]{1,0:T(8,128)(2,1)S(1)} %copy-done.5), channel_id=1, source_target_pairs={{0,16},{8,24},{16,0},{24,8},{1,17},{9,25},{17,1},{25,9},{2,18},{10... | collective-permute-start | bytes 393224 | tf_op jit(solution)/shard_map/ppermute | solution.py:17
  25.2 21.8 %collective-permute-start.9 = (bf16[2,4,16,4096]{3,2,1,0:T(8,128)(2,1)S(1)}, bf16[2,4,16,4096]{3,2,1,0:T(8,128)(2,1)}, u32[]{:S(2)}, u32[]{:S(2)}) collective-permute-start(bf16[2,4,16,4096]{3,2,1,0:T(8,128)(2,1)S(1)} %pad_maximum_fusion.4), channel_id=1, source_target_pairs={{0,1},{1,0},{2,3},{3,2},{4,5},{5,4},{6,7},{7,6},{8,9},{9,8},{10,11... | collective-permute-start | bytes 3145736 | tf_op jit(solution)/shard_map/ppermute | solution.py:48
  29.1 46.3 %collective-permute-start.8 = (bf16[4,16,4096]{2,1,0:T(8,128)(2,1)}, bf16[4,16,4096]{2,1,0:T(8,128)(2,1)}, u32[]{:S(2)}, u32[]{:S(2)}) collective-permute-start(bf16[4,16,4096]{2,1,0:T(8,128)(2,1)} %get-tuple-element.7), channel_id=1, source_target_pairs={{0,2},{2,4},{4,6},{6,0},{1,3},{3,5},{5,7},{7,1},{8,10},{10,12},{12... | collective-permute-start | bytes 1572872 | tf_op jit(solution)/shard_map/ppermute | solution.py:17
  30.8 31.0 %collective-permute-start.7 = (bf16[4,16,4096]{2,1,0:T(8,128)(2,1)}, bf16[4,16,4096]{2,1,0:T(8,128)(2,1)S(1)}, u32[]{:S(2)}, u32[]{:S(2)}) collective-permute-start(bf16[4,16,4096]{2,1,0:T(8,128)(2,1)} %get-tuple-element.7), channel_id=1, source_target_pairs={{0,4},{2,6},{4,0},{6,2},{1,5},{3,7},{5,1},{7,3},{8,12},{10,14},{12... | collective-permute-start | bytes 1572872 | tf_op jit(solution)/shard_map/ppermute | solution.py:17
  31.7 43.8 %collective-permute-start.6 = (bf16[4,16,4096]{2,1,0:T(8,128)(2,1)}, bf16[4,16,4096]{2,1,0:T(8,128)(2,1)}, u32[]{:S(2)}, u32[]{:S(2)}) collective-permute-start(bf16[4,16,4096]{2,1,0:T(8,128)(2,1)} %get-tuple-element.7), channel_id=1, source_target_pairs={{0,6},{2,0},{4,2},{6,4},{1,7},{3,1},{5,3},{7,5},{8,14},{10,8},{12,... | collective-permute-start | bytes 1572872 | tf_op jit(solution)/shard_map/ppermute | solution.py:17
  35.1 54.4 %all-to-all-start.1 = ((bf16[2,16,32,640]{3,1,0,2:T(8,128)(2,1)}), bf16[2,16,32,640]{3,1,0,2:T(8,128)(2,1)S(1)}, u32[]{:S(2)}, u32[]{:S(2)}) async-start(bf16[2,16,32,640]{3,1,0,2:T(8,128)(2,1)} %copy.39), calls=%async_computation.1 | async-start | bytes 2621440 | tf_op jit(solution)/shard_map/all_to_all | solution.py:54
  44.0 29.0 %collective-permute-start.13 = (bf16[4,16,4096]{2,1,0:T(8,128)(2,1)}, bf16[4,16,4096]{2,1,0:T(8,128)(2,1)S(1)}, u32[]{:S(2)}, u32[]{:S(2)}) collective-permute-start(bf16[4,16,4096]{2,1,0:T(8,128)(2,1)} %get-tuple-element.8), channel_id=1, source_target_pairs={{0,16},{8,24},{16,0},{24,8},{1,17},{9,25},{17,1},{25,9},{2,18},{10... | collective-permute-start | bytes 1572872 | tf_op jit(solution)/shard_map/ppermute | solution.py:17
  47.0 36.9 %collective-permute-start.11 = (bf16[4,16,4096]{2,1,0:T(8,128)(2,1)}, bf16[4,16,4096]{2,1,0:T(8,128)(2,1)S(1)}, u32[]{:S(2)}, u32[]{:S(2)}) collective-permute-start(bf16[4,16,4096]{2,1,0:T(8,128)(2,1)} %get-tuple-element.8), channel_id=1, source_target_pairs={{0,8},{8,16},{16,24},{24,0},{1,9},{9,17},{17,25},{25,1},{2,10},{10... | collective-permute-start | bytes 1572872 | tf_op jit(solution)/shard_map/ppermute | solution.py:17
  61.8 0.8 copy-start.2
  62.6 21.4 %collective-permute-start.10 = (bf16[4,16,4096]{2,1,0:T(8,128)(2,1)}, bf16[4,16,4096]{2,1,0:T(8,128)(2,1)S(1)}, u32[]{:S(2)}, u32[]{:S(2)}) collective-permute-start(bf16[4,16,4096]{2,1,0:T(8,128)(2,1)} %get-tuple-element.8), channel_id=1, source_target_pairs={{0,24},{8,0},{16,8},{24,16},{1,25},{9,1},{17,9},{25,17},{2,26},{10... | collective-permute-start | bytes 1572872 | tf_op jit(solution)/shard_map/ppermute | solution.py:17
  66.2 6.8 %copy-start.3 = (bf16[4,16,4096]{2,1,0:T(8,128)(2,1)S(1)}, bf16[4,16,4096]{2,1,0:T(8,128)(2,1)}, u32[]{:S(2)}) copy-start(bf16[4,16,4096]{2,1,0:T(8,128)(2,1)} %copy-done.2) | copy-start | bytes 1572868
  74.1 20.3 %collective-permute-start.14 = (bf16[2,4,16,4096]{3,2,1,0:T(8,128)(2,1)}, bf16[2,4,16,4096]{3,2,1,0:T(8,128)(2,1)}, u32[]{:S(2)}, u32[]{:S(2)}) collective-permute-start(bf16[2,4,16,4096]{3,2,1,0:T(8,128)(2,1)} %pad_maximum_fusion.5), channel_id=1, source_target_pairs={{0,1},{1,0},{2,3},{3,2},{4,5},{5,4},{6,7},{7,6},{8,9},{9,8},{10,11... | collective-permute-start | bytes 3145736 | tf_op jit(solution)/shard_map/ppermute | solution.py:61
  88.6 7.1 %collective-permute-start.12 = (bf16[4,4,16,4096]{3,2,1,0:T(8,128)(2,1)}, bf16[4,4,16,4096]{3,2,1,0:T(8,128)(2,1)}, u32[]{:S(2)}, u32[]{:S(2)}) collective-permute-start(bf16[4,4,16,4096]{3,2,1,0:T(8,128)(2,1)} %get-tuple-element.23), channel_id=1, source_target_pairs={{0,1},{1,0},{2,3},{3,2},{4,5},{5,4},{6,7},{7,6},{8,9},{9,8},{10,11... | collective-permute-start | bytes 6291464 | tf_op jit(solution)/shard_map/ppermute | solution.py:59
  89.6 0.7 copy-start.7
  89.6 0.7 copy-start.8
  97.3 1.6 %copy-start = (bf16[1,4,4,16,4096]{4,3,2,1,0:T(8,128)(2,1)S(1)}, bf16[1,4,4,16,4096]{4,3,2,1,0:T(8,128)(2,1)}, u32[]{:S(2)}) copy-start(bf16[1,4,4,16,4096]{4,3,2,1,0:T(8,128)(2,1)} %get-tuple-element.22) | copy-start | bytes 6291460
  97.3 2.2 %copy-start.1 = (bf16[1,4,4,16,4096]{4,3,2,1,0:T(8,128)(2,1)S(1)}, bf16[1,4,4,16,4096]{4,3,2,1,0:T(8,128)(2,1)}, u32[]{:S(2)}) copy-start(bf16[1,4,4,16,4096]{4,3,2,1,0:T(8,128)(2,1)} %get-tuple-element.24) | copy-start | bytes 6291460

commit v9 on v6

--- a/solution.py
+++ b/solution.py
@@ -48,11 +48,10 @@
     copies = jnp.broadcast_to(both[None], (nrow,) + both.shape)
     spread = lax.all_to_all(copies, "row", 0, 0, tiled=True)
     spread = spread.reshape(nrow, 2, local_pairs, local_g // width, width)
+    left_imag = lax.all_gather(matrix_imag, cols, axis=0, tiled=True)
     row_real = jnp.stack((matrix_real,) + ring_gather(matrix_real, "x"))
-    col_imag = jnp.stack((matrix_imag,) + ring_gather(matrix_imag, "y"))
-    first = jnp.stack([row_real, col_imag])
-    first_other = lax.ppermute(first, "core", CORE_PAIRS)
-    spread, row_real, col_imag, first = lax.optimization_barrier((spread, row_real, col_imag, first))
+    first_other = lax.ppermute(row_real, "core", CORE_PAIRS)
+    spread, row_real = lax.optimization_barrier((spread, row_real))
     payload = spread.transpose(1, 2, 0, 3, 4).reshape(2, local_pairs, ncol, width)
     bands = jnp.stack([valence_index, conduction_index]).astype(jnp.bfloat16)
     tags = jnp.broadcast_to(bands[:, :, None, None], (2, local_pairs, ncol, 128))
@@ -60,18 +59,12 @@
     column = lax.all_to_all(payload, cols, split_axis=2, concat_axis=1, tiled=True)
     column = column.reshape(2, pairs, width + 128)
     real_plus, real_far, real_minus = ring_gather(row_real, "y")
-    imag_plus, imag_far, imag_minus = ring_gather(col_imag, "x")
-    near = jnp.stack([real_plus, real_minus, imag_plus, imag_minus])
+    near = jnp.stack([real_plus, real_minus])
     near_other = lax.ppermute(near, "core", CORE_PAIRS)
-    far = jnp.stack([real_far, imag_far])
-    far_other = lax.ppermute(far, "core", CORE_PAIRS)
-    parts = []
-    for part in range(2):
-        for src_first, src_near, src_far in ((first, near, far), (first_other, near_other, far_other)):
-            parts.append(
-                jnp.stack([src_first[part], src_near[2 * part], src_far[part], src_near[2 * part + 1]])
-            )
-    left = jnp.stack(parts).reshape(2 * pairs, local_g)
+    far_other = lax.ppermute(real_far, "core", CORE_PAIRS)
+    own = jnp.stack([row_real, real_plus, real_far, real_minus])
+    other = jnp.stack([first_other, near_other[0], far_other, near_other[1]])
+    left = jnp.concatenate([own.reshape(pairs // 2, local_g), other.reshape(pairs // 2, local_g), left_imag])
 
     all_bands = column[:, :, width].astype(jnp.int32)
     gap = lookup(all_bands[1], conduction_energy) - lookup(all_bands[0], valence_energy)
@@ -87,7 +80,6 @@
         return grid.transpose(order + (3, 4)).reshape(pairs, width)
 
     real_order = (2, 1, 0)
-    imag_order = (2, 0, 1)
     right_real = []
     right_imag = []
     for index in range(frequency.shape[0]):
@@ -96,11 +88,9 @@
         scaled_real = (weight[:, None] * wide[0]).astype(jnp.bfloat16)
         scaled_imag = (weight[:, None] * wide[1]).astype(jnp.bfloat16)
         real_a = relative(scaled_real, real_order)
-        imag_b = relative(scaled_imag, imag_order)
-        real_b = relative(scaled_real, imag_order)
         imag_a = relative(scaled_imag, real_order)
-        right_real.append(jnp.concatenate([-real_a, -imag_b], axis=0))
-        right_imag.append(jnp.concatenate([-imag_a, real_b], axis=0))
+        right_real.append(jnp.concatenate([-real_a, -scaled_imag], axis=0))
+        right_imag.append(jnp.concatenate([-imag_a, scaled_real], axis=0))
     dims = (((0,), (0,)), ((), ()))
     chi_real = lax.dot_general(left, jnp.stack(right_real, axis=1), dims, preferred_element_type=jnp.float32)
     chi_imag = lax.dot_general(left, jnp.stack(right_imag, axis=1), dims, preferred_element_type=jnp.float32)

time: 109 us -> 134 us (1.23)
  between operations: 3.77 us -> 17.1 us
  starting transfers between devices: 40.2 us -> 50.8 us
  waiting for transfers between devices: 14.6 us -> 8.12 us
  local copies, waits for them, and re-layouts: 12.8 us -> 19.1 us
  matrix products: 22.6 us -> 24.4 us
    ppermute x1, starting transfers between devices: 0.01 us -> 24.4 us  [on_device(): near_other = lax.ppermute(near, 'core', CORE_PAIRS)]
    ppermute x16 -> x8, waiting for transfers between devices: 14.6 us -> 1.61 us  [shift(): lax.ppermute(value, axis, [(i, (i + step) % size) for i in range(size)])]
    ppermute x16 -> x8, starting transfers between devices: 24.5 us -> 12 us  [shift(): lax.ppermute(value, axis, [(i, (i + step) % size) for i in range(size)])]
    all_gather x0 -> x1, local copies, waits for them, and re-layouts: none -> 6.55 us  [on_device(): left_imag = lax.all_gather(matrix_imag, cols, axis=0, tiled=True)]
    all_to_all x1, waiting for transfers between devices: 0.01 us -> 6.48 us  [on_device(): spread = lax.all_to_all(copies, 'row', 0, 0, tiled=True)]
    reshape x1 -> x3, local copies, waits for them, and re-layouts: 0.11 us -> 5.04 us  [the longest x1 2.47 us: on_device(): other.reshape(pairs // 2, local_g)]
    another operation x10 -> x3, other arithmetic: 9.06 us -> 4.34 us  [the longest x1 1.78 us: on_device(): own = jnp.stack([row_real, real_plus, real_far, real_minus])]
    slice x5 -> x2, local copies, waits for them, and re-layouts: 4.45 us -> 1.44 us  [the longest x1 1.27 us: on_device(): other = jnp.stack([first_other, near_other[0], far_other, near_other[1]])]
  transfers between devices with their start and end apart: 21 -> 14, of which waited for: 4 -> 3; matrix products, arithmetic and copies ran while one was open for 20% -> 19% of each run, Pallas kernels for 0% -> 0%
where the time goes in v9:
time: 134 us; the launch traced here: 133 us
  starting transfers between devices  50.8 us (38%)
  matrix products  24.4 us (18%)
  local copies, waits for them, and re-layouts  19.1 us (14%)
  between operations  17.1 us (13%)
  other arithmetic  13.6 us (10%)
  waiting for transfers between devices  8.12 us (6%)
    ppermute x1, starting transfers between devices, on_device(): near_other = lax.ppermute(near, 'core', CORE_PAIRS)  24.4 us
    dot_general x1, matrix products, on_device(): lax.dot_general(left, jnp.stack(right_imag, axis=1), dims, preferred_elem...  13.4 us
    ppermute x8, starting transfers between devices, shift(): lax.ppermute(value, axis, [(i, (i + step) % size) for i in range(size)])  12 us
    dot_general x1, matrix products, on_device(): lax.dot_general(left, jnp.stack(right_real, axis=1), dims, preferred_elem...  10.9 us
    all_gather x1, local copies, waits for them, and re-layouts, on_device(): left_imag = lax.all_gather(matrix_imag, cols, axis=0, tiled=True)  6.55 us
    all_to_all x1, waiting for transfers between devices, on_device(): spread = lax.all_to_all(copies, 'row', 0, 0, tiled=True)  6.48 us
    all_to_all x1, starting transfers between devices, on_device(): spread = lax.all_to_all(copies, 'row', 0, 0, tiled=True)  5.14 us
    all_to_all x1, starting transfers between devices, on_device(): lax.all_to_all(payload, cols, split_axis=2, concat_axis=1, tiled=True)  4.78 us
  transfers between devices with their start and end apart: 14, of which 3 were waited for; matrix products, arithmetic and copies ran while one was open for 19% of the time, Pallas kernels for 0%

profile of v9, /device:TPU:1, one launch (start us, length us, event | category | flops | bytes accessed | tf_op | source)
XLA Modules:
  0.0 133.1 jit_solution(9622938842540524167)
XLA Ops:
  7.2 2.1 %collective-permute-start.1 = (bf16[16,4096]{1,0:T(8,128)(2,1)}, bf16[16,4096]{1,0:T(8,128)(2,1)S(1)}, u32[]{:S(2)}, u32[]{:S(2)}) collective-permute-start(bf16[16,4096]{1,0:T(8,128)(2,1)} %param.7), channel_id=1, source_target_pairs={{0,8},{8,16},{16,24},{24,0},{1,9},{9,17},{17,25},{25,1},{2,10},{10... | collective-permute-start | bytes 393224 | tf_op jit(solution)/shard_map/ppermute | solution.py:17
  9.3 1.4 %collective-permute-start = (bf16[16,4096]{1,0:T(8,128)(2,1)}, bf16[16,4096]{1,0:T(8,128)(2,1)S(1)}, u32[]{:S(2)}, u32[]{:S(2)}) collective-permute-start(bf16[16,4096]{1,0:T(8,128)(2,1)} %param.7), channel_id=1, source_target_pairs={{0,24},{8,0},{16,8},{24,16},{1,25},{9,1},{17,9},{25,17},{2,26},{10... | collective-permute-start | bytes 393224 | tf_op jit(solution)/shard_map/ppermute | solution.py:17
  10.7 1.0 pad_maximum_fusion.5
  11.7 1.1 broadcast_in_dim.28
  12.8 5.1 %all-to-all-start = ((bf16[4,2,16,4096]{3,2,1,0:T(8,128)(2,1)}), bf16[4,2,16,4096]{3,2,1,0:T(8,128)(2,1)S(1)}, u32[]{:S(2)}, u32[]{:S(2)}) async-start(bf16[4,2,16,4096]{3,2,1,0:T(8,128)(2,1)} %broadcast_in_dim.28), calls=%async_computation | async-start | bytes 2097152 | tf_op jit(solution)/shard_map/all_to_all | solution.py:49
  18.1 2.7 %collective-permute-start.3 = (bf16[16,2048]{1,0:T(8,128)(2,1)S(1)}, bf16[16,2048]{1,0:T(8,128)(2,1)S(1)}, u32[]{:S(2)}, u32[]{:S(2)}) collective-permute-start(bf16[16,2048]{1,0:T(8,128)(2,1)S(1)} %slice.61), channel_id=1, source_target_pairs={{0,24},{8,0},{16,8},{24,16},{1,25},{9,1},{17,9},{25,17},{2,26},{10... | collective-permute-start | bytes 196616 | tf_op jit(solution)/shard_map/ppermute | solution.py:17
  24.2 0.9 pad_maximum_fusion.4
  25.1 6.5 %all-to-all-done = bf16[4,2,16,4096]{3,2,1,0:T(8,128)(2,1)S(1)} async-done(((bf16[4,2,16,4096]{3,2,1,0:T(8,128)(2,1)}), bf16[4,2,16,4096]{3,2,1,0:T(8,128)(2,1)S(1)}, u32[]{:S(2)}, u32[]{:S(2)}) %all-to-all-start) | async-done | bytes 1048608 | tf_op jit(solution)/shard_map/all_to_all | solution.py:49
  32.0 1.4 %collective-permute-start.5 = (bf16[4,16,4096]{2,1,0:T(8,128)(2,1)}, bf16[4,16,4096]{2,1,0:T(8,128)(2,1)S(1)}, u32[]{:S(2)}, u32[]{:S(2)}) collective-permute-start(bf16[4,16,4096]{2,1,0:T(8,128)(2,1)} %pad_maximum_fusion.4), channel_id=1, source_target_pairs={{0,2},{2,4},{4,6},{6,0},{1,3},{3,5},{5,7},{7,1},{8,10},{10,12},{12... | collective-permute-start | bytes 1572872 | tf_op jit(solution)/shard_map/ppermute | solution.py:17
  33.3 1.5 %collective-permute-start.4 = (bf16[4,16,4096]{2,1,0:T(8,128)(2,1)}, bf16[4,16,4096]{2,1,0:T(8,128)(2,1)S(1)}, u32[]{:S(2)}, u32[]{:S(2)}) collective-permute-start(bf16[4,16,4096]{2,1,0:T(8,128)(2,1)} %pad_maximum_fusion.4), channel_id=1, source_target_pairs={{0,6},{2,0},{4,2},{6,4},{1,7},{3,1},{5,3},{7,5},{8,14},{10,8},{12,... | collective-permute-start | bytes 1572872 | tf_op jit(solution)/shard_map/ppermute | solution.py:17
  34.9 2.9 %collective-permute-start.8 = (bf16[4,16,4096]{2,1,0:T(8,128)(2,1)}, bf16[4,16,4096]{2,1,0:T(8,128)(2,1)}, u32[]{:S(2)}, u32[]{:S(2)}) collective-permute-start(bf16[4,16,4096]{2,1,0:T(8,128)(2,1)} %pad_maximum_fusion.4), channel_id=1, source_target_pairs={{0,1},{1,0},{2,3},{3,2},{4,5},{5,4},{6,7},{7,6},{8,9},{9,8},{10,11... | collective-permute-start | bytes 1572872 | tf_op jit(solution)/shard_map/ppermute | solution.py:53
  38.2 1.5 %copy.49 = bf16[2,16,32,640]{3,1,0,2:T(8,128)(2,1)} copy(bf16[2,16,32,640]{3,2,1,0:T(8,128)(2,1)S(1)} %pad_maximum_fusion.2) | data formatting | bytes 2621440 | tf_op jit(solution)/shard_map/concatenate | solution.py:58
  39.6 4.8 %all-to-all-start.1 = ((bf16[2,16,32,640]{3,1,0,2:T(8,128)(2,1)}), bf16[2,16,32,640]{3,1,0,2:T(8,128)(2,1)S(1)}, u32[]{:S(2)}, u32[]{:S(2)}) async-start(bf16[2,16,32,640]{3,1,0,2:T(8,128)(2,1)} %copy.49), calls=%async_computation.1 | async-start | bytes 2621440 | tf_op jit(solution)/shard_map/all_to_all | solution.py:59
  44.6 1.4 %collective-permute-start.6 = (bf16[4,16,2048]{2,1,0:T(8,128)(2,1)S(1)}, bf16[4,16,2048]{2,1,0:T(8,128)(2,1)S(1)}, u32[]{:S(2)}, u32[]{:S(2)}) collective-permute-start(bf16[4,16,2048]{2,1,0:T(8,128)(2,1)S(1)} %slice.62), channel_id=1, source_target_pairs={{0,2},{2,4},{4,6},{6,0},{1,3},{3,5},{5,7},{7,1},{8,10},{10,12},{12... | collective-permute-start | bytes 786440 | tf_op jit(solution)/shard_map/ppermute | solution.py:17
  46.0 1.5 %collective-permute-start.7 = (bf16[4,16,2048]{2,1,0:T(8,128)(2,1)S(1)}, bf16[4,16,2048]{2,1,0:T(8,128)(2,1)S(1)}, u32[]{:S(2)}, u32[]{:S(2)}) collective-permute-start(bf16[4,16,2048]{2,1,0:T(8,128)(2,1)S(1)} %slice.63), channel_id=1, source_target_pairs={{0,6},{2,0},{4,2},{6,4},{1,7},{3,1},{5,3},{7,5},{8,14},{10,8},{12,... | collective-permute-start | bytes 786440 | tf_op jit(solution)/shard_map/ppermute | solution.py:17
  47.4 1.1 pad_maximum_fusion.3
  48.5 24.4 %collective-permute-start.9 = (bf16[2,4,16,4096]{3,2,1,0:T(8,128)(2,1)}, bf16[2,4,16,4096]{3,2,1,0:T(8,128)(2,1)}, u32[]{:S(2)}, u32[]{:S(2)}) collective-permute-start(bf16[2,4,16,4096]{3,2,1,0:T(8,128)(2,1)} %pad_maximum_fusion.3), channel_id=1, source_target_pairs={{0,1},{1,0},{2,3},{3,2},{4,5},{5,4},{6,7},{7,6},{8,9},{9,8},{10,11... | collective-permute-start | bytes 3145736 | tf_op jit(solution)/shard_map/ppermute | solution.py:63
  72.9 1.5 %collective-permute-done.6 = bf16[4,16,2048]{2,1,0:T(8,128)(2,1)S(1)} collective-permute-done((bf16[4,16,2048]{2,1,0:T(8,128)(2,1)S(1)}, bf16[4,16,2048]{2,1,0:T(8,128)(2,1)S(1)}, u32[]{:S(2)}, u32[]{:S(2)}) %collective-permute-start.6) | collective-permute-done | bytes 262176 | tf_op jit(solution)/shard_map/ppermute | solution.py:17
  74.4 0.7 constant_dynamic-update-slice_fusion.1
  75.1 0.7 constant_dynamic-update-slice_fusion
  75.8 1.5 %collective-permute-start.10 = (bf16[4,16,4096]{2,1,0:T(8,128)(2,1)}, bf16[4,16,4096]{2,1,0:T(8,128)(2,1)}, u32[]{:S(2)}, u32[]{:S(2)}) collective-permute-start(bf16[4,16,4096]{2,1,0:T(8,128)(2,1)} %constant_dynamic-update-slice_fusion), channel_id=1, source_target_pairs={{0,1},{1,0},{2,3},{3,2},{4,5},{5,4},{6,7},{7,6},{8,9},{9,8},{10,11... | collective-permute-start | bytes 1572872 | tf_op jit(solution)/shard_map/ppermute | solution.py:64
  77.4 1.8 %pad_maximum_fusion = bf16[4,4,16,4096]{3,2,1,0:T(8,128)(2,1)S(1)} fusion(bf16[1,4,16,4096]{3,2,1,0:T(8,128)(2,1)} %bitcast.94, bf16[1,4,16,4096]{3,2,1,0:T(8,128)(2,1)} %bitcast.7, bf16[1,4,16,4096]{3,2,1,0:T(8,128)(2,1)} %bitcast.96, bf16[1,4,16,4096]{3,2,1,0:T(8,128)(2,1)} %bitcast.5), kind=kLoop, calls=%fused_computation.3 | loop fusion | flops 3145728 | bytes 4194304 | tf_op jit(solution)/shard_map/stack | solution.py:65
  79.2 2.5 %copy.45 = bf16[256,4096]{0,1:T(8,128)(2,1)} copy(bf16[256,4096]{1,0:T(8,128)(2,1)S(1)} %bitcast.87) | data formatting | bytes 4194304 | tf_op jit(solution)/shard_map/reshape | solution.py:67
  86.5 1.1 maximum_bitcast_fusion.6
  87.9 1.2 maximum_bitcast_fusion.3
  89.0 1.0 maximum_bitcast_fusion.4
  90.1 1.3 fusion.35
  91.4 1.5 %pad_maximum_fusion.1 = bf16[4,4,16,4096]{3,2,1,0:T(8,128)(2,1)S(1)} fusion(bf16[1,4,16,4096]{3,2,1,0:T(8,128)(2,1)S(1)} %get-tuple-element.15, bf16[1,4,16,4096]{3,2,1,0:T(8,128)(2,1)} %bitcast.11, bf16[1,4,16,4096]{3,2,1,0:T(8,128)(2,1)S(1)} %get-tuple-element.14, bf16[1,4,16,4096]{3,2,1,0:T(8,128)(2,1)} %bitcast.10), kind=kLoop, calls=%fused_computation.4 | loop fusion | flops 3145728 | bytes 4194304 | tf_op jit(solution)/shard_map/stack | solution.py:66
  92.8 2.5 %copy.46 = bf16[256,4096]{0,1:T(8,128)(2,1)} copy(bf16[256,4096]{1,0:T(8,128)(2,1)S(1)} %bitcast.86) | data formatting | bytes 4194304 | tf_op jit(solution)/shard_map/reshape | solution.py:67
  95.3 6.5 %copy.47 = bf16[512,4096]{0,1:T(8,128)(2,1)} copy(bf16[512,4096]{1,0:T(8,128)(2,1)} %all-gather.2.cloned.1.call-done) | data formatting | bytes 8388608 | tf_op jit(solution)/shard_map/all_gather | solution.py:51
  101.9 13.4 %convert_bitcast_fusion = bf16[2,4096,512]{2,1,0:T(8,128)(2,1)} fusion(bf16[512,4096]{0,1:T(8,128)(2,1)} %copy.47, bf16[256,4096]{0,1:T(8,128)(2,1)} %copy.46, bf16[256,4096]{0,1:T(8,128)(2,1)S(1)} %copy-done.3, bf16[1024,1,512]{2,0,1:T(8,128)(2,1)} %maximum_bitcast_fusion.6, bf16[1024,1,512]{2,0,1:T(8,128)(2,1)S(1)} %maximum_bitcast_fusion.5), kind=kOutput, calls=%fused_computation.1 | convolution fusion | flops 8623489024 | bytes 18874368 | tf_op jit(solution)/shard_map/dot_general | solution.py:96
  115.3 10.9 %convert_bitcast_fusion.1 = bf16[2,4096,512]{2,1,0:T(8,128)(2,1)} fusion(bf16[512,4096]{0,1:T(8,128)(2,1)S(1)} %copy-done, bf16[256,4096]{0,1:T(8,128)(2,1)S(1)} %copy-done.4, bf16[256,4096]{0,1:T(8,128)(2,1)S(1)} %copy-done.3, bf16[1024,1,512]{2,0,1:T(8,128)(2,1)S(1)} %copy-done.6, bf16[1024,1,512]{2,0,1:T(8,128)(2,1)S(1)} %copy-done.5), kind=kOutput, calls=%fused_computation.2 | convolution fusion | flops 8623489024 | bytes 18874368 | tf_op jit(solution)/shard_map/dot_general | solution.py:95
  (83 shorter events, 6.7 us)
Async XLA Ops:
  7.2 10.8 %copy-start.11 = (s32[16]{0:T(128)S(1)}, s32[16]{0:T(128)}, u32[]{:S(2)}) copy-start(s32[16]{0:T(128)} %param.10) | copy-start | bytes 196
  7.2 10.8 %copy-start.12 = (s32[16]{0:T(128)S(1)}, s32[16]{0:T(128)}, u32[]{:S(2)}) copy-start(s32[16]{0:T(128)} %param.9) | copy-start | bytes 196
  7.2 88.1 %all-gather.2.cloned.1.call-start = ((), (), s32[]{:S(2)}) async-start(), calls=%async_computation.2 | async-start | bytes 4325376 | tf_op jit(solution)/shard_map/all_gather | solution.py:51
  7.2 10.7 %collective-permute-start.1 = (bf16[16,4096]{1,0:T(8,128)(2,1)}, bf16[16,4096]{1,0:T(8,128)(2,1)S(1)}, u32[]{:S(2)}, u32[]{:S(2)}) collective-permute-start(bf16[16,4096]{1,0:T(8,128)(2,1)} %param.7), channel_id=1, source_target_pairs={{0,8},{8,16},{16,24},{24,0},{1,9},{9,17},{17,25},{25,1},{2,10},{10... | collective-permute-start | bytes 393224 | tf_op jit(solution)/shard_map/ppermute | solution.py:17
  9.3 8.7 %collective-permute-start = (bf16[16,4096]{1,0:T(8,128)(2,1)}, bf16[16,4096]{1,0:T(8,128)(2,1)S(1)}, u32[]{:S(2)}, u32[]{:S(2)}) collective-permute-start(bf16[16,4096]{1,0:T(8,128)(2,1)} %param.7), channel_id=1, source_target_pairs={{0,24},{8,0},{16,8},{24,16},{1,25},{9,1},{17,9},{25,17},{2,26},{10... | collective-permute-start | bytes 393224 | tf_op jit(solution)/shard_map/ppermute | solution.py:17
  10.7 10.1 %copy-start.8 = (f32[2]{0:T(128)S(1)}, f32[2]{0:T(128)}, u32[]{:S(2)}) copy-start(f32[2]{0:T(128)} %param.13) | copy-start | bytes 28
  11.7 12.5 %copy-start.7 = (bf16[16,4096]{1,0:T(8,128)(2,1)S(1)}, bf16[16,4096]{1,0:T(8,128)(2,1)}, u32[]{:S(2)}) copy-start(bf16[16,4096]{1,0:T(8,128)(2,1)} %param.7) | copy-start | bytes 393220
  12.8 18.8 %all-to-all-start = ((bf16[4,2,16,4096]{3,2,1,0:T(8,128)(2,1)}), bf16[4,2,16,4096]{3,2,1,0:T(8,128)(2,1)S(1)}, u32[]{:S(2)}, u32[]{:S(2)}) async-start(bf16[4,2,16,4096]{3,2,1,0:T(8,128)(2,1)} %broadcast_in_dim.28), calls=%async_computation | async-start | bytes 2097152 | tf_op jit(solution)/shard_map/all_to_all | solution.py:49
  18.0 6.1 %collective-permute-start.2 = (bf16[16,2048]{1,0:T(8,128)(2,1)S(1)}, bf16[16,2048]{1,0:T(8,128)(2,1)S(1)}, u32[]{:S(2)}, u32[]{:S(2)}) collective-permute-start(bf16[16,2048]{1,0:T(8,128)(2,1)S(1)} %slice.60), channel_id=1, source_target_pairs={{0,8},{8,16},{16,24},{24,0},{1,9},{9,17},{17,25},{25,1},{2,10},{10... | collective-permute-start | bytes 196616 | tf_op jit(solution)/shard_map/ppermute | solution.py:17
  18.1 6.0 %collective-permute-start.3 = (bf16[16,2048]{1,0:T(8,128)(2,1)S(1)}, bf16[16,2048]{1,0:T(8,128)(2,1)S(1)}, u32[]{:S(2)}, u32[]{:S(2)}) collective-permute-start(bf16[16,2048]{1,0:T(8,128)(2,1)S(1)} %slice.61), channel_id=1, source_target_pairs={{0,24},{8,0},{16,8},{24,16},{1,25},{9,1},{17,9},{25,17},{2,26},{10... | collective-permute-start | bytes 196616 | tf_op jit(solution)/shard_map/ppermute | solution.py:17
  32.0 12.6 %collective-permute-start.5 = (bf16[4,16,4096]{2,1,0:T(8,128)(2,1)}, bf16[4,16,4096]{2,1,0:T(8,128)(2,1)S(1)}, u32[]{:S(2)}, u32[]{:S(2)}) collective-permute-start(bf16[4,16,4096]{2,1,0:T(8,128)(2,1)} %pad_maximum_fusion.4), channel_id=1, source_target_pairs={{0,2},{2,4},{4,6},{6,0},{1,3},{3,5},{5,7},{7,1},{8,10},{10,12},{12... | collective-permute-start | bytes 1572872 | tf_op jit(solution)/shard_map/ppermute | solution.py:17
  33.3 12.6 %collective-permute-start.4 = (bf16[4,16,4096]{2,1,0:T(8,128)(2,1)}, bf16[4,16,4096]{2,1,0:T(8,128)(2,1)S(1)}, u32[]{:S(2)}, u32[]{:S(2)}) collective-permute-start(bf16[4,16,4096]{2,1,0:T(8,128)(2,1)} %pad_maximum_fusion.4), channel_id=1, source_target_pairs={{0,6},{2,0},{4,2},{6,4},{1,7},{3,1},{5,3},{7,5},{8,14},{10,8},{12,... | collective-permute-start | bytes 1572872 | tf_op jit(solution)/shard_map/ppermute | solution.py:17
  34.9 56.5 %collective-permute-start.8 = (bf16[4,16,4096]{2,1,0:T(8,128)(2,1)}, bf16[4,16,4096]{2,1,0:T(8,128)(2,1)}, u32[]{:S(2)}, u32[]{:S(2)}) collective-permute-start(bf16[4,16,4096]{2,1,0:T(8,128)(2,1)} %pad_maximum_fusion.4), channel_id=1, source_target_pairs={{0,1},{1,0},{2,3},{3,2},{4,5},{5,4},{6,7},{7,6},{8,9},{9,8},{10,11... | collective-permute-start | bytes 1572872 | tf_op jit(solution)/shard_map/ppermute | solution.py:53
  39.6 42.0 %all-to-all-start.1 = ((bf16[2,16,32,640]{3,1,0,2:T(8,128)(2,1)}), bf16[2,16,32,640]{3,1,0,2:T(8,128)(2,1)S(1)}, u32[]{:S(2)}, u32[]{:S(2)}) async-start(bf16[2,16,32,640]{3,1,0,2:T(8,128)(2,1)} %copy.49), calls=%async_computation.1 | async-start | bytes 2621440 | tf_op jit(solution)/shard_map/all_to_all | solution.py:59
  44.6 31.3 %copy-start.1 = (bf16[4,16,4096]{2,1,0:T(8,128)(2,1)}, bf16[4,16,4096]{2,1,0:T(8,128)(2,1)S(1)}, u32[]{:S(2)}) copy-start(bf16[4,16,4096]{2,1,0:T(8,128)(2,1)S(1)} %collective-permute-done.5) | copy-start | bytes 1572868
  44.6 29.8 %collective-permute-start.6 = (bf16[4,16,2048]{2,1,0:T(8,128)(2,1)S(1)}, bf16[4,16,2048]{2,1,0:T(8,128)(2,1)S(1)}, u32[]{:S(2)}, u32[]{:S(2)}) collective-permute-start(bf16[4,16,2048]{2,1,0:T(8,128)(2,1)S(1)} %slice.62), channel_id=1, source_target_pairs={{0,2},{2,4},{4,6},{6,0},{1,3},{3,5},{5,7},{7,1},{8,10},{10,12},{12... | collective-permute-start | bytes 786440 | tf_op jit(solution)/shard_map/ppermute | solution.py:17
  45.9 31.4 %copy-start.2 = (bf16[4,16,4096]{2,1,0:T(8,128)(2,1)}, bf16[4,16,4096]{2,1,0:T(8,128)(2,1)S(1)}, u32[]{:S(2)}) copy-start(bf16[4,16,4096]{2,1,0:T(8,128)(2,1)S(1)} %collective-permute-done.4) | copy-start | bytes 1572868
  46.0 29.2 %collective-permute-start.7 = (bf16[4,16,2048]{2,1,0:T(8,128)(2,1)S(1)}, bf16[4,16,2048]{2,1,0:T(8,128)(2,1)S(1)}, u32[]{:S(2)}, u32[]{:S(2)}) collective-permute-start(bf16[4,16,2048]{2,1,0:T(8,128)(2,1)S(1)} %slice.63), channel_id=1, source_target_pairs={{0,6},{2,0},{4,2},{6,4},{1,7},{3,1},{5,3},{7,5},{8,14},{10,8},{12,... | collective-permute-start | bytes 786440 | tf_op jit(solution)/shard_map/ppermute | solution.py:17
  48.5 41.5 %collective-permute-start.9 = (bf16[2,4,16,4096]{3,2,1,0:T(8,128)(2,1)}, bf16[2,4,16,4096]{3,2,1,0:T(8,128)(2,1)}, u32[]{:S(2)}, u32[]{:S(2)}) collective-permute-start(bf16[2,4,16,4096]{3,2,1,0:T(8,128)(2,1)} %pad_maximum_fusion.3), channel_id=1, source_target_pairs={{0,1},{1,0},{2,3},{3,2},{4,5},{5,4},{6,7},{7,6},{8,9},{9,8},{10,11... | collective-permute-start | bytes 3145736 | tf_op jit(solution)/shard_map/ppermute | solution.py:63
  75.8 15.5 %collective-permute-start.10 = (bf16[4,16,4096]{2,1,0:T(8,128)(2,1)}, bf16[4,16,4096]{2,1,0:T(8,128)(2,1)}, u32[]{:S(2)}, u32[]{:S(2)}) collective-permute-start(bf16[4,16,4096]{2,1,0:T(8,128)(2,1)} %constant_dynamic-update-slice_fusion), channel_id=1, source_target_pairs={{0,1},{1,0},{2,3},{3,2},{4,5},{5,4},{6,7},{7,6},{8,9},{9,8},{10,11... | collective-permute-start | bytes 1572872 | tf_op jit(solution)/shard_map/ppermute | solution.py:64
  81.6 0.7 copy-start.9
  81.6 0.7 copy-start.10
  95.3 6.6 %copy-start.3 = (bf16[256,4096]{0,1:T(8,128)(2,1)S(1)}, bf16[256,4096]{0,1:T(8,128)(2,1)}, u32[]{:S(2)}) copy-start(bf16[256,4096]{0,1:T(8,128)(2,1)} %copy.45) | copy-start | bytes 6291460
  101.9 13.5 %copy-start = (bf16[512,4096]{0,1:T(8,128)(2,1)S(1)}, bf16[512,4096]{0,1:T(8,128)(2,1)}, u32[]{:S(2)}) copy-start(bf16[512,4096]{0,1:T(8,128)(2,1)} %copy.47) | copy-start | bytes 12582916
  101.9 13.5 %copy-start.4 = (bf16[256,4096]{0,1:T(8,128)(2,1)S(1)}, bf16[256,4096]{0,1:T(8,128)(2,1)}, u32[]{:S(2)}) copy-start(bf16[256,4096]{0,1:T(8,128)(2,1)} %copy.46) | copy-start | bytes 6291460
  101.9 13.5 %copy-start.5 = (bf16[1024,1,512]{2,0,1:T(8,128)(2,1)S(1)}, bf16[1024,1,512]{2,0,1:T(8,128)(2,1)}, u32[]{:S(2)}) copy-start(bf16[1024,1,512]{2,0,1:T(8,128)(2,1)} %maximum_bitcast_fusion.3) | copy-start | bytes 3145732
  101.9 13.5 %copy-start.6 = (bf16[1024,1,512]{2,0,1:T(8,128)(2,1)S(1)}, bf16[1024,1,512]{2,0,1:T(8,128)(2,1)}, u32[]{:S(2)}) copy-start(bf16[1024,1,512]{2,0,1:T(8,128)(2,1)} %maximum_bitcast_fusion.4) | copy-start | bytes 3145732
Sparse Core Ops, SparseCore 0:
  10.8 65.8 all-gather.1

commit v10 on v6

--- a/solution.py
+++ b/solution.py
@@ -23,8 +23,13 @@
     from_plus = shift(block, axis, -1)
     far_first = shift(from_minus[..., :half], axis, 1)
     far_second = shift(from_plus[..., half:], axis, -1)
+    return from_plus, far_first, far_second, from_minus
+
+
+def ring_block(block, axis):
+    from_plus, far_first, far_second, from_minus = ring_gather(block, axis)
     far = jnp.concatenate([far_first, far_second], axis=-1)
-    return from_plus, far, from_minus
+    return jnp.stack([block, from_plus, far, from_minus])
 
 
 def on_device(
@@ -48,8 +53,8 @@
     copies = jnp.broadcast_to(both[None], (nrow,) + both.shape)
     spread = lax.all_to_all(copies, "row", 0, 0, tiled=True)
     spread = spread.reshape(nrow, 2, local_pairs, local_g // width, width)
-    row_real = jnp.stack((matrix_real,) + ring_gather(matrix_real, "x"))
-    col_imag = jnp.stack((matrix_imag,) + ring_gather(matrix_imag, "y"))
+    row_real = ring_block(matrix_real, "x")
+    col_imag = ring_block(matrix_imag, "y")
     first = jnp.stack([row_real, col_imag])
     first_other = lax.ppermute(first, "core", CORE_PAIRS)
     spread, row_real, col_imag, first = lax.optimization_barrier((spread, row_real, col_imag, first))
@@ -59,19 +64,24 @@
     payload = jnp.concatenate([payload, tags], axis=3)
     column = lax.all_to_all(payload, cols, split_axis=2, concat_axis=1, tiled=True)
     column = column.reshape(2, pairs, width + 128)
-    real_plus, real_far, real_minus = ring_gather(row_real, "y")
-    imag_plus, imag_far, imag_minus = ring_gather(col_imag, "x")
+    real_plus, real_far_a, real_far_b, real_minus = ring_gather(row_real, "y")
+    imag_plus, imag_far_a, imag_far_b, imag_minus = ring_gather(col_imag, "x")
     near = jnp.stack([real_plus, real_minus, imag_plus, imag_minus])
     near_other = lax.ppermute(near, "core", CORE_PAIRS)
-    far = jnp.stack([real_far, imag_far])
-    far_other = lax.ppermute(far, "core", CORE_PAIRS)
-    parts = []
+    far_a = jnp.stack([real_far_a, imag_far_a])
+    far_a_other = lax.ppermute(far_a, "core", CORE_PAIRS)
+    far_b = jnp.stack([real_far_b, imag_far_b])
+    far_b_other = lax.ppermute(far_b, "core", CORE_PAIRS)
+    pieces = []
     for part in range(2):
-        for src_first, src_near, src_far in ((first, near, far), (first_other, near_other, far_other)):
-            parts.append(
-                jnp.stack([src_first[part], src_near[2 * part], src_far[part], src_near[2 * part + 1]])
-            )
-    left = jnp.stack(parts).reshape(2 * pairs, local_g)
+        for src_first, src_near, src_a, src_b in (
+            (first, near, far_a, far_b),
+            (first_other, near_other, far_a_other, far_b_other),
+        ):
+            src_far = jnp.concatenate([src_a[part], src_b[part]], axis=-1)
+            for piece in (src_first[part], src_near[2 * part], src_far, src_near[2 * part + 1]):
+                pieces.append(piece.reshape(-1, local_g))
+    left = jnp.concatenate(pieces, axis=0)
 
     all_bands = column[:, :, width].astype(jnp.int32)
     gap = lookup(all_bands[1], conduction_energy) - lookup(all_bands[0], valence_energy)

time: 109 us -> 172 us (1.58); the launches traced: 108 us -> 168 us
  local copies, waits for them, and re-layouts: 12.8 us -> 75.4 us
  other arithmetic: 13.8 us -> 26.3 us
  waiting for transfers between devices: 14.6 us -> 3.75 us
  starting transfers between devices: 40.2 us -> 33.7 us
  matrix products: 22.6 us -> 25.8 us
    another operation x0 -> x12, local copies, waits for them, and re-layouts: none -> 24.8 us  [on_device(): pieces.append(piece.reshape(-1, local_g))]
    concatenate x0 -> x5, local copies, waits for them, and re-layouts: none -> 23.4 us  [the longest x1 18.9 us: on_device(): left = jnp.concatenate(pieces, axis=0)]
    ppermute x16, waiting for transfers between devices: 14.6 us -> 3.73 us  [shift(): lax.ppermute(value, axis, [(i, (i + step) % size) for i in range(size)])]
    concatenate x0 -> x3, other arithmetic: none -> 6.59 us  [on_device(): src_far = jnp.concatenate([src_a[part], src_b[part]], axis=-1)]
    ppermute x16, starting transfers between devices: 24.5 us -> 18.8 us  [shift(): lax.ppermute(value, axis, [(i, (i + step) % size) for i in range(size)])]
    reshape x0 -> x2, local copies, waits for them, and re-layouts: none -> 4.77 us  [on_device(): pieces.append(piece.reshape(-1, local_g))]
    dot_general x1, matrix products: 11.3 us -> 15 us  [on_device(): lax.dot_general(left, jnp.stack(right_real, axis=1), dims, preferred_elem...]
    slice x2, local copies, waits for them, and re-layouts: 1.36 us -> 4.37 us  [on_device(): src_first[part]]
  transfers between devices with their start and end apart: 21 -> 22, of which waited for: 4 -> 3; matrix products, arithmetic and copies ran while one was open for 20% -> 42% of each run, Pallas kernels for 0% -> 0%
where the time goes in v10:
time: 172 us; the launch traced here: 168 us
  local copies, waits for them, and re-layouts  75.4 us (44%)
  starting transfers between devices  33.7 us (20%)
  other arithmetic  26.3 us (15%)
  matrix products  25.8 us (15%)
  waiting for transfers between devices  3.75 us (2%)
  between operations  3.56 us (2%)
    another operation x12, local copies, waits for them, and re-layouts, on_device(): pieces.append(piece.reshape(-1, local_g))  24.8 us
    concatenate x1, local copies, waits for them, and re-layouts, on_device(): left = jnp.concatenate(pieces, axis=0)  18.9 us
    ppermute x16, starting transfers between devices, shift(): lax.ppermute(value, axis, [(i, (i + step) % size) for i in range(size)])  18.8 us
    dot_general x1, matrix products, on_device(): lax.dot_general(left, jnp.stack(right_real, axis=1), dims, preferred_elem...  15 us
    dot_general x1, matrix products, on_device(): lax.dot_general(left, jnp.stack(right_imag, axis=1), dims, preferred_elem...  10.9 us
    concatenate x3, other arithmetic, on_device(): src_far = jnp.concatenate([src_a[part], src_b[part]], axis=-1)  6.59 us
    all_to_all x1, starting transfers between devices, on_device(): spread = lax.all_to_all(copies, 'row', 0, 0, tiled=True)  5.16 us
    all_to_all x1, starting transfers between devices, on_device(): lax.all_to_all(payload, cols, split_axis=2, concat_axis=1, tiled=True)  4.85 us
  transfers between devices with their start and end apart: 22, of which 3 were waited for; matrix products, arithmetic and copies ran while one was open for 42% of the time, Pallas kernels for 0%

profile of v10, /device:TPU:1, one launch (start us, length us, event | category | flops | bytes accessed | tf_op | source)
XLA Modules:
  0.0 168.5 jit_solution(11739047043077782984)
XLA Ops:
  0.7 2.1 %collective-permute-start.1 = (bf16[16,4096]{1,0:T(8,128)(2,1)}, bf16[16,4096]{1,0:T(8,128)(2,1)S(1)}, u32[]{:S(2)}, u32[]{:S(2)}) collective-permute-start(bf16[16,4096]{1,0:T(8,128)(2,1)} %param.7), channel_id=1, source_target_pairs={{0,8},{8,16},{16,24},{24,0},{1,9},{9,17},{17,25},{25,1},{2,10},{10... | collective-permute-start | bytes 393224 | tf_op jit(solution)/shard_map/ppermute | solution.py:17
  9.1 5.2 %all-to-all-start = ((bf16[4,2,16,4096]{3,2,1,0:T(8,128)(2,1)}), bf16[4,2,16,4096]{3,2,1,0:T(8,128)(2,1)S(1)}, u32[]{:S(2)}, u32[]{:S(2)}) async-start(bf16[4,2,16,4096]{3,2,1,0:T(8,128)(2,1)} %broadcast_in_dim.28), calls=%async_computation | async-start | bytes 2097152 | tf_op jit(solution)/shard_map/all_to_all | solution.py:54
  20.8 2.6 %collective-permute-done.2 = bf16[16,2048]{1,0:T(8,128)(2,1)S(1)} collective-permute-done((bf16[16,2048]{1,0:T(8,128)(2,1)S(1)}, bf16[16,2048]{1,0:T(8,128)(2,1)S(1)}, u32[]{:S(2)}, u32[]{:S(2)}) %collective-permute-start.2) | collective-permute-done | bytes 65568 | tf_op jit(solution)/shard_map/ppermute | solution.py:17
  27.2 3.8 %collective-permute-start.12 = (bf16[2,4,16,4096]{3,2,1,0:T(8,128)(2,1)}, bf16[2,4,16,4096]{3,2,1,0:T(8,128)(2,1)}, u32[]{:S(2)}, u32[]{:S(2)}) collective-permute-start(bf16[2,4,16,4096]{3,2,1,0:T(8,128)(2,1)} %pad_maximum_fusion.2), channel_id=1, source_target_pairs={{0,1},{1,0},{2,3},{3,2},{4,5},{5,4},{6,7},{7,6},{8,9},{9,8},{10,11... | collective-permute-start | bytes 3145736 | tf_op jit(solution)/shard_map/ppermute | solution.py:59
  33.0 2.7 %collective-permute-start.13 = (bf16[4,16,4096]{2,1,0:T(8,128)(2,1)}, bf16[4,16,4096]{2,1,0:T(8,128)(2,1)}, u32[]{:S(2)}, u32[]{:S(2)}) collective-permute-start(bf16[4,16,4096]{2,1,0:T(8,128)(2,1)} %get-tuple-element.8), channel_id=1, source_target_pairs={{0,24},{8,0},{16,8},{24,16},{1,25},{9,1},{17,9},{25,17},{2,26},{10... | collective-permute-start | bytes 1572872 | tf_op jit(solution)/shard_map/ppermute | solution.py:17
  35.7 2.1 %fusion.41 = (bf16[1,4,16,4096]{3,2,1,0:T(8,128)(2,1)}, bf16[1,4,16,4096]{3,2,1,0:T(8,128)(2,1)S(1)}) fusion(bf16[2,4,16,4096]{3,2,1,0:T(8,128)(2,1)} %pad_maximum_fusion.2), kind=kLoop, calls=%fused_computation.100 | loop fusion | bytes 2097152 | tf_op jit(solution)/shard_map/slice | solution.py:82
  41.5 4.9 %all-to-all-start.1 = ((bf16[2,16,32,640]{3,1,0,2:T(8,128)(2,1)}), bf16[2,16,32,640]{3,1,0,2:T(8,128)(2,1)S(1)}, u32[]{:S(2)}, u32[]{:S(2)}) async-start(bf16[2,16,32,640]{3,1,0,2:T(8,128)(2,1)} %copy.106), calls=%async_computation.1 | async-start | bytes 2621440 | tf_op jit(solution)/shard_map/all_to_all | solution.py:65
  46.4 2.3 %fusion.40 = (bf16[1,4,16,4096]{3,2,1,0:T(8,128)(2,1)}, bf16[1,4,16,4096]{3,2,1,0:T(8,128)(2,1)}) fusion(bf16[2,4,16,4096]{3,2,1,0:T(8,128)(2,1)} %collective-permute-done.12), kind=kLoop, calls=%fused_computation.99 | loop fusion | bytes 2097152 | tf_op jit(solution)/shard_map/slice | solution.py:82
  48.7 2.4 %copy.96 = bf16[64,4096]{0,1:T(8,128)(2,1)} copy(bf16[64,4096]{1,0:T(8,128)(2,1)} %bitcast.117) | data formatting | bytes 1048576 | tf_op jit(solution)/shard_map/reshape;squeeze | solution.py:83
  51.0 2.4 %copy.103 = bf16[64,4096]{0,1:T(8,128)(2,1)} copy(bf16[64,4096]{1,0:T(8,128)(2,1)} %bitcast.115) | data formatting | bytes 1048576 | tf_op jit(solution)/shard_map/reshape;squeeze | solution.py:83
  53.5 2.4 %copy.93 = bf16[64,4096]{0,1:T(8,128)(2,1)} copy(bf16[64,4096]{1,0:T(8,128)(2,1)} %bitcast.11) | data formatting | bytes 1048576 | tf_op jit(solution)/shard_map/reshape;squeeze;stack | solution.py:83
  57.5 2.6 %collective-permute-start.11 = (bf16[4,16,2048]{2,1,0:T(8,128)(2,1)}, bf16[4,16,2048]{2,1,0:T(8,128)(2,1)}, u32[]{:S(2)}, u32[]{:S(2)}) collective-permute-start(bf16[4,16,2048]{2,1,0:T(8,128)(2,1)} %slice.121), channel_id=1, source_target_pairs={{0,6},{2,0},{4,2},{6,4},{1,7},{3,1},{5,3},{7,5},{8,14},{10,8},{12,... | collective-permute-start | bytes 786440 | tf_op jit(solution)/shard_map/ppermute | solution.py:17
  61.7 2.4 %copy.95 = bf16[64,4096]{0,1:T(8,128)(2,1)} copy(bf16[64,4096]{1,0:T(8,128)(2,1)} %bitcast.13) | data formatting | bytes 1048576 | tf_op jit(solution)/shard_map/reshape;squeeze;stack | solution.py:83
  64.1 3.1 %pad_maximum_fusion = bf16[4,4,16,4096]{3,2,1,0:T(8,128)(2,1)} fusion(bf16[1,4,16,4096]{3,2,1,0:T(8,128)(2,1)} %bitcast.18, bf16[1,4,16,4096]{3,2,1,0:T(8,128)(2,1)} %bitcast.17, bf16[1,4,16,4096]{3,2,1,0:T(8,128)(2,1)} %bitcast.16, bf16[1,4,16,4096]{3,2,1,0:T(8,128)(2,1)} %bitcast.15), kind=kLoop, calls=%fused_computation.6 | loop fusion | flops 3145728 | bytes 4194304 | tf_op jit(solution)/shard_map/stack | solution.py:69
  69.5 2.5 %collective-permute-start.18 = (bf16[4,16,2048]{2,1,0:T(8,128)(2,1)}, bf16[4,16,2048]{2,1,0:T(8,128)(2,1)}, u32[]{:S(2)}, u32[]{:S(2)}) collective-permute-start(bf16[4,16,2048]{2,1,0:T(8,128)(2,1)} %slice.126), channel_id=1, source_target_pairs={{0,24},{8,0},{16,8},{24,16},{1,25},{9,1},{17,9},{25,17},{2,26},{10... | collective-permute-start | bytes 786440 | tf_op jit(solution)/shard_map/ppermute | solution.py:17
  73.7 2.4 %copy.100 = bf16[64,4096]{0,1:T(8,128)(2,1)} copy(bf16[64,4096]{1,0:T(8,128)(2,1)} %bitcast.28) | data formatting | bytes 1048576 | tf_op jit(solution)/shard_map/reshape;squeeze;stack | solution.py:83
  76.0 2.5 %copy.102 = bf16[64,4096]{0,1:T(8,128)(2,1)} copy(bf16[64,4096]{1,0:T(8,128)(2,1)} %bitcast.30) | data formatting | bytes 1048576 | tf_op jit(solution)/shard_map/reshape;squeeze;stack | solution.py:83
  78.5 1.8 %pad_maximum_fusion.7 = bf16[4,16,4096]{2,1,0:T(8,128)(2,1)} fusion(bf16[4,16,2048]{2,1,0:T(8,128)(2,1)} %collective-permute-done.11, bf16[4,16,2048]{2,1,0:T(8,128)(2,1)} %collective-permute-done.10), kind=kLoop, calls=%fused_computation.66 | loop fusion | flops 1048576 | bytes 1048576 | tf_op jit(solution)/shard_map/concatenate | solution.py:81
  80.3 2.4 %copy.94 = bf16[64,4096]{0,1:T(8,128)(2,1)} copy(bf16[64,4096]{1,0:T(8,128)(2,1)} %bitcast.114) | data formatting | bytes 1048576 | tf_op jit(solution)/shard_map/reshape | solution.py:83
  82.7 1.9 %pad_maximum_fusion.9 = bf16[2,4,16,2048]{3,2,1,0:T(8,128)(2,1)} fusion(bf16[1,4,16,2048]{3,2,1,0:T(8,128)(2,1)} %bitcast.24, bf16[1,4,16,2048]{3,2,1,0:T(8,128)(2,1)} %bitcast.23), kind=kLoop, calls=%fused_computation.68 | loop fusion | flops 262144 | bytes 1048576 | tf_op jit(solution)/shard_map/stack | solution.py:73
  84.9 1.9 %pad_maximum_fusion.8 = bf16[2,4,16,2048]{3,2,1,0:T(8,128)(2,1)} fusion(bf16[1,4,16,2048]{3,2,1,0:T(8,128)(2,1)} %bitcast.21, bf16[1,4,16,2048]{3,2,1,0:T(8,128)(2,1)} %bitcast.20), kind=kLoop, calls=%fused_computation.67 | loop fusion | flops 262144 | bytes 1048576 | tf_op jit(solution)/shard_map/stack | solution.py:71
  88.9 2.4 %copy.101 = bf16[64,4096]{0,1:T(8,128)(2,1)} copy(bf16[64,4096]{1,0:T(8,128)(2,1)} %bitcast.113) | data formatting | bytes 1048576 | tf_op jit(solution)/shard_map/reshape | solution.py:83
  103.6 1.9 %fusion.42 = (bf16[1,4,16,2048]{3,2,1,0:T(8,128)(2,1)}, bf16[1,4,16,2048]{3,2,1,0:T(8,128)(2,1)}) fusion(bf16[2,4,16,2048]{3,2,1,0:T(8,128)(2,1)} %collective-permute-done.17), kind=kLoop, calls=%fused_computation.101 | loop fusion | bytes 1048576 | tf_op jit(solution)/shard_map/slice | solution.py:81
  107.7 1.9 %copy.90 = bf16[64,2048]{0,1:T(8,128)(2,1)} copy(bf16[64,2048]{1,0:T(8,128)(2,1)} %bitcast.132) | data formatting | bytes 524288 | tf_op jit(solution)/shard_map/concatenate | solution.py:81
  109.6 2.9 %pad_maximum_fusion.3 = (bf16[64,4096]{0,1:T(8,128)(2,1)}, bf16[64,4096]{0,1:T(8,128)(2,1)}) fusion(bf16[64,2048]{0,1:T(8,128)(2,1)S(1)} %copy.89, bf16[64,2048]{0,1:T(8,128)(2,1)S(1)} %copy.88, bf16[64,2048]{0,1:T(8,128)(2,1)} %copy.91, bf16[64,2048]{0,1:T(8,128)(2,1)} %copy.90), kind=kLoop, calls=%fused_computation.16 | loop fusion | flops 2097152 | bytes 2097152 | tf_op jit(solution)/shard_map/concatenate | solution.py:81
  112.5 2.7 %fusion.39 = (bf16[1,4,16,4096]{3,2,1,0:T(8,128)(2,1)}, bf16[1,4,16,4096]{3,2,1,0:T(8,128)(2,1)}, bf16[1,4,16,4096]{3,2,1,0:T(8,128)(2,1)}, bf16[1,4,16,4096]{3,2,1,0:T(8,128)(2,1)S(1)}) fusion(bf16[4,4,16,4096]{3,2,1,0:T(8,128)(2,1)} %collective-permute-done.15), kind=kLoop, calls=%fused_computation.98 | loop fusion | bytes 4194304 | tf_op jit(solution)/shard_map/slice | solution.py:82
  116.5 2.4 %copy.98 = bf16[64,4096]{0,1:T(8,128)(2,1)} copy(bf16[64,4096]{1,0:T(8,128)(2,1)} %bitcast.129) | data formatting | bytes 1048576 | tf_op jit(solution)/shard_map/reshape;squeeze | solution.py:83
  119.0 2.4 %copy.104 = bf16[64,4096]{0,1:T(8,128)(2,1)} copy(bf16[64,4096]{1,0:T(8,128)(2,1)} %bitcast.128) | data formatting | bytes 1048576 | tf_op jit(solution)/shard_map/reshape;squeeze | solution.py:83
  121.3 2.4 %copy.105 = bf16[64,4096]{0,1:T(8,128)(2,1)} copy(bf16[64,4096]{1,0:T(8,128)(2,1)} %bitcast.127) | data formatting | bytes 1048576 | tf_op jit(solution)/shard_map/reshape;squeeze | solution.py:83
  123.7 18.9 %concatenate.109 = bf16[1024,4096]{0,1:T(8,128)(2,1)} concatenate(bf16[64,4096]{0,1:T(8,128)(2,1)S(1)} %copy.92, bf16[64,4096]{0,1:T(8,128)(2,1)} %copy.93, bf16[64,4096]{0,1:T(8,128)(2,1)} %copy.94, bf16[64,4096]{0,1:T(8,128)(2,1)} %copy.95, bf16[64,4096]{0,1:T(8,128)(2,1)S(1)} %copy-done.1, bf16[64,4096]{0,1:T(8,128)(2,1)} %copy.97, bf16[64,4096]{0,1:T(8,128)(2,1)} %get-tuple-element.48, ...), dimensions={0} | concatenate | bytes 16777216 | tf_op jit(solution)/shard_map/concatenate | solution.py:84
  142.6 15.0 %convert_bitcast_fusion.1 = bf16[2,4096,512]{2,1,0:T(8,128)(2,1)} fusion(bf16[1024,4096]{0,1:T(8,128)(2,1)} %concatenate.109, bf16[1024,1,512]{2,0,1:T(8,128)(2,1)} %maximum_bitcast_fusion.1, bf16[1024,1,512]{2,0,1:T(8,128)(2,1)} %maximum_bitcast_fusion), kind=kOutput, calls=%fused_computation.5 | convolution fusion | flops 8598323200 | bytes 18874368 | tf_op jit(solution)/shard_map/dot_general | solution.py:115
  157.6 10.9 %convert_bitcast_fusion = bf16[2,4096,512]{2,1,0:T(8,128)(2,1)} fusion(bf16[1024,4096]{0,1:T(8,128)(2,1)S(1)} %copy-done, bf16[1024,1,512]{2,0,1:T(8,128)(2,1)S(1)} %copy-done.2, bf16[1024,1,512]{2,0,1:T(8,128)(2,1)S(1)} %copy-done.3), kind=kOutput, calls=%fused_computation.4 | convolution fusion | flops 8598323200 | bytes 18874368 | tf_op jit(solution)/shard_map/dot_general | solution.py:116
  (123 shorter events, 45.2 us)
Async XLA Ops:
  0.6 13.6 %copy-start.9 = (s32[16]{0:T(128)S(1)}, s32[16]{0:T(128)}, u32[]{:S(2)}) copy-start(s32[16]{0:T(128)} %param.10) | copy-start | bytes 196
  0.6 13.6 %copy-start.10 = (s32[16]{0:T(128)S(1)}, s32[16]{0:T(128)}, u32[]{:S(2)}) copy-start(s32[16]{0:T(128)} %param.9) | copy-start | bytes 196
  0.7 13.6 %copy-start.6 = (f32[2]{0:T(128)S(1)}, f32[2]{0:T(128)}, u32[]{:S(2)}) copy-start(f32[2]{0:T(128)} %param.13) | copy-start | bytes 28
  0.7 18.0 %collective-permute-start.1 = (bf16[16,4096]{1,0:T(8,128)(2,1)}, bf16[16,4096]{1,0:T(8,128)(2,1)S(1)}, u32[]{:S(2)}, u32[]{:S(2)}) collective-permute-start(bf16[16,4096]{1,0:T(8,128)(2,1)} %param.7), channel_id=1, source_target_pairs={{0,8},{8,16},{16,24},{24,0},{1,9},{9,17},{17,25},{25,1},{2,10},{10... | collective-permute-start | bytes 393224 | tf_op jit(solution)/shard_map/ppermute | solution.py:17
  2.8 14.5 %collective-permute-start = (bf16[16,4096]{1,0:T(8,128)(2,1)}, bf16[16,4096]{1,0:T(8,128)(2,1)S(1)}, u32[]{:S(2)}, u32[]{:S(2)}) collective-permute-start(bf16[16,4096]{1,0:T(8,128)(2,1)} %param.7), channel_id=1, source_target_pairs={{0,24},{8,0},{16,8},{24,16},{1,25},{9,1},{17,9},{25,17},{2,26},{10... | collective-permute-start | bytes 393224 | tf_op jit(solution)/shard_map/ppermute | solution.py:17
  4.1 16.4 %collective-permute-start.5 = (bf16[16,4096]{1,0:T(8,128)(2,1)}, bf16[16,4096]{1,0:T(8,128)(2,1)S(1)}, u32[]{:S(2)}, u32[]{:S(2)}) collective-permute-start(bf16[16,4096]{1,0:T(8,128)(2,1)} %param.8), channel_id=1, source_target_pairs={{0,2},{2,4},{4,6},{6,0},{1,3},{3,5},{5,7},{7,1},{8,10},{10,12},{12... | collective-permute-start | bytes 393224 | tf_op jit(solution)/shard_map/ppermute | solution.py:17
  5.5 13.4 %collective-permute-start.4 = (bf16[16,4096]{1,0:T(8,128)(2,1)}, bf16[16,4096]{1,0:T(8,128)(2,1)S(1)}, u32[]{:S(2)}, u32[]{:S(2)}) collective-permute-start(bf16[16,4096]{1,0:T(8,128)(2,1)} %param.8), channel_id=1, source_target_pairs={{0,6},{2,0},{4,2},{6,4},{1,7},{3,1},{5,3},{7,5},{8,14},{10,8},{12,... | collective-permute-start | bytes 393224 | tf_op jit(solution)/shard_map/ppermute | solution.py:17
  8.0 15.4 %copy-start.4 = (bf16[16,4096]{1,0:T(8,128)(2,1)S(1)}, bf16[16,4096]{1,0:T(8,128)(2,1)}, u32[]{:S(2)}) copy-start(bf16[16,4096]{1,0:T(8,128)(2,1)} %param.7) | copy-start | bytes 393220
  9.1 16.1 %copy-start.5 = (bf16[16,4096]{1,0:T(8,128)(2,1)S(1)}, bf16[16,4096]{1,0:T(8,128)(2,1)}, u32[]{:S(2)}) copy-start(bf16[16,4096]{1,0:T(8,128)(2,1)} %param.8) | copy-start | bytes 393220
  9.1 21.9 %all-to-all-start = ((bf16[4,2,16,4096]{3,2,1,0:T(8,128)(2,1)}), bf16[4,2,16,4096]{3,2,1,0:T(8,128)(2,1)S(1)}, u32[]{:S(2)}, u32[]{:S(2)}) async-start(bf16[4,2,16,4096]{3,2,1,0:T(8,128)(2,1)} %broadcast_in_dim.28), calls=%async_computation | async-start | bytes 2097152 | tf_op jit(solution)/shard_map/all_to_all | solution.py:54
  17.3 3.5 %collective-permute-start.3 = (bf16[16,2048]{1,0:T(8,128)(2,1)S(1)}, bf16[16,2048]{1,0:T(8,128)(2,1)S(1)}, u32[]{:S(2)}, u32[]{:S(2)}) collective-permute-start(bf16[16,2048]{1,0:T(8,128)(2,1)S(1)} %slice.117), channel_id=1, source_target_pairs={{0,24},{8,0},{16,8},{24,16},{1,25},{9,1},{17,9},{25,17},{2,26},{10... | collective-permute-start | bytes 196616 | tf_op jit(solution)/shard_map/ppermute | solution.py:17
  18.6 4.7 %collective-permute-start.2 = (bf16[16,2048]{1,0:T(8,128)(2,1)S(1)}, bf16[16,2048]{1,0:T(8,128)(2,1)S(1)}, u32[]{:S(2)}, u32[]{:S(2)}) collective-permute-start(bf16[16,2048]{1,0:T(8,128)(2,1)S(1)} %slice.116), channel_id=1, source_target_pairs={{0,8},{8,16},{16,24},{24,0},{1,9},{9,17},{17,25},{25,1},{2,10},{10... | collective-permute-start | bytes 196616 | tf_op jit(solution)/shard_map/ppermute | solution.py:17
  18.9 5.3 %collective-permute-start.7 = (bf16[16,2048]{1,0:T(8,128)(2,1)S(1)}, bf16[16,2048]{1,0:T(8,128)(2,1)S(1)}, u32[]{:S(2)}, u32[]{:S(2)}) collective-permute-start(bf16[16,2048]{1,0:T(8,128)(2,1)S(1)} %slice.119), channel_id=1, source_target_pairs={{0,6},{2,0},{4,2},{6,4},{1,7},{3,1},{5,3},{7,5},{8,14},{10,8},{12,... | collective-permute-start | bytes 196616 | tf_op jit(solution)/shard_map/ppermute | solution.py:17
  20.5 4.7 %collective-permute-start.6 = (bf16[16,2048]{1,0:T(8,128)(2,1)S(1)}, bf16[16,2048]{1,0:T(8,128)(2,1)S(1)}, u32[]{:S(2)}, u32[]{:S(2)}) collective-permute-start(bf16[16,2048]{1,0:T(8,128)(2,1)S(1)} %slice.118), channel_id=1, source_target_pairs={{0,2},{2,4},{4,6},{6,0},{1,3},{3,5},{5,7},{7,1},{8,10},{10,12},{12... | collective-permute-start | bytes 196616 | tf_op jit(solution)/shard_map/ppermute | solution.py:17
  27.2 19.2 %collective-permute-start.12 = (bf16[2,4,16,4096]{3,2,1,0:T(8,128)(2,1)}, bf16[2,4,16,4096]{3,2,1,0:T(8,128)(2,1)}, u32[]{:S(2)}, u32[]{:S(2)}) collective-permute-start(bf16[2,4,16,4096]{3,2,1,0:T(8,128)(2,1)} %pad_maximum_fusion.2), channel_id=1, source_target_pairs={{0,1},{1,0},{2,3},{3,2},{4,5},{5,4},{6,7},{7,6},{8,9},{9,8},{10,11... | collective-permute-start | bytes 3145736 | tf_op jit(solution)/shard_map/ppermute | solution.py:59
  31.5 22.0 %collective-permute-start.8 = (bf16[4,16,4096]{2,1,0:T(8,128)(2,1)}, bf16[4,16,4096]{2,1,0:T(8,128)(2,1)}, u32[]{:S(2)}, u32[]{:S(2)}) collective-permute-start(bf16[4,16,4096]{2,1,0:T(8,128)(2,1)} %get-tuple-element.7), channel_id=1, source_target_pairs={{0,6},{2,0},{4,2},{6,4},{1,7},{3,1},{5,3},{7,5},{8,14},{10,8},{12,... | collective-permute-start | bytes 1572872 | tf_op jit(solution)/shard_map/ppermute | solution.py:17
  31.6 28.5 %collective-permute-start.9 = (bf16[4,16,4096]{2,1,0:T(8,128)(2,1)}, bf16[4,16,4096]{2,1,0:T(8,128)(2,1)}, u32[]{:S(2)}, u32[]{:S(2)}) collective-permute-start(bf16[4,16,4096]{2,1,0:T(8,128)(2,1)} %get-tuple-element.7), channel_id=1, source_target_pairs={{0,2},{2,4},{4,6},{6,0},{1,3},{3,5},{5,7},{7,1},{8,10},{10,12},{12... | collective-permute-start | bytes 1572872 | tf_op jit(solution)/shard_map/ppermute | solution.py:17
  33.0 31.1 %collective-permute-start.14 = (bf16[4,16,4096]{2,1,0:T(8,128)(2,1)}, bf16[4,16,4096]{2,1,0:T(8,128)(2,1)}, u32[]{:S(2)}, u32[]{:S(2)}) collective-permute-start(bf16[4,16,4096]{2,1,0:T(8,128)(2,1)} %get-tuple-element.8), channel_id=1, source_target_pairs={{0,8},{8,16},{16,24},{24,0},{1,9},{9,17},{17,25},{25,1},{2,10},{10... | collective-permute-start | bytes 1572872 | tf_op jit(solution)/shard_map/ppermute | solution.py:17
  33.0 31.1 %collective-permute-start.13 = (bf16[4,16,4096]{2,1,0:T(8,128)(2,1)}, bf16[4,16,4096]{2,1,0:T(8,128)(2,1)}, u32[]{:S(2)}, u32[]{:S(2)}) collective-permute-start(bf16[4,16,4096]{2,1,0:T(8,128)(2,1)} %get-tuple-element.8), channel_id=1, source_target_pairs={{0,24},{8,0},{16,8},{24,16},{1,25},{9,1},{17,9},{25,17},{2,26},{10... | collective-permute-start | bytes 1572872 | tf_op jit(solution)/shard_map/ppermute | solution.py:17
  41.5 49.8 %all-to-all-start.1 = ((bf16[2,16,32,640]{3,1,0,2:T(8,128)(2,1)}), bf16[2,16,32,640]{3,1,0,2:T(8,128)(2,1)S(1)}, u32[]{:S(2)}, u32[]{:S(2)}) async-start(bf16[2,16,32,640]{3,1,0,2:T(8,128)(2,1)} %copy.106), calls=%async_computation.1 | async-start | bytes 2621440 | tf_op jit(solution)/shard_map/all_to_all | solution.py:65
  57.5 21.0 %collective-permute-start.11 = (bf16[4,16,2048]{2,1,0:T(8,128)(2,1)}, bf16[4,16,2048]{2,1,0:T(8,128)(2,1)}, u32[]{:S(2)}, u32[]{:S(2)}) collective-permute-start(bf16[4,16,2048]{2,1,0:T(8,128)(2,1)} %slice.121), channel_id=1, source_target_pairs={{0,6},{2,0},{4,2},{6,4},{1,7},{3,1},{5,3},{7,5},{8,14},{10,8},{12,... | collective-permute-start | bytes 786440 | tf_op jit(solution)/shard_map/ppermute | solution.py:17
  61.7 16.8 %collective-permute-start.10 = (bf16[4,16,2048]{2,1,0:T(8,128)(2,1)}, bf16[4,16,2048]{2,1,0:T(8,128)(2,1)}, u32[]{:S(2)}, u32[]{:S(2)}) collective-permute-start(bf16[4,16,2048]{2,1,0:T(8,128)(2,1)} %slice.120), channel_id=1, source_target_pairs={{0,2},{2,4},{4,6},{6,0},{1,3},{3,5},{5,7},{7,1},{8,10},{10,12},{12... | collective-permute-start | bytes 786440 | tf_op jit(solution)/shard_map/ppermute | solution.py:17
  67.2 45.3 %collective-permute-start.15 = (bf16[4,4,16,4096]{3,2,1,0:T(8,128)(2,1)}, bf16[4,4,16,4096]{3,2,1,0:T(8,128)(2,1)}, u32[]{:S(2)}, u32[]{:S(2)}) collective-permute-start(bf16[4,4,16,4096]{3,2,1,0:T(8,128)(2,1)} %pad_maximum_fusion), channel_id=1, source_target_pairs={{0,1},{1,0},{2,3},{3,2},{4,5},{5,4},{6,7},{7,6},{8,9},{9,8},{10,11... | collective-permute-start | bytes 6291464 | tf_op jit(solution)/shard_map/ppermute | solution.py:70
  69.5 13.2 %collective-permute-start.18 = (bf16[4,16,2048]{2,1,0:T(8,128)(2,1)}, bf16[4,16,2048]{2,1,0:T(8,128)(2,1)}, u32[]{:S(2)}, u32[]{:S(2)}) collective-permute-start(bf16[4,16,2048]{2,1,0:T(8,128)(2,1)} %slice.126), channel_id=1, source_target_pairs={{0,24},{8,0},{16,8},{24,16},{1,25},{9,1},{17,9},{25,17},{2,26},{10... | collective-permute-start | bytes 786440 | tf_op jit(solution)/shard_map/ppermute | solution.py:17
  73.7 11.2 %collective-permute-start.16 = (bf16[4,16,2048]{2,1,0:T(8,128)(2,1)}, bf16[4,16,2048]{2,1,0:T(8,128)(2,1)}, u32[]{:S(2)}, u32[]{:S(2)}) collective-permute-start(bf16[4,16,2048]{2,1,0:T(8,128)(2,1)} %slice.124), channel_id=1, source_target_pairs={{0,8},{8,16},{16,24},{24,0},{1,9},{9,17},{17,25},{25,1},{2,10},{10... | collective-permute-start | bytes 786440 | tf_op jit(solution)/shard_map/ppermute | solution.py:17
  84.6 17.6 %collective-permute-start.19 = (bf16[2,4,16,2048]{3,2,1,0:T(8,128)(2,1)}, bf16[2,4,16,2048]{3,2,1,0:T(8,128)(2,1)}, u32[]{:S(2)}, u32[]{:S(2)}) collective-permute-start(bf16[2,4,16,2048]{3,2,1,0:T(8,128)(2,1)} %pad_maximum_fusion.9), channel_id=1, source_target_pairs={{0,1},{1,0},{2,3},{3,2},{4,5},{5,4},{6,7},{7,6},{8,9},{9,8},{10,11... | collective-permute-start | bytes 1572872 | tf_op jit(solution)/shard_map/ppermute | solution.py:74
  86.8 16.7 %collective-permute-start.17 = (bf16[2,4,16,2048]{3,2,1,0:T(8,128)(2,1)}, bf16[2,4,16,2048]{3,2,1,0:T(8,128)(2,1)}, u32[]{:S(2)}, u32[]{:S(2)}) collective-permute-start(bf16[2,4,16,2048]{3,2,1,0:T(8,128)(2,1)} %pad_maximum_fusion.8), channel_id=1, source_target_pairs={{0,1},{1,0},{2,3},{3,2},{4,5},{5,4},{6,7},{7,6},{8,9},{9,8},{10,11... | collective-permute-start | bytes 1572872 | tf_op jit(solution)/shard_map/ppermute | solution.py:72
  91.7 1.5 copy-start.8
  116.5 7.2 %copy-start.1 = (bf16[64,4096]{0,1:T(8,128)(2,1)S(1)}, bf16[64,4096]{0,1:T(8,128)(2,1)}, u32[]{:S(2)}) copy-start(bf16[64,4096]{0,1:T(8,128)(2,1)} %copy.96) | copy-start | bytes 1572868
  142.6 15.0 %copy-start = (bf16[1024,4096]{0,1:T(8,128)(2,1)S(1)}, bf16[1024,4096]{0,1:T(8,128)(2,1)}, u32[]{:S(2)}) copy-start(bf16[1024,4096]{0,1:T(8,128)(2,1)} %concatenate.109) | copy-start | bytes 25165828
  142.6 15.0 %copy-start.2 = (bf16[1024,1,512]{2,0,1:T(8,128)(2,1)S(1)}, bf16[1024,1,512]{2,0,1:T(8,128)(2,1)}, u32[]{:S(2)}) copy-start(bf16[1024,1,512]{2,0,1:T(8,128)(2,1)} %maximum_bitcast_fusion.3) | copy-start | bytes 3145732
  142.6 15.0 %copy-start.3 = (bf16[1024,1,512]{2,0,1:T(8,128)(2,1)S(1)}, bf16[1024,1,512]{2,0,1:T(8,128)(2,1)}, u32[]{:S(2)}) copy-start(bf16[1024,1,512]{2,0,1:T(8,128)(2,1)} %maximum_bitcast_fusion.2) | copy-start | bytes 3145732
  (1 other events, 1.4 us)

commit v11 on v6

--- a/solution.py
+++ b/solution.py
@@ -61,9 +61,9 @@
     column = column.reshape(2, pairs, width + 128)
     real_plus, real_far, real_minus = ring_gather(row_real, "y")
     imag_plus, imag_far, imag_minus = ring_gather(col_imag, "x")
-    near = jnp.stack([real_plus, real_minus, imag_plus, imag_minus])
+    near = lax.optimization_barrier(jnp.stack([real_plus, real_minus, imag_plus, imag_minus]))
     near_other = lax.ppermute(near, "core", CORE_PAIRS)
-    far = jnp.stack([real_far, imag_far])
+    far = lax.optimization_barrier(jnp.stack([real_far, imag_far]))
     far_other = lax.ppermute(far, "core", CORE_PAIRS)
     parts = []
     for part in range(2):

time: 109 us -> 114 us (1.046)
  the two profiles are of different devices: /device:TPU:1 before, /device:TPU:39 now
where the time goes in v11:
time: 114 us; the launch traced here: 113 us
  starting transfers between devices  43.1 us (38%)
  matrix products  22.6 us (20%)
  local copies, waits for them, and re-layouts  17.7 us (16%)
  other arithmetic  14.8 us (13%)
  waiting for transfers between devices  11.3 us (10%)
  between operations  3.78 us (3%)
    ppermute x16, starting transfers between devices, shift(): lax.ppermute(value, axis, [(i, (i + step) % size) for i in range(size)])  17.3 us
    dot_general x1, matrix products, on_device(): lax.dot_general(left, jnp.stack(right_imag, axis=1), dims, preferred_elem...  11.3 us
    ppermute x16, waiting for transfers between devices, shift(): lax.ppermute(value, axis, [(i, (i + step) % size) for i in range(size)])  11.3 us
    dot_general x1, matrix products, on_device(): lax.dot_general(left, jnp.stack(right_real, axis=1), dims, preferred_elem...  11.3 us
    ppermute x1, starting transfers between devices, on_device(): near_other = lax.ppermute(near, 'core', CORE_PAIRS)  9.12 us
    all_to_all x1, starting transfers between devices, on_device(): lax.all_to_all(payload, cols, split_axis=2, concat_axis=1, tiled=True)  5.76 us
    all_to_all x1, starting transfers between devices, on_device(): spread = lax.all_to_all(copies, 'row', 0, 0, tiled=True)  4.98 us
    ppermute x1, starting transfers between devices, on_device(): first_other = lax.ppermute(first, 'core', CORE_PAIRS)  4.23 us
  transfers between devices with their start and end apart: 21, of which 6 were waited for; matrix products, arithmetic and copies ran while one was open for 23% of the time, Pallas kernels for 0%

profile of v11, /device:TPU:39, one launch (start us, length us, event | category | flops | bytes accessed | tf_op | source)
XLA Modules:
  0.0 113.4 jit_solution(7720697772550338733)
XLA Ops:
  0.9 1.3 %collective-permute-start = (bf16[16,4096]{1,0:T(8,128)(2,1)}, bf16[16,4096]{1,0:T(8,128)(2,1)S(1)}, u32[]{:S(2)}, u32[]{:S(2)}) collective-permute-start(bf16[16,4096]{1,0:T(8,128)(2,1)} %param.7), channel_id=1, source_target_pairs={{0,24},{8,0},{16,8},{24,16},{1,25},{9,1},{17,9},{25,17},{2,26},{10... | collective-permute-start | bytes 393224 | tf_op jit(solution)/shard_map/ppermute | solution.py:17
  2.2 1.3 %collective-permute-start.5 = (bf16[16,4096]{1,0:T(8,128)(2,1)}, bf16[16,4096]{1,0:T(8,128)(2,1)S(1)}, u32[]{:S(2)}, u32[]{:S(2)}) collective-permute-start(bf16[16,4096]{1,0:T(8,128)(2,1)} %param.8), channel_id=1, source_target_pairs={{0,2},{2,4},{4,6},{6,0},{1,3},{3,5},{5,7},{7,1},{8,10},{10,12},{12... | collective-permute-start | bytes 393224 | tf_op jit(solution)/shard_map/ppermute | solution.py:17
  3.5 1.4 %collective-permute-start.4 = (bf16[16,4096]{1,0:T(8,128)(2,1)}, bf16[16,4096]{1,0:T(8,128)(2,1)S(1)}, u32[]{:S(2)}, u32[]{:S(2)}) collective-permute-start(bf16[16,4096]{1,0:T(8,128)(2,1)} %param.8), channel_id=1, source_target_pairs={{0,6},{2,0},{4,2},{6,4},{1,7},{3,1},{5,3},{7,5},{8,14},{10,8},{12,... | collective-permute-start | bytes 393224 | tf_op jit(solution)/shard_map/ppermute | solution.py:17
  5.9 1.1 broadcast_in_dim.28
  7.0 5.0 %all-to-all-start = ((bf16[4,2,16,4096]{3,2,1,0:T(8,128)(2,1)}), bf16[4,2,16,4096]{3,2,1,0:T(8,128)(2,1)S(1)}, u32[]{:S(2)}, u32[]{:S(2)}) async-start(bf16[4,2,16,4096]{3,2,1,0:T(8,128)(2,1)} %broadcast_in_dim.28), calls=%async_computation | async-start | bytes 2097152 | tf_op jit(solution)/shard_map/all_to_all | solution.py:49
  15.3 2.7 %collective-permute-start.7 = (bf16[16,2048]{1,0:T(8,128)(2,1)S(1)}, bf16[16,2048]{1,0:T(8,128)(2,1)S(1)}, u32[]{:S(2)}, u32[]{:S(2)}) collective-permute-start(bf16[16,2048]{1,0:T(8,128)(2,1)S(1)} %slice.135), channel_id=1, source_target_pairs={{0,6},{2,0},{4,2},{6,4},{1,7},{3,1},{5,3},{7,5},{8,14},{10,8},{12,... | collective-permute-start | bytes 196616 | tf_op jit(solution)/shard_map/ppermute | solution.py:17
  18.1 1.5 %collective-permute-start.2 = (bf16[16,2048]{1,0:T(8,128)(2,1)S(1)}, bf16[16,2048]{1,0:T(8,128)(2,1)S(1)}, u32[]{:S(2)}, u32[]{:S(2)}) collective-permute-start(bf16[16,2048]{1,0:T(8,128)(2,1)S(1)} %slice.132), channel_id=1, source_target_pairs={{0,8},{8,16},{16,24},{24,0},{1,9},{9,17},{17,25},{25,1},{2,10},{10... | collective-permute-start | bytes 196616 | tf_op jit(solution)/shard_map/ppermute | solution.py:17
  21.6 2.5 %collective-permute-done.3 = bf16[16,2048]{1,0:T(8,128)(2,1)S(1)} collective-permute-done((bf16[16,2048]{1,0:T(8,128)(2,1)S(1)}, bf16[16,2048]{1,0:T(8,128)(2,1)S(1)}, u32[]{:S(2)}, u32[]{:S(2)}) %collective-permute-start.3) | collective-permute-done | bytes 65568 | tf_op jit(solution)/shard_map/ppermute | solution.py:17
  25.1 4.2 %collective-permute-start.16 = (bf16[2,4,16,4096]{3,2,1,0:T(8,128)(2,1)S(1)}, bf16[2,4,16,4096]{3,2,1,0:T(8,128)(2,1)}, u32[]{:S(2)}, u32[]{:S(2)}) collective-permute-start(bf16[2,4,16,4096]{3,2,1,0:T(8,128)(2,1)S(1)} %pad_maximum_fusion.3), channel_id=1, source_target_pairs={{0,1},{1,0},{2,3},{3,2},{4,5},{5,4},{6,7},{7,6},{8,9},{9,8},{10,11... | collective-permute-start | bytes 3145736 | tf_op jit(solution)/shard_map/ppermute | solution.py:54
  30.0 2.7 %collective-permute-start.8 = (bf16[4,16,4096]{2,1,0:T(8,128)(2,1)}, bf16[4,16,4096]{2,1,0:T(8,128)(2,1)}, u32[]{:S(2)}, u32[]{:S(2)}) collective-permute-start(bf16[4,16,4096]{2,1,0:T(8,128)(2,1)} %get-tuple-element.7), channel_id=1, source_target_pairs={{0,6},{2,0},{4,2},{6,4},{1,7},{3,1},{5,3},{7,5},{8,14},{10,8},{12,... | collective-permute-start | bytes 1572872 | tf_op jit(solution)/shard_map/ppermute | solution.py:17
  32.6 1.5 %collective-permute-start.10 = (bf16[4,16,4096]{2,1,0:T(8,128)(2,1)}, bf16[4,16,4096]{2,1,0:T(8,128)(2,1)S(1)}, u32[]{:S(2)}, u32[]{:S(2)}) collective-permute-start(bf16[4,16,4096]{2,1,0:T(8,128)(2,1)} %get-tuple-element.8), channel_id=1, source_target_pairs={{0,24},{8,0},{16,8},{24,16},{1,25},{9,1},{17,9},{25,17},{2,26},{10... | collective-permute-start | bytes 1572872 | tf_op jit(solution)/shard_map/ppermute | solution.py:17
  34.3 1.5 %copy.39 = bf16[2,16,32,640]{3,1,0,2:T(8,128)(2,1)} copy(bf16[2,16,32,640]{3,2,1,0:T(8,128)(2,1)S(1)} %pad_maximum_fusion.2) | data formatting | bytes 2621440 | tf_op jit(solution)/shard_map/concatenate | solution.py:59
  35.8 5.8 %all-to-all-start.1 = ((bf16[2,16,32,640]{3,1,0,2:T(8,128)(2,1)}), bf16[2,16,32,640]{3,1,0,2:T(8,128)(2,1)S(1)}, u32[]{:S(2)}, u32[]{:S(2)}) async-start(bf16[2,16,32,640]{3,1,0,2:T(8,128)(2,1)} %copy.39), calls=%async_computation.1 | async-start | bytes 2621440 | tf_op jit(solution)/shard_map/all_to_all | solution.py:60
  41.7 2.3 %fusion.35 = (bf16[1,4,16,4096]{3,2,1,0:T(8,128)(2,1)}, bf16[1,4,16,4096]{3,2,1,0:T(8,128)(2,1)}) fusion(bf16[2,4,16,4096]{3,2,1,0:T(8,128)(2,1)} %collective-permute-done.16), kind=kLoop, calls=%fused_computation.100 | loop fusion | bytes 2097152 | tf_op jit(solution)/shard_map/slice | solution.py:72
  47.2 2.6 %collective-permute-start.13 = (bf16[4,16,2048]{2,1,0:T(8,128)(2,1)S(1)}, bf16[4,16,2048]{2,1,0:T(8,128)(2,1)S(1)}, u32[]{:S(2)}, u32[]{:S(2)}) collective-permute-start(bf16[4,16,2048]{2,1,0:T(8,128)(2,1)S(1)} %slice.138), channel_id=1, source_target_pairs={{0,6},{2,0},{4,2},{6,4},{1,7},{3,1},{5,3},{7,5},{8,14},{10,8},{12,... | collective-permute-start | bytes 786440 | tf_op jit(solution)/shard_map/ppermute | solution.py:17
  50.7 1.8 %pad_maximum_fusion.1 = bf16[4,4,16,4096]{3,2,1,0:T(8,128)(2,1)S(1)} fusion(bf16[1,4,16,4096]{3,2,1,0:T(8,128)(2,1)} %bitcast.111, bf16[1,4,16,4096]{3,2,1,0:T(8,128)(2,1)} %bitcast.110, bf16[1,4,16,4096]{3,2,1,0:T(8,128)(2,1)} %bitcast.11, bf16[1,4,16,4096]{3,2,1,0:T(8,128)(2,1)} %bitcast.10), kind=kLoop, calls=%fused_computation.3 | loop fusion | flops 3145728 | bytes 4194304 | tf_op jit(solution)/shard_map/stack | solution.py:64
  52.7 9.1 %collective-permute-start.17 = (bf16[4,4,16,4096]{3,2,1,0:T(8,128)(2,1)S(1)}, bf16[4,4,16,4096]{3,2,1,0:T(8,128)(2,1)}, u32[]{:S(2)}, u32[]{:S(2)}) collective-permute-start(bf16[4,4,16,4096]{3,2,1,0:T(8,128)(2,1)S(1)} %pad_maximum_fusion.1), channel_id=1, source_target_pairs={{0,1},{1,0},{2,3},{3,2},{4,5},{5,4},{6,7},{7,6},{8,9},{9,8},{10,11... | collective-permute-start | bytes 6291464 | tf_op jit(solution)/shard_map/ppermute | solution.py:65
  61.9 1.5 %collective-permute-start.15 = (bf16[4,16,2048]{2,1,0:T(8,128)(2,1)S(1)}, bf16[4,16,2048]{2,1,0:T(8,128)(2,1)S(1)}, u32[]{:S(2)}, u32[]{:S(2)}) collective-permute-start(bf16[4,16,2048]{2,1,0:T(8,128)(2,1)S(1)} %slice.140), channel_id=1, source_target_pairs={{0,24},{8,0},{16,8},{24,16},{1,25},{9,1},{17,9},{25,17},{2,26},{10... | collective-permute-start | bytes 786440 | tf_op jit(solution)/shard_map/ppermute | solution.py:17
  63.5 1.1 collective-permute-done.12
  64.6 4.3 %collective-permute-done.14 = bf16[4,16,2048]{2,1,0:T(8,128)(2,1)S(1)} collective-permute-done((bf16[4,16,2048]{2,1,0:T(8,128)(2,1)S(1)}, bf16[4,16,2048]{2,1,0:T(8,128)(2,1)S(1)}, u32[]{:S(2)}, u32[]{:S(2)}) %collective-permute-start.14) | collective-permute-done | bytes 262176 | tf_op jit(solution)/shard_map/ppermute | solution.py:17
  68.9 1.3 %collective-permute-done.15 = bf16[4,16,2048]{2,1,0:T(8,128)(2,1)S(1)} collective-permute-done((bf16[4,16,2048]{2,1,0:T(8,128)(2,1)S(1)}, bf16[4,16,2048]{2,1,0:T(8,128)(2,1)S(1)}, u32[]{:S(2)}, u32[]{:S(2)}) %collective-permute-start.15) | collective-permute-done | bytes 262176 | tf_op jit(solution)/shard_map/ppermute | solution.py:17
  70.3 1.1 pad_maximum_fusion.4
  71.3 1.7 %collective-permute-start.18 = (bf16[2,4,16,4096]{3,2,1,0:T(8,128)(2,1)}, bf16[2,4,16,4096]{3,2,1,0:T(8,128)(2,1)}, u32[]{:S(2)}, u32[]{:S(2)}) collective-permute-start(bf16[2,4,16,4096]{3,2,1,0:T(8,128)(2,1)} %pad_maximum_fusion.4), channel_id=1, source_target_pairs={{0,1},{1,0},{2,3},{3,2},{4,5},{5,4},{6,7},{7,6},{8,9},{9,8},{10,11... | collective-permute-start | bytes 3145736 | tf_op jit(solution)/shard_map/ppermute | solution.py:67
  73.1 1.3 %fusion.34 = (bf16[1,4,16,4096]{3,2,1,0:T(8,128)(2,1)S(1)}, bf16[1,4,16,4096]{3,2,1,0:T(8,128)(2,1)S(1)}) fusion(bf16[2,4,16,4096]{3,2,1,0:T(8,128)(2,1)} %pad_maximum_fusion.4), kind=kLoop, calls=%fused_computation.99 | loop fusion | bytes 2097152 | tf_op jit(solution)/shard_map/slice | solution.py:72
  74.4 2.3 %maximum_bitcast_fusion = (bf16[1,4,4,16,4096]{4,3,2,1,0:T(8,128)(2,1)}, bf16[1,4,4,16,4096]{4,3,2,1,0:T(8,128)(2,1)}) fusion(bf16[1,4,16,4096]{3,2,1,0:T(8,128)(2,1)S(1)} %get-tuple-element.17, bf16[1,4,16,4096]{3,2,1,0:T(8,128)(2,1)S(1)} %get-tuple-element.28, bf16[1,4,16,4096]{3,2,1,0:T(8,128)(2,1)S(1)} %get-tuple-element.14, ...), kind=kLoop, calls=%fused_computation.4 | loop fusion | flops 6291456 | bytes 8388608 | tf_op jit(solution)/shard_map/stack | solution.py:74
  76.9 1.6 %slice_convert_fusion = f32[2,512,512]{2,1,0:T(8,128)} fusion(bf16[2,512,640]{2,1,0:T(8,128)(2,1)S(1)} %bitcast.96), kind=kLoop, calls=%fused_computation.15 | loop fusion | flops 524288 | bytes 3145728 | tf_op jit(solution)/shard_map/convert_element_type | solution.py:78
  79.1 1.7 %fusion.30 = (f32[1,512,512]{2,1,0:T(8,128)S(1)}, f32[1,512,512]{2,1,0:T(8,128)S(1)}) fusion(f32[2,512,512]{2,1,0:T(8,128)} %slice_convert_fusion), kind=kLoop, calls=%fused_computation.95 | loop fusion | bytes 4194304 | tf_op jit(solution)/shard_map/slice | solution.py:96
  84.3 1.3 %fusion.36 = (bf16[1,4,16,4096]{3,2,1,0:T(8,128)(2,1)S(1)}, bf16[1,4,16,4096]{3,2,1,0:T(8,128)(2,1)S(1)}) fusion(bf16[2,4,16,4096]{3,2,1,0:T(8,128)(2,1)} %collective-permute-done.18), kind=kLoop, calls=%fused_computation.101 | loop fusion | bytes 2097152 | tf_op jit(solution)/shard_map/slice | solution.py:72
  85.6 1.7 %fusion.32 = (bf16[1,4,16,4096]{3,2,1,0:T(8,128)(2,1)S(1)}, bf16[1,4,16,4096]{3,2,1,0:T(8,128)(2,1)S(1)}, bf16[1,4,16,4096]{3,2,1,0:T(8,128)(2,1)S(1)}, bf16[1,4,16,4096]{3,2,1,0:T(8,128)(2,1)S(1)}) fusion(bf16[4,4,16,4096]{3,2,1,0:T(8,128)(2,1)} %collective-permute-done.17), kind=kLoop, calls=%fused_computation.97 | loop fusion | bytes 4194304 | tf_op jit(solution)/shard_map/slice | solution.py:72
  89.7 1.1 pad_maximum_fusion
  90.8 11.3 %convert_bitcast_fusion = bf16[2,4096,512]{2,1,0:T(8,128)(2,1)} fusion(bf16[1024,4096,1]{1,0,2:T(8,128)(2,1)S(1)} %bitcast.93, bf16[1024,1,512]{2,0,1:T(8,128)(2,1)S(1)} %maximum_bitcast_fusion.7, bf16[1024,1,512]{2,0,1:T(8,128)(2,1)S(1)} %maximum_bitcast_fusion.6), kind=kOutput, calls=%fused_computation.1 | convolution fusion | flops 8598323200 | bytes 18874368 | tf_op jit(solution)/shard_map/dot_general | solution.py:106
  102.1 11.3 %convert_bitcast_fusion.1 = bf16[2,4096,512]{2,1,0:T(8,128)(2,1)} fusion(bf16[1024,4096,1]{1,0,2:T(8,128)(2,1)S(1)} %bitcast.94, bf16[1024,1,512]{2,0,1:T(8,128)(2,1)S(1)} %maximum_bitcast_fusion.5, bf16[1024,1,512]{2,0,1:T(8,128)(2,1)S(1)} %maximum_bitcast_fusion.4), kind=kOutput, calls=%fused_computation.2 | convolution fusion | flops 8598323200 | bytes 18874368 | tf_op jit(solution)/shard_map/dot_general | solution.py:105
  (112 shorter events, 16.8 us)
Async XLA Ops:
  0.6 11.4 %copy-start.13 = (s32[16]{0:T(128)S(1)}, s32[16]{0:T(128)}, u32[]{:S(2)}) copy-start(s32[16]{0:T(128)} %param.9) | copy-start | bytes 196
  0.6 11.4 %copy-start.14 = (s32[16]{0:T(128)S(1)}, s32[16]{0:T(128)}, u32[]{:S(2)}) copy-start(s32[16]{0:T(128)} %param.10) | copy-start | bytes 196
  0.7 11.4 %copy-start.10 = (f32[2]{0:T(128)S(1)}, f32[2]{0:T(128)}, u32[]{:S(2)}) copy-start(f32[2]{0:T(128)} %param.13) | copy-start | bytes 28
  0.7 17.4 %collective-permute-start.1 = (bf16[16,4096]{1,0:T(8,128)(2,1)}, bf16[16,4096]{1,0:T(8,128)(2,1)S(1)}, u32[]{:S(2)}, u32[]{:S(2)}) collective-permute-start(bf16[16,4096]{1,0:T(8,128)(2,1)} %param.7), channel_id=1, source_target_pairs={{0,8},{8,16},{16,24},{24,0},{1,9},{9,17},{17,25},{25,1},{2,10},{10... | collective-permute-start | bytes 393224 | tf_op jit(solution)/shard_map/ppermute | solution.py:17
  0.9 18.7 %collective-permute-start = (bf16[16,4096]{1,0:T(8,128)(2,1)}, bf16[16,4096]{1,0:T(8,128)(2,1)S(1)}, u32[]{:S(2)}, u32[]{:S(2)}) collective-permute-start(bf16[16,4096]{1,0:T(8,128)(2,1)} %param.7), channel_id=1, source_target_pairs={{0,24},{8,0},{16,8},{24,16},{1,25},{9,1},{17,9},{25,17},{2,26},{10... | collective-permute-start | bytes 393224 | tf_op jit(solution)/shard_map/ppermute | solution.py:17
  2.2 13.0 %collective-permute-start.5 = (bf16[16,4096]{1,0:T(8,128)(2,1)}, bf16[16,4096]{1,0:T(8,128)(2,1)S(1)}, u32[]{:S(2)}, u32[]{:S(2)}) collective-permute-start(bf16[16,4096]{1,0:T(8,128)(2,1)} %param.8), channel_id=1, source_target_pairs={{0,2},{2,4},{4,6},{6,0},{1,3},{3,5},{5,7},{7,1},{8,10},{10,12},{12... | collective-permute-start | bytes 393224 | tf_op jit(solution)/shard_map/ppermute | solution.py:17
  3.5 11.8 %collective-permute-start.4 = (bf16[16,4096]{1,0:T(8,128)(2,1)}, bf16[16,4096]{1,0:T(8,128)(2,1)S(1)}, u32[]{:S(2)}, u32[]{:S(2)}) collective-permute-start(bf16[16,4096]{1,0:T(8,128)(2,1)} %param.8), channel_id=1, source_target_pairs={{0,6},{2,0},{4,2},{6,4},{1,7},{3,1},{5,3},{7,5},{8,14},{10,8},{12,... | collective-permute-start | bytes 393224 | tf_op jit(solution)/shard_map/ppermute | solution.py:17
  5.9 13.8 %copy-start.8 = (bf16[16,4096]{1,0:T(8,128)(2,1)S(1)}, bf16[16,4096]{1,0:T(8,128)(2,1)}, u32[]{:S(2)}) copy-start(bf16[16,4096]{1,0:T(8,128)(2,1)} %param.8) | copy-start | bytes 393220
  7.0 17.1 %copy-start.9 = (bf16[16,4096]{1,0:T(8,128)(2,1)S(1)}, bf16[16,4096]{1,0:T(8,128)(2,1)}, u32[]{:S(2)}) copy-start(bf16[16,4096]{1,0:T(8,128)(2,1)} %param.7) | copy-start | bytes 393220
  7.0 22.3 %all-to-all-start = ((bf16[4,2,16,4096]{3,2,1,0:T(8,128)(2,1)}), bf16[4,2,16,4096]{3,2,1,0:T(8,128)(2,1)S(1)}, u32[]{:S(2)}, u32[]{:S(2)}) async-start(bf16[4,2,16,4096]{3,2,1,0:T(8,128)(2,1)} %broadcast_in_dim.28), calls=%async_computation | async-start | bytes 2097152 | tf_op jit(solution)/shard_map/all_to_all | solution.py:49
  15.2 4.5 %collective-permute-start.6 = (bf16[16,2048]{1,0:T(8,128)(2,1)S(1)}, bf16[16,2048]{1,0:T(8,128)(2,1)S(1)}, u32[]{:S(2)}, u32[]{:S(2)}) collective-permute-start(bf16[16,2048]{1,0:T(8,128)(2,1)S(1)} %slice.134), channel_id=1, source_target_pairs={{0,2},{2,4},{4,6},{6,0},{1,3},{3,5},{5,7},{7,1},{8,10},{10,12},{12... | collective-permute-start | bytes 196616 | tf_op jit(solution)/shard_map/ppermute | solution.py:17
  15.3 4.4 %collective-permute-start.7 = (bf16[16,2048]{1,0:T(8,128)(2,1)S(1)}, bf16[16,2048]{1,0:T(8,128)(2,1)S(1)}, u32[]{:S(2)}, u32[]{:S(2)}) collective-permute-start(bf16[16,2048]{1,0:T(8,128)(2,1)S(1)} %slice.135), channel_id=1, source_target_pairs={{0,6},{2,0},{4,2},{6,4},{1,7},{3,1},{5,3},{7,5},{8,14},{10,8},{12,... | collective-permute-start | bytes 196616 | tf_op jit(solution)/shard_map/ppermute | solution.py:17
  18.1 3.5 %collective-permute-start.2 = (bf16[16,2048]{1,0:T(8,128)(2,1)S(1)}, bf16[16,2048]{1,0:T(8,128)(2,1)S(1)}, u32[]{:S(2)}, u32[]{:S(2)}) collective-permute-start(bf16[16,2048]{1,0:T(8,128)(2,1)S(1)} %slice.132), channel_id=1, source_target_pairs={{0,8},{8,16},{16,24},{24,0},{1,9},{9,17},{17,25},{25,1},{2,10},{10... | collective-permute-start | bytes 196616 | tf_op jit(solution)/shard_map/ppermute | solution.py:17
  19.6 4.5 %collective-permute-start.3 = (bf16[16,2048]{1,0:T(8,128)(2,1)S(1)}, bf16[16,2048]{1,0:T(8,128)(2,1)S(1)}, u32[]{:S(2)}, u32[]{:S(2)}) collective-permute-start(bf16[16,2048]{1,0:T(8,128)(2,1)S(1)} %slice.133), channel_id=1, source_target_pairs={{0,24},{8,0},{16,8},{24,16},{1,25},{9,1},{17,9},{25,17},{2,26},{10... | collective-permute-start | bytes 196616 | tf_op jit(solution)/shard_map/ppermute | solution.py:17
  25.1 16.5 %collective-permute-start.16 = (bf16[2,4,16,4096]{3,2,1,0:T(8,128)(2,1)S(1)}, bf16[2,4,16,4096]{3,2,1,0:T(8,128)(2,1)}, u32[]{:S(2)}, u32[]{:S(2)}) collective-permute-start(bf16[2,4,16,4096]{3,2,1,0:T(8,128)(2,1)S(1)} %pad_maximum_fusion.3), channel_id=1, source_target_pairs={{0,1},{1,0},{2,3},{3,2},{4,5},{5,4},{6,7},{7,6},{8,9},{9,8},{10,11... | collective-permute-start | bytes 3145736 | tf_op jit(solution)/shard_map/ppermute | solution.py:54
  29.9 15.1 %collective-permute-start.9 = (bf16[4,16,4096]{2,1,0:T(8,128)(2,1)}, bf16[4,16,4096]{2,1,0:T(8,128)(2,1)}, u32[]{:S(2)}, u32[]{:S(2)}) collective-permute-start(bf16[4,16,4096]{2,1,0:T(8,128)(2,1)} %get-tuple-element.7), channel_id=1, source_target_pairs={{0,2},{2,4},{4,6},{6,0},{1,3},{3,5},{5,7},{7,1},{8,10},{10,12},{12... | collective-permute-start | bytes 1572872 | tf_op jit(solution)/shard_map/ppermute | solution.py:17
  30.0 16.2 %collective-permute-start.8 = (bf16[4,16,4096]{2,1,0:T(8,128)(2,1)}, bf16[4,16,4096]{2,1,0:T(8,128)(2,1)}, u32[]{:S(2)}, u32[]{:S(2)}) collective-permute-start(bf16[4,16,4096]{2,1,0:T(8,128)(2,1)} %get-tuple-element.7), channel_id=1, source_target_pairs={{0,6},{2,0},{4,2},{6,4},{1,7},{3,1},{5,3},{7,5},{8,14},{10,8},{12,... | collective-permute-start | bytes 1572872 | tf_op jit(solution)/shard_map/ppermute | solution.py:17
  32.6 17.1 %collective-permute-start.11 = (bf16[4,16,4096]{2,1,0:T(8,128)(2,1)}, bf16[4,16,4096]{2,1,0:T(8,128)(2,1)S(1)}, u32[]{:S(2)}, u32[]{:S(2)}) collective-permute-start(bf16[4,16,4096]{2,1,0:T(8,128)(2,1)} %get-tuple-element.8), channel_id=1, source_target_pairs={{0,8},{8,16},{16,24},{24,0},{1,9},{9,17},{17,25},{25,1},{2,10},{10... | collective-permute-start | bytes 1572872 | tf_op jit(solution)/shard_map/ppermute | solution.py:17
  32.6 17.1 %collective-permute-start.10 = (bf16[4,16,4096]{2,1,0:T(8,128)(2,1)}, bf16[4,16,4096]{2,1,0:T(8,128)(2,1)S(1)}, u32[]{:S(2)}, u32[]{:S(2)}) collective-permute-start(bf16[4,16,4096]{2,1,0:T(8,128)(2,1)} %get-tuple-element.8), channel_id=1, source_target_pairs={{0,24},{8,0},{16,8},{24,16},{1,25},{9,1},{17,9},{25,17},{2,26},{10... | collective-permute-start | bytes 1572872 | tf_op jit(solution)/shard_map/ppermute | solution.py:17
  35.8 40.8 %all-to-all-start.1 = ((bf16[2,16,32,640]{3,1,0,2:T(8,128)(2,1)}), bf16[2,16,32,640]{3,1,0,2:T(8,128)(2,1)S(1)}, u32[]{:S(2)}, u32[]{:S(2)}) async-start(bf16[2,16,32,640]{3,1,0,2:T(8,128)(2,1)} %copy.39), calls=%async_computation.1 | async-start | bytes 2621440 | tf_op jit(solution)/shard_map/all_to_all | solution.py:60
  46.0 18.6 %collective-permute-start.12 = (bf16[4,16,2048]{2,1,0:T(8,128)(2,1)S(1)}, bf16[4,16,2048]{2,1,0:T(8,128)(2,1)S(1)}, u32[]{:S(2)}, u32[]{:S(2)}) collective-permute-start(bf16[4,16,2048]{2,1,0:T(8,128)(2,1)S(1)} %slice.137), channel_id=1, source_target_pairs={{0,2},{2,4},{4,6},{6,0},{1,3},{3,5},{5,7},{7,1},{8,10},{10,12},{12... | collective-permute-start | bytes 786440 | tf_op jit(solution)/shard_map/ppermute | solution.py:17
  47.2 17.4 %collective-permute-start.13 = (bf16[4,16,2048]{2,1,0:T(8,128)(2,1)S(1)}, bf16[4,16,2048]{2,1,0:T(8,128)(2,1)S(1)}, u32[]{:S(2)}, u32[]{:S(2)}) collective-permute-start(bf16[4,16,2048]{2,1,0:T(8,128)(2,1)S(1)} %slice.138), channel_id=1, source_target_pairs={{0,6},{2,0},{4,2},{6,4},{1,7},{3,1},{5,3},{7,5},{8,14},{10,8},{12,... | collective-permute-start | bytes 786440 | tf_op jit(solution)/shard_map/ppermute | solution.py:17
  52.5 9.3 %copy-start.7 = (bf16[4,16,4096]{2,1,0:T(8,128)(2,1)S(1)}, bf16[4,16,4096]{2,1,0:T(8,128)(2,1)}, u32[]{:S(2)}) copy-start(bf16[4,16,4096]{2,1,0:T(8,128)(2,1)} %copy-done.6) | copy-start | bytes 1572868
  52.5 9.4 %copy-start.5 = (bf16[4,16,4096]{2,1,0:T(8,128)(2,1)S(1)}, bf16[4,16,4096]{2,1,0:T(8,128)(2,1)}, u32[]{:S(2)}) copy-start(bf16[4,16,4096]{2,1,0:T(8,128)(2,1)} %copy-done.4) | copy-start | bytes 1572868
  52.7 33.0 %collective-permute-start.17 = (bf16[4,4,16,4096]{3,2,1,0:T(8,128)(2,1)S(1)}, bf16[4,4,16,4096]{3,2,1,0:T(8,128)(2,1)}, u32[]{:S(2)}, u32[]{:S(2)}) collective-permute-start(bf16[4,4,16,4096]{3,2,1,0:T(8,128)(2,1)S(1)} %pad_maximum_fusion.1), channel_id=1, source_target_pairs={{0,1},{1,0},{2,3},{3,2},{4,5},{5,4},{6,7},{7,6},{8,9},{9,8},{10,11... | collective-permute-start | bytes 6291464 | tf_op jit(solution)/shard_map/ppermute | solution.py:65
  61.8 7.1 %collective-permute-start.14 = (bf16[4,16,2048]{2,1,0:T(8,128)(2,1)S(1)}, bf16[4,16,2048]{2,1,0:T(8,128)(2,1)S(1)}, u32[]{:S(2)}, u32[]{:S(2)}) collective-permute-start(bf16[4,16,2048]{2,1,0:T(8,128)(2,1)S(1)} %slice.139), channel_id=1, source_target_pairs={{0,8},{8,16},{16,24},{24,0},{1,9},{9,17},{17,25},{25,1},{2,10},{10... | collective-permute-start | bytes 786440 | tf_op jit(solution)/shard_map/ppermute | solution.py:17
  61.9 8.3 %collective-permute-start.15 = (bf16[4,16,2048]{2,1,0:T(8,128)(2,1)S(1)}, bf16[4,16,2048]{2,1,0:T(8,128)(2,1)S(1)}, u32[]{:S(2)}, u32[]{:S(2)}) collective-permute-start(bf16[4,16,2048]{2,1,0:T(8,128)(2,1)S(1)} %slice.140), channel_id=1, source_target_pairs={{0,24},{8,0},{16,8},{24,16},{1,25},{9,1},{17,9},{25,17},{2,26},{10... | collective-permute-start | bytes 786440 | tf_op jit(solution)/shard_map/ppermute | solution.py:17
  71.3 13.0 %collective-permute-start.18 = (bf16[2,4,16,4096]{3,2,1,0:T(8,128)(2,1)}, bf16[2,4,16,4096]{3,2,1,0:T(8,128)(2,1)}, u32[]{:S(2)}, u32[]{:S(2)}) collective-permute-start(bf16[2,4,16,4096]{3,2,1,0:T(8,128)(2,1)} %pad_maximum_fusion.4), channel_id=1, source_target_pairs={{0,1},{1,0},{2,3},{3,2},{4,5},{5,4},{6,7},{7,6},{8,9},{9,8},{10,11... | collective-permute-start | bytes 3145736 | tf_op jit(solution)/shard_map/ppermute | solution.py:67
  76.8 1.9 %copy-start.11 = (f32[16]{0:T(128)S(1)}, f32[16]{0:T(128)}, u32[]{:S(2)}) copy-start(f32[16]{0:T(128)} %param.11) | copy-start | bytes 196
  76.8 2.0 %copy-start.12 = (f32[32]{0:T(128)S(1)}, f32[32]{0:T(128)}, u32[]{:S(2)}) copy-start(f32[32]{0:T(128)} %param.12) | copy-start | bytes 388
  85.6 1.8 %copy-start.3 = (bf16[1,4,16,4096]{3,2,1,0:T(8,128)(2,1)S(1)}, bf16[1,4,16,4096]{3,2,1,0:T(8,128)(2,1)}, u32[]{:S(2)}) copy-start(bf16[1,4,16,4096]{3,2,1,0:T(8,128)(2,1)} %get-tuple-element.31) | copy-start | bytes 1572868
  87.5 2.2 %copy-start.1 = (bf16[1,4,4,16,4096]{4,3,2,1,0:T(8,128)(2,1)S(1)}, bf16[1,4,4,16,4096]{4,3,2,1,0:T(8,128)(2,1)}, u32[]{:S(2)}) copy-start(bf16[1,4,4,16,4096]{4,3,2,1,0:T(8,128)(2,1)} %get-tuple-element.55) | copy-start | bytes 6291460
  (4 other events, 5.1 us)

commit v12 on v6

--- a/solution.py
+++ b/solution.py
@@ -45,8 +45,7 @@
     width = local_g * nrow // ncol
     both = jnp.stack([matrix_real, matrix_imag])
 
-    copies = jnp.broadcast_to(both[None], (nrow,) + both.shape)
-    spread = lax.all_to_all(copies, "row", 0, 0, tiled=True)
+    spread = lax.all_gather(both, "row", axis=0)
     spread = spread.reshape(nrow, 2, local_pairs, local_g // width, width)
     row_real = jnp.stack((matrix_real,) + ring_gather(matrix_real, "x"))
     col_imag = jnp.stack((matrix_imag,) + ring_gather(matrix_imag, "y"))

time: 109 us -> 131 us (1.20)
  between operations: 3.77 us -> 17 us
  waiting for transfers between devices: 14.6 us -> 26.6 us
  starting transfers between devices: 40.2 us -> 34.4 us
  other arithmetic: 13.8 us -> 16.1 us
    all_gather x0 -> x1, waiting for transfers between devices: none -> 12.5 us  [on_device(): spread = lax.all_gather(both, 'row', axis=0)]
    all_to_all x1 -> x0, starting transfers between devices: 5.16 us -> none  [on_device(): spread = lax.all_to_all(copies, 'row', 0, 0, tiled=True)]
    all_to_all x1, starting transfers between devices: 5.14 us -> 7.14 us  [on_device(): lax.all_to_all(payload, cols, split_axis=2, concat_axis=1, tiled=True)]
    ppermute x16, starting transfers between devices: 24.5 us -> 23.1 us  [shift(): lax.ppermute(value, axis, [(i, (i + step) % size) for i in range(size)])]
    unnamed x27 -> x17, local copies, waits for them, and re-layouts: 2.16 us -> 3.36 us
  transfers between devices with their start and end apart: 21 -> 21, of which waited for: 4 -> 3; matrix products, arithmetic and copies ran while one was open for 20% -> 19% of each run, Pallas kernels for 0% -> 0%
where the time goes in v12:
time: 131 us; the launch traced here: 130 us
  starting transfers between devices  34.4 us (26%)
  waiting for transfers between devices  26.6 us (20%)
  matrix products  22.6 us (17%)
  between operations  17 us (13%)
  other arithmetic  16.1 us (12%)
  local copies, waits for them, and re-layouts  13.7 us (10%)
    ppermute x16, starting transfers between devices, shift(): lax.ppermute(value, axis, [(i, (i + step) % size) for i in range(size)])  23.1 us
    ppermute x16, waiting for transfers between devices, shift(): lax.ppermute(value, axis, [(i, (i + step) % size) for i in range(size)])  14.1 us
    all_gather x1, waiting for transfers between devices, on_device(): spread = lax.all_gather(both, 'row', axis=0)  12.5 us
    dot_general x1, matrix products, on_device(): lax.dot_general(left, jnp.stack(right_imag, axis=1), dims, preferred_elem...  11.3 us
    dot_general x1, matrix products, on_device(): lax.dot_general(left, jnp.stack(right_real, axis=1), dims, preferred_elem...  11.3 us
    all_to_all x1, starting transfers between devices, on_device(): lax.all_to_all(payload, cols, split_axis=2, concat_axis=1, tiled=True)  7.14 us
    another operation x3, other arithmetic, on_device(): left = jnp.stack(parts).reshape(2 * pairs, local_g)  6.7 us
    unnamed x17, local copies, waits for them, and re-layouts  3.36 us
  transfers between devices with their start and end apart: 21, of which 3 were waited for; matrix products, arithmetic and copies ran while one was open for 19% of the time, Pallas kernels for 0%

profile of v12, /device:TPU:1, one launch (start us, length us, event | category | flops | bytes accessed | tf_op | source)
XLA Modules:
  0.0 130.4 jit_solution(3115227120799873819)
XLA Ops:
  7.2 2.2 %collective-permute-start.5 = (bf16[16,4096]{1,0:T(8,128)(2,1)}, bf16[16,4096]{1,0:T(8,128)(2,1)S(1)}, u32[]{:S(2)}, u32[]{:S(2)}) collective-permute-start(bf16[16,4096]{1,0:T(8,128)(2,1)} %param.8), channel_id=1, source_target_pairs={{0,2},{2,4},{4,6},{6,0},{1,3},{3,5},{5,7},{7,1},{8,10},{10,12},{12... | collective-permute-start | bytes 393224 | tf_op jit(solution)/shard_map/ppermute | solution.py:17
  9.4 1.5 %collective-permute-start.4 = (bf16[16,4096]{1,0:T(8,128)(2,1)}, bf16[16,4096]{1,0:T(8,128)(2,1)S(1)}, u32[]{:S(2)}, u32[]{:S(2)}) collective-permute-start(bf16[16,4096]{1,0:T(8,128)(2,1)} %param.8), channel_id=1, source_target_pairs={{0,6},{2,0},{4,2},{6,4},{1,7},{3,1},{5,3},{7,5},{8,14},{10,8},{12,... | collective-permute-start | bytes 393224 | tf_op jit(solution)/shard_map/ppermute | solution.py:17
  10.9 1.2 collective-permute-start.1
  12.1 1.5 %collective-permute-start = (bf16[16,4096]{1,0:T(8,128)(2,1)}, bf16[16,4096]{1,0:T(8,128)(2,1)S(1)}, u32[]{:S(2)}, u32[]{:S(2)}) collective-permute-start(bf16[16,4096]{1,0:T(8,128)(2,1)} %param.7), channel_id=1, source_target_pairs={{0,24},{8,0},{16,8},{24,16},{1,25},{9,1},{17,9},{25,17},{2,26},{10... | collective-permute-start | bytes 393224 | tf_op jit(solution)/shard_map/ppermute | solution.py:17
  14.2 2.7 %collective-permute-start.7 = (bf16[16,2048]{1,0:T(8,128)(2,1)S(1)}, bf16[16,2048]{1,0:T(8,128)(2,1)S(1)}, u32[]{:S(2)}, u32[]{:S(2)}) collective-permute-start(bf16[16,2048]{1,0:T(8,128)(2,1)S(1)} %slice.111), channel_id=1, source_target_pairs={{0,6},{2,0},{4,2},{6,4},{1,7},{3,1},{5,3},{7,5},{8,14},{10,8},{12,... | collective-permute-start | bytes 196616 | tf_op jit(solution)/shard_map/ppermute | solution.py:17
  16.9 1.7 %pad_maximum_fusion.8 = bf16[2,16,4096]{2,1,0:T(8,128)(2,1)} fusion(bf16[1,16,4096]{2,1,0:T(8,128)(2,1)} %bitcast.110, bf16[1,16,4096]{2,1,0:T(8,128)(2,1)} %bitcast.112), kind=kLoop, calls=%fused_computation.75 | loop fusion | flops 131072 | bytes 524288 | tf_op jit(solution)/shard_map/stack | solution.py:46
  18.7 1.2 collective-permute-start.2
  19.9 1.6 %collective-permute-start.3 = (bf16[16,2048]{1,0:T(8,128)(2,1)S(1)}, bf16[16,2048]{1,0:T(8,128)(2,1)S(1)}, u32[]{:S(2)}, u32[]{:S(2)}) collective-permute-start(bf16[16,2048]{1,0:T(8,128)(2,1)S(1)} %slice.109), channel_id=1, source_target_pairs={{0,24},{8,0},{16,8},{24,16},{1,25},{9,1},{17,9},{25,17},{2,26},{10... | collective-permute-start | bytes 196616 | tf_op jit(solution)/shard_map/ppermute | solution.py:17
  21.5 1.8 %fusion.29 = (bf16[1,4,16,4096]{3,2,1,0:T(8,128)(2,1)S(1)}, bf16[4,16,4096]{2,1,0:T(8,128)(2,1)}) fusion(bf16[1,16,4096]{2,1,0:T(8,128)(2,1)S(1)} %bitcast.116, bf16[1,16,4096]{2,1,0:T(8,128)(2,1)S(1)} %maximum_bitcast_fusion.10, bf16[1,16,4096]{2,1,0:T(8,128)(2,1)S(1)} %bitcast.117, bf16[1,16,4096]{2,1,0:T(8,128)(2,1)} %bitcast.111), kind=kLoop, calls=%fused_computation.95 | loop fusion | flops 786432 | bytes 1572864 | tf_op jit(solution)/shard_map/stack | solution.py:52
  24.3 3.3 %collective-permute-start.12 = (bf16[2,4,16,4096]{3,2,1,0:T(8,128)(2,1)S(1)}, bf16[2,4,16,4096]{3,2,1,0:T(8,128)(2,1)S(1)}, u32[]{:S(2)}, u32[]{:S(2)}) collective-permute-start(bf16[2,4,16,4096]{3,2,1,0:T(8,128)(2,1)S(1)} %pad_maximum_fusion.4), channel_id=1, source_target_pairs={{0,1},{1,0},{2,3},{3,2},{4,5},{5,4},{6,7},{7,6},{8,9},{9,8},{10,11... | collective-permute-start | bytes 3145736 | tf_op jit(solution)/shard_map/ppermute | solution.py:53
  30.7 12.5 %all-gather.3.cloned.1.call-done = bf16[8,16,4096]{2,1,0:T(8,128)(2,1)} async-done(((bf16[2,16,4096]{2,1,0:T(8,128)(2,1)}), bf16[8,16,4096]{2,1,0:T(8,128)(2,1)}) %all-gather.3.cloned.1.call-update) | async-done | bytes 1048592 | tf_op jit(solution)/shard_map/all_gather | solution.py:48
  43.2 1.6 %copy.68 = bf16[16,8,8,512]{3,2,1,0:T(8,128)(2,1)S(1)} copy(bf16[16,8,8,512]{3,1,2,0:T(8,128)(2,1)} %bitcast.109) | data formatting | bytes 2097152
  44.8 1.3 collective-permute-start.9
  46.1 1.5 %collective-permute-start.8 = (bf16[4,16,4096]{2,1,0:T(8,128)(2,1)}, bf16[4,16,4096]{2,1,0:T(8,128)(2,1)}, u32[]{:S(2)}, u32[]{:S(2)}) collective-permute-start(bf16[4,16,4096]{2,1,0:T(8,128)(2,1)} %get-tuple-element.7), channel_id=1, source_target_pairs={{0,6},{2,0},{4,2},{6,4},{1,7},{3,1},{5,3},{7,5},{8,14},{10,8},{12,... | collective-permute-start | bytes 1572872 | tf_op jit(solution)/shard_map/ppermute | solution.py:17
  47.7 1.3 collective-permute-start.14
  48.9 1.5 %collective-permute-start.13 = (bf16[4,16,4096]{2,1,0:T(8,128)(2,1)}, bf16[4,16,4096]{2,1,0:T(8,128)(2,1)}, u32[]{:S(2)}, u32[]{:S(2)}) collective-permute-start(bf16[4,16,4096]{2,1,0:T(8,128)(2,1)} %get-tuple-element.8), channel_id=1, source_target_pairs={{0,24},{8,0},{16,8},{24,16},{1,25},{9,1},{17,9},{25,17},{2,26},{10... | collective-permute-start | bytes 1572872 | tf_op jit(solution)/shard_map/ppermute | solution.py:17
  50.8 1.5 %copy.52 = bf16[2,16,32,640]{3,1,0,2:T(8,128)(2,1)} copy(bf16[2,16,32,640]{3,2,1,0:T(8,128)(2,1)S(1)} %pad_maximum_fusion.3) | data formatting | bytes 2621440 | tf_op jit(solution)/shard_map/concatenate | solution.py:58
  52.4 7.1 %all-to-all-start = ((bf16[2,16,32,640]{3,1,0,2:T(8,128)(2,1)}), bf16[2,16,32,640]{3,1,0,2:T(8,128)(2,1)S(1)}, u32[]{:S(2)}, u32[]{:S(2)}) async-start(bf16[2,16,32,640]{3,1,0,2:T(8,128)(2,1)} %copy.52), calls=%async_computation | async-start | bytes 2621440 | tf_op jit(solution)/shard_map/all_to_all | solution.py:59
  60.5 1.5 %collective-permute-start.10 = (bf16[4,16,2048]{2,1,0:T(8,128)(2,1)S(1)}, bf16[4,16,2048]{2,1,0:T(8,128)(2,1)S(1)}, u32[]{:S(2)}, u32[]{:S(2)}) collective-permute-start(bf16[4,16,2048]{2,1,0:T(8,128)(2,1)S(1)} %slice.112), channel_id=1, source_target_pairs={{0,2},{2,4},{4,6},{6,0},{1,3},{3,5},{5,7},{7,1},{8,10},{10,12},{12... | collective-permute-start | bytes 786440 | tf_op jit(solution)/shard_map/ppermute | solution.py:17
  62.9 1.4 %collective-permute-start.11 = (bf16[4,16,2048]{2,1,0:T(8,128)(2,1)S(1)}, bf16[4,16,2048]{2,1,0:T(8,128)(2,1)S(1)}, u32[]{:S(2)}, u32[]{:S(2)}) collective-permute-start(bf16[4,16,2048]{2,1,0:T(8,128)(2,1)S(1)} %slice.113), channel_id=1, source_target_pairs={{0,6},{2,0},{4,2},{6,4},{1,7},{3,1},{5,3},{7,5},{8,14},{10,8},{12,... | collective-permute-start | bytes 786440 | tf_op jit(solution)/shard_map/ppermute | solution.py:17
  64.4 1.0 slice.116
  65.3 1.5 %collective-permute-start.16 = (bf16[4,16,2048]{2,1,0:T(8,128)(2,1)S(1)}, bf16[4,16,2048]{2,1,0:T(8,128)(2,1)S(1)}, u32[]{:S(2)}, u32[]{:S(2)}) collective-permute-start(bf16[4,16,2048]{2,1,0:T(8,128)(2,1)S(1)} %slice.116), channel_id=1, source_target_pairs={{0,8},{8,16},{16,24},{24,0},{1,9},{9,17},{17,25},{25,1},{2,10},{10... | collective-permute-start | bytes 786440 | tf_op jit(solution)/shard_map/ppermute | solution.py:17
  67.8 1.4 %collective-permute-start.17 = (bf16[4,16,2048]{2,1,0:T(8,128)(2,1)S(1)}, bf16[4,16,2048]{2,1,0:T(8,128)(2,1)S(1)}, u32[]{:S(2)}, u32[]{:S(2)}) collective-permute-start(bf16[4,16,2048]{2,1,0:T(8,128)(2,1)S(1)} %slice.117), channel_id=1, source_target_pairs={{0,24},{8,0},{16,8},{24,16},{1,25},{9,1},{17,9},{25,17},{2,26},{10... | collective-permute-start | bytes 786440 | tf_op jit(solution)/shard_map/ppermute | solution.py:17
  69.1 13.5 %collective-permute-done.10 = bf16[4,16,2048]{2,1,0:T(8,128)(2,1)S(1)} collective-permute-done((bf16[4,16,2048]{2,1,0:T(8,128)(2,1)S(1)}, bf16[4,16,2048]{2,1,0:T(8,128)(2,1)S(1)}, u32[]{:S(2)}, u32[]{:S(2)}) %collective-permute-start.10) | collective-permute-done | bytes 262176 | tf_op jit(solution)/shard_map/ppermute | solution.py:17
  82.7 1.1 pad_maximum_fusion.5
  84.7 5.0 %maximum_bitcast_fusion = (bf16[1,4,4,16,4096]{4,3,2,1,0:T(8,128)(2,1)}, bf16[4,4,16,4096]{3,2,1,0:T(8,128)(2,1)}, bf16[1,4,4,16,4096]{4,3,2,1,0:T(8,128)(2,1)}) fusion(bf16[1,4,16,4096]{3,2,1,0:T(8,128)(2,1)} %bitcast.12, bf16[1,4,16,4096]{3,2,1,0:T(8,128)(2,1)S(1)} %maximum_bitcast_fusion.7, bf16[1,4,16,4096]{3,2,1,0:T(8,128)(2,1)} %bitcast.10, ...), kind=kLoop, calls=%fused_computation.6 | loop fusion | flops 9437184 | bytes 10485760 | tf_op jit(solution)/shard_map/stack | solution.py:73
  94.6 1.3 fusion.35
  95.9 1.7 %fusion.32 = (bf16[1,4,16,4096]{3,2,1,0:T(8,128)(2,1)S(1)}, bf16[1,4,16,4096]{3,2,1,0:T(8,128)(2,1)S(1)}, bf16[1,4,16,4096]{3,2,1,0:T(8,128)(2,1)S(1)}, bf16[1,4,16,4096]{3,2,1,0:T(8,128)(2,1)S(1)}) fusion(bf16[4,4,16,4096]{3,2,1,0:T(8,128)(2,1)} %collective-permute-done.15), kind=kLoop, calls=%fused_computation.98 | loop fusion | bytes 4194304 | tf_op jit(solution)/shard_map/slice | solution.py:71
  98.2 1.0 copy-done
  99.8 1.1 pad_maximum_fusion
  100.9 11.3 %convert_bitcast_fusion = bf16[2,4096,512]{2,1,0:T(8,128)(2,1)} fusion(bf16[1024,4096,1]{1,0,2:T(8,128)(2,1)S(1)} %bitcast.94, bf16[1024,1,512]{2,0,1:T(8,128)(2,1)S(1)} %maximum_bitcast_fusion.6, bf16[1024,1,512]{2,0,1:T(8,128)(2,1)S(1)} %maximum_bitcast_fusion.5), kind=kOutput, calls=%fused_computation.1 | convolution fusion | flops 8598323200 | bytes 18874368 | tf_op jit(solution)/shard_map/dot_general | solution.py:105
  112.2 11.3 %convert_bitcast_fusion.1 = bf16[2,4096,512]{2,1,0:T(8,128)(2,1)} fusion(bf16[1024,4096,1]{1,0,2:T(8,128)(2,1)S(1)} %bitcast.95, bf16[1024,1,512]{2,0,1:T(8,128)(2,1)S(1)} %maximum_bitcast_fusion.4, bf16[1024,1,512]{2,0,1:T(8,128)(2,1)S(1)} %maximum_bitcast_fusion.3), kind=kOutput, calls=%fused_computation.2 | convolution fusion | flops 8598323200 | bytes 18874368 | tf_op jit(solution)/shard_map/dot_general | solution.py:104
  (95 shorter events, 12.5 us)
Async XLA Ops:
  7.2 16.2 %copy-start.2 = (bf16[16,4096]{1,0:T(8,128)(2,1)S(1)}, bf16[16,4096]{1,0:T(8,128)(2,1)}, u32[]{:S(2)}) copy-start(bf16[16,4096]{1,0:T(8,128)(2,1)} %param.7) | copy-start | bytes 393220
  7.2 36.0 %all-gather.3.cloned.1.call-start = ((), (), s32[]{:S(2)}) async-start(), calls=%async_computation.1 | async-start | bytes 1310720 | tf_op jit(solution)/shard_map/all_gather | solution.py:48
  7.2 6.9 %collective-permute-start.5 = (bf16[16,4096]{1,0:T(8,128)(2,1)}, bf16[16,4096]{1,0:T(8,128)(2,1)S(1)}, u32[]{:S(2)}, u32[]{:S(2)}) collective-permute-start(bf16[16,4096]{1,0:T(8,128)(2,1)} %param.8), channel_id=1, source_target_pairs={{0,2},{2,4},{4,6},{6,0},{1,3},{3,5},{5,7},{7,1},{8,10},{10,12},{12... | collective-permute-start | bytes 393224 | tf_op jit(solution)/shard_map/ppermute | solution.py:17
  9.4 4.7 %collective-permute-start.4 = (bf16[16,4096]{1,0:T(8,128)(2,1)}, bf16[16,4096]{1,0:T(8,128)(2,1)S(1)}, u32[]{:S(2)}, u32[]{:S(2)}) collective-permute-start(bf16[16,4096]{1,0:T(8,128)(2,1)} %param.8), channel_id=1, source_target_pairs={{0,6},{2,0},{4,2},{6,4},{1,7},{3,1},{5,3},{7,5},{8,14},{10,8},{12,... | collective-permute-start | bytes 393224 | tf_op jit(solution)/shard_map/ppermute | solution.py:17
  10.9 7.7 %collective-permute-start.1 = (bf16[16,4096]{1,0:T(8,128)(2,1)}, bf16[16,4096]{1,0:T(8,128)(2,1)S(1)}, u32[]{:S(2)}, u32[]{:S(2)}) collective-permute-start(bf16[16,4096]{1,0:T(8,128)(2,1)} %param.7), channel_id=1, source_target_pairs={{0,8},{8,16},{16,24},{24,0},{1,9},{9,17},{17,25},{25,1},{2,10},{10... | collective-permute-start | bytes 393224 | tf_op jit(solution)/shard_map/ppermute | solution.py:17
  12.1 7.7 %collective-permute-start = (bf16[16,4096]{1,0:T(8,128)(2,1)}, bf16[16,4096]{1,0:T(8,128)(2,1)S(1)}, u32[]{:S(2)}, u32[]{:S(2)}) collective-permute-start(bf16[16,4096]{1,0:T(8,128)(2,1)} %param.7), channel_id=1, source_target_pairs={{0,24},{8,0},{16,8},{24,16},{1,25},{9,1},{17,9},{25,17},{2,26},{10... | collective-permute-start | bytes 393224 | tf_op jit(solution)/shard_map/ppermute | solution.py:17
  14.1 7.3 %collective-permute-start.6 = (bf16[16,2048]{1,0:T(8,128)(2,1)S(1)}, bf16[16,2048]{1,0:T(8,128)(2,1)S(1)}, u32[]{:S(2)}, u32[]{:S(2)}) collective-permute-start(bf16[16,2048]{1,0:T(8,128)(2,1)S(1)} %slice.110), channel_id=1, source_target_pairs={{0,2},{2,4},{4,6},{6,0},{1,3},{3,5},{5,7},{7,1},{8,10},{10,12},{12... | collective-permute-start | bytes 196616 | tf_op jit(solution)/shard_map/ppermute | solution.py:17
  14.2 7.3 %collective-permute-start.7 = (bf16[16,2048]{1,0:T(8,128)(2,1)S(1)}, bf16[16,2048]{1,0:T(8,128)(2,1)S(1)}, u32[]{:S(2)}, u32[]{:S(2)}) collective-permute-start(bf16[16,2048]{1,0:T(8,128)(2,1)S(1)} %slice.111), channel_id=1, source_target_pairs={{0,6},{2,0},{4,2},{6,4},{1,7},{3,1},{5,3},{7,5},{8,14},{10,8},{12,... | collective-permute-start | bytes 196616 | tf_op jit(solution)/shard_map/ppermute | solution.py:17
  18.7 4.6 %collective-permute-start.2 = (bf16[16,2048]{1,0:T(8,128)(2,1)S(1)}, bf16[16,2048]{1,0:T(8,128)(2,1)S(1)}, u32[]{:S(2)}, u32[]{:S(2)}) collective-permute-start(bf16[16,2048]{1,0:T(8,128)(2,1)S(1)} %slice.108), channel_id=1, source_target_pairs={{0,8},{8,16},{16,24},{24,0},{1,9},{9,17},{17,25},{25,1},{2,10},{10... | collective-permute-start | bytes 196616 | tf_op jit(solution)/shard_map/ppermute | solution.py:17
  19.9 3.5 %collective-permute-start.3 = (bf16[16,2048]{1,0:T(8,128)(2,1)S(1)}, bf16[16,2048]{1,0:T(8,128)(2,1)S(1)}, u32[]{:S(2)}, u32[]{:S(2)}) collective-permute-start(bf16[16,2048]{1,0:T(8,128)(2,1)S(1)} %slice.109), channel_id=1, source_target_pairs={{0,24},{8,0},{16,8},{24,16},{1,25},{9,1},{17,9},{25,17},{2,26},{10... | collective-permute-start | bytes 196616 | tf_op jit(solution)/shard_map/ppermute | solution.py:17
  23.3 4.3 %copy-start.3 = (f32[2]{0:T(128)S(1)}, f32[2]{0:T(128)}, u32[]{:S(2)}) copy-start(f32[2]{0:T(128)} %param.13) | copy-start | bytes 28
  23.3 7.3 %copy-start.6 = (s32[16]{0:T(128)S(1)}, s32[16]{0:T(128)}, u32[]{:S(2)}) copy-start(s32[16]{0:T(128)} %param.9) | copy-start | bytes 196
  23.3 7.4 %copy-start.7 = (s32[16]{0:T(128)S(1)}, s32[16]{0:T(128)}, u32[]{:S(2)}) copy-start(s32[16]{0:T(128)} %param.10) | copy-start | bytes 196
  24.3 23.3 %collective-permute-start.12 = (bf16[2,4,16,4096]{3,2,1,0:T(8,128)(2,1)S(1)}, bf16[2,4,16,4096]{3,2,1,0:T(8,128)(2,1)S(1)}, u32[]{:S(2)}, u32[]{:S(2)}) collective-permute-start(bf16[2,4,16,4096]{3,2,1,0:T(8,128)(2,1)S(1)} %pad_maximum_fusion.4), channel_id=1, source_target_pairs={{0,1},{1,0},{2,3},{3,2},{4,5},{5,4},{6,7},{7,6},{8,9},{9,8},{10,11... | collective-permute-start | bytes 3145736 | tf_op jit(solution)/shard_map/ppermute | solution.py:53
  44.8 14.7 %collective-permute-start.9 = (bf16[4,16,4096]{2,1,0:T(8,128)(2,1)}, bf16[4,16,4096]{2,1,0:T(8,128)(2,1)}, u32[]{:S(2)}, u32[]{:S(2)}) collective-permute-start(bf16[4,16,4096]{2,1,0:T(8,128)(2,1)} %get-tuple-element.7), channel_id=1, source_target_pairs={{0,2},{2,4},{4,6},{6,0},{1,3},{3,5},{5,7},{7,1},{8,10},{10,12},{12... | collective-permute-start | bytes 1572872 | tf_op jit(solution)/shard_map/ppermute | solution.py:17
  46.1 15.8 %collective-permute-start.8 = (bf16[4,16,4096]{2,1,0:T(8,128)(2,1)}, bf16[4,16,4096]{2,1,0:T(8,128)(2,1)}, u32[]{:S(2)}, u32[]{:S(2)}) collective-permute-start(bf16[4,16,4096]{2,1,0:T(8,128)(2,1)} %get-tuple-element.7), channel_id=1, source_target_pairs={{0,6},{2,0},{4,2},{6,4},{1,7},{3,1},{5,3},{7,5},{8,14},{10,8},{12,... | collective-permute-start | bytes 1572872 | tf_op jit(solution)/shard_map/ppermute | solution.py:17
  47.7 16.7 %collective-permute-start.14 = (bf16[4,16,4096]{2,1,0:T(8,128)(2,1)}, bf16[4,16,4096]{2,1,0:T(8,128)(2,1)}, u32[]{:S(2)}, u32[]{:S(2)}) collective-permute-start(bf16[4,16,4096]{2,1,0:T(8,128)(2,1)} %get-tuple-element.8), channel_id=1, source_target_pairs={{0,8},{8,16},{16,24},{24,0},{1,9},{9,17},{17,25},{25,1},{2,10},{10... | collective-permute-start | bytes 1572872 | tf_op jit(solution)/shard_map/ppermute | solution.py:17
  48.9 17.9 %collective-permute-start.13 = (bf16[4,16,4096]{2,1,0:T(8,128)(2,1)}, bf16[4,16,4096]{2,1,0:T(8,128)(2,1)}, u32[]{:S(2)}, u32[]{:S(2)}) collective-permute-start(bf16[4,16,4096]{2,1,0:T(8,128)(2,1)} %get-tuple-element.8), channel_id=1, source_target_pairs={{0,24},{8,0},{16,8},{24,16},{1,25},{9,1},{17,9},{25,17},{2,26},{10... | collective-permute-start | bytes 1572872 | tf_op jit(solution)/shard_map/ppermute | solution.py:17
  52.4 37.4 %all-to-all-start = ((bf16[2,16,32,640]{3,1,0,2:T(8,128)(2,1)}), bf16[2,16,32,640]{3,1,0,2:T(8,128)(2,1)S(1)}, u32[]{:S(2)}, u32[]{:S(2)}) async-start(bf16[2,16,32,640]{3,1,0,2:T(8,128)(2,1)} %copy.52), calls=%async_computation | async-start | bytes 2621440 | tf_op jit(solution)/shard_map/all_to_all | solution.py:59
  60.5 22.2 %collective-permute-start.10 = (bf16[4,16,2048]{2,1,0:T(8,128)(2,1)S(1)}, bf16[4,16,2048]{2,1,0:T(8,128)(2,1)S(1)}, u32[]{:S(2)}, u32[]{:S(2)}) collective-permute-start(bf16[4,16,2048]{2,1,0:T(8,128)(2,1)S(1)} %slice.112), channel_id=1, source_target_pairs={{0,2},{2,4},{4,6},{6,0},{1,3},{3,5},{5,7},{7,1},{8,10},{10,12},{12... | collective-permute-start | bytes 786440 | tf_op jit(solution)/shard_map/ppermute | solution.py:17
  62.9 19.7 %collective-permute-start.11 = (bf16[4,16,2048]{2,1,0:T(8,128)(2,1)S(1)}, bf16[4,16,2048]{2,1,0:T(8,128)(2,1)S(1)}, u32[]{:S(2)}, u32[]{:S(2)}) collective-permute-start(bf16[4,16,2048]{2,1,0:T(8,128)(2,1)S(1)} %slice.113), channel_id=1, source_target_pairs={{0,6},{2,0},{4,2},{6,4},{1,7},{3,1},{5,3},{7,5},{8,14},{10,8},{12,... | collective-permute-start | bytes 786440 | tf_op jit(solution)/shard_map/ppermute | solution.py:17
  65.3 17.3 %collective-permute-start.16 = (bf16[4,16,2048]{2,1,0:T(8,128)(2,1)S(1)}, bf16[4,16,2048]{2,1,0:T(8,128)(2,1)S(1)}, u32[]{:S(2)}, u32[]{:S(2)}) collective-permute-start(bf16[4,16,2048]{2,1,0:T(8,128)(2,1)S(1)} %slice.116), channel_id=1, source_target_pairs={{0,8},{8,16},{16,24},{24,0},{1,9},{9,17},{17,25},{25,1},{2,10},{10... | collective-permute-start | bytes 786440 | tf_op jit(solution)/shard_map/ppermute | solution.py:17
  67.8 14.9 %collective-permute-start.17 = (bf16[4,16,2048]{2,1,0:T(8,128)(2,1)S(1)}, bf16[4,16,2048]{2,1,0:T(8,128)(2,1)S(1)}, u32[]{:S(2)}, u32[]{:S(2)}) collective-permute-start(bf16[4,16,2048]{2,1,0:T(8,128)(2,1)S(1)} %slice.117), channel_id=1, source_target_pairs={{0,24},{8,0},{16,8},{24,16},{1,25},{9,1},{17,9},{25,17},{2,26},{10... | collective-permute-start | bytes 786440 | tf_op jit(solution)/shard_map/ppermute | solution.py:17
  83.8 10.8 %collective-permute-start.18 = (bf16[2,4,16,4096]{3,2,1,0:T(8,128)(2,1)}, bf16[2,4,16,4096]{3,2,1,0:T(8,128)(2,1)}, u32[]{:S(2)}, u32[]{:S(2)}) collective-permute-start(bf16[2,4,16,4096]{3,2,1,0:T(8,128)(2,1)} %pad_maximum_fusion.5), channel_id=1, source_target_pairs={{0,1},{1,0},{2,3},{3,2},{4,5},{5,4},{6,7},{7,6},{8,9},{9,8},{10,11... | collective-permute-start | bytes 3145736 | tf_op jit(solution)/shard_map/ppermute | solution.py:66
  89.7 6.2 %collective-permute-start.15 = (bf16[4,4,16,4096]{3,2,1,0:T(8,128)(2,1)}, bf16[4,4,16,4096]{3,2,1,0:T(8,128)(2,1)}, u32[]{:S(2)}, u32[]{:S(2)}) collective-permute-start(bf16[4,4,16,4096]{3,2,1,0:T(8,128)(2,1)} %get-tuple-element.23), channel_id=1, source_target_pairs={{0,1},{1,0},{2,3},{3,2},{4,5},{5,4},{6,7},{7,6},{8,9},{9,8},{10,11... | collective-permute-start | bytes 6291464 | tf_op jit(solution)/shard_map/ppermute | solution.py:64
  89.9 0.7 copy-start.4
  89.9 0.7 copy-start.5
  97.6 1.6 %copy-start = (bf16[1,4,4,16,4096]{4,3,2,1,0:T(8,128)(2,1)S(1)}, bf16[1,4,4,16,4096]{4,3,2,1,0:T(8,128)(2,1)}, u32[]{:S(2)}) copy-start(bf16[1,4,4,16,4096]{4,3,2,1,0:T(8,128)(2,1)} %get-tuple-element.22) | copy-start | bytes 6291460
  97.6 2.2 %copy-start.1 = (bf16[1,4,4,16,4096]{4,3,2,1,0:T(8,128)(2,1)S(1)}, bf16[1,4,4,16,4096]{4,3,2,1,0:T(8,128)(2,1)}, u32[]{:S(2)}) copy-start(bf16[1,4,4,16,4096]{4,3,2,1,0:T(8,128)(2,1)} %get-tuple-element.24) | copy-start | bytes 6291460
Sparse Core Ops, SparseCore 0:
  18.7 24.4 all-gather.2

commit v13 on v6

--- a/solution.py
+++ b/solution.py
@@ -65,13 +65,9 @@
     near_other = lax.ppermute(near, "core", CORE_PAIRS)
     far = jnp.stack([real_far, imag_far])
     far_other = lax.ppermute(far, "core", CORE_PAIRS)
-    parts = []
-    for part in range(2):
-        for src_first, src_near, src_far in ((first, near, far), (first_other, near_other, far_other)):
-            parts.append(
-                jnp.stack([src_first[part], src_near[2 * part], src_far[part], src_near[2 * part + 1]])
-            )
-    left = jnp.stack(parts).reshape(2 * pairs, local_g)
+    buffers = (first, near, far, first_other, near_other, far_other)
+    left = jnp.concatenate([piece.reshape(-1, local_pairs, local_g) for piece in buffers], axis=0)
+    left = left.reshape(2 * pairs, local_g)
 
     all_bands = column[:, :, width].astype(jnp.int32)
     gap = lookup(all_bands[1], conduction_energy) - lookup(all_bands[0], valence_energy)
@@ -88,6 +84,12 @@
 
     real_order = (2, 1, 0)
     imag_order = (2, 0, 1)
+    slots = ((0, 0), (1, 0), (0, 1), (0, 3), (1, 1), (1, 3), (0, 2), (1, 2))
+
+    def arrange(real_rows, imag_rows):
+        grids = [rows.reshape(ncore, 4, 4 * local_pairs, width) for rows in (real_rows, imag_rows)]
+        return jnp.stack([grids[part][:, outer] for part, outer in slots], axis=1).reshape(pairs * 2, width)
+
     right_real = []
     right_imag = []
     for index in range(frequency.shape[0]):
@@ -99,8 +101,8 @@
         imag_b = relative(scaled_imag, imag_order)
         real_b = relative(scaled_real, imag_order)
         imag_a = relative(scaled_imag, real_order)
-        right_real.append(jnp.concatenate([-real_a, -imag_b], axis=0))
-        right_imag.append(jnp.concatenate([-imag_a, real_b], axis=0))
+        right_real.append(arrange(-real_a, -imag_b))
+        right_imag.append(arrange(-imag_a, real_b))
     dims = (((0,), (0,)), ((), ()))
     chi_real = lax.dot_general(left, jnp.stack(right_real, axis=1), dims, preferred_element_type=jnp.float32)
     chi_imag = lax.dot_general(left, jnp.stack(right_imag, axis=1), dims, preferred_element_type=jnp.float32)

time: 109 us -> 128 us (1.17)
  local copies, waits for them, and re-layouts: 12.8 us -> 22.2 us
  matrix products: 22.6 us -> 29.1 us
  waiting for transfers between devices: 14.6 us -> 17.2 us
  starting transfers between devices: 40.2 us -> 42 us
    unnamed x27 -> x52, local copies, waits for them, and re-layouts: 2.16 us -> 13.1 us
    ppermute x1, starting transfers between devices: 0.01 us -> 4.65 us  [on_device(): near_other = lax.ppermute(near, 'core', CORE_PAIRS)]
    another operation x7 -> x1, other arithmetic: 6.32 us -> 1.83 us  [on_device(): near = jnp.stack([real_plus, real_minus, imag_plus, imag_minus])]
    ppermute x16, starting transfers between devices: 24.5 us -> 20.3 us  [shift(): lax.ppermute(value, axis, [(i, (i + step) % size) for i in range(size)])]
    dot_general x1, matrix products: 11.3 us -> 14.6 us  [on_device(): lax.dot_general(left, jnp.stack(right_real, axis=1), dims, preferred_elem...]
    dot_general x1, matrix products: 11.3 us -> 14.6 us  [on_device(): lax.dot_general(left, jnp.stack(right_imag, axis=1), dims, preferred_elem...]
    slice x5 -> x1, local copies, waits for them, and re-layouts: 4.45 us -> 1.72 us  [on_device(): scaled_imag = (weight[:, None] * wide[1]).astype(jnp.bfloat16)]
    ppermute x16, waiting for transfers between devices: 14.6 us -> 17.2 us  [shift(): lax.ppermute(value, axis, [(i, (i + step) % size) for i in range(size)])]
  transfers between devices with their start and end apart: 21 -> 21, of which waited for: 4 -> 4; matrix products, arithmetic and copies ran while one was open for 20% -> 25% of each run, Pallas kernels for 0% -> 0%
where the time goes in v13:
time: 128 us; the launch traced here: 127 us
  starting transfers between devices  42 us (33%)
  matrix products  29.1 us (23%)
  local copies, waits for them, and re-layouts  22.2 us (17%)
  waiting for transfers between devices  17.2 us (13%)
  other arithmetic  13 us (10%)
  between operations  3.91 us (3%)
    ppermute x16, starting transfers between devices, shift(): lax.ppermute(value, axis, [(i, (i + step) % size) for i in range(size)])  20.3 us
    ppermute x16, waiting for transfers between devices, shift(): lax.ppermute(value, axis, [(i, (i + step) % size) for i in range(size)])  17.2 us
    dot_general x1, matrix products, on_device(): lax.dot_general(left, jnp.stack(right_real, axis=1), dims, preferred_elem...  14.6 us
    dot_general x1, matrix products, on_device(): lax.dot_general(left, jnp.stack(right_imag, axis=1), dims, preferred_elem...  14.6 us
    unnamed x52, local copies, waits for them, and re-layouts  13.1 us
    all_to_all x1, starting transfers between devices, on_device(): lax.all_to_all(payload, cols, split_axis=2, concat_axis=1, tiled=True)  6.49 us
    all_to_all x1, starting transfers between devices, on_device(): spread = lax.all_to_all(copies, 'row', 0, 0, tiled=True)  5.03 us
    ppermute x1, starting transfers between devices, on_device(): near_other = lax.ppermute(near, 'core', CORE_PAIRS)  4.65 us
  transfers between devices with their start and end apart: 21, of which 4 were waited for; matrix products, arithmetic and copies ran while one was open for 25% of the time, Pallas kernels for 0%

profile of v13, /device:TPU:1, one launch (start us, length us, event | category | flops | bytes accessed | tf_op | source)
XLA Modules:
  0.0 127.4 jit_solution(11210174445250660206)
XLA Ops:
  0.6 2.1 %collective-permute-start.1 = (bf16[16,4096]{1,0:T(8,128)(2,1)}, bf16[16,4096]{1,0:T(8,128)(2,1)S(1)}, u32[]{:S(2)}, u32[]{:S(2)}) collective-permute-start(bf16[16,4096]{1,0:T(8,128)(2,1)} %param.7), channel_id=1, source_target_pairs={{0,8},{8,16},{16,24},{24,0},{1,9},{9,17},{17,25},{25,1},{2,10},{10... | collective-permute-start | bytes 393224 | tf_op jit(solution)/shard_map/ppermute | solution.py:17
  2.8 1.3 %collective-permute-start = (bf16[16,4096]{1,0:T(8,128)(2,1)}, bf16[16,4096]{1,0:T(8,128)(2,1)S(1)}, u32[]{:S(2)}, u32[]{:S(2)}) collective-permute-start(bf16[16,4096]{1,0:T(8,128)(2,1)} %param.7), channel_id=1, source_target_pairs={{0,24},{8,0},{16,8},{24,16},{1,25},{9,1},{17,9},{25,17},{2,26},{10... | collective-permute-start | bytes 393224 | tf_op jit(solution)/shard_map/ppermute | solution.py:17
  4.1 1.4 %collective-permute-start.5 = (bf16[16,4096]{1,0:T(8,128)(2,1)}, bf16[16,4096]{1,0:T(8,128)(2,1)S(1)}, u32[]{:S(2)}, u32[]{:S(2)}) collective-permute-start(bf16[16,4096]{1,0:T(8,128)(2,1)} %param.8), channel_id=1, source_target_pairs={{0,2},{2,4},{4,6},{6,0},{1,3},{3,5},{5,7},{7,1},{8,10},{10,12},{12... | collective-permute-start | bytes 393224 | tf_op jit(solution)/shard_map/ppermute | solution.py:17
  5.5 1.4 %collective-permute-start.4 = (bf16[16,4096]{1,0:T(8,128)(2,1)}, bf16[16,4096]{1,0:T(8,128)(2,1)S(1)}, u32[]{:S(2)}, u32[]{:S(2)}) collective-permute-start(bf16[16,4096]{1,0:T(8,128)(2,1)} %param.8), channel_id=1, source_target_pairs={{0,6},{2,0},{4,2},{6,4},{1,7},{3,1},{5,3},{7,5},{8,14},{10,8},{12,... | collective-permute-start | bytes 393224 | tf_op jit(solution)/shard_map/ppermute | solution.py:17
  8.0 1.1 broadcast_in_dim.28
  9.0 5.0 %all-to-all-start = ((bf16[4,2,16,4096]{3,2,1,0:T(8,128)(2,1)}), bf16[4,2,16,4096]{3,2,1,0:T(8,128)(2,1)S(1)}, u32[]{:S(2)}, u32[]{:S(2)}) async-start(bf16[4,2,16,4096]{3,2,1,0:T(8,128)(2,1)} %broadcast_in_dim.28), calls=%async_computation | async-start | bytes 2097152 | tf_op jit(solution)/shard_map/all_to_all | solution.py:49
  15.4 1.3 %fusion.31 = (f32[1]{0:T(128)}, f32[1]{0:T(128)}) fusion(f32[2]{0:T(128)} %param.13), kind=kLoop, calls=%fused_computation.125 | loop fusion | bytes 16 | tf_op jit(solution)/shard_map/slice | solution.py:96
  19.4 2.7 %collective-permute-start.3 = (bf16[16,2048]{1,0:T(8,128)(2,1)S(1)}, bf16[16,2048]{1,0:T(8,128)(2,1)S(1)}, u32[]{:S(2)}, u32[]{:S(2)}) collective-permute-start(bf16[16,2048]{1,0:T(8,128)(2,1)S(1)} %slice.197), channel_id=1, source_target_pairs={{0,24},{8,0},{16,8},{24,16},{1,25},{9,1},{17,9},{25,17},{2,26},{10... | collective-permute-start | bytes 196616 | tf_op jit(solution)/shard_map/ppermute | solution.py:17
  22.3 2.7 %collective-permute-start.7 = (bf16[16,2048]{1,0:T(8,128)(2,1)S(1)}, bf16[16,2048]{1,0:T(8,128)(2,1)S(1)}, u32[]{:S(2)}, u32[]{:S(2)}) collective-permute-start(bf16[16,2048]{1,0:T(8,128)(2,1)S(1)} %slice.199), channel_id=1, source_target_pairs={{0,6},{2,0},{4,2},{6,4},{1,7},{3,1},{5,3},{7,5},{8,14},{10,8},{12,... | collective-permute-start | bytes 196616 | tf_op jit(solution)/shard_map/ppermute | solution.py:17
  28.9 3.4 %collective-permute-start.16 = (bf16[2,4,16,4096]{3,2,1,0:T(8,128)(2,1)}, bf16[2,4,16,4096]{3,2,1,0:T(8,128)(2,1)}, u32[]{:S(2)}, u32[]{:S(2)}) collective-permute-start(bf16[2,4,16,4096]{3,2,1,0:T(8,128)(2,1)} %pad_maximum_fusion.2), channel_id=1, source_target_pairs={{0,1},{1,0},{2,3},{3,2},{4,5},{5,4},{6,7},{7,6},{8,9},{9,8},{10,11... | collective-permute-start | bytes 3145736 | tf_op jit(solution)/shard_map/ppermute | solution.py:54
  32.8 3.1 %collective-permute-start.8 = (bf16[4,16,4096]{2,1,0:T(8,128)(2,1)}, bf16[4,16,4096]{2,1,0:T(8,128)(2,1)S(1)}, u32[]{:S(2)}, u32[]{:S(2)}) collective-permute-start(bf16[4,16,4096]{2,1,0:T(8,128)(2,1)} %get-tuple-element.7), channel_id=1, source_target_pairs={{0,6},{2,0},{4,2},{6,4},{1,7},{3,1},{5,3},{7,5},{8,14},{10,8},{12,... | collective-permute-start | bytes 1572872 | tf_op jit(solution)/shard_map/ppermute | solution.py:17
  36.0 1.4 %collective-permute-start.11 = (bf16[4,16,4096]{2,1,0:T(8,128)(2,1)}, bf16[4,16,4096]{2,1,0:T(8,128)(2,1)S(1)}, u32[]{:S(2)}, u32[]{:S(2)}) collective-permute-start(bf16[4,16,4096]{2,1,0:T(8,128)(2,1)} %get-tuple-element.8), channel_id=1, source_target_pairs={{0,8},{8,16},{16,24},{24,0},{1,9},{9,17},{17,25},{25,1},{2,10},{10... | collective-permute-start | bytes 1572872 | tf_op jit(solution)/shard_map/ppermute | solution.py:17
  37.7 1.5 %copy.47 = bf16[2,16,32,640]{3,1,0,2:T(8,128)(2,1)} copy(bf16[2,16,32,640]{3,2,1,0:T(8,128)(2,1)S(1)} %pad_maximum_fusion.1) | data formatting | bytes 2621440 | tf_op jit(solution)/shard_map/concatenate | solution.py:59
  39.1 6.5 %all-to-all-start.1 = ((bf16[2,16,32,640]{3,1,0,2:T(8,128)(2,1)}), bf16[2,16,32,640]{3,1,0,2:T(8,128)(2,1)S(1)}, u32[]{:S(2)}, u32[]{:S(2)}) async-start(bf16[2,16,32,640]{3,1,0,2:T(8,128)(2,1)} %copy.47), calls=%async_computation.1 | async-start | bytes 2621440 | tf_op jit(solution)/shard_map/all_to_all | solution.py:60
  45.6 2.3 %constant_dynamic-update-slice_fusion.5 = bf16[64,16,4096]{2,1,0:T(8,128)(2,1)} fusion(bf16[8,16,4096]{2,1,0:T(8,128)(2,1)} %bitcast.10), kind=kLoop, calls=%fused_computation.104 | loop fusion | bytes 2097152
  48.0 3.5 %collective-permute-done.9 = bf16[4,16,4096]{2,1,0:T(8,128)(2,1)S(1)} collective-permute-done((bf16[4,16,4096]{2,1,0:T(8,128)(2,1)}, bf16[4,16,4096]{2,1,0:T(8,128)(2,1)S(1)}, u32[]{:S(2)}, u32[]{:S(2)}) %collective-permute-start.9) | collective-permute-done | bytes 524320 | tf_op jit(solution)/shard_map/ppermute | solution.py:17
  51.6 2.7 %collective-permute-start.13 = (bf16[4,16,2048]{2,1,0:T(8,128)(2,1)S(1)}, bf16[4,16,2048]{2,1,0:T(8,128)(2,1)S(1)}, u32[]{:S(2)}, u32[]{:S(2)}) collective-permute-start(bf16[4,16,2048]{2,1,0:T(8,128)(2,1)S(1)} %slice.201), channel_id=1, source_target_pairs={{0,6},{2,0},{4,2},{6,4},{1,7},{3,1},{5,3},{7,5},{8,14},{10,8},{12,... | collective-permute-start | bytes 786440 | tf_op jit(solution)/shard_map/ppermute | solution.py:17
  55.3 1.8 %pad_maximum_fusion = bf16[4,4,16,4096]{3,2,1,0:T(8,128)(2,1)S(1)} fusion(bf16[1,4,16,4096]{3,2,1,0:T(8,128)(2,1)} %bitcast.130, bf16[1,4,16,4096]{3,2,1,0:T(8,128)(2,1)} %bitcast.128, bf16[1,4,16,4096]{3,2,1,0:T(8,128)(2,1)} %bitcast.129, bf16[1,4,16,4096]{3,2,1,0:T(8,128)(2,1)} %bitcast.127), kind=kLoop, calls=%fused_computation.2 | loop fusion | flops 3145728 | bytes 4194304 | tf_op jit(solution)/shard_map/stack | solution.py:64
  57.2 4.7 %collective-permute-start.17 = (bf16[4,4,16,4096]{3,2,1,0:T(8,128)(2,1)S(1)}, bf16[4,4,16,4096]{3,2,1,0:T(8,128)(2,1)}, u32[]{:S(2)}, u32[]{:S(2)}) collective-permute-start(bf16[4,4,16,4096]{3,2,1,0:T(8,128)(2,1)S(1)} %pad_maximum_fusion), channel_id=1, source_target_pairs={{0,1},{1,0},{2,3},{3,2},{4,5},{5,4},{6,7},{7,6},{8,9},{9,8},{10,11... | collective-permute-start | bytes 6291464 | tf_op jit(solution)/shard_map/ppermute | solution.py:65
  61.9 1.4 %constant_dynamic-update-slice_fusion.4 = bf16[64,16,4096]{2,1,0:T(8,128)(2,1)} fusion(bf16[64,16,4096]{2,1,0:T(8,128)(2,1)} %constant_dynamic-update-slice_fusion.5, bf16[16,16,4096]{2,1,0:T(8,128)(2,1)S(1)} %bitcast.87), kind=kLoop, calls=%fused_computation.103 | loop fusion | bytes 4194304
  63.3 7.0 %collective-permute-done.12 = bf16[4,16,2048]{2,1,0:T(8,128)(2,1)S(1)} collective-permute-done((bf16[4,16,2048]{2,1,0:T(8,128)(2,1)S(1)}, bf16[4,16,2048]{2,1,0:T(8,128)(2,1)S(1)}, u32[]{:S(2)}, u32[]{:S(2)}) %collective-permute-start.12) | collective-permute-done | bytes 262176 | tf_op jit(solution)/shard_map/ppermute | solution.py:17
  71.3 5.7 %collective-permute-done.15 = bf16[4,16,2048]{2,1,0:T(8,128)(2,1)S(1)} collective-permute-done((bf16[4,16,2048]{2,1,0:T(8,128)(2,1)S(1)}, bf16[4,16,2048]{2,1,0:T(8,128)(2,1)S(1)}, u32[]{:S(2)}, u32[]{:S(2)}) %collective-permute-start.15) | collective-permute-done | bytes 262176 | tf_op jit(solution)/shard_map/ppermute | solution.py:17
  77.0 1.1 pad_maximum_fusion.3
  78.1 2.0 %collective-permute-start.18 = (bf16[2,4,16,4096]{3,2,1,0:T(8,128)(2,1)}, bf16[2,4,16,4096]{3,2,1,0:T(8,128)(2,1)}, u32[]{:S(2)}, u32[]{:S(2)}) collective-permute-start(bf16[2,4,16,4096]{3,2,1,0:T(8,128)(2,1)} %pad_maximum_fusion.3), channel_id=1, source_target_pairs={{0,1},{1,0},{2,3},{3,2},{4,5},{5,4},{6,7},{7,6},{8,9},{9,8},{10,11... | collective-permute-start | bytes 3145736 | tf_op jit(solution)/shard_map/ppermute | solution.py:67
  80.1 2.3 %constant_dynamic-update-slice_fusion.3 = bf16[64,16,4096]{2,1,0:T(8,128)(2,1)} fusion(bf16[64,16,4096]{2,1,0:T(8,128)(2,1)} %constant_dynamic-update-slice_fusion.4, bf16[8,16,4096]{2,1,0:T(8,128)(2,1)} %bitcast.18), kind=kLoop, calls=%fused_computation.102 | loop fusion | bytes 2097152
  82.4 2.4 %constant_dynamic-update-slice_fusion.2 = bf16[64,16,4096]{2,1,0:T(8,128)(2,1)} fusion(bf16[64,16,4096]{2,1,0:T(8,128)(2,1)} %constant_dynamic-update-slice_fusion.3, bf16[8,16,4096]{2,1,0:T(8,128)(2,1)} %bitcast.19), kind=kLoop, calls=%fused_computation.101 | loop fusion | bytes 2097152
  85.0 1.6 %slice_convert_fusion = f32[2,512,512]{2,1,0:T(8,128)} fusion(bf16[2,512,640]{2,1,0:T(8,128)(2,1)S(1)} %bitcast.89), kind=kLoop, calls=%fused_computation.10 | loop fusion | flops 524288 | bytes 3145728 | tf_op jit(solution)/shard_map/convert_element_type | solution.py:74
  87.2 1.7 %fusion.30 = (f32[1,512,512]{2,1,0:T(8,128)S(1)}, f32[1,512,512]{2,1,0:T(8,128)S(1)}) fusion(f32[2,512,512]{2,1,0:T(8,128)} %slice_convert_fusion), kind=kLoop, calls=%fused_computation.124 | loop fusion | bytes 4194304 | tf_op jit(solution)/shard_map/slice | solution.py:99
  92.7 3.1 %constant_dynamic-update-slice_fusion.1 = bf16[64,16,4096]{2,1,0:T(8,128)(2,1)} fusion(bf16[64,16,4096]{2,1,0:T(8,128)(2,1)} %constant_dynamic-update-slice_fusion.2, bf16[16,16,4096]{2,1,0:T(8,128)(2,1)} %bitcast.20), kind=kLoop, calls=%fused_computation.100 | loop fusion | bytes 4194304
  95.9 2.4 %constant_dynamic-update-slice_fusion = bf16[64,16,4096]{2,1,0:T(8,128)(2,1)} fusion(bf16[64,16,4096]{2,1,0:T(8,128)(2,1)} %constant_dynamic-update-slice_fusion.1, bf16[8,16,4096]{2,1,0:T(8,128)(2,1)} %bitcast.21), kind=kLoop, calls=%fused_computation.99 | loop fusion | bytes 2097152 | tf_op jit(solution)/shard_map/concatenate | solution.py:69
  98.3 14.6 %convert_bitcast_fusion = bf16[2,4096,512]{2,1,0:T(8,128)(2,1)} fusion(bf16[1024,4096,1]{1,0,2:T(8,128)(2,1)} %bitcast.23, bf16[1024,1,512]{2,0,1:T(8,128)(2,1)S(1)} %bitcast.140, bf16[1024,1,512]{2,0,1:T(8,128)(2,1)S(1)} %bitcast.139), kind=kOutput, calls=%fused_computation | convolution fusion | flops 8598323200 | bytes 18874368 | tf_op jit(solution)/shard_map/dot_general | solution.py:108
  112.8 14.6 %convert_bitcast_fusion.1 = bf16[2,4096,512]{2,1,0:T(8,128)(2,1)} fusion(bf16[1024,4096,1]{1,0,2:T(8,128)(2,1)} %bitcast.23, bf16[1024,1,512]{2,0,1:T(8,128)(2,1)S(1)} %bitcast.142, bf16[1024,1,512]{2,0,1:T(8,128)(2,1)S(1)} %bitcast.141), kind=kOutput, calls=%fused_computation.1 | convolution fusion | flops 8598323200 | bytes 18874368 | tf_op jit(solution)/shard_map/dot_general | solution.py:107
  (125 shorter events, 13.6 us)
Async XLA Ops:
  0.6 24.4 %copy-start.5 = (bf16[16,4096]{1,0:T(8,128)(2,1)S(1)}, bf16[16,4096]{1,0:T(8,128)(2,1)}, u32[]{:S(2)}) copy-start(bf16[16,4096]{1,0:T(8,128)(2,1)} %param.7) | copy-start | bytes 393220
  0.6 26.2 %copy-start.6 = (bf16[16,4096]{1,0:T(8,128)(2,1)S(1)}, bf16[16,4096]{1,0:T(8,128)(2,1)}, u32[]{:S(2)}) copy-start(bf16[16,4096]{1,0:T(8,128)(2,1)} %param.8) | copy-start | bytes 393220
  0.6 18.6 %collective-permute-start.1 = (bf16[16,4096]{1,0:T(8,128)(2,1)}, bf16[16,4096]{1,0:T(8,128)(2,1)S(1)}, u32[]{:S(2)}, u32[]{:S(2)}) collective-permute-start(bf16[16,4096]{1,0:T(8,128)(2,1)} %param.7), channel_id=1, source_target_pairs={{0,8},{8,16},{16,24},{24,0},{1,9},{9,17},{17,25},{25,1},{2,10},{10... | collective-permute-start | bytes 393224 | tf_op jit(solution)/shard_map/ppermute | solution.py:17
  2.8 16.6 %collective-permute-start = (bf16[16,4096]{1,0:T(8,128)(2,1)}, bf16[16,4096]{1,0:T(8,128)(2,1)S(1)}, u32[]{:S(2)}, u32[]{:S(2)}) collective-permute-start(bf16[16,4096]{1,0:T(8,128)(2,1)} %param.7), channel_id=1, source_target_pairs={{0,24},{8,0},{16,8},{24,16},{1,25},{9,1},{17,9},{25,17},{2,26},{10... | collective-permute-start | bytes 393224 | tf_op jit(solution)/shard_map/ppermute | solution.py:17
  4.1 18.0 %collective-permute-start.5 = (bf16[16,4096]{1,0:T(8,128)(2,1)}, bf16[16,4096]{1,0:T(8,128)(2,1)S(1)}, u32[]{:S(2)}, u32[]{:S(2)}) collective-permute-start(bf16[16,4096]{1,0:T(8,128)(2,1)} %param.8), channel_id=1, source_target_pairs={{0,2},{2,4},{4,6},{6,0},{1,3},{3,5},{5,7},{7,1},{8,10},{10,12},{12... | collective-permute-start | bytes 393224 | tf_op jit(solution)/shard_map/ppermute | solution.py:17
  5.5 16.7 %collective-permute-start.4 = (bf16[16,4096]{1,0:T(8,128)(2,1)}, bf16[16,4096]{1,0:T(8,128)(2,1)S(1)}, u32[]{:S(2)}, u32[]{:S(2)}) collective-permute-start(bf16[16,4096]{1,0:T(8,128)(2,1)} %param.8), channel_id=1, source_target_pairs={{0,6},{2,0},{4,2},{6,4},{1,7},{3,1},{5,3},{7,5},{8,14},{10,8},{12,... | collective-permute-start | bytes 393224 | tf_op jit(solution)/shard_map/ppermute | solution.py:17
  9.0 23.3 %all-to-all-start = ((bf16[4,2,16,4096]{3,2,1,0:T(8,128)(2,1)}), bf16[4,2,16,4096]{3,2,1,0:T(8,128)(2,1)S(1)}, u32[]{:S(2)}, u32[]{:S(2)}) async-start(bf16[4,2,16,4096]{3,2,1,0:T(8,128)(2,1)} %broadcast_in_dim.28), calls=%async_computation | async-start | bytes 2097152 | tf_op jit(solution)/shard_map/all_to_all | solution.py:49
  19.3 5.7 %collective-permute-start.2 = (bf16[16,2048]{1,0:T(8,128)(2,1)S(1)}, bf16[16,2048]{1,0:T(8,128)(2,1)S(1)}, u32[]{:S(2)}, u32[]{:S(2)}) collective-permute-start(bf16[16,2048]{1,0:T(8,128)(2,1)S(1)} %slice.196), channel_id=1, source_target_pairs={{0,8},{8,16},{16,24},{24,0},{1,9},{9,17},{17,25},{25,1},{2,10},{10... | collective-permute-start | bytes 196616 | tf_op jit(solution)/shard_map/ppermute | solution.py:17
  19.4 5.6 %collective-permute-start.3 = (bf16[16,2048]{1,0:T(8,128)(2,1)S(1)}, bf16[16,2048]{1,0:T(8,128)(2,1)S(1)}, u32[]{:S(2)}, u32[]{:S(2)}) collective-permute-start(bf16[16,2048]{1,0:T(8,128)(2,1)S(1)} %slice.197), channel_id=1, source_target_pairs={{0,24},{8,0},{16,8},{24,16},{1,25},{9,1},{17,9},{25,17},{2,26},{10... | collective-permute-start | bytes 196616 | tf_op jit(solution)/shard_map/ppermute | solution.py:17
  22.2 4.7 %collective-permute-start.6 = (bf16[16,2048]{1,0:T(8,128)(2,1)S(1)}, bf16[16,2048]{1,0:T(8,128)(2,1)S(1)}, u32[]{:S(2)}, u32[]{:S(2)}) collective-permute-start(bf16[16,2048]{1,0:T(8,128)(2,1)S(1)} %slice.198), channel_id=1, source_target_pairs={{0,2},{2,4},{4,6},{6,0},{1,3},{3,5},{5,7},{7,1},{8,10},{10,12},{12... | collective-permute-start | bytes 196616 | tf_op jit(solution)/shard_map/ppermute | solution.py:17
  22.3 4.6 %collective-permute-start.7 = (bf16[16,2048]{1,0:T(8,128)(2,1)S(1)}, bf16[16,2048]{1,0:T(8,128)(2,1)S(1)}, u32[]{:S(2)}, u32[]{:S(2)}) collective-permute-start(bf16[16,2048]{1,0:T(8,128)(2,1)S(1)} %slice.199), channel_id=1, source_target_pairs={{0,6},{2,0},{4,2},{6,4},{1,7},{3,1},{5,3},{7,5},{8,14},{10,8},{12,... | collective-permute-start | bytes 196616 | tf_op jit(solution)/shard_map/ppermute | solution.py:17
  28.9 53.5 %collective-permute-start.16 = (bf16[2,4,16,4096]{3,2,1,0:T(8,128)(2,1)}, bf16[2,4,16,4096]{3,2,1,0:T(8,128)(2,1)}, u32[]{:S(2)}, u32[]{:S(2)}) collective-permute-start(bf16[2,4,16,4096]{3,2,1,0:T(8,128)(2,1)} %pad_maximum_fusion.2), channel_id=1, source_target_pairs={{0,1},{1,0},{2,3},{3,2},{4,5},{5,4},{6,7},{7,6},{8,9},{9,8},{10,11... | collective-permute-start | bytes 3145736 | tf_op jit(solution)/shard_map/ppermute | solution.py:54
  32.8 18.7 %collective-permute-start.8 = (bf16[4,16,4096]{2,1,0:T(8,128)(2,1)}, bf16[4,16,4096]{2,1,0:T(8,128)(2,1)S(1)}, u32[]{:S(2)}, u32[]{:S(2)}) collective-permute-start(bf16[4,16,4096]{2,1,0:T(8,128)(2,1)} %get-tuple-element.7), channel_id=1, source_target_pairs={{0,6},{2,0},{4,2},{6,4},{1,7},{3,1},{5,3},{7,5},{8,14},{10,8},{12,... | collective-permute-start | bytes 1572872 | tf_op jit(solution)/shard_map/ppermute | solution.py:17
  35.9 15.5 %collective-permute-start.9 = (bf16[4,16,4096]{2,1,0:T(8,128)(2,1)}, bf16[4,16,4096]{2,1,0:T(8,128)(2,1)S(1)}, u32[]{:S(2)}, u32[]{:S(2)}) collective-permute-start(bf16[4,16,4096]{2,1,0:T(8,128)(2,1)} %get-tuple-element.7), channel_id=1, source_target_pairs={{0,2},{2,4},{4,6},{6,0},{1,3},{3,5},{5,7},{7,1},{8,10},{10,12},{12... | collective-permute-start | bytes 1572872 | tf_op jit(solution)/shard_map/ppermute | solution.py:17
  36.0 18.5 %collective-permute-start.10 = (bf16[4,16,4096]{2,1,0:T(8,128)(2,1)}, bf16[4,16,4096]{2,1,0:T(8,128)(2,1)S(1)}, u32[]{:S(2)}, u32[]{:S(2)}) collective-permute-start(bf16[4,16,4096]{2,1,0:T(8,128)(2,1)} %get-tuple-element.8), channel_id=1, source_target_pairs={{0,24},{8,0},{16,8},{24,16},{1,25},{9,1},{17,9},{25,17},{2,26},{10... | collective-permute-start | bytes 1572872 | tf_op jit(solution)/shard_map/ppermute | solution.py:17
  36.0 18.3 %collective-permute-start.11 = (bf16[4,16,4096]{2,1,0:T(8,128)(2,1)}, bf16[4,16,4096]{2,1,0:T(8,128)(2,1)S(1)}, u32[]{:S(2)}, u32[]{:S(2)}) collective-permute-start(bf16[4,16,4096]{2,1,0:T(8,128)(2,1)} %get-tuple-element.8), channel_id=1, source_target_pairs={{0,8},{8,16},{16,24},{24,0},{1,9},{9,17},{17,25},{25,1},{2,10},{10... | collective-permute-start | bytes 1572872 | tf_op jit(solution)/shard_map/ppermute | solution.py:17
  39.1 45.6 %all-to-all-start.1 = ((bf16[2,16,32,640]{3,1,0,2:T(8,128)(2,1)}), bf16[2,16,32,640]{3,1,0,2:T(8,128)(2,1)S(1)}, u32[]{:S(2)}, u32[]{:S(2)}) async-start(bf16[2,16,32,640]{3,1,0,2:T(8,128)(2,1)} %copy.47), calls=%async_computation.1 | async-start | bytes 2621440 | tf_op jit(solution)/shard_map/all_to_all | solution.py:60
  51.5 3.0 %copy-start.3 = (bf16[4,16,4096]{2,1,0:T(8,128)(2,1)}, bf16[4,16,4096]{2,1,0:T(8,128)(2,1)S(1)}, u32[]{:S(2)}) copy-start(bf16[4,16,4096]{2,1,0:T(8,128)(2,1)S(1)} %collective-permute-done.9) | copy-start | bytes 1572868
  51.5 18.8 %collective-permute-start.12 = (bf16[4,16,2048]{2,1,0:T(8,128)(2,1)S(1)}, bf16[4,16,2048]{2,1,0:T(8,128)(2,1)S(1)}, u32[]{:S(2)}, u32[]{:S(2)}) collective-permute-start(bf16[4,16,2048]{2,1,0:T(8,128)(2,1)S(1)} %slice.200), channel_id=1, source_target_pairs={{0,2},{2,4},{4,6},{6,0},{1,3},{3,5},{5,7},{7,1},{8,10},{10,12},{12... | collective-permute-start | bytes 786440 | tf_op jit(solution)/shard_map/ppermute | solution.py:17
  51.6 2.9 %copy-start = (bf16[4,16,4096]{2,1,0:T(8,128)(2,1)}, bf16[4,16,4096]{2,1,0:T(8,128)(2,1)S(1)}, u32[]{:S(2)}) copy-start(bf16[4,16,4096]{2,1,0:T(8,128)(2,1)S(1)} %collective-permute-done.8) | copy-start | bytes 1572868
  51.6 19.6 %collective-permute-start.13 = (bf16[4,16,2048]{2,1,0:T(8,128)(2,1)S(1)}, bf16[4,16,2048]{2,1,0:T(8,128)(2,1)S(1)}, u32[]{:S(2)}, u32[]{:S(2)}) collective-permute-start(bf16[4,16,2048]{2,1,0:T(8,128)(2,1)S(1)} %slice.201), channel_id=1, source_target_pairs={{0,6},{2,0},{4,2},{6,4},{1,7},{3,1},{5,3},{7,5},{8,14},{10,8},{12,... | collective-permute-start | bytes 786440 | tf_op jit(solution)/shard_map/ppermute | solution.py:17
  54.4 0.8 copy-start.4
  54.4 16.9 %collective-permute-start.14 = (bf16[4,16,2048]{2,1,0:T(8,128)(2,1)S(1)}, bf16[4,16,2048]{2,1,0:T(8,128)(2,1)S(1)}, u32[]{:S(2)}, u32[]{:S(2)}) collective-permute-start(bf16[4,16,2048]{2,1,0:T(8,128)(2,1)S(1)} %slice.202), channel_id=1, source_target_pairs={{0,8},{8,16},{16,24},{24,0},{1,9},{9,17},{17,25},{25,1},{2,10},{10... | collective-permute-start | bytes 786440 | tf_op jit(solution)/shard_map/ppermute | solution.py:17
  54.5 0.9 copy-start.1
  55.3 6.5 %copy-start.2 = (bf16[4,16,4096]{2,1,0:T(8,128)(2,1)S(1)}, bf16[4,16,4096]{2,1,0:T(8,128)(2,1)}, u32[]{:S(2)}) copy-start(bf16[4,16,4096]{2,1,0:T(8,128)(2,1)} %copy-done.1) | copy-start | bytes 1572868
  57.2 35.6 %collective-permute-start.17 = (bf16[4,4,16,4096]{3,2,1,0:T(8,128)(2,1)S(1)}, bf16[4,4,16,4096]{3,2,1,0:T(8,128)(2,1)}, u32[]{:S(2)}, u32[]{:S(2)}) collective-permute-start(bf16[4,4,16,4096]{3,2,1,0:T(8,128)(2,1)S(1)} %pad_maximum_fusion), channel_id=1, source_target_pairs={{0,1},{1,0},{2,3},{3,2},{4,5},{5,4},{6,7},{7,6},{8,9},{9,8},{10,11... | collective-permute-start | bytes 6291464 | tf_op jit(solution)/shard_map/ppermute | solution.py:65
  70.3 6.7 %collective-permute-start.15 = (bf16[4,16,2048]{2,1,0:T(8,128)(2,1)S(1)}, bf16[4,16,2048]{2,1,0:T(8,128)(2,1)S(1)}, u32[]{:S(2)}, u32[]{:S(2)}) collective-permute-start(bf16[4,16,2048]{2,1,0:T(8,128)(2,1)S(1)} %slice.203), channel_id=1, source_target_pairs={{0,24},{8,0},{16,8},{24,16},{1,25},{9,1},{17,9},{25,17},{2,26},{10... | collective-permute-start | bytes 786440 | tf_op jit(solution)/shard_map/ppermute | solution.py:17
  78.1 17.8 %collective-permute-start.18 = (bf16[2,4,16,4096]{3,2,1,0:T(8,128)(2,1)}, bf16[2,4,16,4096]{3,2,1,0:T(8,128)(2,1)}, u32[]{:S(2)}, u32[]{:S(2)}) collective-permute-start(bf16[2,4,16,4096]{3,2,1,0:T(8,128)(2,1)} %pad_maximum_fusion.3), channel_id=1, source_target_pairs={{0,1},{1,0},{2,3},{3,2},{4,5},{5,4},{6,7},{7,6},{8,9},{9,8},{10,11... | collective-permute-start | bytes 3145736 | tf_op jit(solution)/shard_map/ppermute | solution.py:67
  82.4 4.4 %copy-start.7 = (f32[32]{0:T(128)S(1)}, f32[32]{0:T(128)}, u32[]{:S(2)}) copy-start(f32[32]{0:T(128)} %param.12) | copy-start | bytes 388
  82.4 4.4 %copy-start.8 = (f32[16]{0:T(128)S(1)}, f32[16]{0:T(128)}, u32[]{:S(2)}) copy-start(f32[16]{0:T(128)} %param.11) | copy-start | bytes 196

commit v14 on v6

--- a/solution.py
+++ b/solution.py
@@ -53,12 +53,12 @@
     first = jnp.stack([row_real, col_imag])
     first_other = lax.ppermute(first, "core", CORE_PAIRS)
     spread, row_real, col_imag, first = lax.optimization_barrier((spread, row_real, col_imag, first))
-    payload = spread.transpose(1, 2, 0, 3, 4).reshape(2, local_pairs, ncol, width)
+    payload = spread.transpose(0, 3, 1, 2, 4).reshape(ncol, 2, local_pairs, width)
     bands = jnp.stack([valence_index, conduction_index]).astype(jnp.bfloat16)
-    tags = jnp.broadcast_to(bands[:, :, None, None], (2, local_pairs, ncol, 128))
+    tags = jnp.broadcast_to(bands[None, :, :, None], (ncol, 2, local_pairs, 128))
     payload = jnp.concatenate([payload, tags], axis=3)
-    column = lax.all_to_all(payload, cols, split_axis=2, concat_axis=1, tiled=True)
-    column = column.reshape(2, pairs, width + 128)
+    column = lax.all_to_all(payload, cols, split_axis=0, concat_axis=0, tiled=True)
+    column = column.transpose(1, 0, 2, 3).reshape(2, pairs, width + 128)
     real_plus, real_far, real_minus = ring_gather(row_real, "y")
     imag_plus, imag_far, imag_minus = ring_gather(col_imag, "x")
     near = jnp.stack([real_plus, real_minus, imag_plus, imag_minus])

time: 109 us -> 108 us (level)
  local copies, waits for them, and re-layouts: 12.8 us -> 11.5 us
  other arithmetic: 13.8 us -> 14.9 us
    concatenate x1 -> x0, local copies, waits for them, and re-layouts: 1.52 us -> none  [on_device(): payload = jnp.concatenate([payload, tags], axis=3)]
    concatenate x1, other arithmetic: 0.14 us -> 1.24 us  [on_device(): payload = jnp.concatenate([payload, tags], axis=3)]
where the time goes in v14:
time: 108 us
  starting transfers between devices  40.2 us (37%)
  matrix products  22.6 us (21%)
  other arithmetic  14.9 us (14%)
  waiting for transfers between devices  14.7 us (14%)
  local copies, waits for them, and re-layouts  11.5 us (11%)
  between operations  3.75 us (3%)
    ppermute x16, starting transfers between devices, shift(): lax.ppermute(value, axis, [(i, (i + step) % size) for i in range(size)])  24.5 us
    ppermute x16, waiting for transfers between devices, shift(): lax.ppermute(value, axis, [(i, (i + step) % size) for i in range(size)])  14.7 us
    dot_general x1, matrix products, on_device(): lax.dot_general(left, jnp.stack(right_imag, axis=1), dims, preferred_elem...  11.3 us
    dot_general x1, matrix products, on_device(): lax.dot_general(left, jnp.stack(right_real, axis=1), dims, preferred_elem...  11.3 us
    another operation x3, other arithmetic, on_device(): left = jnp.stack(parts).reshape(2 * pairs, local_g)  6.04 us
    all_to_all x1, starting transfers between devices, on_device(): spread = lax.all_to_all(copies, 'row', 0, 0, tiled=True)  5.16 us
    all_to_all x1, starting transfers between devices, on_device(): lax.all_to_all(payload, cols, split_axis=0, concat_axis=0, tiled=True)  5.14 us
    ppermute x1, starting transfers between devices, on_device(): first_other = lax.ppermute(first, 'core', CORE_PAIRS)  3.51 us
  transfers between devices with their start and end apart: 21, of which 4 were waited for; matrix products, arithmetic and copies ran while one was open for 20% of the time, Pallas kernels for 0%

profile of v14, /device:TPU:1, one launch (start us, length us, event | category | flops | bytes accessed | tf_op | source)
XLA Modules:
  0.0 107.7 jit_solution(7372600981392940540)
XLA Ops:
  0.7 2.1 %collective-permute-start.1 = (bf16[16,4096]{1,0:T(8,128)(2,1)}, bf16[16,4096]{1,0:T(8,128)(2,1)S(1)}, u32[]{:S(2)}, u32[]{:S(2)}) collective-permute-start(bf16[16,4096]{1,0:T(8,128)(2,1)} %param.7), channel_id=1, source_target_pairs={{0,8},{8,16},{16,24},{24,0},{1,9},{9,17},{17,25},{25,1},{2,10},{10... | collective-permute-start | bytes 393224 | tf_op jit(solution)/shard_map/ppermute | solution.py:17
  2.8 1.4 %collective-permute-start = (bf16[16,4096]{1,0:T(8,128)(2,1)}, bf16[16,4096]{1,0:T(8,128)(2,1)S(1)}, u32[]{:S(2)}, u32[]{:S(2)}) collective-permute-start(bf16[16,4096]{1,0:T(8,128)(2,1)} %param.7), channel_id=1, source_target_pairs={{0,24},{8,0},{16,8},{24,16},{1,25},{9,1},{17,9},{25,17},{2,26},{10... | collective-permute-start | bytes 393224 | tf_op jit(solution)/shard_map/ppermute | solution.py:17
  4.1 1.4 %collective-permute-start.5 = (bf16[16,4096]{1,0:T(8,128)(2,1)}, bf16[16,4096]{1,0:T(8,128)(2,1)S(1)}, u32[]{:S(2)}, u32[]{:S(2)}) collective-permute-start(bf16[16,4096]{1,0:T(8,128)(2,1)} %param.8), channel_id=1, source_target_pairs={{0,2},{2,4},{4,6},{6,0},{1,3},{3,5},{5,7},{7,1},{8,10},{10,12},{12... | collective-permute-start | bytes 393224 | tf_op jit(solution)/shard_map/ppermute | solution.py:17
  5.5 1.4 %collective-permute-start.4 = (bf16[16,4096]{1,0:T(8,128)(2,1)}, bf16[16,4096]{1,0:T(8,128)(2,1)S(1)}, u32[]{:S(2)}, u32[]{:S(2)}) collective-permute-start(bf16[16,4096]{1,0:T(8,128)(2,1)} %param.8), channel_id=1, source_target_pairs={{0,6},{2,0},{4,2},{6,4},{1,7},{3,1},{5,3},{7,5},{8,14},{10,8},{12,... | collective-permute-start | bytes 393224 | tf_op jit(solution)/shard_map/ppermute | solution.py:17
  7.0 1.0 pad_maximum_fusion.8
  8.0 1.1 broadcast_in_dim.28
  9.1 5.2 %all-to-all-start = ((bf16[4,2,16,4096]{3,2,1,0:T(8,128)(2,1)}), bf16[4,2,16,4096]{3,2,1,0:T(8,128)(2,1)S(1)}, u32[]{:S(2)}, u32[]{:S(2)}) async-start(bf16[4,2,16,4096]{3,2,1,0:T(8,128)(2,1)} %broadcast_in_dim.28), calls=%async_computation | async-start | bytes 2097152 | tf_op jit(solution)/shard_map/all_to_all | solution.py:49
  17.5 2.7 %collective-permute-start.7 = (bf16[16,2048]{1,0:T(8,128)(2,1)S(1)}, bf16[16,2048]{1,0:T(8,128)(2,1)S(1)}, u32[]{:S(2)}, u32[]{:S(2)}) collective-permute-start(bf16[16,2048]{1,0:T(8,128)(2,1)S(1)} %slice.111), channel_id=1, source_target_pairs={{0,6},{2,0},{4,2},{6,4},{1,7},{3,1},{5,3},{7,5},{8,14},{10,8},{12,... | collective-permute-start | bytes 196616 | tf_op jit(solution)/shard_map/ppermute | solution.py:17
  20.4 2.7 %collective-permute-start.3 = (bf16[16,2048]{1,0:T(8,128)(2,1)S(1)}, bf16[16,2048]{1,0:T(8,128)(2,1)S(1)}, u32[]{:S(2)}, u32[]{:S(2)}) collective-permute-start(bf16[16,2048]{1,0:T(8,128)(2,1)S(1)} %slice.109), channel_id=1, source_target_pairs={{0,24},{8,0},{16,8},{24,16},{1,25},{9,1},{17,9},{25,17},{2,26},{10... | collective-permute-start | bytes 196616 | tf_op jit(solution)/shard_map/ppermute | solution.py:17
  23.1 0.9 fusion.29
  24.0 0.9 collective-permute-done.2
  26.0 3.5 %collective-permute-start.12 = (bf16[2,4,16,4096]{3,2,1,0:T(8,128)(2,1)S(1)}, bf16[2,4,16,4096]{3,2,1,0:T(8,128)(2,1)}, u32[]{:S(2)}, u32[]{:S(2)}) collective-permute-start(bf16[2,4,16,4096]{3,2,1,0:T(8,128)(2,1)S(1)} %pad_maximum_fusion.4), channel_id=1, source_target_pairs={{0,1},{1,0},{2,3},{3,2},{4,5},{5,4},{6,7},{7,6},{8,9},{9,8},{10,11... | collective-permute-start | bytes 3145736 | tf_op jit(solution)/shard_map/ppermute | solution.py:54
  30.0 2.7 %collective-permute-start.8 = (bf16[4,16,4096]{2,1,0:T(8,128)(2,1)}, bf16[4,16,4096]{2,1,0:T(8,128)(2,1)S(1)}, u32[]{:S(2)}, u32[]{:S(2)}) collective-permute-start(bf16[4,16,4096]{2,1,0:T(8,128)(2,1)} %get-tuple-element.7), channel_id=1, source_target_pairs={{0,6},{2,0},{4,2},{6,4},{1,7},{3,1},{5,3},{7,5},{8,14},{10,8},{12,... | collective-permute-start | bytes 1572872 | tf_op jit(solution)/shard_map/ppermute | solution.py:17
  33.0 2.7 %collective-permute-start.13 = (bf16[4,16,4096]{2,1,0:T(8,128)(2,1)}, bf16[4,16,4096]{2,1,0:T(8,128)(2,1)}, u32[]{:S(2)}, u32[]{:S(2)}) collective-permute-start(bf16[4,16,4096]{2,1,0:T(8,128)(2,1)} %get-tuple-element.8), channel_id=1, source_target_pairs={{0,24},{8,0},{16,8},{24,16},{1,25},{9,1},{17,9},{25,17},{2,26},{10... | collective-permute-start | bytes 1572872 | tf_op jit(solution)/shard_map/ppermute | solution.py:17
  36.1 1.2 %pad_maximum_fusion.3 = bf16[32,2,16,640]{3,2,1,0:T(8,128)(2,1)} fusion(bf16[32,2,16,128]{3,2,1,0:T(8,128)(2,1)S(1)} %broadcast_in_dim.29, bf16[32,2,16,512]{3,2,1,0:T(8,128)(2,1)S(1)} %bitcast.96), kind=kLoop, calls=%fused_computation.15 | loop fusion | flops 2621440 | bytes 2621440 | tf_op jit(solution)/shard_map/concatenate | solution.py:59
  37.3 5.1 %all-to-all-start.1 = ((bf16[32,2,16,640]{3,2,1,0:T(8,128)(2,1)}), bf16[32,2,16,640]{3,2,1,0:T(8,128)(2,1)S(1)}, u32[]{:S(2)}, u32[]{:S(2)}) async-start(bf16[32,2,16,640]{3,2,1,0:T(8,128)(2,1)} %pad_maximum_fusion.3), calls=%async_computation.1 | async-start | bytes 2621440 | tf_op jit(solution)/shard_map/all_to_all | solution.py:60
  42.6 1.6 %collective-permute-done.9 = bf16[4,16,4096]{2,1,0:T(8,128)(2,1)S(1)} collective-permute-done((bf16[4,16,4096]{2,1,0:T(8,128)(2,1)}, bf16[4,16,4096]{2,1,0:T(8,128)(2,1)S(1)}, u32[]{:S(2)}, u32[]{:S(2)}) %collective-permute-start.9) | collective-permute-done | bytes 524320 | tf_op jit(solution)/shard_map/ppermute | solution.py:17
  44.3 2.7 %collective-permute-start.11 = (bf16[4,16,2048]{2,1,0:T(8,128)(2,1)S(1)}, bf16[4,16,2048]{2,1,0:T(8,128)(2,1)S(1)}, u32[]{:S(2)}, u32[]{:S(2)}) collective-permute-start(bf16[4,16,2048]{2,1,0:T(8,128)(2,1)S(1)} %slice.113), channel_id=1, source_target_pairs={{0,6},{2,0},{4,2},{6,4},{1,7},{3,1},{5,3},{7,5},{8,14},{10,8},{12,... | collective-permute-start | bytes 786440 | tf_op jit(solution)/shard_map/ppermute | solution.py:17
  47.0 1.3 %fusion.34 = (bf16[1,4,16,4096]{3,2,1,0:T(8,128)(2,1)S(1)}, bf16[1,4,16,4096]{3,2,1,0:T(8,128)(2,1)S(1)}) fusion(bf16[2,4,16,4096]{3,2,1,0:T(8,128)(2,1)} %collective-permute-done.12), kind=kLoop, calls=%fused_computation.99 | loop fusion | bytes 2097152 | tf_op jit(solution)/shard_map/slice | solution.py:72
  48.3 1.0 slice.116
  50.0 1.0 slice.117
  51.0 3.3 %collective-permute-start.17 = (bf16[4,16,2048]{2,1,0:T(8,128)(2,1)S(1)}, bf16[4,16,2048]{2,1,0:T(8,128)(2,1)S(1)}, u32[]{:S(2)}, u32[]{:S(2)}) collective-permute-start(bf16[4,16,2048]{2,1,0:T(8,128)(2,1)S(1)} %slice.117), channel_id=1, source_target_pairs={{0,24},{8,0},{16,8},{24,16},{1,25},{9,1},{17,9},{25,17},{2,26},{10... | collective-permute-start | bytes 786440 | tf_op jit(solution)/shard_map/ppermute | solution.py:17
  54.3 11.3 %collective-permute-done.10 = bf16[4,16,2048]{2,1,0:T(8,128)(2,1)S(1)} collective-permute-done((bf16[4,16,2048]{2,1,0:T(8,128)(2,1)S(1)}, bf16[4,16,2048]{2,1,0:T(8,128)(2,1)S(1)}, u32[]{:S(2)}, u32[]{:S(2)}) %collective-permute-start.10) | collective-permute-done | bytes 262176 | tf_op jit(solution)/shard_map/ppermute | solution.py:17
  66.6 1.1 pad_maximum_fusion.5
  67.6 1.9 %collective-permute-start.18 = (bf16[2,4,16,4096]{3,2,1,0:T(8,128)(2,1)}, bf16[2,4,16,4096]{3,2,1,0:T(8,128)(2,1)}, u32[]{:S(2)}, u32[]{:S(2)}) collective-permute-start(bf16[2,4,16,4096]{3,2,1,0:T(8,128)(2,1)} %pad_maximum_fusion.5), channel_id=1, source_target_pairs={{0,1},{1,0},{2,3},{3,2},{4,5},{5,4},{6,7},{7,6},{8,9},{9,8},{10,11... | collective-permute-start | bytes 3145736 | tf_op jit(solution)/shard_map/ppermute | solution.py:67
  69.5 4.4 %maximum_bitcast_fusion = (bf16[1,4,4,16,4096]{4,3,2,1,0:T(8,128)(2,1)}, bf16[4,4,16,4096]{3,2,1,0:T(8,128)(2,1)}, bf16[1,4,4,16,4096]{4,3,2,1,0:T(8,128)(2,1)}) fusion(bf16[1,4,16,4096]{3,2,1,0:T(8,128)(2,1)S(1)} %bitcast.107, bf16[1,4,16,4096]{3,2,1,0:T(8,128)(2,1)S(1)} %maximum_bitcast_fusion.7, bf16[1,4,16,4096]{3,2,1,0:T(8,128)(2,1)S(1)} %bitcast.108, ...), kind=kLoop, calls=%fused_computation.6 | loop fusion | flops 9437184 | bytes 10485760 | tf_op jit(solution)/shard_map/stack | solution.py:74
  78.8 1.3 %fusion.35 = (bf16[1,4,16,4096]{3,2,1,0:T(8,128)(2,1)S(1)}, bf16[1,4,16,4096]{3,2,1,0:T(8,128)(2,1)S(1)}) fusion(bf16[2,4,16,4096]{3,2,1,0:T(8,128)(2,1)} %collective-permute-done.18), kind=kLoop, calls=%fused_computation.100 | loop fusion | bytes 2097152 | tf_op jit(solution)/shard_map/slice | solution.py:72
  80.1 1.7 %fusion.32 = (bf16[1,4,16,4096]{3,2,1,0:T(8,128)(2,1)S(1)}, bf16[1,4,16,4096]{3,2,1,0:T(8,128)(2,1)S(1)}, bf16[1,4,16,4096]{3,2,1,0:T(8,128)(2,1)S(1)}, bf16[1,4,16,4096]{3,2,1,0:T(8,128)(2,1)S(1)}) fusion(bf16[4,4,16,4096]{3,2,1,0:T(8,128)(2,1)} %collective-permute-done.15), kind=kLoop, calls=%fused_computation.97 | loop fusion | bytes 4194304 | tf_op jit(solution)/shard_map/slice | solution.py:72
  82.4 1.0 copy-done
  84.0 1.1 %pad_maximum_fusion = bf16[4,4,4,16,4096]{4,3,2,1,0:T(8,128)(2,1)S(1)} fusion(bf16[1,4,4,16,4096]{4,3,2,1,0:T(8,128)(2,1)S(1)} %get-tuple-element.50, bf16[1,4,4,16,4096]{4,3,2,1,0:T(8,128)(2,1)S(1)} %copy-done.1, bf16[1,4,4,16,4096]{4,3,2,1,0:T(8,128)(2,1)S(1)} %get-tuple-element.49, bf16[1,4,4,16,4096]{4,3,2,1,0:T(8,128)(2,1)S(1)} %copy-done), kind=kLoop, calls=%fused_computation | loop fusion | flops 12582912 | bytes 16777216 | tf_op jit(solution)/shard_map/stack | solution.py:74
  85.1 11.3 %convert_bitcast_fusion = bf16[2,4096,512]{2,1,0:T(8,128)(2,1)} fusion(bf16[1024,4096,1]{1,0,2:T(8,128)(2,1)S(1)} %bitcast.89, bf16[1024,1,512]{2,0,1:T(8,128)(2,1)S(1)} %maximum_bitcast_fusion.6, bf16[1024,1,512]{2,0,1:T(8,128)(2,1)S(1)} %maximum_bitcast_fusion.5), kind=kOutput, calls=%fused_computation.1 | convolution fusion | flops 8598323200 | bytes 18874368 | tf_op jit(solution)/shard_map/dot_general | solution.py:106
  96.4 11.3 %convert_bitcast_fusion.1 = bf16[2,4096,512]{2,1,0:T(8,128)(2,1)} fusion(bf16[1024,4096,1]{1,0,2:T(8,128)(2,1)S(1)} %bitcast.90, bf16[1024,1,512]{2,0,1:T(8,128)(2,1)S(1)} %maximum_bitcast_fusion.4, bf16[1024,1,512]{2,0,1:T(8,128)(2,1)S(1)} %maximum_bitcast_fusion.3), kind=kOutput, calls=%fused_computation.2 | convolution fusion | flops 8598323200 | bytes 18874368 | tf_op jit(solution)/shard_map/dot_general | solution.py:105
  (104 shorter events, 10.9 us)
Async XLA Ops:
  0.6 13.6 %copy-start.11 = (s32[16]{0:T(128)S(1)}, s32[16]{0:T(128)}, u32[]{:S(2)}) copy-start(s32[16]{0:T(128)} %param.9) | copy-start | bytes 196
  0.6 13.6 %copy-start.12 = (s32[16]{0:T(128)S(1)}, s32[16]{0:T(128)}, u32[]{:S(2)}) copy-start(s32[16]{0:T(128)} %param.10) | copy-start | bytes 196
  0.7 13.6 %copy-start.8 = (f32[2]{0:T(128)S(1)}, f32[2]{0:T(128)}, u32[]{:S(2)}) copy-start(f32[2]{0:T(128)} %param.13) | copy-start | bytes 28
  0.7 19.6 %collective-permute-start.1 = (bf16[16,4096]{1,0:T(8,128)(2,1)}, bf16[16,4096]{1,0:T(8,128)(2,1)S(1)}, u32[]{:S(2)}, u32[]{:S(2)}) collective-permute-start(bf16[16,4096]{1,0:T(8,128)(2,1)} %param.7), channel_id=1, source_target_pairs={{0,8},{8,16},{16,24},{24,0},{1,9},{9,17},{17,25},{25,1},{2,10},{10... | collective-permute-start | bytes 393224 | tf_op jit(solution)/shard_map/ppermute | solution.py:17
  2.8 17.6 %collective-permute-start = (bf16[16,4096]{1,0:T(8,128)(2,1)}, bf16[16,4096]{1,0:T(8,128)(2,1)S(1)}, u32[]{:S(2)}, u32[]{:S(2)}) collective-permute-start(bf16[16,4096]{1,0:T(8,128)(2,1)} %param.7), channel_id=1, source_target_pairs={{0,24},{8,0},{16,8},{24,16},{1,25},{9,1},{17,9},{25,17},{2,26},{10... | collective-permute-start | bytes 393224 | tf_op jit(solution)/shard_map/ppermute | solution.py:17
  4.1 13.3 %collective-permute-start.5 = (bf16[16,4096]{1,0:T(8,128)(2,1)}, bf16[16,4096]{1,0:T(8,128)(2,1)S(1)}, u32[]{:S(2)}, u32[]{:S(2)}) collective-permute-start(bf16[16,4096]{1,0:T(8,128)(2,1)} %param.8), channel_id=1, source_target_pairs={{0,2},{2,4},{4,6},{6,0},{1,3},{3,5},{5,7},{7,1},{8,10},{10,12},{12... | collective-permute-start | bytes 393224 | tf_op jit(solution)/shard_map/ppermute | solution.py:17
  5.5 12.0 %collective-permute-start.4 = (bf16[16,4096]{1,0:T(8,128)(2,1)}, bf16[16,4096]{1,0:T(8,128)(2,1)S(1)}, u32[]{:S(2)}, u32[]{:S(2)}) collective-permute-start(bf16[16,4096]{1,0:T(8,128)(2,1)} %param.8), channel_id=1, source_target_pairs={{0,6},{2,0},{4,2},{6,4},{1,7},{3,1},{5,3},{7,5},{8,14},{10,8},{12,... | collective-permute-start | bytes 393224 | tf_op jit(solution)/shard_map/ppermute | solution.py:17
  8.0 15.2 %copy-start.6 = (bf16[16,4096]{1,0:T(8,128)(2,1)S(1)}, bf16[16,4096]{1,0:T(8,128)(2,1)}, u32[]{:S(2)}) copy-start(bf16[16,4096]{1,0:T(8,128)(2,1)} %param.8) | copy-start | bytes 393220
  9.1 15.9 %copy-start.7 = (bf16[16,4096]{1,0:T(8,128)(2,1)S(1)}, bf16[16,4096]{1,0:T(8,128)(2,1)}, u32[]{:S(2)}) copy-start(bf16[16,4096]{1,0:T(8,128)(2,1)} %param.7) | copy-start | bytes 393220
  9.1 20.4 %all-to-all-start = ((bf16[4,2,16,4096]{3,2,1,0:T(8,128)(2,1)}), bf16[4,2,16,4096]{3,2,1,0:T(8,128)(2,1)S(1)}, u32[]{:S(2)}, u32[]{:S(2)}) async-start(bf16[4,2,16,4096]{3,2,1,0:T(8,128)(2,1)} %broadcast_in_dim.28), calls=%async_computation | async-start | bytes 2097152 | tf_op jit(solution)/shard_map/all_to_all | solution.py:49
  17.4 5.7 %collective-permute-start.6 = (bf16[16,2048]{1,0:T(8,128)(2,1)S(1)}, bf16[16,2048]{1,0:T(8,128)(2,1)S(1)}, u32[]{:S(2)}, u32[]{:S(2)}) collective-permute-start(bf16[16,2048]{1,0:T(8,128)(2,1)S(1)} %slice.110), channel_id=1, source_target_pairs={{0,2},{2,4},{4,6},{6,0},{1,3},{3,5},{5,7},{7,1},{8,10},{10,12},{12... | collective-permute-start | bytes 196616 | tf_op jit(solution)/shard_map/ppermute | solution.py:17
  17.5 5.6 %collective-permute-start.7 = (bf16[16,2048]{1,0:T(8,128)(2,1)S(1)}, bf16[16,2048]{1,0:T(8,128)(2,1)S(1)}, u32[]{:S(2)}, u32[]{:S(2)}) collective-permute-start(bf16[16,2048]{1,0:T(8,128)(2,1)S(1)} %slice.111), channel_id=1, source_target_pairs={{0,6},{2,0},{4,2},{6,4},{1,7},{3,1},{5,3},{7,5},{8,14},{10,8},{12,... | collective-permute-start | bytes 196616 | tf_op jit(solution)/shard_map/ppermute | solution.py:17
  20.3 4.7 %collective-permute-start.2 = (bf16[16,2048]{1,0:T(8,128)(2,1)S(1)}, bf16[16,2048]{1,0:T(8,128)(2,1)S(1)}, u32[]{:S(2)}, u32[]{:S(2)}) collective-permute-start(bf16[16,2048]{1,0:T(8,128)(2,1)S(1)} %slice.108), channel_id=1, source_target_pairs={{0,8},{8,16},{16,24},{24,0},{1,9},{9,17},{17,25},{25,1},{2,10},{10... | collective-permute-start | bytes 196616 | tf_op jit(solution)/shard_map/ppermute | solution.py:17
  20.4 4.6 %collective-permute-start.3 = (bf16[16,2048]{1,0:T(8,128)(2,1)S(1)}, bf16[16,2048]{1,0:T(8,128)(2,1)S(1)}, u32[]{:S(2)}, u32[]{:S(2)}) collective-permute-start(bf16[16,2048]{1,0:T(8,128)(2,1)S(1)} %slice.109), channel_id=1, source_target_pairs={{0,24},{8,0},{16,8},{24,16},{1,25},{9,1},{17,9},{25,17},{2,26},{10... | collective-permute-start | bytes 196616 | tf_op jit(solution)/shard_map/ppermute | solution.py:17
  26.0 21.1 %collective-permute-start.12 = (bf16[2,4,16,4096]{3,2,1,0:T(8,128)(2,1)S(1)}, bf16[2,4,16,4096]{3,2,1,0:T(8,128)(2,1)}, u32[]{:S(2)}, u32[]{:S(2)}) collective-permute-start(bf16[2,4,16,4096]{3,2,1,0:T(8,128)(2,1)S(1)} %pad_maximum_fusion.4), channel_id=1, source_target_pairs={{0,1},{1,0},{2,3},{3,2},{4,5},{5,4},{6,7},{7,6},{8,9},{9,8},{10,11... | collective-permute-start | bytes 3145736 | tf_op jit(solution)/shard_map/ppermute | solution.py:54
  29.9 14.3 %collective-permute-start.9 = (bf16[4,16,4096]{2,1,0:T(8,128)(2,1)}, bf16[4,16,4096]{2,1,0:T(8,128)(2,1)S(1)}, u32[]{:S(2)}, u32[]{:S(2)}) collective-permute-start(bf16[4,16,4096]{2,1,0:T(8,128)(2,1)} %get-tuple-element.7), channel_id=1, source_target_pairs={{0,2},{2,4},{4,6},{6,0},{1,3},{3,5},{5,7},{7,1},{8,10},{10,12},{12... | collective-permute-start | bytes 1572872 | tf_op jit(solution)/shard_map/ppermute | solution.py:17
  30.0 14.3 %collective-permute-start.8 = (bf16[4,16,4096]{2,1,0:T(8,128)(2,1)}, bf16[4,16,4096]{2,1,0:T(8,128)(2,1)S(1)}, u32[]{:S(2)}, u32[]{:S(2)}) collective-permute-start(bf16[4,16,4096]{2,1,0:T(8,128)(2,1)} %get-tuple-element.7), channel_id=1, source_target_pairs={{0,6},{2,0},{4,2},{6,4},{1,7},{3,1},{5,3},{7,5},{8,14},{10,8},{12,... | collective-permute-start | bytes 1572872 | tf_op jit(solution)/shard_map/ppermute | solution.py:17
  32.6 15.7 %collective-permute-start.14 = (bf16[4,16,4096]{2,1,0:T(8,128)(2,1)}, bf16[4,16,4096]{2,1,0:T(8,128)(2,1)}, u32[]{:S(2)}, u32[]{:S(2)}) collective-permute-start(bf16[4,16,4096]{2,1,0:T(8,128)(2,1)} %get-tuple-element.8), channel_id=1, source_target_pairs={{0,8},{8,16},{16,24},{24,0},{1,9},{9,17},{17,25},{25,1},{2,10},{10... | collective-permute-start | bytes 1572872 | tf_op jit(solution)/shard_map/ppermute | solution.py:17
  33.0 17.0 %collective-permute-start.13 = (bf16[4,16,4096]{2,1,0:T(8,128)(2,1)}, bf16[4,16,4096]{2,1,0:T(8,128)(2,1)}, u32[]{:S(2)}, u32[]{:S(2)}) collective-permute-start(bf16[4,16,4096]{2,1,0:T(8,128)(2,1)} %get-tuple-element.8), channel_id=1, source_target_pairs={{0,24},{8,0},{16,8},{24,16},{1,25},{9,1},{17,9},{25,17},{2,26},{10... | collective-permute-start | bytes 1572872 | tf_op jit(solution)/shard_map/ppermute | solution.py:17
  37.3 36.6 %all-to-all-start.1 = ((bf16[32,2,16,640]{3,2,1,0:T(8,128)(2,1)}), bf16[32,2,16,640]{3,2,1,0:T(8,128)(2,1)S(1)}, u32[]{:S(2)}, u32[]{:S(2)}) async-start(bf16[32,2,16,640]{3,2,1,0:T(8,128)(2,1)} %pad_maximum_fusion.3), calls=%async_computation.1 | async-start | bytes 2621440 | tf_op jit(solution)/shard_map/all_to_all | solution.py:60
  44.2 2.9 %copy-start.2 = (bf16[4,16,4096]{2,1,0:T(8,128)(2,1)}, bf16[4,16,4096]{2,1,0:T(8,128)(2,1)S(1)}, u32[]{:S(2)}) copy-start(bf16[4,16,4096]{2,1,0:T(8,128)(2,1)S(1)} %collective-permute-done.9) | copy-start | bytes 1572868
  44.2 21.5 %collective-permute-start.10 = (bf16[4,16,2048]{2,1,0:T(8,128)(2,1)S(1)}, bf16[4,16,2048]{2,1,0:T(8,128)(2,1)S(1)}, u32[]{:S(2)}, u32[]{:S(2)}) collective-permute-start(bf16[4,16,2048]{2,1,0:T(8,128)(2,1)S(1)} %slice.112), channel_id=1, source_target_pairs={{0,2},{2,4},{4,6},{6,0},{1,3},{3,5},{5,7},{7,1},{8,10},{10,12},{12... | collective-permute-start | bytes 786440 | tf_op jit(solution)/shard_map/ppermute | solution.py:17
  44.3 2.8 %copy-start.4 = (bf16[4,16,4096]{2,1,0:T(8,128)(2,1)}, bf16[4,16,4096]{2,1,0:T(8,128)(2,1)S(1)}, u32[]{:S(2)}) copy-start(bf16[4,16,4096]{2,1,0:T(8,128)(2,1)S(1)} %collective-permute-done.8) | copy-start | bytes 1572868
  44.3 21.3 %collective-permute-start.11 = (bf16[4,16,2048]{2,1,0:T(8,128)(2,1)S(1)}, bf16[4,16,2048]{2,1,0:T(8,128)(2,1)S(1)}, u32[]{:S(2)}, u32[]{:S(2)}) collective-permute-start(bf16[4,16,2048]{2,1,0:T(8,128)(2,1)S(1)} %slice.113), channel_id=1, source_target_pairs={{0,6},{2,0},{4,2},{6,4},{1,7},{3,1},{5,3},{7,5},{8,14},{10,8},{12,... | collective-permute-start | bytes 786440 | tf_op jit(solution)/shard_map/ppermute | solution.py:17
  49.3 17.2 %collective-permute-start.16 = (bf16[4,16,2048]{2,1,0:T(8,128)(2,1)S(1)}, bf16[4,16,2048]{2,1,0:T(8,128)(2,1)S(1)}, u32[]{:S(2)}, u32[]{:S(2)}) collective-permute-start(bf16[4,16,2048]{2,1,0:T(8,128)(2,1)S(1)} %slice.116), channel_id=1, source_target_pairs={{0,8},{8,16},{16,24},{24,0},{1,9},{9,17},{17,25},{25,1},{2,10},{10... | collective-permute-start | bytes 786440 | tf_op jit(solution)/shard_map/ppermute | solution.py:17
  51.0 18.5 %copy-start.3 = (bf16[4,16,4096]{2,1,0:T(8,128)(2,1)S(1)}, bf16[4,16,4096]{2,1,0:T(8,128)(2,1)}, u32[]{:S(2)}) copy-start(bf16[4,16,4096]{2,1,0:T(8,128)(2,1)} %copy-done.2) | copy-start | bytes 1572868
  51.0 18.5 %copy-start.5 = (bf16[4,16,4096]{2,1,0:T(8,128)(2,1)S(1)}, bf16[4,16,4096]{2,1,0:T(8,128)(2,1)}, u32[]{:S(2)}) copy-start(bf16[4,16,4096]{2,1,0:T(8,128)(2,1)} %copy-done.4) | copy-start | bytes 1572868
  51.0 15.5 %collective-permute-start.17 = (bf16[4,16,2048]{2,1,0:T(8,128)(2,1)S(1)}, bf16[4,16,2048]{2,1,0:T(8,128)(2,1)S(1)}, u32[]{:S(2)}, u32[]{:S(2)}) collective-permute-start(bf16[4,16,2048]{2,1,0:T(8,128)(2,1)S(1)} %slice.117), channel_id=1, source_target_pairs={{0,24},{8,0},{16,8},{24,16},{1,25},{9,1},{17,9},{25,17},{2,26},{10... | collective-permute-start | bytes 786440 | tf_op jit(solution)/shard_map/ppermute | solution.py:17
  67.6 11.2 %collective-permute-start.18 = (bf16[2,4,16,4096]{3,2,1,0:T(8,128)(2,1)}, bf16[2,4,16,4096]{3,2,1,0:T(8,128)(2,1)}, u32[]{:S(2)}, u32[]{:S(2)}) collective-permute-start(bf16[2,4,16,4096]{3,2,1,0:T(8,128)(2,1)} %pad_maximum_fusion.5), channel_id=1, source_target_pairs={{0,1},{1,0},{2,3},{3,2},{4,5},{5,4},{6,7},{7,6},{8,9},{9,8},{10,11... | collective-permute-start | bytes 3145736 | tf_op jit(solution)/shard_map/ppermute | solution.py:67
  73.9 6.2 %collective-permute-start.15 = (bf16[4,4,16,4096]{3,2,1,0:T(8,128)(2,1)}, bf16[4,4,16,4096]{3,2,1,0:T(8,128)(2,1)}, u32[]{:S(2)}, u32[]{:S(2)}) collective-permute-start(bf16[4,4,16,4096]{3,2,1,0:T(8,128)(2,1)} %get-tuple-element.23), channel_id=1, source_target_pairs={{0,1},{1,0},{2,3},{3,2},{4,5},{5,4},{6,7},{7,6},{8,9},{9,8},{10,11... | collective-permute-start | bytes 6291464 | tf_op jit(solution)/shard_map/ppermute | solution.py:65
  81.8 1.6 %copy-start = (bf16[1,4,4,16,4096]{4,3,2,1,0:T(8,128)(2,1)S(1)}, bf16[1,4,4,16,4096]{4,3,2,1,0:T(8,128)(2,1)}, u32[]{:S(2)}) copy-start(bf16[1,4,4,16,4096]{4,3,2,1,0:T(8,128)(2,1)} %get-tuple-element.22) | copy-start | bytes 6291460
  81.8 2.2 %copy-start.1 = (bf16[1,4,4,16,4096]{4,3,2,1,0:T(8,128)(2,1)S(1)}, bf16[1,4,4,16,4096]{4,3,2,1,0:T(8,128)(2,1)}, u32[]{:S(2)}) copy-start(bf16[1,4,4,16,4096]{4,3,2,1,0:T(8,128)(2,1)} %get-tuple-element.24) | copy-start | bytes 6291460
  (2 other events, 1.4 us)

commit v15 on v14

--- a/solution.py
+++ b/solution.py
@@ -27,6 +27,10 @@
     return from_plus, far, from_minus
 
 
+def ring_direct(block, axis):
+    return jnp.stack([block, shift(block, axis, -1), shift(block, axis, 2), shift(block, axis, 1)])
+
+
 def on_device(
     matrix_real,
     matrix_imag,
@@ -48,8 +52,8 @@
     copies = jnp.broadcast_to(both[None], (nrow,) + both.shape)
     spread = lax.all_to_all(copies, "row", 0, 0, tiled=True)
     spread = spread.reshape(nrow, 2, local_pairs, local_g // width, width)
-    row_real = jnp.stack((matrix_real,) + ring_gather(matrix_real, "x"))
-    col_imag = jnp.stack((matrix_imag,) + ring_gather(matrix_imag, "y"))
+    row_real = ring_direct(matrix_real, "x")
+    col_imag = ring_direct(matrix_imag, "y")
     first = jnp.stack([row_real, col_imag])
     first_other = lax.ppermute(first, "core", CORE_PAIRS)
     spread, row_real, col_imag, first = lax.optimization_barrier((spread, row_real, col_imag, first))

time: 108 us -> 108 us (level)
  starting transfers between devices: 40.2 us -> 37.6 us
  waiting for transfers between devices: 14.7 us -> 16.8 us
    ppermute x16 -> x14, starting transfers between devices: 24.5 us -> 21 us  [shift(): lax.ppermute(value, axis, [(i, (i + step) % size) for i in range(size)])]
    all_to_all x1, starting transfers between devices: 5.14 us -> 7.42 us  [on_device(): lax.all_to_all(payload, cols, split_axis=0, concat_axis=0, tiled=True)]
    ppermute x16 -> x14, waiting for transfers between devices: 14.7 us -> 16.8 us  [shift(): lax.ppermute(value, axis, [(i, (i + step) % size) for i in range(size)])]
  transfers between devices with their start and end apart: 21 -> 19, of which waited for: 4 -> 3; matrix products, arithmetic and copies ran while one was open for 20% -> 20% of each run, Pallas kernels for 0% -> 0%
where the time goes in v15:
time: 108 us; the launch traced here: 107 us
  starting transfers between devices  37.6 us (35%)
  matrix products  22.6 us (21%)
  waiting for transfers between devices  16.8 us (16%)
  other arithmetic  14.9 us (14%)
  local copies, waits for them, and re-layouts  11.5 us (11%)
  between operations  3.8 us (4%)
    ppermute x14, starting transfers between devices, shift(): lax.ppermute(value, axis, [(i, (i + step) % size) for i in range(size)])  21 us
    ppermute x14, waiting for transfers between devices, shift(): lax.ppermute(value, axis, [(i, (i + step) % size) for i in range(size)])  16.8 us
    dot_general x1, matrix products, on_device(): lax.dot_general(left, jnp.stack(right_imag, axis=1), dims, preferred_elem...  11.3 us
    dot_general x1, matrix products, on_device(): lax.dot_general(left, jnp.stack(right_real, axis=1), dims, preferred_elem...  11.3 us
    all_to_all x1, starting transfers between devices, on_device(): lax.all_to_all(payload, cols, split_axis=0, concat_axis=0, tiled=True)  7.42 us
    another operation x3, other arithmetic, on_device(): left = jnp.stack(parts).reshape(2 * pairs, local_g)  6.02 us
    all_to_all x1, starting transfers between devices, on_device(): spread = lax.all_to_all(copies, 'row', 0, 0, tiled=True)  5.03 us
    ppermute x1, starting transfers between devices, on_device(): first_other = lax.ppermute(first, 'core', CORE_PAIRS)  3.3 us
  transfers between devices with their start and end apart: 19, of which 3 were waited for; matrix products, arithmetic and copies ran while one was open for 20% of the time, Pallas kernels for 0%

profile of v15, /device:TPU:1, one launch (start us, length us, event | category | flops | bytes accessed | tf_op | source)
XLA Modules:
  0.0 107.3 jit_solution(9484776174220694307)
XLA Ops:
  0.7 3.4 %collective-permute-start = (bf16[16,4096]{1,0:T(8,128)(2,1)}, bf16[16,4096]{1,0:T(8,128)(2,1)S(1)}, u32[]{:S(2)}, u32[]{:S(2)}) collective-permute-start(bf16[16,4096]{1,0:T(8,128)(2,1)} %param.7), channel_id=1, source_target_pairs={{0,24},{8,0},{16,8},{24,16},{1,25},{9,1},{17,9},{25,17},{2,26},{10... | collective-permute-start | bytes 393224 | tf_op jit(solution)/shard_map/ppermute | solution.py:17
  4.1 2.7 %collective-permute-start.3 = (bf16[16,4096]{1,0:T(8,128)(2,1)}, bf16[16,4096]{1,0:T(8,128)(2,1)S(1)}, u32[]{:S(2)}, u32[]{:S(2)}) collective-permute-start(bf16[16,4096]{1,0:T(8,128)(2,1)} %param.8), channel_id=1, source_target_pairs={{0,6},{2,0},{4,2},{6,4},{1,7},{3,1},{5,3},{7,5},{8,14},{10,8},{12,... | collective-permute-start | bytes 393224 | tf_op jit(solution)/shard_map/ppermute | solution.py:17
  6.8 1.6 %collective-permute-start.4 = (bf16[16,4096]{1,0:T(8,128)(2,1)}, bf16[16,4096]{1,0:T(8,128)(2,1)S(1)}, u32[]{:S(2)}, u32[]{:S(2)}) collective-permute-start(bf16[16,4096]{1,0:T(8,128)(2,1)} %param.8), channel_id=1, source_target_pairs={{0,4},{2,6},{4,0},{6,2},{1,5},{3,7},{5,1},{7,3},{8,12},{10,14},{12... | collective-permute-start | bytes 393224 | tf_op jit(solution)/shard_map/ppermute | solution.py:17
  8.4 1.0 pad_maximum_fusion.8
  9.4 1.1 %broadcast_in_dim.28 = bf16[4,2,16,4096]{3,2,1,0:T(8,128)(2,1)} broadcast(bf16[2,16,4096]{2,1,0:T(8,128)(2,1)S(1)} %pad_maximum_fusion.8), dimensions={1,2,3} | broadcast | bytes 1310720 | tf_op jit(solution)/shard_map/broadcast_in_dim | solution.py:52
  10.5 5.0 %all-to-all-start = ((bf16[4,2,16,4096]{3,2,1,0:T(8,128)(2,1)}), bf16[4,2,16,4096]{3,2,1,0:T(8,128)(2,1)S(1)}, u32[]{:S(2)}, u32[]{:S(2)}) async-start(bf16[4,2,16,4096]{3,2,1,0:T(8,128)(2,1)} %broadcast_in_dim.28), calls=%async_computation | async-start | bytes 2097152 | tf_op jit(solution)/shard_map/all_to_all | solution.py:53
  18.9 1.8 %collective-permute-start.1 = (bf16[16,4096]{1,0:T(8,128)(2,1)S(1)}, bf16[16,4096]{1,0:T(8,128)(2,1)S(1)}, u32[]{:S(2)}, u32[]{:S(2)}) collective-permute-start(bf16[16,4096]{1,0:T(8,128)(2,1)S(1)} %copy-done.7), channel_id=1, source_target_pairs={{0,16},{8,24},{16,0},{24,8},{1,17},{9,25},{17,1},{25,9},{2,18},{10... | collective-permute-start | bytes 393224 | tf_op jit(solution)/shard_map/ppermute | solution.py:17
  20.7 0.9 fusion.29
  21.6 2.7 %collective-permute-done.1 = bf16[16,4096]{1,0:T(8,128)(2,1)S(1)} collective-permute-done((bf16[16,4096]{1,0:T(8,128)(2,1)S(1)}, bf16[16,4096]{1,0:T(8,128)(2,1)S(1)}, u32[]{:S(2)}, u32[]{:S(2)}) %collective-permute-start.1) | collective-permute-done | bytes 131104 | tf_op jit(solution)/shard_map/ppermute | solution.py:17
  24.3 0.9 fusion.30
  25.3 3.3 %collective-permute-start.10 = (bf16[2,4,16,4096]{3,2,1,0:T(8,128)(2,1)S(1)}, bf16[2,4,16,4096]{3,2,1,0:T(8,128)(2,1)}, u32[]{:S(2)}, u32[]{:S(2)}) collective-permute-start(bf16[2,4,16,4096]{3,2,1,0:T(8,128)(2,1)S(1)} %pad_maximum_fusion.4), channel_id=1, source_target_pairs={{0,1},{1,0},{2,3},{3,2},{4,5},{5,4},{6,7},{7,6},{8,9},{9,8},{10,11... | collective-permute-start | bytes 3145736 | tf_op jit(solution)/shard_map/ppermute | solution.py:58
  29.0 1.7 %collective-permute-start.7 = (bf16[4,16,4096]{2,1,0:T(8,128)(2,1)}, bf16[4,16,4096]{2,1,0:T(8,128)(2,1)S(1)}, u32[]{:S(2)}, u32[]{:S(2)}) collective-permute-start(bf16[4,16,4096]{2,1,0:T(8,128)(2,1)} %get-tuple-element.7), channel_id=1, source_target_pairs={{0,2},{2,4},{4,6},{6,0},{1,3},{3,5},{5,7},{7,1},{8,10},{10,12},{12... | collective-permute-start | bytes 1572872 | tf_op jit(solution)/shard_map/ppermute | solution.py:17
  30.7 1.1 collective-permute-start.6
  32.2 2.5 %collective-permute-start.11 = (bf16[4,16,4096]{2,1,0:T(8,128)(2,1)}, bf16[4,16,4096]{2,1,0:T(8,128)(2,1)}, u32[]{:S(2)}, u32[]{:S(2)}) collective-permute-start(bf16[4,16,4096]{2,1,0:T(8,128)(2,1)} %get-tuple-element.8), channel_id=1, source_target_pairs={{0,24},{8,0},{16,8},{24,16},{1,25},{9,1},{17,9},{25,17},{2,26},{10... | collective-permute-start | bytes 1572872 | tf_op jit(solution)/shard_map/ppermute | solution.py:17
  35.2 1.2 %pad_maximum_fusion.3 = bf16[32,2,16,640]{3,2,1,0:T(8,128)(2,1)} fusion(bf16[32,2,16,128]{3,2,1,0:T(8,128)(2,1)S(1)} %broadcast_in_dim.29, bf16[32,2,16,512]{3,2,1,0:T(8,128)(2,1)S(1)} %bitcast.94), kind=kLoop, calls=%fused_computation.15 | loop fusion | flops 2621440 | bytes 2621440 | tf_op jit(solution)/shard_map/concatenate | solution.py:63
  36.4 7.4 %all-to-all-start.1 = ((bf16[32,2,16,640]{3,2,1,0:T(8,128)(2,1)}), bf16[32,2,16,640]{3,2,1,0:T(8,128)(2,1)S(1)}, u32[]{:S(2)}, u32[]{:S(2)}) async-start(bf16[32,2,16,640]{3,2,1,0:T(8,128)(2,1)} %pad_maximum_fusion.3), calls=%async_computation.1 | async-start | bytes 2621440 | tf_op jit(solution)/shard_map/all_to_all | solution.py:64
  44.0 1.5 %collective-permute-start.8 = (bf16[4,16,2048]{2,1,0:T(8,128)(2,1)S(1)}, bf16[4,16,2048]{2,1,0:T(8,128)(2,1)S(1)}, u32[]{:S(2)}, u32[]{:S(2)}) collective-permute-start(bf16[4,16,2048]{2,1,0:T(8,128)(2,1)S(1)} %slice.92), channel_id=1, source_target_pairs={{0,2},{2,4},{4,6},{6,0},{1,3},{3,5},{5,7},{7,1},{8,10},{10,12},{12... | collective-permute-start | bytes 786440 | tf_op jit(solution)/shard_map/ppermute | solution.py:17
  45.5 1.4 %collective-permute-start.9 = (bf16[4,16,2048]{2,1,0:T(8,128)(2,1)S(1)}, bf16[4,16,2048]{2,1,0:T(8,128)(2,1)S(1)}, u32[]{:S(2)}, u32[]{:S(2)}) collective-permute-start(bf16[4,16,2048]{2,1,0:T(8,128)(2,1)S(1)} %slice.93), channel_id=1, source_target_pairs={{0,6},{2,0},{4,2},{6,4},{1,7},{3,1},{5,3},{7,5},{8,14},{10,8},{12,... | collective-permute-start | bytes 786440 | tf_op jit(solution)/shard_map/ppermute | solution.py:17
  46.8 1.3 %fusion.34 = (bf16[1,4,16,4096]{3,2,1,0:T(8,128)(2,1)S(1)}, bf16[1,4,16,4096]{3,2,1,0:T(8,128)(2,1)S(1)}) fusion(bf16[2,4,16,4096]{3,2,1,0:T(8,128)(2,1)} %collective-permute-done.10), kind=kLoop, calls=%fused_computation.97 | loop fusion | bytes 2097152 | tf_op jit(solution)/shard_map/slice | solution.py:76
  48.1 1.0 slice.96
  49.1 1.5 %collective-permute-start.14 = (bf16[4,16,2048]{2,1,0:T(8,128)(2,1)S(1)}, bf16[4,16,2048]{2,1,0:T(8,128)(2,1)S(1)}, u32[]{:S(2)}, u32[]{:S(2)}) collective-permute-start(bf16[4,16,2048]{2,1,0:T(8,128)(2,1)S(1)} %slice.96), channel_id=1, source_target_pairs={{0,8},{8,16},{16,24},{24,0},{1,9},{9,17},{17,25},{25,1},{2,10},{10... | collective-permute-start | bytes 786440 | tf_op jit(solution)/shard_map/ppermute | solution.py:17
  50.6 1.0 slice.97
  51.6 1.4 %collective-permute-start.15 = (bf16[4,16,2048]{2,1,0:T(8,128)(2,1)S(1)}, bf16[4,16,2048]{2,1,0:T(8,128)(2,1)S(1)}, u32[]{:S(2)}, u32[]{:S(2)}) collective-permute-start(bf16[4,16,2048]{2,1,0:T(8,128)(2,1)S(1)} %slice.97), channel_id=1, source_target_pairs={{0,24},{8,0},{16,8},{24,16},{1,25},{9,1},{17,9},{25,17},{2,26},{10... | collective-permute-start | bytes 786440 | tf_op jit(solution)/shard_map/ppermute | solution.py:17
  53.0 14.0 %collective-permute-done.8 = bf16[4,16,2048]{2,1,0:T(8,128)(2,1)S(1)} collective-permute-done((bf16[4,16,2048]{2,1,0:T(8,128)(2,1)S(1)}, bf16[4,16,2048]{2,1,0:T(8,128)(2,1)S(1)}, u32[]{:S(2)}, u32[]{:S(2)}) %collective-permute-start.8) | collective-permute-done | bytes 262176 | tf_op jit(solution)/shard_map/ppermute | solution.py:17
  67.1 1.1 %pad_maximum_fusion.5 = bf16[2,4,16,4096]{3,2,1,0:T(8,128)(2,1)} fusion(bf16[1,4,16,4096]{3,2,1,0:T(8,128)(2,1)S(1)} %maximum_bitcast_fusion.8, bf16[1,4,16,4096]{3,2,1,0:T(8,128)(2,1)S(1)} %maximum_bitcast_fusion.7), kind=kLoop, calls=%fused_computation.18 | loop fusion | flops 524288 | bytes 2097152 | tf_op jit(solution)/shard_map/stack | solution.py:70
  69.1 4.4 %maximum_bitcast_fusion = (bf16[1,4,4,16,4096]{4,3,2,1,0:T(8,128)(2,1)}, bf16[4,4,16,4096]{3,2,1,0:T(8,128)(2,1)}, bf16[1,4,4,16,4096]{4,3,2,1,0:T(8,128)(2,1)}) fusion(bf16[1,4,16,4096]{3,2,1,0:T(8,128)(2,1)S(1)} %bitcast.105, bf16[1,4,16,4096]{3,2,1,0:T(8,128)(2,1)S(1)} %maximum_bitcast_fusion.7, bf16[1,4,16,4096]{3,2,1,0:T(8,128)(2,1)S(1)} %bitcast.106, ...), kind=kLoop, calls=%fused_computation.6 | loop fusion | flops 9437184 | bytes 10485760 | tf_op jit(solution)/shard_map/stack | solution.py:78
  78.4 1.3 %fusion.35 = (bf16[1,4,16,4096]{3,2,1,0:T(8,128)(2,1)S(1)}, bf16[1,4,16,4096]{3,2,1,0:T(8,128)(2,1)S(1)}) fusion(bf16[2,4,16,4096]{3,2,1,0:T(8,128)(2,1)} %collective-permute-done.16), kind=kLoop, calls=%fused_computation.98 | loop fusion | bytes 2097152 | tf_op jit(solution)/shard_map/slice | solution.py:76
  79.7 1.7 %fusion.32 = (bf16[1,4,16,4096]{3,2,1,0:T(8,128)(2,1)S(1)}, bf16[1,4,16,4096]{3,2,1,0:T(8,128)(2,1)S(1)}, bf16[1,4,16,4096]{3,2,1,0:T(8,128)(2,1)S(1)}, bf16[1,4,16,4096]{3,2,1,0:T(8,128)(2,1)S(1)}) fusion(bf16[4,4,16,4096]{3,2,1,0:T(8,128)(2,1)} %collective-permute-done.13), kind=kLoop, calls=%fused_computation.95 | loop fusion | bytes 4194304 | tf_op jit(solution)/shard_map/slice | solution.py:76
  81.9 1.0 copy-done
  83.5 1.1 %pad_maximum_fusion = bf16[4,4,4,16,4096]{4,3,2,1,0:T(8,128)(2,1)S(1)} fusion(bf16[1,4,4,16,4096]{4,3,2,1,0:T(8,128)(2,1)S(1)} %get-tuple-element.50, bf16[1,4,4,16,4096]{4,3,2,1,0:T(8,128)(2,1)S(1)} %copy-done.1, bf16[1,4,4,16,4096]{4,3,2,1,0:T(8,128)(2,1)S(1)} %get-tuple-element.49, bf16[1,4,4,16,4096]{4,3,2,1,0:T(8,128)(2,1)S(1)} %copy-done), kind=kLoop, calls=%fused_computation | loop fusion | flops 12582912 | bytes 16777216 | tf_op jit(solution)/shard_map/stack | solution.py:78
  84.6 11.3 %convert_bitcast_fusion = bf16[2,4096,512]{2,1,0:T(8,128)(2,1)} fusion(bf16[1024,4096,1]{1,0,2:T(8,128)(2,1)S(1)} %bitcast.87, bf16[1024,1,512]{2,0,1:T(8,128)(2,1)S(1)} %maximum_bitcast_fusion.6, bf16[1024,1,512]{2,0,1:T(8,128)(2,1)S(1)} %maximum_bitcast_fusion.5), kind=kOutput, calls=%fused_computation.1 | convolution fusion | flops 8598323200 | bytes 18874368 | tf_op jit(solution)/shard_map/dot_general | solution.py:110
  96.0 11.3 %convert_bitcast_fusion.1 = bf16[2,4096,512]{2,1,0:T(8,128)(2,1)} fusion(bf16[1024,4096,1]{1,0,2:T(8,128)(2,1)S(1)} %bitcast.88, bf16[1024,1,512]{2,0,1:T(8,128)(2,1)S(1)} %maximum_bitcast_fusion.4, bf16[1024,1,512]{2,0,1:T(8,128)(2,1)S(1)} %maximum_bitcast_fusion.3), kind=kOutput, calls=%fused_computation.2 | convolution fusion | flops 8598323200 | bytes 18874368 | tf_op jit(solution)/shard_map/dot_general | solution.py:109
  (94 shorter events, 9.2 us)
Async XLA Ops:
  0.6 18.3 %copy-start.7 = (bf16[16,4096]{1,0:T(8,128)(2,1)S(1)}, bf16[16,4096]{1,0:T(8,128)(2,1)}, u32[]{:S(2)}) copy-start(bf16[16,4096]{1,0:T(8,128)(2,1)} %param.7) | copy-start | bytes 393220
  0.6 20.1 %copy-start.6 = (bf16[16,4096]{1,0:T(8,128)(2,1)S(1)}, bf16[16,4096]{1,0:T(8,128)(2,1)}, u32[]{:S(2)}) copy-start(bf16[16,4096]{1,0:T(8,128)(2,1)} %param.8) | copy-start | bytes 393220
  0.7 14.9 %copy-start.11 = (s32[16]{0:T(128)S(1)}, s32[16]{0:T(128)}, u32[]{:S(2)}) copy-start(s32[16]{0:T(128)} %param.9) | copy-start | bytes 196
  0.7 14.9 %copy-start.12 = (s32[16]{0:T(128)S(1)}, s32[16]{0:T(128)}, u32[]{:S(2)}) copy-start(s32[16]{0:T(128)} %param.10) | copy-start | bytes 196
  0.7 14.9 %copy-start.8 = (f32[2]{0:T(128)S(1)}, f32[2]{0:T(128)}, u32[]{:S(2)}) copy-start(f32[2]{0:T(128)} %param.13) | copy-start | bytes 28
  0.7 20.9 %collective-permute-start = (bf16[16,4096]{1,0:T(8,128)(2,1)}, bf16[16,4096]{1,0:T(8,128)(2,1)S(1)}, u32[]{:S(2)}, u32[]{:S(2)}) collective-permute-start(bf16[16,4096]{1,0:T(8,128)(2,1)} %param.7), channel_id=1, source_target_pairs={{0,24},{8,0},{16,8},{24,16},{1,25},{9,1},{17,9},{25,17},{2,26},{10... | collective-permute-start | bytes 393224 | tf_op jit(solution)/shard_map/ppermute | solution.py:17
  4.1 17.6 %collective-permute-start.2 = (bf16[16,4096]{1,0:T(8,128)(2,1)}, bf16[16,4096]{1,0:T(8,128)(2,1)S(1)}, u32[]{:S(2)}, u32[]{:S(2)}) collective-permute-start(bf16[16,4096]{1,0:T(8,128)(2,1)} %param.7), channel_id=1, source_target_pairs={{0,8},{8,16},{16,24},{24,0},{1,9},{9,17},{17,25},{25,1},{2,10},{10... | collective-permute-start | bytes 393224 | tf_op jit(solution)/shard_map/ppermute | solution.py:17
  4.1 14.8 %collective-permute-start.3 = (bf16[16,4096]{1,0:T(8,128)(2,1)}, bf16[16,4096]{1,0:T(8,128)(2,1)S(1)}, u32[]{:S(2)}, u32[]{:S(2)}) collective-permute-start(bf16[16,4096]{1,0:T(8,128)(2,1)} %param.8), channel_id=1, source_target_pairs={{0,6},{2,0},{4,2},{6,4},{1,7},{3,1},{5,3},{7,5},{8,14},{10,8},{12,... | collective-permute-start | bytes 393224 | tf_op jit(solution)/shard_map/ppermute | solution.py:17
  6.8 13.9 %collective-permute-start.5 = (bf16[16,4096]{1,0:T(8,128)(2,1)}, bf16[16,4096]{1,0:T(8,128)(2,1)S(1)}, u32[]{:S(2)}, u32[]{:S(2)}) collective-permute-start(bf16[16,4096]{1,0:T(8,128)(2,1)} %param.8), channel_id=1, source_target_pairs={{0,2},{2,4},{4,6},{6,0},{1,3},{3,5},{5,7},{7,1},{8,10},{10,12},{12... | collective-permute-start | bytes 393224 | tf_op jit(solution)/shard_map/ppermute | solution.py:17
  6.8 13.9 %collective-permute-start.4 = (bf16[16,4096]{1,0:T(8,128)(2,1)}, bf16[16,4096]{1,0:T(8,128)(2,1)S(1)}, u32[]{:S(2)}, u32[]{:S(2)}) collective-permute-start(bf16[16,4096]{1,0:T(8,128)(2,1)} %param.8), channel_id=1, source_target_pairs={{0,4},{2,6},{4,0},{6,2},{1,5},{3,7},{5,1},{7,3},{8,12},{10,14},{12... | collective-permute-start | bytes 393224 | tf_op jit(solution)/shard_map/ppermute | solution.py:17
  10.5 18.1 %all-to-all-start = ((bf16[4,2,16,4096]{3,2,1,0:T(8,128)(2,1)}), bf16[4,2,16,4096]{3,2,1,0:T(8,128)(2,1)S(1)}, u32[]{:S(2)}, u32[]{:S(2)}) async-start(bf16[4,2,16,4096]{3,2,1,0:T(8,128)(2,1)} %broadcast_in_dim.28), calls=%async_computation | async-start | bytes 2097152 | tf_op jit(solution)/shard_map/all_to_all | solution.py:53
  18.9 5.4 %collective-permute-start.1 = (bf16[16,4096]{1,0:T(8,128)(2,1)S(1)}, bf16[16,4096]{1,0:T(8,128)(2,1)S(1)}, u32[]{:S(2)}, u32[]{:S(2)}) collective-permute-start(bf16[16,4096]{1,0:T(8,128)(2,1)S(1)} %copy-done.7), channel_id=1, source_target_pairs={{0,16},{8,24},{16,0},{24,8},{1,17},{9,25},{17,1},{25,9},{2,18},{10... | collective-permute-start | bytes 393224 | tf_op jit(solution)/shard_map/ppermute | solution.py:17
  25.3 21.5 %collective-permute-start.10 = (bf16[2,4,16,4096]{3,2,1,0:T(8,128)(2,1)S(1)}, bf16[2,4,16,4096]{3,2,1,0:T(8,128)(2,1)}, u32[]{:S(2)}, u32[]{:S(2)}) collective-permute-start(bf16[2,4,16,4096]{3,2,1,0:T(8,128)(2,1)S(1)} %pad_maximum_fusion.4), channel_id=1, source_target_pairs={{0,1},{1,0},{2,3},{3,2},{4,5},{5,4},{6,7},{7,6},{8,9},{9,8},{10,11... | collective-permute-start | bytes 3145736 | tf_op jit(solution)/shard_map/ppermute | solution.py:58
  29.0 14.9 %collective-permute-start.7 = (bf16[4,16,4096]{2,1,0:T(8,128)(2,1)}, bf16[4,16,4096]{2,1,0:T(8,128)(2,1)S(1)}, u32[]{:S(2)}, u32[]{:S(2)}) collective-permute-start(bf16[4,16,4096]{2,1,0:T(8,128)(2,1)} %get-tuple-element.7), channel_id=1, source_target_pairs={{0,2},{2,4},{4,6},{6,0},{1,3},{3,5},{5,7},{7,1},{8,10},{10,12},{12... | collective-permute-start | bytes 1572872 | tf_op jit(solution)/shard_map/ppermute | solution.py:17
  30.7 14.7 %collective-permute-start.6 = (bf16[4,16,4096]{2,1,0:T(8,128)(2,1)}, bf16[4,16,4096]{2,1,0:T(8,128)(2,1)S(1)}, u32[]{:S(2)}, u32[]{:S(2)}) collective-permute-start(bf16[4,16,4096]{2,1,0:T(8,128)(2,1)} %get-tuple-element.7), channel_id=1, source_target_pairs={{0,6},{2,0},{4,2},{6,4},{1,7},{3,1},{5,3},{7,5},{8,14},{10,8},{12,... | collective-permute-start | bytes 1572872 | tf_op jit(solution)/shard_map/ppermute | solution.py:17
  31.8 16.3 %collective-permute-start.12 = (bf16[4,16,4096]{2,1,0:T(8,128)(2,1)}, bf16[4,16,4096]{2,1,0:T(8,128)(2,1)}, u32[]{:S(2)}, u32[]{:S(2)}) collective-permute-start(bf16[4,16,4096]{2,1,0:T(8,128)(2,1)} %get-tuple-element.8), channel_id=1, source_target_pairs={{0,8},{8,16},{16,24},{24,0},{1,9},{9,17},{17,25},{25,1},{2,10},{10... | collective-permute-start | bytes 1572872 | tf_op jit(solution)/shard_map/ppermute | solution.py:17
  32.2 18.4 %collective-permute-start.11 = (bf16[4,16,4096]{2,1,0:T(8,128)(2,1)}, bf16[4,16,4096]{2,1,0:T(8,128)(2,1)}, u32[]{:S(2)}, u32[]{:S(2)}) collective-permute-start(bf16[4,16,4096]{2,1,0:T(8,128)(2,1)} %get-tuple-element.8), channel_id=1, source_target_pairs={{0,24},{8,0},{16,8},{24,16},{1,25},{9,1},{17,9},{25,17},{2,26},{10... | collective-permute-start | bytes 1572872 | tf_op jit(solution)/shard_map/ppermute | solution.py:17
  36.4 37.1 %all-to-all-start.1 = ((bf16[32,2,16,640]{3,2,1,0:T(8,128)(2,1)}), bf16[32,2,16,640]{3,2,1,0:T(8,128)(2,1)S(1)}, u32[]{:S(2)}, u32[]{:S(2)}) async-start(bf16[32,2,16,640]{3,2,1,0:T(8,128)(2,1)} %pad_maximum_fusion.3), calls=%async_computation.1 | async-start | bytes 2621440 | tf_op jit(solution)/shard_map/all_to_all | solution.py:64
  43.9 2.9 %copy-start.2 = (bf16[4,16,4096]{2,1,0:T(8,128)(2,1)}, bf16[4,16,4096]{2,1,0:T(8,128)(2,1)S(1)}, u32[]{:S(2)}) copy-start(bf16[4,16,4096]{2,1,0:T(8,128)(2,1)S(1)} %collective-permute-done.7) | copy-start | bytes 1572868
  44.0 23.0 %collective-permute-start.8 = (bf16[4,16,2048]{2,1,0:T(8,128)(2,1)S(1)}, bf16[4,16,2048]{2,1,0:T(8,128)(2,1)S(1)}, u32[]{:S(2)}, u32[]{:S(2)}) collective-permute-start(bf16[4,16,2048]{2,1,0:T(8,128)(2,1)S(1)} %slice.92), channel_id=1, source_target_pairs={{0,2},{2,4},{4,6},{6,0},{1,3},{3,5},{5,7},{7,1},{8,10},{10,12},{12... | collective-permute-start | bytes 786440 | tf_op jit(solution)/shard_map/ppermute | solution.py:17
  45.4 1.4 %copy-start.4 = (bf16[4,16,4096]{2,1,0:T(8,128)(2,1)}, bf16[4,16,4096]{2,1,0:T(8,128)(2,1)S(1)}, u32[]{:S(2)}) copy-start(bf16[4,16,4096]{2,1,0:T(8,128)(2,1)S(1)} %collective-permute-done.6) | copy-start | bytes 1572868
  45.5 21.5 %collective-permute-start.9 = (bf16[4,16,2048]{2,1,0:T(8,128)(2,1)S(1)}, bf16[4,16,2048]{2,1,0:T(8,128)(2,1)S(1)}, u32[]{:S(2)}, u32[]{:S(2)}) collective-permute-start(bf16[4,16,2048]{2,1,0:T(8,128)(2,1)S(1)} %slice.93), channel_id=1, source_target_pairs={{0,6},{2,0},{4,2},{6,4},{1,7},{3,1},{5,3},{7,5},{8,14},{10,8},{12,... | collective-permute-start | bytes 786440 | tf_op jit(solution)/shard_map/ppermute | solution.py:17
  49.1 18.0 %collective-permute-start.14 = (bf16[4,16,2048]{2,1,0:T(8,128)(2,1)S(1)}, bf16[4,16,2048]{2,1,0:T(8,128)(2,1)S(1)}, u32[]{:S(2)}, u32[]{:S(2)}) collective-permute-start(bf16[4,16,2048]{2,1,0:T(8,128)(2,1)S(1)} %slice.96), channel_id=1, source_target_pairs={{0,8},{8,16},{16,24},{24,0},{1,9},{9,17},{17,25},{25,1},{2,10},{10... | collective-permute-start | bytes 786440 | tf_op jit(solution)/shard_map/ppermute | solution.py:17
  51.6 17.5 %copy-start.3 = (bf16[4,16,4096]{2,1,0:T(8,128)(2,1)S(1)}, bf16[4,16,4096]{2,1,0:T(8,128)(2,1)}, u32[]{:S(2)}) copy-start(bf16[4,16,4096]{2,1,0:T(8,128)(2,1)} %copy-done.2) | copy-start | bytes 1572868
  51.6 17.5 %copy-start.5 = (bf16[4,16,4096]{2,1,0:T(8,128)(2,1)S(1)}, bf16[4,16,4096]{2,1,0:T(8,128)(2,1)}, u32[]{:S(2)}) copy-start(bf16[4,16,4096]{2,1,0:T(8,128)(2,1)} %copy-done.4) | copy-start | bytes 1572868
  51.6 15.5 %collective-permute-start.15 = (bf16[4,16,2048]{2,1,0:T(8,128)(2,1)S(1)}, bf16[4,16,2048]{2,1,0:T(8,128)(2,1)S(1)}, u32[]{:S(2)}, u32[]{:S(2)}) collective-permute-start(bf16[4,16,2048]{2,1,0:T(8,128)(2,1)S(1)} %slice.97), channel_id=1, source_target_pairs={{0,24},{8,0},{16,8},{24,16},{1,25},{9,1},{17,9},{25,17},{2,26},{10... | collective-permute-start | bytes 786440 | tf_op jit(solution)/shard_map/ppermute | solution.py:17
  68.2 10.1 %collective-permute-start.16 = (bf16[2,4,16,4096]{3,2,1,0:T(8,128)(2,1)}, bf16[2,4,16,4096]{3,2,1,0:T(8,128)(2,1)}, u32[]{:S(2)}, u32[]{:S(2)}) collective-permute-start(bf16[2,4,16,4096]{3,2,1,0:T(8,128)(2,1)} %pad_maximum_fusion.5), channel_id=1, source_target_pairs={{0,1},{1,0},{2,3},{3,2},{4,5},{5,4},{6,7},{7,6},{8,9},{9,8},{10,11... | collective-permute-start | bytes 3145736 | tf_op jit(solution)/shard_map/ppermute | solution.py:71
  73.5 6.2 %collective-permute-start.13 = (bf16[4,4,16,4096]{3,2,1,0:T(8,128)(2,1)}, bf16[4,4,16,4096]{3,2,1,0:T(8,128)(2,1)}, u32[]{:S(2)}, u32[]{:S(2)}) collective-permute-start(bf16[4,4,16,4096]{3,2,1,0:T(8,128)(2,1)} %get-tuple-element.23), channel_id=1, source_target_pairs={{0,1},{1,0},{2,3},{3,2},{4,5},{5,4},{6,7},{7,6},{8,9},{9,8},{10,11... | collective-permute-start | bytes 6291464 | tf_op jit(solution)/shard_map/ppermute | solution.py:69
  73.6 0.7 copy-start.9
  73.6 0.7 copy-start.10
  81.3 1.6 %copy-start = (bf16[1,4,4,16,4096]{4,3,2,1,0:T(8,128)(2,1)S(1)}, bf16[1,4,4,16,4096]{4,3,2,1,0:T(8,128)(2,1)}, u32[]{:S(2)}) copy-start(bf16[1,4,4,16,4096]{4,3,2,1,0:T(8,128)(2,1)} %get-tuple-element.22) | copy-start | bytes 6291460
  81.3 2.2 %copy-start.1 = (bf16[1,4,4,16,4096]{4,3,2,1,0:T(8,128)(2,1)S(1)}, bf16[1,4,4,16,4096]{4,3,2,1,0:T(8,128)(2,1)}, u32[]{:S(2)}) copy-start(bf16[1,4,4,16,4096]{4,3,2,1,0:T(8,128)(2,1)} %get-tuple-element.24) | copy-start | bytes 6291460

commit v16 on v15

--- a/solution.py
+++ b/solution.py
@@ -18,12 +18,12 @@
 
 
 def ring_gather(block, axis):
-    half = block.shape[-1] // 2
+    half = block.shape[0] // 2
     from_minus = shift(block, axis, 1)
     from_plus = shift(block, axis, -1)
-    far_first = shift(from_minus[..., :half], axis, 1)
-    far_second = shift(from_plus[..., half:], axis, -1)
-    far = jnp.concatenate([far_first, far_second], axis=-1)
+    far_first = shift(from_minus[:half], axis, 1)
+    far_second = shift(from_plus[half:], axis, -1)
+    far = jnp.concatenate([far_first, far_second], axis=0)
     return from_plus, far, from_minus
 
 

time: 108 us -> 108 us (level)
  no operation moved by 1% of the time
where the time goes in v16:
time: 108 us; the launch traced here: 107 us
  starting transfers between devices  37.6 us (35%)
  matrix products  22.6 us (21%)
  waiting for transfers between devices  16.8 us (16%)
  other arithmetic  14.9 us (14%)
  local copies, waits for them, and re-layouts  11.5 us (11%)
  between operations  3.8 us (4%)
    ppermute x14, starting transfers between devices, shift(): lax.ppermute(value, axis, [(i, (i + step) % size) for i in range(size)])  21 us
    ppermute x14, waiting for transfers between devices, shift(): lax.ppermute(value, axis, [(i, (i + step) % size) for i in range(size)])  16.8 us
    dot_general x1, matrix products, on_device(): lax.dot_general(left, jnp.stack(right_imag, axis=1), dims, preferred_elem...  11.3 us
    dot_general x1, matrix products, on_device(): lax.dot_general(left, jnp.stack(right_real, axis=1), dims, preferred_elem...  11.3 us
    all_to_all x1, starting transfers between devices, on_device(): lax.all_to_all(payload, cols, split_axis=0, concat_axis=0, tiled=True)  7.42 us
    another operation x3, other arithmetic, on_device(): left = jnp.stack(parts).reshape(2 * pairs, local_g)  6.02 us
    all_to_all x1, starting transfers between devices, on_device(): spread = lax.all_to_all(copies, 'row', 0, 0, tiled=True)  5.03 us
    ppermute x1, starting transfers between devices, on_device(): first_other = lax.ppermute(first, 'core', CORE_PAIRS)  3.3 us
  transfers between devices with their start and end apart: 19, of which 3 were waited for; matrix products, arithmetic and copies ran while one was open for 20% of the time, Pallas kernels for 0%

profile of v16, /device:TPU:1, one launch (start us, length us, event | category | flops | bytes accessed | tf_op | source)
XLA Modules:
  0.0 107.3 jit_solution(9036653773300651158)
XLA Ops:
  0.7 3.4 %collective-permute-start = (bf16[16,4096]{1,0:T(8,128)(2,1)}, bf16[16,4096]{1,0:T(8,128)(2,1)S(1)}, u32[]{:S(2)}, u32[]{:S(2)}) collective-permute-start(bf16[16,4096]{1,0:T(8,128)(2,1)} %param.7), channel_id=1, source_target_pairs={{0,24},{8,0},{16,8},{24,16},{1,25},{9,1},{17,9},{25,17},{2,26},{10... | collective-permute-start | bytes 393224 | tf_op jit(solution)/shard_map/ppermute | solution.py:17
  4.1 2.7 %collective-permute-start.3 = (bf16[16,4096]{1,0:T(8,128)(2,1)}, bf16[16,4096]{1,0:T(8,128)(2,1)S(1)}, u32[]{:S(2)}, u32[]{:S(2)}) collective-permute-start(bf16[16,4096]{1,0:T(8,128)(2,1)} %param.8), channel_id=1, source_target_pairs={{0,6},{2,0},{4,2},{6,4},{1,7},{3,1},{5,3},{7,5},{8,14},{10,8},{12,... | collective-permute-start | bytes 393224 | tf_op jit(solution)/shard_map/ppermute | solution.py:17
  6.8 1.6 %collective-permute-start.4 = (bf16[16,4096]{1,0:T(8,128)(2,1)}, bf16[16,4096]{1,0:T(8,128)(2,1)S(1)}, u32[]{:S(2)}, u32[]{:S(2)}) collective-permute-start(bf16[16,4096]{1,0:T(8,128)(2,1)} %param.8), channel_id=1, source_target_pairs={{0,4},{2,6},{4,0},{6,2},{1,5},{3,7},{5,1},{7,3},{8,12},{10,14},{12... | collective-permute-start | bytes 393224 | tf_op jit(solution)/shard_map/ppermute | solution.py:17
  8.4 1.0 pad_maximum_fusion.8
  9.4 1.1 %broadcast_in_dim.28 = bf16[4,2,16,4096]{3,2,1,0:T(8,128)(2,1)} broadcast(bf16[2,16,4096]{2,1,0:T(8,128)(2,1)S(1)} %pad_maximum_fusion.8), dimensions={1,2,3} | broadcast | bytes 1310720 | tf_op jit(solution)/shard_map/broadcast_in_dim | solution.py:52
  10.5 5.0 %all-to-all-start = ((bf16[4,2,16,4096]{3,2,1,0:T(8,128)(2,1)}), bf16[4,2,16,4096]{3,2,1,0:T(8,128)(2,1)S(1)}, u32[]{:S(2)}, u32[]{:S(2)}) async-start(bf16[4,2,16,4096]{3,2,1,0:T(8,128)(2,1)} %broadcast_in_dim.28), calls=%async_computation | async-start | bytes 2097152 | tf_op jit(solution)/shard_map/all_to_all | solution.py:53
  18.9 1.8 %collective-permute-start.1 = (bf16[16,4096]{1,0:T(8,128)(2,1)S(1)}, bf16[16,4096]{1,0:T(8,128)(2,1)S(1)}, u32[]{:S(2)}, u32[]{:S(2)}) collective-permute-start(bf16[16,4096]{1,0:T(8,128)(2,1)S(1)} %copy-done.7), channel_id=1, source_target_pairs={{0,16},{8,24},{16,0},{24,8},{1,17},{9,25},{17,1},{25,9},{2,18},{10... | collective-permute-start | bytes 393224 | tf_op jit(solution)/shard_map/ppermute | solution.py:17
  20.7 0.9 fusion.29
  21.6 2.7 %collective-permute-done.1 = bf16[16,4096]{1,0:T(8,128)(2,1)S(1)} collective-permute-done((bf16[16,4096]{1,0:T(8,128)(2,1)S(1)}, bf16[16,4096]{1,0:T(8,128)(2,1)S(1)}, u32[]{:S(2)}, u32[]{:S(2)}) %collective-permute-start.1) | collective-permute-done | bytes 131104 | tf_op jit(solution)/shard_map/ppermute | solution.py:17
  24.3 0.9 fusion.30
  25.3 3.3 %collective-permute-start.10 = (bf16[2,4,16,4096]{3,2,1,0:T(8,128)(2,1)S(1)}, bf16[2,4,16,4096]{3,2,1,0:T(8,128)(2,1)}, u32[]{:S(2)}, u32[]{:S(2)}) collective-permute-start(bf16[2,4,16,4096]{3,2,1,0:T(8,128)(2,1)S(1)} %pad_maximum_fusion.4), channel_id=1, source_target_pairs={{0,1},{1,0},{2,3},{3,2},{4,5},{5,4},{6,7},{7,6},{8,9},{9,8},{10,11... | collective-permute-start | bytes 3145736 | tf_op jit(solution)/shard_map/ppermute | solution.py:58
  29.0 1.7 %collective-permute-start.7 = (bf16[4,16,4096]{2,1,0:T(8,128)(2,1)}, bf16[4,16,4096]{2,1,0:T(8,128)(2,1)S(1)}, u32[]{:S(2)}, u32[]{:S(2)}) collective-permute-start(bf16[4,16,4096]{2,1,0:T(8,128)(2,1)} %get-tuple-element.7), channel_id=1, source_target_pairs={{0,2},{2,4},{4,6},{6,0},{1,3},{3,5},{5,7},{7,1},{8,10},{10,12},{12... | collective-permute-start | bytes 1572872 | tf_op jit(solution)/shard_map/ppermute | solution.py:17
  30.7 1.1 collective-permute-start.6
  32.2 2.5 %collective-permute-start.11 = (bf16[4,16,4096]{2,1,0:T(8,128)(2,1)}, bf16[4,16,4096]{2,1,0:T(8,128)(2,1)}, u32[]{:S(2)}, u32[]{:S(2)}) collective-permute-start(bf16[4,16,4096]{2,1,0:T(8,128)(2,1)} %get-tuple-element.8), channel_id=1, source_target_pairs={{0,24},{8,0},{16,8},{24,16},{1,25},{9,1},{17,9},{25,17},{2,26},{10... | collective-permute-start | bytes 1572872 | tf_op jit(solution)/shard_map/ppermute | solution.py:17
  35.2 1.2 %pad_maximum_fusion.3 = bf16[32,2,16,640]{3,2,1,0:T(8,128)(2,1)} fusion(bf16[32,2,16,128]{3,2,1,0:T(8,128)(2,1)S(1)} %broadcast_in_dim.29, bf16[32,2,16,512]{3,2,1,0:T(8,128)(2,1)S(1)} %bitcast.94), kind=kLoop, calls=%fused_computation.15 | loop fusion | flops 2621440 | bytes 2621440 | tf_op jit(solution)/shard_map/concatenate | solution.py:63
  36.4 7.4 %all-to-all-start.1 = ((bf16[32,2,16,640]{3,2,1,0:T(8,128)(2,1)}), bf16[32,2,16,640]{3,2,1,0:T(8,128)(2,1)S(1)}, u32[]{:S(2)}, u32[]{:S(2)}) async-start(bf16[32,2,16,640]{3,2,1,0:T(8,128)(2,1)} %pad_maximum_fusion.3), calls=%async_computation.1 | async-start | bytes 2621440 | tf_op jit(solution)/shard_map/all_to_all | solution.py:64
  44.0 1.5 %collective-permute-start.8 = (bf16[2,16,4096]{2,1,0:T(8,128)(2,1)S(1)}, bf16[2,16,4096]{2,1,0:T(8,128)(2,1)S(1)}, u32[]{:S(2)}, u32[]{:S(2)}) collective-permute-start(bf16[2,16,4096]{2,1,0:T(8,128)(2,1)S(1)} %slice.92), channel_id=1, source_target_pairs={{0,2},{2,4},{4,6},{6,0},{1,3},{3,5},{5,7},{7,1},{8,10},{10,12},{12... | collective-permute-start | bytes 786440 | tf_op jit(solution)/shard_map/ppermute | solution.py:17
  45.5 1.4 %collective-permute-start.9 = (bf16[2,16,4096]{2,1,0:T(8,128)(2,1)S(1)}, bf16[2,16,4096]{2,1,0:T(8,128)(2,1)S(1)}, u32[]{:S(2)}, u32[]{:S(2)}) collective-permute-start(bf16[2,16,4096]{2,1,0:T(8,128)(2,1)S(1)} %slice.93), channel_id=1, source_target_pairs={{0,6},{2,0},{4,2},{6,4},{1,7},{3,1},{5,3},{7,5},{8,14},{10,8},{12,... | collective-permute-start | bytes 786440 | tf_op jit(solution)/shard_map/ppermute | solution.py:17
  46.8 1.3 %fusion.34 = (bf16[1,4,16,4096]{3,2,1,0:T(8,128)(2,1)S(1)}, bf16[1,4,16,4096]{3,2,1,0:T(8,128)(2,1)S(1)}) fusion(bf16[2,4,16,4096]{3,2,1,0:T(8,128)(2,1)} %collective-permute-done.10), kind=kLoop, calls=%fused_computation.97 | loop fusion | bytes 2097152 | tf_op jit(solution)/shard_map/slice | solution.py:76
  48.1 1.0 slice.96
  49.1 1.5 %collective-permute-start.14 = (bf16[2,16,4096]{2,1,0:T(8,128)(2,1)S(1)}, bf16[2,16,4096]{2,1,0:T(8,128)(2,1)S(1)}, u32[]{:S(2)}, u32[]{:S(2)}) collective-permute-start(bf16[2,16,4096]{2,1,0:T(8,128)(2,1)S(1)} %slice.96), channel_id=1, source_target_pairs={{0,8},{8,16},{16,24},{24,0},{1,9},{9,17},{17,25},{25,1},{2,10},{10... | collective-permute-start | bytes 786440 | tf_op jit(solution)/shard_map/ppermute | solution.py:17
  50.6 1.0 slice.97
  51.6 1.4 %collective-permute-start.15 = (bf16[2,16,4096]{2,1,0:T(8,128)(2,1)S(1)}, bf16[2,16,4096]{2,1,0:T(8,128)(2,1)S(1)}, u32[]{:S(2)}, u32[]{:S(2)}) collective-permute-start(bf16[2,16,4096]{2,1,0:T(8,128)(2,1)S(1)} %slice.97), channel_id=1, source_target_pairs={{0,24},{8,0},{16,8},{24,16},{1,25},{9,1},{17,9},{25,17},{2,26},{10... | collective-permute-start | bytes 786440 | tf_op jit(solution)/shard_map/ppermute | solution.py:17
  53.0 14.0 %collective-permute-done.8 = bf16[2,16,4096]{2,1,0:T(8,128)(2,1)S(1)} collective-permute-done((bf16[2,16,4096]{2,1,0:T(8,128)(2,1)S(1)}, bf16[2,16,4096]{2,1,0:T(8,128)(2,1)S(1)}, u32[]{:S(2)}, u32[]{:S(2)}) %collective-permute-start.8) | collective-permute-done | bytes 262176 | tf_op jit(solution)/shard_map/ppermute | solution.py:17
  67.2 1.1 %pad_maximum_fusion.5 = bf16[2,4,16,4096]{3,2,1,0:T(8,128)(2,1)} fusion(bf16[1,4,16,4096]{3,2,1,0:T(8,128)(2,1)S(1)} %maximum_bitcast_fusion.8, bf16[1,4,16,4096]{3,2,1,0:T(8,128)(2,1)S(1)} %maximum_bitcast_fusion.7), kind=kLoop, calls=%fused_computation.18 | loop fusion | flops 524288 | bytes 2097152 | tf_op jit(solution)/shard_map/stack | solution.py:70
  69.1 4.4 %maximum_bitcast_fusion = (bf16[1,4,4,16,4096]{4,3,2,1,0:T(8,128)(2,1)}, bf16[4,4,16,4096]{3,2,1,0:T(8,128)(2,1)}, bf16[1,4,4,16,4096]{4,3,2,1,0:T(8,128)(2,1)}) fusion(bf16[1,4,16,4096]{3,2,1,0:T(8,128)(2,1)S(1)} %bitcast.105, bf16[1,4,16,4096]{3,2,1,0:T(8,128)(2,1)S(1)} %maximum_bitcast_fusion.7, bf16[1,4,16,4096]{3,2,1,0:T(8,128)(2,1)S(1)} %bitcast.106, ...), kind=kLoop, calls=%fused_computation.6 | loop fusion | flops 9437184 | bytes 10485760 | tf_op jit(solution)/shard_map/stack | solution.py:78
  78.4 1.3 %fusion.35 = (bf16[1,4,16,4096]{3,2,1,0:T(8,128)(2,1)S(1)}, bf16[1,4,16,4096]{3,2,1,0:T(8,128)(2,1)S(1)}) fusion(bf16[2,4,16,4096]{3,2,1,0:T(8,128)(2,1)} %collective-permute-done.16), kind=kLoop, calls=%fused_computation.98 | loop fusion | bytes 2097152 | tf_op jit(solution)/shard_map/slice | solution.py:76
  79.7 1.7 %fusion.32 = (bf16[1,4,16,4096]{3,2,1,0:T(8,128)(2,1)S(1)}, bf16[1,4,16,4096]{3,2,1,0:T(8,128)(2,1)S(1)}, bf16[1,4,16,4096]{3,2,1,0:T(8,128)(2,1)S(1)}, bf16[1,4,16,4096]{3,2,1,0:T(8,128)(2,1)S(1)}) fusion(bf16[4,4,16,4096]{3,2,1,0:T(8,128)(2,1)} %collective-permute-done.13), kind=kLoop, calls=%fused_computation.95 | loop fusion | bytes 4194304 | tf_op jit(solution)/shard_map/slice | solution.py:76
  81.9 1.0 copy-done
  83.6 1.1 %pad_maximum_fusion = bf16[4,4,4,16,4096]{4,3,2,1,0:T(8,128)(2,1)S(1)} fusion(bf16[1,4,4,16,4096]{4,3,2,1,0:T(8,128)(2,1)S(1)} %get-tuple-element.50, bf16[1,4,4,16,4096]{4,3,2,1,0:T(8,128)(2,1)S(1)} %copy-done.1, bf16[1,4,4,16,4096]{4,3,2,1,0:T(8,128)(2,1)S(1)} %get-tuple-element.49, bf16[1,4,4,16,4096]{4,3,2,1,0:T(8,128)(2,1)S(1)} %copy-done), kind=kLoop, calls=%fused_computation | loop fusion | flops 12582912 | bytes 16777216 | tf_op jit(solution)/shard_map/stack | solution.py:78
  84.7 11.3 %convert_bitcast_fusion = bf16[2,4096,512]{2,1,0:T(8,128)(2,1)} fusion(bf16[1024,4096,1]{1,0,2:T(8,128)(2,1)S(1)} %bitcast.87, bf16[1024,1,512]{2,0,1:T(8,128)(2,1)S(1)} %maximum_bitcast_fusion.6, bf16[1024,1,512]{2,0,1:T(8,128)(2,1)S(1)} %maximum_bitcast_fusion.5), kind=kOutput, calls=%fused_computation.1 | convolution fusion | flops 8598323200 | bytes 18874368 | tf_op jit(solution)/shard_map/dot_general | solution.py:110
  96.0 11.3 %convert_bitcast_fusion.1 = bf16[2,4096,512]{2,1,0:T(8,128)(2,1)} fusion(bf16[1024,4096,1]{1,0,2:T(8,128)(2,1)S(1)} %bitcast.88, bf16[1024,1,512]{2,0,1:T(8,128)(2,1)S(1)} %maximum_bitcast_fusion.4, bf16[1024,1,512]{2,0,1:T(8,128)(2,1)S(1)} %maximum_bitcast_fusion.3), kind=kOutput, calls=%fused_computation.2 | convolution fusion | flops 8598323200 | bytes 18874368 | tf_op jit(solution)/shard_map/dot_general | solution.py:109
  (94 shorter events, 9.2 us)
Async XLA Ops:
  0.6 18.3 %copy-start.7 = (bf16[16,4096]{1,0:T(8,128)(2,1)S(1)}, bf16[16,4096]{1,0:T(8,128)(2,1)}, u32[]{:S(2)}) copy-start(bf16[16,4096]{1,0:T(8,128)(2,1)} %param.7) | copy-start | bytes 393220
  0.6 20.1 %copy-start.6 = (bf16[16,4096]{1,0:T(8,128)(2,1)S(1)}, bf16[16,4096]{1,0:T(8,128)(2,1)}, u32[]{:S(2)}) copy-start(bf16[16,4096]{1,0:T(8,128)(2,1)} %param.8) | copy-start | bytes 393220
  0.7 14.9 %copy-start.11 = (s32[16]{0:T(128)S(1)}, s32[16]{0:T(128)}, u32[]{:S(2)}) copy-start(s32[16]{0:T(128)} %param.9) | copy-start | bytes 196
  0.7 14.9 %copy-start.12 = (s32[16]{0:T(128)S(1)}, s32[16]{0:T(128)}, u32[]{:S(2)}) copy-start(s32[16]{0:T(128)} %param.10) | copy-start | bytes 196
  0.7 14.9 %copy-start.8 = (f32[2]{0:T(128)S(1)}, f32[2]{0:T(128)}, u32[]{:S(2)}) copy-start(f32[2]{0:T(128)} %param.13) | copy-start | bytes 28
  0.7 20.9 %collective-permute-start = (bf16[16,4096]{1,0:T(8,128)(2,1)}, bf16[16,4096]{1,0:T(8,128)(2,1)S(1)}, u32[]{:S(2)}, u32[]{:S(2)}) collective-permute-start(bf16[16,4096]{1,0:T(8,128)(2,1)} %param.7), channel_id=1, source_target_pairs={{0,24},{8,0},{16,8},{24,16},{1,25},{9,1},{17,9},{25,17},{2,26},{10... | collective-permute-start | bytes 393224 | tf_op jit(solution)/shard_map/ppermute | solution.py:17
  4.1 17.6 %collective-permute-start.2 = (bf16[16,4096]{1,0:T(8,128)(2,1)}, bf16[16,4096]{1,0:T(8,128)(2,1)S(1)}, u32[]{:S(2)}, u32[]{:S(2)}) collective-permute-start(bf16[16,4096]{1,0:T(8,128)(2,1)} %param.7), channel_id=1, source_target_pairs={{0,8},{8,16},{16,24},{24,0},{1,9},{9,17},{17,25},{25,1},{2,10},{10... | collective-permute-start | bytes 393224 | tf_op jit(solution)/shard_map/ppermute | solution.py:17
  4.1 14.8 %collective-permute-start.3 = (bf16[16,4096]{1,0:T(8,128)(2,1)}, bf16[16,4096]{1,0:T(8,128)(2,1)S(1)}, u32[]{:S(2)}, u32[]{:S(2)}) collective-permute-start(bf16[16,4096]{1,0:T(8,128)(2,1)} %param.8), channel_id=1, source_target_pairs={{0,6},{2,0},{4,2},{6,4},{1,7},{3,1},{5,3},{7,5},{8,14},{10,8},{12,... | collective-permute-start | bytes 393224 | tf_op jit(solution)/shard_map/ppermute | solution.py:17
  6.8 13.9 %collective-permute-start.5 = (bf16[16,4096]{1,0:T(8,128)(2,1)}, bf16[16,4096]{1,0:T(8,128)(2,1)S(1)}, u32[]{:S(2)}, u32[]{:S(2)}) collective-permute-start(bf16[16,4096]{1,0:T(8,128)(2,1)} %param.8), channel_id=1, source_target_pairs={{0,2},{2,4},{4,6},{6,0},{1,3},{3,5},{5,7},{7,1},{8,10},{10,12},{12... | collective-permute-start | bytes 393224 | tf_op jit(solution)/shard_map/ppermute | solution.py:17
  6.8 13.9 %collective-permute-start.4 = (bf16[16,4096]{1,0:T(8,128)(2,1)}, bf16[16,4096]{1,0:T(8,128)(2,1)S(1)}, u32[]{:S(2)}, u32[]{:S(2)}) collective-permute-start(bf16[16,4096]{1,0:T(8,128)(2,1)} %param.8), channel_id=1, source_target_pairs={{0,4},{2,6},{4,0},{6,2},{1,5},{3,7},{5,1},{7,3},{8,12},{10,14},{12... | collective-permute-start | bytes 393224 | tf_op jit(solution)/shard_map/ppermute | solution.py:17
  10.5 18.1 %all-to-all-start = ((bf16[4,2,16,4096]{3,2,1,0:T(8,128)(2,1)}), bf16[4,2,16,4096]{3,2,1,0:T(8,128)(2,1)S(1)}, u32[]{:S(2)}, u32[]{:S(2)}) async-start(bf16[4,2,16,4096]{3,2,1,0:T(8,128)(2,1)} %broadcast_in_dim.28), calls=%async_computation | async-start | bytes 2097152 | tf_op jit(solution)/shard_map/all_to_all | solution.py:53
  18.9 5.4 %collective-permute-start.1 = (bf16[16,4096]{1,0:T(8,128)(2,1)S(1)}, bf16[16,4096]{1,0:T(8,128)(2,1)S(1)}, u32[]{:S(2)}, u32[]{:S(2)}) collective-permute-start(bf16[16,4096]{1,0:T(8,128)(2,1)S(1)} %copy-done.7), channel_id=1, source_target_pairs={{0,16},{8,24},{16,0},{24,8},{1,17},{9,25},{17,1},{25,9},{2,18},{10... | collective-permute-start | bytes 393224 | tf_op jit(solution)/shard_map/ppermute | solution.py:17
  25.3 21.5 %collective-permute-start.10 = (bf16[2,4,16,4096]{3,2,1,0:T(8,128)(2,1)S(1)}, bf16[2,4,16,4096]{3,2,1,0:T(8,128)(2,1)}, u32[]{:S(2)}, u32[]{:S(2)}) collective-permute-start(bf16[2,4,16,4096]{3,2,1,0:T(8,128)(2,1)S(1)} %pad_maximum_fusion.4), channel_id=1, source_target_pairs={{0,1},{1,0},{2,3},{3,2},{4,5},{5,4},{6,7},{7,6},{8,9},{9,8},{10,11... | collective-permute-start | bytes 3145736 | tf_op jit(solution)/shard_map/ppermute | solution.py:58
  29.0 14.9 %collective-permute-start.7 = (bf16[4,16,4096]{2,1,0:T(8,128)(2,1)}, bf16[4,16,4096]{2,1,0:T(8,128)(2,1)S(1)}, u32[]{:S(2)}, u32[]{:S(2)}) collective-permute-start(bf16[4,16,4096]{2,1,0:T(8,128)(2,1)} %get-tuple-element.7), channel_id=1, source_target_pairs={{0,2},{2,4},{4,6},{6,0},{1,3},{3,5},{5,7},{7,1},{8,10},{10,12},{12... | collective-permute-start | bytes 1572872 | tf_op jit(solution)/shard_map/ppermute | solution.py:17
  30.7 14.7 %collective-permute-start.6 = (bf16[4,16,4096]{2,1,0:T(8,128)(2,1)}, bf16[4,16,4096]{2,1,0:T(8,128)(2,1)S(1)}, u32[]{:S(2)}, u32[]{:S(2)}) collective-permute-start(bf16[4,16,4096]{2,1,0:T(8,128)(2,1)} %get-tuple-element.7), channel_id=1, source_target_pairs={{0,6},{2,0},{4,2},{6,4},{1,7},{3,1},{5,3},{7,5},{8,14},{10,8},{12,... | collective-permute-start | bytes 1572872 | tf_op jit(solution)/shard_map/ppermute | solution.py:17
  31.8 16.3 %collective-permute-start.12 = (bf16[4,16,4096]{2,1,0:T(8,128)(2,1)}, bf16[4,16,4096]{2,1,0:T(8,128)(2,1)}, u32[]{:S(2)}, u32[]{:S(2)}) collective-permute-start(bf16[4,16,4096]{2,1,0:T(8,128)(2,1)} %get-tuple-element.8), channel_id=1, source_target_pairs={{0,8},{8,16},{16,24},{24,0},{1,9},{9,17},{17,25},{25,1},{2,10},{10... | collective-permute-start | bytes 1572872 | tf_op jit(solution)/shard_map/ppermute | solution.py:17
  32.2 18.4 %collective-permute-start.11 = (bf16[4,16,4096]{2,1,0:T(8,128)(2,1)}, bf16[4,16,4096]{2,1,0:T(8,128)(2,1)}, u32[]{:S(2)}, u32[]{:S(2)}) collective-permute-start(bf16[4,16,4096]{2,1,0:T(8,128)(2,1)} %get-tuple-element.8), channel_id=1, source_target_pairs={{0,24},{8,0},{16,8},{24,16},{1,25},{9,1},{17,9},{25,17},{2,26},{10... | collective-permute-start | bytes 1572872 | tf_op jit(solution)/shard_map/ppermute | solution.py:17
  36.4 37.1 %all-to-all-start.1 = ((bf16[32,2,16,640]{3,2,1,0:T(8,128)(2,1)}), bf16[32,2,16,640]{3,2,1,0:T(8,128)(2,1)S(1)}, u32[]{:S(2)}, u32[]{:S(2)}) async-start(bf16[32,2,16,640]{3,2,1,0:T(8,128)(2,1)} %pad_maximum_fusion.3), calls=%async_computation.1 | async-start | bytes 2621440 | tf_op jit(solution)/shard_map/all_to_all | solution.py:64
  43.9 2.9 %copy-start.2 = (bf16[4,16,4096]{2,1,0:T(8,128)(2,1)}, bf16[4,16,4096]{2,1,0:T(8,128)(2,1)S(1)}, u32[]{:S(2)}) copy-start(bf16[4,16,4096]{2,1,0:T(8,128)(2,1)S(1)} %collective-permute-done.7) | copy-start | bytes 1572868
  44.0 23.0 %collective-permute-start.8 = (bf16[2,16,4096]{2,1,0:T(8,128)(2,1)S(1)}, bf16[2,16,4096]{2,1,0:T(8,128)(2,1)S(1)}, u32[]{:S(2)}, u32[]{:S(2)}) collective-permute-start(bf16[2,16,4096]{2,1,0:T(8,128)(2,1)S(1)} %slice.92), channel_id=1, source_target_pairs={{0,2},{2,4},{4,6},{6,0},{1,3},{3,5},{5,7},{7,1},{8,10},{10,12},{12... | collective-permute-start | bytes 786440 | tf_op jit(solution)/shard_map/ppermute | solution.py:17
  45.4 1.4 %copy-start.4 = (bf16[4,16,4096]{2,1,0:T(8,128)(2,1)}, bf16[4,16,4096]{2,1,0:T(8,128)(2,1)S(1)}, u32[]{:S(2)}) copy-start(bf16[4,16,4096]{2,1,0:T(8,128)(2,1)S(1)} %collective-permute-done.6) | copy-start | bytes 1572868
  45.5 21.5 %collective-permute-start.9 = (bf16[2,16,4096]{2,1,0:T(8,128)(2,1)S(1)}, bf16[2,16,4096]{2,1,0:T(8,128)(2,1)S(1)}, u32[]{:S(2)}, u32[]{:S(2)}) collective-permute-start(bf16[2,16,4096]{2,1,0:T(8,128)(2,1)S(1)} %slice.93), channel_id=1, source_target_pairs={{0,6},{2,0},{4,2},{6,4},{1,7},{3,1},{5,3},{7,5},{8,14},{10,8},{12,... | collective-permute-start | bytes 786440 | tf_op jit(solution)/shard_map/ppermute | solution.py:17
  49.1 18.0 %collective-permute-start.14 = (bf16[2,16,4096]{2,1,0:T(8,128)(2,1)S(1)}, bf16[2,16,4096]{2,1,0:T(8,128)(2,1)S(1)}, u32[]{:S(2)}, u32[]{:S(2)}) collective-permute-start(bf16[2,16,4096]{2,1,0:T(8,128)(2,1)S(1)} %slice.96), channel_id=1, source_target_pairs={{0,8},{8,16},{16,24},{24,0},{1,9},{9,17},{17,25},{25,1},{2,10},{10... | collective-permute-start | bytes 786440 | tf_op jit(solution)/shard_map/ppermute | solution.py:17
  51.6 17.6 %copy-start.3 = (bf16[4,16,4096]{2,1,0:T(8,128)(2,1)S(1)}, bf16[4,16,4096]{2,1,0:T(8,128)(2,1)}, u32[]{:S(2)}) copy-start(bf16[4,16,4096]{2,1,0:T(8,128)(2,1)} %copy-done.2) | copy-start | bytes 1572868
  51.6 17.5 %copy-start.5 = (bf16[4,16,4096]{2,1,0:T(8,128)(2,1)S(1)}, bf16[4,16,4096]{2,1,0:T(8,128)(2,1)}, u32[]{:S(2)}) copy-start(bf16[4,16,4096]{2,1,0:T(8,128)(2,1)} %copy-done.4) | copy-start | bytes 1572868
  51.6 15.5 %collective-permute-start.15 = (bf16[2,16,4096]{2,1,0:T(8,128)(2,1)S(1)}, bf16[2,16,4096]{2,1,0:T(8,128)(2,1)S(1)}, u32[]{:S(2)}, u32[]{:S(2)}) collective-permute-start(bf16[2,16,4096]{2,1,0:T(8,128)(2,1)S(1)} %slice.97), channel_id=1, source_target_pairs={{0,24},{8,0},{16,8},{24,16},{1,25},{9,1},{17,9},{25,17},{2,26},{10... | collective-permute-start | bytes 786440 | tf_op jit(solution)/shard_map/ppermute | solution.py:17
  68.2 10.1 %collective-permute-start.16 = (bf16[2,4,16,4096]{3,2,1,0:T(8,128)(2,1)}, bf16[2,4,16,4096]{3,2,1,0:T(8,128)(2,1)}, u32[]{:S(2)}, u32[]{:S(2)}) collective-permute-start(bf16[2,4,16,4096]{3,2,1,0:T(8,128)(2,1)} %pad_maximum_fusion.5), channel_id=1, source_target_pairs={{0,1},{1,0},{2,3},{3,2},{4,5},{5,4},{6,7},{7,6},{8,9},{9,8},{10,11... | collective-permute-start | bytes 3145736 | tf_op jit(solution)/shard_map/ppermute | solution.py:71
  73.5 6.2 %collective-permute-start.13 = (bf16[4,4,16,4096]{3,2,1,0:T(8,128)(2,1)}, bf16[4,4,16,4096]{3,2,1,0:T(8,128)(2,1)}, u32[]{:S(2)}, u32[]{:S(2)}) collective-permute-start(bf16[4,4,16,4096]{3,2,1,0:T(8,128)(2,1)} %get-tuple-element.23), channel_id=1, source_target_pairs={{0,1},{1,0},{2,3},{3,2},{4,5},{5,4},{6,7},{7,6},{8,9},{9,8},{10,11... | collective-permute-start | bytes 6291464 | tf_op jit(solution)/shard_map/ppermute | solution.py:69
  73.6 0.7 copy-start.9
  73.6 0.7 copy-start.10
  81.3 1.6 %copy-start = (bf16[1,4,4,16,4096]{4,3,2,1,0:T(8,128)(2,1)S(1)}, bf16[1,4,4,16,4096]{4,3,2,1,0:T(8,128)(2,1)}, u32[]{:S(2)}) copy-start(bf16[1,4,4,16,4096]{4,3,2,1,0:T(8,128)(2,1)} %get-tuple-element.22) | copy-start | bytes 6291460
  81.3 2.2 %copy-start.1 = (bf16[1,4,4,16,4096]{4,3,2,1,0:T(8,128)(2,1)S(1)}, bf16[1,4,4,16,4096]{4,3,2,1,0:T(8,128)(2,1)}, u32[]{:S(2)}) copy-start(bf16[1,4,4,16,4096]{4,3,2,1,0:T(8,128)(2,1)} %get-tuple-element.24) | copy-start | bytes 6291460

commit v17 on v15

--- a/solution.py
+++ b/solution.py
@@ -69,13 +69,11 @@
     near_other = lax.ppermute(near, "core", CORE_PAIRS)
     far = jnp.stack([real_far, imag_far])
     far_other = lax.ppermute(far, "core", CORE_PAIRS)
-    parts = []
+    pieces = []
     for part in range(2):
         for src_first, src_near, src_far in ((first, near, far), (first_other, near_other, far_other)):
-            parts.append(
-                jnp.stack([src_first[part], src_near[2 * part], src_far[part], src_near[2 * part + 1]])
-            )
-    left = jnp.stack(parts).reshape(2 * pairs, local_g)
+            pieces.extend([src_first[part], src_near[2 * part], src_far[part], src_near[2 * part + 1]])
+    left = jnp.stack(pieces).reshape(2 * pairs, local_g)
 
     all_bands = column[:, :, width].astype(jnp.int32)
     gap = lookup(all_bands[1], conduction_energy) - lookup(all_bands[0], valence_energy)

time: 108 us -> 128 us (1.19)
  local copies, waits for them, and re-layouts: 11.5 us -> 28.5 us
  matrix products: 22.6 us -> 29.1 us
  waiting for transfers between devices: 16.8 us -> 11.6 us
  other arithmetic: 14.9 us -> 16.4 us
    unnamed x27 -> x34, local copies, waits for them, and re-layouts: 2.16 us -> 20.8 us
    ppermute x14, waiting for transfers between devices: 16.8 us -> 11.6 us  [shift(): lax.ppermute(value, axis, [(i, (i + step) % size) for i in range(size)])]
    slice x4 -> x0, local copies, waits for them, and re-layouts: 4.28 us -> none  [the longest x1 1.65 us: on_device(): src_near[2 * part]]
    dot_general x1, matrix products: 11.3 us -> 14.6 us  [on_device(): lax.dot_general(left, jnp.stack(right_real, axis=1), dims, preferred_elem...]
    dot_general x1, matrix products: 11.3 us -> 14.6 us  [on_device(): lax.dot_general(left, jnp.stack(right_imag, axis=1), dims, preferred_elem...]
    another operation x3 -> x1, other arithmetic: 6.02 us -> 2.78 us  [on_device(): near = jnp.stack([real_plus, real_minus, imag_plus, imag_minus])]
    ppermute x1, starting transfers between devices: 0.01 us -> 2.02 us  [on_device(): near_other = lax.ppermute(near, 'core', CORE_PAIRS)]
    another operation x0 -> x1, local copies, waits for them, and re-layouts: none -> 1.93 us  [on_device(): left = jnp.stack(pieces).reshape(2 * pairs, local_g)]
  transfers between devices with their start and end apart: 19 -> 19, of which waited for: 3 -> 3; matrix products, arithmetic and copies ran while one was open for 20% -> 24% of each run, Pallas kernels for 0% -> 0%
where the time goes in v17:
time: 128 us; the launch traced here: 127 us
  starting transfers between devices  37.5 us (29%)
  matrix products  29.1 us (23%)
  local copies, waits for them, and re-layouts  28.5 us (22%)
  other arithmetic  16.4 us (13%)
  waiting for transfers between devices  11.6 us (9%)
  between operations  3.75 us (3%)
    ppermute x14, starting transfers between devices, shift(): lax.ppermute(value, axis, [(i, (i + step) % size) for i in range(size)])  21 us
    unnamed x34, local copies, waits for them, and re-layouts  20.8 us
    dot_general x1, matrix products, on_device(): lax.dot_general(left, jnp.stack(right_real, axis=1), dims, preferred_elem...  14.6 us
    dot_general x1, matrix products, on_device(): lax.dot_general(left, jnp.stack(right_imag, axis=1), dims, preferred_elem...  14.6 us
    ppermute x14, waiting for transfers between devices, shift(): lax.ppermute(value, axis, [(i, (i + step) % size) for i in range(size)])  11.6 us
    all_to_all x1, starting transfers between devices, on_device(): lax.all_to_all(payload, cols, split_axis=0, concat_axis=0, tiled=True)  5.53 us
    all_to_all x1, starting transfers between devices, on_device(): spread = lax.all_to_all(copies, 'row', 0, 0, tiled=True)  5.03 us
    another operation x3, other arithmetic, on_device(): first = jnp.stack([row_real, col_imag])  3.67 us
  transfers between devices with their start and end apart: 19, of which 3 were waited for; matrix products, arithmetic and copies ran while one was open for 24% of the time, Pallas kernels for 0%

profile of v17, /device:TPU:1, one launch (start us, length us, event | category | flops | bytes accessed | tf_op | source)
XLA Modules:
  0.0 127.0 jit_solution(9890910671423300137)
XLA Ops:
  0.6 2.1 %collective-permute-start.2 = (bf16[16,4096]{1,0:T(8,128)(2,1)}, bf16[16,4096]{1,0:T(8,128)(2,1)S(1)}, u32[]{:S(2)}, u32[]{:S(2)}) collective-permute-start(bf16[16,4096]{1,0:T(8,128)(2,1)} %param.7), channel_id=1, source_target_pairs={{0,8},{8,16},{16,24},{24,0},{1,9},{9,17},{17,25},{25,1},{2,10},{10... | collective-permute-start | bytes 393224 | tf_op jit(solution)/shard_map/ppermute | solution.py:17
  2.7 2.5 %collective-permute-start.1 = (bf16[16,4096]{1,0:T(8,128)(2,1)}, bf16[16,4096]{1,0:T(8,128)(2,1)S(1)}, u32[]{:S(2)}, u32[]{:S(2)}) collective-permute-start(bf16[16,4096]{1,0:T(8,128)(2,1)} %param.7), channel_id=1, source_target_pairs={{0,16},{8,24},{16,0},{24,8},{1,17},{9,25},{17,1},{25,9},{2,18},{10... | collective-permute-start | bytes 393224 | tf_op jit(solution)/shard_map/ppermute | solution.py:17
  5.2 1.2 collective-permute-start
  6.3 1.3 %collective-permute-start.5 = (bf16[16,4096]{1,0:T(8,128)(2,1)}, bf16[16,4096]{1,0:T(8,128)(2,1)S(1)}, u32[]{:S(2)}, u32[]{:S(2)}) collective-permute-start(bf16[16,4096]{1,0:T(8,128)(2,1)} %param.8), channel_id=1, source_target_pairs={{0,2},{2,4},{4,6},{6,0},{1,3},{3,5},{5,7},{7,1},{8,10},{10,12},{12... | collective-permute-start | bytes 393224 | tf_op jit(solution)/shard_map/ppermute | solution.py:17
  7.6 2.6 %collective-permute-start.4 = (bf16[16,4096]{1,0:T(8,128)(2,1)}, bf16[16,4096]{1,0:T(8,128)(2,1)S(1)}, u32[]{:S(2)}, u32[]{:S(2)}) collective-permute-start(bf16[16,4096]{1,0:T(8,128)(2,1)} %param.8), channel_id=1, source_target_pairs={{0,4},{2,6},{4,0},{6,2},{1,5},{3,7},{5,1},{7,3},{8,12},{10,14},{12... | collective-permute-start | bytes 393224 | tf_op jit(solution)/shard_map/ppermute | solution.py:17
  12.3 5.0 %all-to-all-start = ((bf16[4,2,16,4096]{3,2,1,0:T(8,128)(2,1)}), bf16[4,2,16,4096]{3,2,1,0:T(8,128)(2,1)S(1)}, u32[]{:S(2)}, u32[]{:S(2)}) async-start(bf16[4,2,16,4096]{3,2,1,0:T(8,128)(2,1)} %broadcast_in_dim.28), calls=%async_computation | async-start | bytes 2097152 | tf_op jit(solution)/shard_map/all_to_all | solution.py:53
  18.7 1.4 %fusion.31 = (f32[1]{0:T(128)}, f32[1]{0:T(128)}) fusion(f32[2]{0:T(128)} %param.13), kind=kLoop, calls=%fused_computation.105 | loop fusion | bytes 16 | tf_op jit(solution)/shard_map/slice | solution.py:96
  22.8 1.1 collective-permute-start.3
  23.9 1.8 %fusion.29 = (bf16[1,4,16,4096]{3,2,1,0:T(8,128)(2,1)S(1)}, bf16[4,16,4096]{2,1,0:T(8,128)(2,1)}) fusion(bf16[1,16,4096]{2,1,0:T(8,128)(2,1)S(1)} %bitcast.110, bf16[1,16,4096]{2,1,0:T(8,128)(2,1)S(1)} %bitcast.112, bf16[1,16,4096]{2,1,0:T(8,128)(2,1)S(1)} %bitcast.113, bf16[1,16,4096]{2,1,0:T(8,128)(2,1)} %bitcast.106), kind=kLoop, calls=%fused_computation.103 | loop fusion | flops 786432 | bytes 1572864 | tf_op jit(solution)/shard_map/stack | solution.py:57
  25.7 1.5 %collective-permute-done.3 = bf16[16,4096]{1,0:T(8,128)(2,1)S(1)} collective-permute-done((bf16[16,4096]{1,0:T(8,128)(2,1)}, bf16[16,4096]{1,0:T(8,128)(2,1)S(1)}, u32[]{:S(2)}, u32[]{:S(2)}) %collective-permute-start.3) | collective-permute-done | bytes 131104 | tf_op jit(solution)/shard_map/ppermute | solution.py:17
  27.2 1.8 %fusion.28 = (bf16[1,4,16,4096]{3,2,1,0:T(8,128)(2,1)S(1)}, bf16[4,16,4096]{2,1,0:T(8,128)(2,1)}) fusion(bf16[1,16,4096]{2,1,0:T(8,128)(2,1)S(1)} %bitcast.109, bf16[1,16,4096]{2,1,0:T(8,128)(2,1)S(1)} %bitcast.111, bf16[1,16,4096]{2,1,0:T(8,128)(2,1)S(1)} %bitcast.114, bf16[1,16,4096]{2,1,0:T(8,128)(2,1)} %bitcast.108), kind=kLoop, calls=%fused_computation.102 | loop fusion | flops 786432 | bytes 1572864 | tf_op jit(solution)/shard_map/stack | solution.py:57
  29.0 3.3 %collective-permute-start.10 = (bf16[2,4,16,4096]{3,2,1,0:T(8,128)(2,1)S(1)}, bf16[2,4,16,4096]{3,2,1,0:T(8,128)(2,1)}, u32[]{:S(2)}, u32[]{:S(2)}) collective-permute-start(bf16[2,4,16,4096]{3,2,1,0:T(8,128)(2,1)S(1)} %pad_maximum_fusion.2), channel_id=1, source_target_pairs={{0,1},{1,0},{2,3},{3,2},{4,5},{5,4},{6,7},{7,6},{8,9},{9,8},{10,11... | collective-permute-start | bytes 3145736 | tf_op jit(solution)/shard_map/ppermute | solution.py:58
  32.7 2.3 %collective-permute-start.6 = (bf16[4,16,4096]{2,1,0:T(8,128)(2,1)}, bf16[4,16,4096]{2,1,0:T(8,128)(2,1)}, u32[]{:S(2)}, u32[]{:S(2)}) collective-permute-start(bf16[4,16,4096]{2,1,0:T(8,128)(2,1)} %get-tuple-element.7), channel_id=1, source_target_pairs={{0,6},{2,0},{4,2},{6,4},{1,7},{3,1},{5,3},{7,5},{8,14},{10,8},{12,... | collective-permute-start | bytes 1572872 | tf_op jit(solution)/shard_map/ppermute | solution.py:17
  35.4 2.4 %collective-permute-start.11 = (bf16[4,16,4096]{2,1,0:T(8,128)(2,1)}, bf16[4,16,4096]{2,1,0:T(8,128)(2,1)S(1)}, u32[]{:S(2)}, u32[]{:S(2)}) collective-permute-start(bf16[4,16,4096]{2,1,0:T(8,128)(2,1)} %get-tuple-element.8), channel_id=1, source_target_pairs={{0,24},{8,0},{16,8},{24,16},{1,25},{9,1},{17,9},{25,17},{2,26},{10... | collective-permute-start | bytes 1572872 | tf_op jit(solution)/shard_map/ppermute | solution.py:17
  38.2 1.2 pad_maximum_fusion.1
  39.4 5.5 %all-to-all-start.1 = ((bf16[32,2,16,640]{3,2,1,0:T(8,128)(2,1)}), bf16[32,2,16,640]{3,2,1,0:T(8,128)(2,1)S(1)}, u32[]{:S(2)}, u32[]{:S(2)}) async-start(bf16[32,2,16,640]{3,2,1,0:T(8,128)(2,1)} %pad_maximum_fusion.1), calls=%async_computation.1 | async-start | bytes 2621440 | tf_op jit(solution)/shard_map/all_to_all | solution.py:64
  47.7 3.5 %collective-permute-start.9 = (bf16[4,16,2048]{2,1,0:T(8,128)(2,1)S(1)}, bf16[4,16,2048]{2,1,0:T(8,128)(2,1)S(1)}, u32[]{:S(2)}, u32[]{:S(2)}) collective-permute-start(bf16[4,16,2048]{2,1,0:T(8,128)(2,1)S(1)} %slice.93), channel_id=1, source_target_pairs={{0,6},{2,0},{4,2},{6,4},{1,7},{3,1},{5,3},{7,5},{8,14},{10,8},{12,... | collective-permute-start | bytes 786440 | tf_op jit(solution)/shard_map/ppermute | solution.py:17
  53.9 1.9 %constant_dynamic-update-slice_fusion.5 = bf16[16,4,16,4096]{3,2,1,0:T(8,128)(2,1)} fusion(bf16[16,4,16,4096]{3,2,1,0:T(8,128)(2,1)} %slice_dynamic-update-slice_fusion.9, bf16[4,16,4096]{2,1,0:T(8,128)(2,1)} %collective-permute-done.6), kind=kLoop, calls=%fused_computation.86 | loop fusion | bytes 1048576
  55.8 2.8 %pad_maximum_fusion = bf16[4,4,16,4096]{3,2,1,0:T(8,128)(2,1)} fusion(bf16[1,4,16,4096]{3,2,1,0:T(8,128)(2,1)S(1)} %bitcast.95, bf16[1,4,16,4096]{3,2,1,0:T(8,128)(2,1)S(1)} %bitcast.96, bf16[1,4,16,4096]{3,2,1,0:T(8,128)(2,1)} %bitcast.12, bf16[1,4,16,4096]{3,2,1,0:T(8,128)(2,1)} %bitcast.10), kind=kLoop, calls=%fused_computation.2 | loop fusion | flops 3145728 | bytes 4194304 | tf_op jit(solution)/shard_map/stack | solution.py:68
  58.6 9.2 %collective-permute-done.15 = bf16[4,16,2048]{2,1,0:T(8,128)(2,1)S(1)} collective-permute-done((bf16[4,16,2048]{2,1,0:T(8,128)(2,1)S(1)}, bf16[4,16,2048]{2,1,0:T(8,128)(2,1)S(1)}, u32[]{:S(2)}, u32[]{:S(2)}) %collective-permute-start.15) | collective-permute-done | bytes 262176 | tf_op jit(solution)/shard_map/ppermute | solution.py:17
  67.8 2.0 %collective-permute-start.13 = (bf16[4,4,16,4096]{3,2,1,0:T(8,128)(2,1)}, bf16[4,4,16,4096]{3,2,1,0:T(8,128)(2,1)}, u32[]{:S(2)}, u32[]{:S(2)}) collective-permute-start(bf16[4,4,16,4096]{3,2,1,0:T(8,128)(2,1)} %pad_maximum_fusion), channel_id=1, source_target_pairs={{0,1},{1,0},{2,3},{3,2},{4,5},{5,4},{6,7},{7,6},{8,9},{9,8},{10,11... | collective-permute-start | bytes 6291464 | tf_op jit(solution)/shard_map/ppermute | solution.py:69
  72.6 1.9 %constant_dynamic-update-slice_fusion.3 = bf16[16,4,16,4096]{3,2,1,0:T(8,128)(2,1)} fusion(bf16[16,4,16,4096]{3,2,1,0:T(8,128)(2,1)} %constant_dynamic-update-slice_fusion.4, bf16[4,16,4096]{2,1,0:T(8,128)(2,1)} %collective-permute-done.7), kind=kLoop, calls=%fused_computation.84 | loop fusion | bytes 1048576
  74.5 1.9 %slice_dynamic-update-slice_fusion.7 = bf16[16,4,16,4096]{3,2,1,0:T(8,128)(2,1)} fusion(bf16[16,4,16,4096]{3,2,1,0:T(8,128)(2,1)} %constant_dynamic-update-slice_fusion.3, bf16[2,4,16,4096]{3,2,1,0:T(8,128)(2,1)} %collective-permute-done.10), kind=kLoop, calls=%fused_computation.66 | loop fusion | bytes 1048576
  81.2 1.9 %slice_dynamic-update-slice_fusion.6 = bf16[16,4,16,4096]{3,2,1,0:T(8,128)(2,1)} fusion(bf16[16,4,16,4096]{3,2,1,0:T(8,128)(2,1)} %slice_dynamic-update-slice_fusion.7, bf16[4,4,16,4096]{3,2,1,0:T(8,128)(2,1)} %collective-permute-done.13), kind=kLoop, calls=%fused_computation.65 | loop fusion | bytes 1048576
  83.1 1.9 %slice_dynamic-update-slice_fusion.5 = bf16[16,4,16,4096]{3,2,1,0:T(8,128)(2,1)} fusion(bf16[16,4,16,4096]{3,2,1,0:T(8,128)(2,1)} %slice_dynamic-update-slice_fusion.6, bf16[2,4,16,4096]{3,2,1,0:T(8,128)(2,1)} %collective-permute-done.16), kind=kLoop, calls=%fused_computation.64 | loop fusion | bytes 1048576
  85.0 1.9 %slice_dynamic-update-slice_fusion.4 = bf16[16,4,16,4096]{3,2,1,0:T(8,128)(2,1)} fusion(bf16[16,4,16,4096]{3,2,1,0:T(8,128)(2,1)} %slice_dynamic-update-slice_fusion.5, bf16[4,4,16,4096]{3,2,1,0:T(8,128)(2,1)} %collective-permute-done.13), kind=kLoop, calls=%fused_computation.63 | loop fusion | bytes 1048576
  90.2 1.9 %slice_dynamic-update-slice_fusion.3 = bf16[16,4,16,4096]{3,2,1,0:T(8,128)(2,1)} fusion(bf16[16,4,16,4096]{3,2,1,0:T(8,128)(2,1)} %constant_dynamic-update-slice_fusion, bf16[2,4,16,4096]{3,2,1,0:T(8,128)(2,1)} %collective-permute-done.10), kind=kLoop, calls=%fused_computation.62 | loop fusion | bytes 1048576
  92.1 1.9 %slice_dynamic-update-slice_fusion.2 = bf16[16,4,16,4096]{3,2,1,0:T(8,128)(2,1)} fusion(bf16[16,4,16,4096]{3,2,1,0:T(8,128)(2,1)} %slice_dynamic-update-slice_fusion.3, bf16[4,4,16,4096]{3,2,1,0:T(8,128)(2,1)} %collective-permute-done.13), kind=kLoop, calls=%fused_computation.61 | loop fusion | bytes 1048576
  94.0 1.9 %slice_dynamic-update-slice_fusion.1 = bf16[16,4,16,4096]{3,2,1,0:T(8,128)(2,1)} fusion(bf16[16,4,16,4096]{3,2,1,0:T(8,128)(2,1)} %slice_dynamic-update-slice_fusion.2, bf16[2,4,16,4096]{3,2,1,0:T(8,128)(2,1)} %collective-permute-done.16), kind=kLoop, calls=%fused_computation.60 | loop fusion | bytes 1048576
  95.9 1.9 %slice_dynamic-update-slice_fusion = bf16[16,4,16,4096]{3,2,1,0:T(8,128)(2,1)} fusion(bf16[16,4,16,4096]{3,2,1,0:T(8,128)(2,1)} %slice_dynamic-update-slice_fusion.1, bf16[4,4,16,4096]{3,2,1,0:T(8,128)(2,1)} %collective-permute-done.13), kind=kLoop, calls=%fused_computation.59 | loop fusion | bytes 1048576 | tf_op jit(solution)/shard_map/stack | solution.py:76
  97.8 14.6 %convert_bitcast_fusion.1 = bf16[2,4096,512]{2,1,0:T(8,128)(2,1)} fusion(bf16[1024,4096,1]{1,0,2:T(8,128)(2,1)} %bitcast.17, bf16[1024,1,512]{2,0,1:T(8,128)(2,1)S(1)} %maximum_bitcast_fusion.1, bf16[1024,1,512]{2,0,1:T(8,128)(2,1)S(1)} %maximum_bitcast_fusion), kind=kOutput, calls=%fused_computation.1 | convolution fusion | flops 8598323200 | bytes 18874368 | tf_op jit(solution)/shard_map/dot_general | solution.py:107
  112.4 14.6 %convert_bitcast_fusion = bf16[2,4096,512]{2,1,0:T(8,128)(2,1)} fusion(bf16[1024,4096,1]{1,0,2:T(8,128)(2,1)} %bitcast.17, bf16[1024,1,512]{2,0,1:T(8,128)(2,1)S(1)} %maximum_bitcast_fusion.3, bf16[1024,1,512]{2,0,1:T(8,128)(2,1)S(1)} %maximum_bitcast_fusion.2), kind=kOutput, calls=%fused_computation | convolution fusion | flops 8598323200 | bytes 18874368 | tf_op jit(solution)/shard_map/dot_general | solution.py:108
  (98 shorter events, 20.9 us)
Async XLA Ops:
  0.6 22.1 %collective-permute-start.2 = (bf16[16,4096]{1,0:T(8,128)(2,1)}, bf16[16,4096]{1,0:T(8,128)(2,1)S(1)}, u32[]{:S(2)}, u32[]{:S(2)}) collective-permute-start(bf16[16,4096]{1,0:T(8,128)(2,1)} %param.7), channel_id=1, source_target_pairs={{0,8},{8,16},{16,24},{24,0},{1,9},{9,17},{17,25},{25,1},{2,10},{10... | collective-permute-start | bytes 393224 | tf_op jit(solution)/shard_map/ppermute | solution.py:17
  2.7 21.2 %collective-permute-start.1 = (bf16[16,4096]{1,0:T(8,128)(2,1)}, bf16[16,4096]{1,0:T(8,128)(2,1)S(1)}, u32[]{:S(2)}, u32[]{:S(2)}) collective-permute-start(bf16[16,4096]{1,0:T(8,128)(2,1)} %param.7), channel_id=1, source_target_pairs={{0,16},{8,24},{16,0},{24,8},{1,17},{9,25},{17,1},{25,9},{2,18},{10... | collective-permute-start | bytes 393224 | tf_op jit(solution)/shard_map/ppermute | solution.py:17
  5.2 18.7 %collective-permute-start = (bf16[16,4096]{1,0:T(8,128)(2,1)}, bf16[16,4096]{1,0:T(8,128)(2,1)S(1)}, u32[]{:S(2)}, u32[]{:S(2)}) collective-permute-start(bf16[16,4096]{1,0:T(8,128)(2,1)} %param.7), channel_id=1, source_target_pairs={{0,24},{8,0},{16,8},{24,16},{1,25},{9,1},{17,9},{25,17},{2,26},{10... | collective-permute-start | bytes 393224 | tf_op jit(solution)/shard_map/ppermute | solution.py:17
  6.3 19.4 %collective-permute-start.5 = (bf16[16,4096]{1,0:T(8,128)(2,1)}, bf16[16,4096]{1,0:T(8,128)(2,1)S(1)}, u32[]{:S(2)}, u32[]{:S(2)}) collective-permute-start(bf16[16,4096]{1,0:T(8,128)(2,1)} %param.8), channel_id=1, source_target_pairs={{0,2},{2,4},{4,6},{6,0},{1,3},{3,5},{5,7},{7,1},{8,10},{10,12},{12... | collective-permute-start | bytes 393224 | tf_op jit(solution)/shard_map/ppermute | solution.py:17
  7.6 18.1 %collective-permute-start.4 = (bf16[16,4096]{1,0:T(8,128)(2,1)}, bf16[16,4096]{1,0:T(8,128)(2,1)S(1)}, u32[]{:S(2)}, u32[]{:S(2)}) collective-permute-start(bf16[16,4096]{1,0:T(8,128)(2,1)} %param.8), channel_id=1, source_target_pairs={{0,4},{2,6},{4,0},{6,2},{1,5},{3,7},{5,1},{7,3},{8,12},{10,14},{12... | collective-permute-start | bytes 393224 | tf_op jit(solution)/shard_map/ppermute | solution.py:17
  12.3 20.0 %all-to-all-start = ((bf16[4,2,16,4096]{3,2,1,0:T(8,128)(2,1)}), bf16[4,2,16,4096]{3,2,1,0:T(8,128)(2,1)S(1)}, u32[]{:S(2)}, u32[]{:S(2)}) async-start(bf16[4,2,16,4096]{3,2,1,0:T(8,128)(2,1)} %broadcast_in_dim.28), calls=%async_computation | async-start | bytes 2097152 | tf_op jit(solution)/shard_map/all_to_all | solution.py:53
  22.8 4.4 %collective-permute-start.3 = (bf16[16,4096]{1,0:T(8,128)(2,1)}, bf16[16,4096]{1,0:T(8,128)(2,1)S(1)}, u32[]{:S(2)}, u32[]{:S(2)}) collective-permute-start(bf16[16,4096]{1,0:T(8,128)(2,1)} %param.8), channel_id=1, source_target_pairs={{0,6},{2,0},{4,2},{6,4},{1,7},{3,1},{5,3},{7,5},{8,14},{10,8},{12,... | collective-permute-start | bytes 393224 | tf_op jit(solution)/shard_map/ppermute | solution.py:17
  29.0 45.4 %collective-permute-start.10 = (bf16[2,4,16,4096]{3,2,1,0:T(8,128)(2,1)S(1)}, bf16[2,4,16,4096]{3,2,1,0:T(8,128)(2,1)}, u32[]{:S(2)}, u32[]{:S(2)}) collective-permute-start(bf16[2,4,16,4096]{3,2,1,0:T(8,128)(2,1)S(1)} %pad_maximum_fusion.2), channel_id=1, source_target_pairs={{0,1},{1,0},{2,3},{3,2},{4,5},{5,4},{6,7},{7,6},{8,9},{9,8},{10,11... | collective-permute-start | bytes 3145736 | tf_op jit(solution)/shard_map/ppermute | solution.py:58
  32.7 14.0 %collective-permute-start.6 = (bf16[4,16,4096]{2,1,0:T(8,128)(2,1)}, bf16[4,16,4096]{2,1,0:T(8,128)(2,1)}, u32[]{:S(2)}, u32[]{:S(2)}) collective-permute-start(bf16[4,16,4096]{2,1,0:T(8,128)(2,1)} %get-tuple-element.7), channel_id=1, source_target_pairs={{0,6},{2,0},{4,2},{6,4},{1,7},{3,1},{5,3},{7,5},{8,14},{10,8},{12,... | collective-permute-start | bytes 1572872 | tf_op jit(solution)/shard_map/ppermute | solution.py:17
  35.1 16.1 %collective-permute-start.7 = (bf16[4,16,4096]{2,1,0:T(8,128)(2,1)}, bf16[4,16,4096]{2,1,0:T(8,128)(2,1)}, u32[]{:S(2)}, u32[]{:S(2)}) collective-permute-start(bf16[4,16,4096]{2,1,0:T(8,128)(2,1)} %get-tuple-element.7), channel_id=1, source_target_pairs={{0,2},{2,4},{4,6},{6,0},{1,3},{3,5},{5,7},{7,1},{8,10},{10,12},{12... | collective-permute-start | bytes 1572872 | tf_op jit(solution)/shard_map/ppermute | solution.py:17
  35.1 18.0 %collective-permute-start.12 = (bf16[4,16,4096]{2,1,0:T(8,128)(2,1)}, bf16[4,16,4096]{2,1,0:T(8,128)(2,1)S(1)}, u32[]{:S(2)}, u32[]{:S(2)}) collective-permute-start(bf16[4,16,4096]{2,1,0:T(8,128)(2,1)} %get-tuple-element.8), channel_id=1, source_target_pairs={{0,8},{8,16},{16,24},{24,0},{1,9},{9,17},{17,25},{25,1},{2,10},{10... | collective-permute-start | bytes 1572872 | tf_op jit(solution)/shard_map/ppermute | solution.py:17
  35.4 16.8 %collective-permute-start.11 = (bf16[4,16,4096]{2,1,0:T(8,128)(2,1)}, bf16[4,16,4096]{2,1,0:T(8,128)(2,1)S(1)}, u32[]{:S(2)}, u32[]{:S(2)}) collective-permute-start(bf16[4,16,4096]{2,1,0:T(8,128)(2,1)} %get-tuple-element.8), channel_id=1, source_target_pairs={{0,24},{8,0},{16,8},{24,16},{1,25},{9,1},{17,9},{25,17},{2,26},{10... | collective-permute-start | bytes 1572872 | tf_op jit(solution)/shard_map/ppermute | solution.py:17
  39.4 37.0 %all-to-all-start.1 = ((bf16[32,2,16,640]{3,2,1,0:T(8,128)(2,1)}), bf16[32,2,16,640]{3,2,1,0:T(8,128)(2,1)S(1)}, u32[]{:S(2)}, u32[]{:S(2)}) async-start(bf16[32,2,16,640]{3,2,1,0:T(8,128)(2,1)} %pad_maximum_fusion.1), calls=%async_computation.1 | async-start | bytes 2621440 | tf_op jit(solution)/shard_map/all_to_all | solution.py:64
  47.7 22.1 %collective-permute-start.9 = (bf16[4,16,2048]{2,1,0:T(8,128)(2,1)S(1)}, bf16[4,16,2048]{2,1,0:T(8,128)(2,1)S(1)}, u32[]{:S(2)}, u32[]{:S(2)}) collective-permute-start(bf16[4,16,2048]{2,1,0:T(8,128)(2,1)S(1)} %slice.93), channel_id=1, source_target_pairs={{0,6},{2,0},{4,2},{6,4},{1,7},{3,1},{5,3},{7,5},{8,14},{10,8},{12,... | collective-permute-start | bytes 786440 | tf_op jit(solution)/shard_map/ppermute | solution.py:17
  52.2 17.7 %collective-permute-start.8 = (bf16[4,16,2048]{2,1,0:T(8,128)(2,1)S(1)}, bf16[4,16,2048]{2,1,0:T(8,128)(2,1)S(1)}, u32[]{:S(2)}, u32[]{:S(2)}) collective-permute-start(bf16[4,16,2048]{2,1,0:T(8,128)(2,1)S(1)} %slice.92), channel_id=1, source_target_pairs={{0,2},{2,4},{4,6},{6,0},{1,3},{3,5},{5,7},{7,1},{8,10},{10,12},{12... | collective-permute-start | bytes 786440 | tf_op jit(solution)/shard_map/ppermute | solution.py:17
  52.2 24.5 %copy-start.2 = (bf16[4,16,4096]{2,1,0:T(8,128)(2,1)}, bf16[4,16,4096]{2,1,0:T(8,128)(2,1)S(1)}, u32[]{:S(2)}) copy-start(bf16[4,16,4096]{2,1,0:T(8,128)(2,1)S(1)} %collective-permute-done.11) | copy-start | bytes 1572868
  52.3 15.5 %collective-permute-start.15 = (bf16[4,16,2048]{2,1,0:T(8,128)(2,1)S(1)}, bf16[4,16,2048]{2,1,0:T(8,128)(2,1)S(1)}, u32[]{:S(2)}, u32[]{:S(2)}) collective-permute-start(bf16[4,16,2048]{2,1,0:T(8,128)(2,1)S(1)} %slice.97), channel_id=1, source_target_pairs={{0,24},{8,0},{16,8},{24,16},{1,25},{9,1},{17,9},{25,17},{2,26},{10... | collective-permute-start | bytes 786440 | tf_op jit(solution)/shard_map/ppermute | solution.py:17
  53.1 23.7 %copy-start = (bf16[4,16,4096]{2,1,0:T(8,128)(2,1)}, bf16[4,16,4096]{2,1,0:T(8,128)(2,1)S(1)}, u32[]{:S(2)}) copy-start(bf16[4,16,4096]{2,1,0:T(8,128)(2,1)S(1)} %collective-permute-done.12) | copy-start | bytes 1572868
  53.1 16.7 %collective-permute-start.14 = (bf16[4,16,2048]{2,1,0:T(8,128)(2,1)S(1)}, bf16[4,16,2048]{2,1,0:T(8,128)(2,1)S(1)}, u32[]{:S(2)}, u32[]{:S(2)}) collective-permute-start(bf16[4,16,2048]{2,1,0:T(8,128)(2,1)S(1)} %slice.96), channel_id=1, source_target_pairs={{0,8},{8,16},{16,24},{24,0},{1,9},{9,17},{17,25},{25,1},{2,10},{10... | collective-permute-start | bytes 786440 | tf_op jit(solution)/shard_map/ppermute | solution.py:17
  67.8 6.7 %copy-start.4 = (bf16[4,16,2048]{2,1,0:T(8,128)(2,1)}, bf16[4,16,2048]{2,1,0:T(8,128)(2,1)S(1)}, u32[]{:S(2)}) copy-start(bf16[4,16,2048]{2,1,0:T(8,128)(2,1)S(1)} %collective-permute-done.15) | copy-start | bytes 786436
  67.8 13.4 %collective-permute-start.13 = (bf16[4,4,16,4096]{3,2,1,0:T(8,128)(2,1)}, bf16[4,4,16,4096]{3,2,1,0:T(8,128)(2,1)}, u32[]{:S(2)}, u32[]{:S(2)}) collective-permute-start(bf16[4,4,16,4096]{3,2,1,0:T(8,128)(2,1)} %pad_maximum_fusion), channel_id=1, source_target_pairs={{0,1},{1,0},{2,3},{3,2},{4,5},{5,4},{6,7},{7,6},{8,9},{9,8},{10,11... | collective-permute-start | bytes 6291464 | tf_op jit(solution)/shard_map/ppermute | solution.py:69
  69.8 4.7 %copy-start.6 = (bf16[4,16,2048]{2,1,0:T(8,128)(2,1)}, bf16[4,16,2048]{2,1,0:T(8,128)(2,1)S(1)}, u32[]{:S(2)}) copy-start(bf16[4,16,2048]{2,1,0:T(8,128)(2,1)S(1)} %collective-permute-done.14) | copy-start | bytes 786436
  69.9 7.3 %copy-start.8 = (f32[32]{0:T(128)S(1)}, f32[32]{0:T(128)}, u32[]{:S(2)}) copy-start(f32[32]{0:T(128)} %param.12) | copy-start | bytes 388
  69.9 7.4 %copy-start.9 = (f32[16]{0:T(128)S(1)}, f32[16]{0:T(128)}, u32[]{:S(2)}) copy-start(f32[16]{0:T(128)} %param.11) | copy-start | bytes 196
  71.0 12.1 %collective-permute-start.16 = (bf16[2,4,16,4096]{3,2,1,0:T(8,128)(2,1)}, bf16[2,4,16,4096]{3,2,1,0:T(8,128)(2,1)}, u32[]{:S(2)}, u32[]{:S(2)}) collective-permute-start(bf16[2,4,16,4096]{3,2,1,0:T(8,128)(2,1)} %pad_maximum_fusion.3), channel_id=1, source_target_pairs={{0,1},{1,0},{2,3},{3,2},{4,5},{5,4},{6,7},{7,6},{8,9},{9,8},{10,11... | collective-permute-start | bytes 3145736 | tf_op jit(solution)/shard_map/ppermute | solution.py:71
  80.7 7.0 %copy-start.3 = (bf16[4,16,4096]{2,1,0:T(8,128)(2,1)S(1)}, bf16[4,16,4096]{2,1,0:T(8,128)(2,1)}, u32[]{:S(2)}) copy-start(bf16[4,16,4096]{2,1,0:T(8,128)(2,1)} %copy-done.2) | copy-start | bytes 1572868
  80.7 7.8 %copy-start.5 = (bf16[4,16,2048]{2,1,0:T(8,128)(2,1)S(1)}, bf16[4,16,2048]{2,1,0:T(8,128)(2,1)}, u32[]{:S(2)}) copy-start(bf16[4,16,2048]{2,1,0:T(8,128)(2,1)} %copy-done.4) | copy-start | bytes 786436
  80.7 7.8 %copy-start.7 = (bf16[4,16,2048]{2,1,0:T(8,128)(2,1)S(1)}, bf16[4,16,2048]{2,1,0:T(8,128)(2,1)}, u32[]{:S(2)}) copy-start(bf16[4,16,2048]{2,1,0:T(8,128)(2,1)} %copy-done.6) | copy-start | bytes 786436
  80.8 8.6 %copy-start.1 = (bf16[4,16,4096]{2,1,0:T(8,128)(2,1)S(1)}, bf16[4,16,4096]{2,1,0:T(8,128)(2,1)}, u32[]{:S(2)}) copy-start(bf16[4,16,4096]{2,1,0:T(8,128)(2,1)} %copy-done) | copy-start | bytes 1572868

commit v18 on v15

--- a/solution.py
+++ b/solution.py
@@ -56,7 +56,7 @@
     col_imag = ring_direct(matrix_imag, "y")
     first = jnp.stack([row_real, col_imag])
     first_other = lax.ppermute(first, "core", CORE_PAIRS)
-    spread, row_real, col_imag, first = lax.optimization_barrier((spread, row_real, col_imag, first))
+    spread, col_imag = lax.optimization_barrier((spread, col_imag))
     payload = spread.transpose(0, 3, 1, 2, 4).reshape(ncol, 2, local_pairs, width)
     bands = jnp.stack([valence_index, conduction_index]).astype(jnp.bfloat16)
     tags = jnp.broadcast_to(bands[None, :, :, None], (ncol, 2, local_pairs, 128))

time: 108 us -> 116 us (1.074)
  waiting for transfers between devices: 16.8 us -> 23.7 us
    ppermute x14, waiting for transfers between devices: 16.8 us -> 23.7 us  [shift(): lax.ppermute(value, axis, [(i, (i + step) % size) for i in range(size)])]
    unnamed x27 -> x35, local copies, waits for them, and re-layouts: 2.16 us -> 3.77 us
    ppermute x1, starting transfers between devices: 3.3 us -> 4.63 us  [on_device(): first_other = lax.ppermute(first, 'core', CORE_PAIRS)]
    another operation x3, other arithmetic: 6.02 us -> 4.78 us  [on_device(): left = jnp.stack(parts).reshape(2 * pairs, local_g)]
  transfers between devices with their start and end apart: 19 -> 19, of which waited for: 3 -> 3; matrix products, arithmetic and copies ran while one was open for 20% -> 18% of each run, Pallas kernels for 0% -> 0%
where the time goes in v18:
time: 116 us
  starting transfers between devices  38.4 us (33%)
  waiting for transfers between devices  23.7 us (20%)
  matrix products  22.6 us (19%)
  other arithmetic  14.8 us (13%)
  local copies, waits for them, and re-layouts  12.5 us (11%)
  between operations  3.51 us (3%)
    ppermute x14, waiting for transfers between devices, shift(): lax.ppermute(value, axis, [(i, (i + step) % size) for i in range(size)])  23.7 us
    ppermute x14, starting transfers between devices, shift(): lax.ppermute(value, axis, [(i, (i + step) % size) for i in range(size)])  20.3 us
    dot_general x1, matrix products, on_device(): lax.dot_general(left, jnp.stack(right_imag, axis=1), dims, preferred_elem...  11.3 us
    dot_general x1, matrix products, on_device(): lax.dot_general(left, jnp.stack(right_real, axis=1), dims, preferred_elem...  11.3 us
    all_to_all x1, starting transfers between devices, on_device(): lax.all_to_all(payload, cols, split_axis=0, concat_axis=0, tiled=True)  7.53 us
    all_to_all x1, starting transfers between devices, on_device(): spread = lax.all_to_all(copies, 'row', 0, 0, tiled=True)  5.03 us
    another operation x3, other arithmetic, on_device(): left = jnp.stack(parts).reshape(2 * pairs, local_g)  4.78 us
    ppermute x1, starting transfers between devices, on_device(): first_other = lax.ppermute(first, 'core', CORE_PAIRS)  4.63 us
  transfers between devices with their start and end apart: 19, of which 3 were waited for; matrix products, arithmetic and copies ran while one was open for 18% of the time, Pallas kernels for 0%

profile of v18, /device:TPU:1, one launch (start us, length us, event | category | flops | bytes accessed | tf_op | source)
XLA Modules:
  0.0 115.5 jit_solution(16606198083581290647)
XLA Ops:
  0.7 3.4 %collective-permute-start = (bf16[16,4096]{1,0:T(8,128)(2,1)}, bf16[16,4096]{1,0:T(8,128)(2,1)S(1)}, u32[]{:S(2)}, u32[]{:S(2)}) collective-permute-start(bf16[16,4096]{1,0:T(8,128)(2,1)} %param.7), channel_id=1, source_target_pairs={{0,24},{8,0},{16,8},{24,16},{1,25},{9,1},{17,9},{25,17},{2,26},{10... | collective-permute-start | bytes 393224 | tf_op jit(solution)/shard_map/ppermute | solution.py:17
  4.0 1.7 %collective-permute-start.1 = (bf16[16,4096]{1,0:T(8,128)(2,1)}, bf16[16,4096]{1,0:T(8,128)(2,1)S(1)}, u32[]{:S(2)}, u32[]{:S(2)}) collective-permute-start(bf16[16,4096]{1,0:T(8,128)(2,1)} %param.7), channel_id=1, source_target_pairs={{0,16},{8,24},{16,0},{24,8},{1,17},{9,25},{17,1},{25,9},{2,18},{10... | collective-permute-start | bytes 393224 | tf_op jit(solution)/shard_map/ppermute | solution.py:17
  5.8 2.7 %collective-permute-start.7 = (bf16[16,4096]{1,0:T(8,128)(2,1)}, bf16[16,4096]{1,0:T(8,128)(2,1)S(1)}, u32[]{:S(2)}, u32[]{:S(2)}) collective-permute-start(bf16[16,4096]{1,0:T(8,128)(2,1)} %param.8), channel_id=1, source_target_pairs={{0,6},{2,0},{4,2},{6,4},{1,7},{3,1},{5,3},{7,5},{8,14},{10,8},{12,... | collective-permute-start | bytes 393224 | tf_op jit(solution)/shard_map/ppermute | solution.py:17
  8.5 1.0 pad_maximum_fusion.8
  9.5 1.1 broadcast_in_dim.28
  10.6 5.0 %all-to-all-start = ((bf16[4,2,16,4096]{3,2,1,0:T(8,128)(2,1)}), bf16[4,2,16,4096]{3,2,1,0:T(8,128)(2,1)S(1)}, u32[]{:S(2)}, u32[]{:S(2)}) async-start(bf16[4,2,16,4096]{3,2,1,0:T(8,128)(2,1)} %broadcast_in_dim.28), calls=%async_computation | async-start | bytes 2097152 | tf_op jit(solution)/shard_map/all_to_all | solution.py:53
  15.6 1.7 %collective-permute-start.8 = (bf16[16,4096]{1,0:T(8,128)(2,1)S(1)}, bf16[16,4096]{1,0:T(8,128)(2,1)S(1)}, u32[]{:S(2)}, u32[]{:S(2)}) collective-permute-start(bf16[16,4096]{1,0:T(8,128)(2,1)S(1)} %copy-done.11), channel_id=1, source_target_pairs={{0,4},{2,6},{4,0},{6,2},{1,5},{3,7},{5,1},{7,3},{8,12},{10,14},{12... | collective-permute-start | bytes 393224 | tf_op jit(solution)/shard_map/ppermute | solution.py:17
  17.5 1.1 collective-permute-start.3
  19.2 1.8 %collective-permute-done.8 = bf16[16,4096]{1,0:T(8,128)(2,1)S(1)} collective-permute-done((bf16[16,4096]{1,0:T(8,128)(2,1)S(1)}, bf16[16,4096]{1,0:T(8,128)(2,1)S(1)}, u32[]{:S(2)}, u32[]{:S(2)}) %collective-permute-start.8) | collective-permute-done | bytes 131104 | tf_op jit(solution)/shard_map/ppermute | solution.py:17
  21.0 0.9 fusion.29
  21.9 1.1 pad_maximum_fusion.4
  23.0 4.6 %collective-permute-start.10 = (bf16[2,4,16,4096]{3,2,1,0:T(8,128)(2,1)}, bf16[2,4,16,4096]{3,2,1,0:T(8,128)(2,1)}, u32[]{:S(2)}, u32[]{:S(2)}) collective-permute-start(bf16[2,4,16,4096]{3,2,1,0:T(8,128)(2,1)} %pad_maximum_fusion.4), channel_id=1, source_target_pairs={{0,1},{1,0},{2,3},{3,2},{4,5},{5,4},{6,7},{7,6},{8,9},{9,8},{10,11... | collective-permute-start | bytes 3145736 | tf_op jit(solution)/shard_map/ppermute | solution.py:58
  27.6 4.1 %collective-permute-done.3 = bf16[4,16,4096]{2,1,0:T(8,128)(2,1)S(1)} collective-permute-done((bf16[4,16,4096]{2,1,0:T(8,128)(2,1)S(1)}, bf16[4,16,4096]{2,1,0:T(8,128)(2,1)S(1)}, u32[]{:S(2)}, u32[]{:S(2)}) %collective-permute-start.3) | collective-permute-done | bytes 524320 | tf_op jit(solution)/shard_map/ppermute | solution.py:17
  33.2 3.4 %collective-permute-start.6 = (bf16[4,16,2048]{2,1,0:T(8,128)(2,1)}, bf16[4,16,2048]{2,1,0:T(8,128)(2,1)}, u32[]{:S(2)}, u32[]{:S(2)}) collective-permute-start(bf16[4,16,2048]{2,1,0:T(8,128)(2,1)} %slice.85), channel_id=1, source_target_pairs={{0,6},{2,0},{4,2},{6,4},{1,7},{3,1},{5,3},{7,5},{8,14},{10,8},{12,... | collective-permute-start | bytes 786440 | tf_op jit(solution)/shard_map/ppermute | solution.py:17
  41.5 1.6 %collective-permute-start.12 = (bf16[4,16,4096]{2,1,0:T(8,128)(2,1)}, bf16[4,16,4096]{2,1,0:T(8,128)(2,1)S(1)}, u32[]{:S(2)}, u32[]{:S(2)}) collective-permute-start(bf16[4,16,4096]{2,1,0:T(8,128)(2,1)} %get-tuple-element.4), channel_id=1, source_target_pairs={{0,8},{8,16},{16,24},{24,0},{1,9},{9,17},{17,25},{25,1},{2,10},{10... | collective-permute-start | bytes 1572872 | tf_op jit(solution)/shard_map/ppermute | solution.py:17
  43.1 1.2 collective-permute-start.11
  44.7 1.2 %pad_maximum_fusion.3 = bf16[32,2,16,640]{3,2,1,0:T(8,128)(2,1)} fusion(bf16[32,2,16,128]{3,2,1,0:T(8,128)(2,1)S(1)} %broadcast_in_dim.29, bf16[32,2,16,512]{3,2,1,0:T(8,128)(2,1)S(1)} %bitcast.94), kind=kLoop, calls=%fused_computation.15 | loop fusion | flops 2621440 | bytes 2621440 | tf_op jit(solution)/shard_map/concatenate | solution.py:63
  45.9 7.5 %all-to-all-start.1 = ((bf16[32,2,16,640]{3,2,1,0:T(8,128)(2,1)}), bf16[32,2,16,640]{3,2,1,0:T(8,128)(2,1)S(1)}, u32[]{:S(2)}, u32[]{:S(2)}) async-start(bf16[32,2,16,640]{3,2,1,0:T(8,128)(2,1)} %pad_maximum_fusion.3), calls=%async_computation.1 | async-start | bytes 2621440 | tf_op jit(solution)/shard_map/all_to_all | solution.py:64
  53.5 1.1 maximum_bitcast_fusion.7
  54.6 1.5 %collective-permute-start.14 = (bf16[4,16,2048]{2,1,0:T(8,128)(2,1)S(1)}, bf16[4,16,2048]{2,1,0:T(8,128)(2,1)S(1)}, u32[]{:S(2)}, u32[]{:S(2)}) collective-permute-start(bf16[4,16,2048]{2,1,0:T(8,128)(2,1)S(1)} %slice.88), channel_id=1, source_target_pairs={{0,8},{8,16},{16,24},{24,0},{1,9},{9,17},{17,25},{25,1},{2,10},{10... | collective-permute-start | bytes 786440 | tf_op jit(solution)/shard_map/ppermute | solution.py:17
  56.1 1.4 %collective-permute-start.15 = (bf16[4,16,2048]{2,1,0:T(8,128)(2,1)S(1)}, bf16[4,16,2048]{2,1,0:T(8,128)(2,1)S(1)}, u32[]{:S(2)}, u32[]{:S(2)}) collective-permute-start(bf16[4,16,2048]{2,1,0:T(8,128)(2,1)S(1)} %slice.89), channel_id=1, source_target_pairs={{0,24},{8,0},{16,8},{24,16},{1,25},{9,1},{17,9},{25,17},{2,26},{10... | collective-permute-start | bytes 786440 | tf_op jit(solution)/shard_map/ppermute | solution.py:17
  57.5 1.3 %fusion.33 = (bf16[1,4,16,4096]{3,2,1,0:T(8,128)(2,1)S(1)}, bf16[1,4,16,4096]{3,2,1,0:T(8,128)(2,1)S(1)}) fusion(bf16[2,4,16,4096]{3,2,1,0:T(8,128)(2,1)} %collective-permute-done.10), kind=kLoop, calls=%fused_computation.96 | loop fusion | bytes 2097152 | tf_op jit(solution)/shard_map/slice | solution.py:76
  58.8 17.9 %collective-permute-done.14 = bf16[4,16,2048]{2,1,0:T(8,128)(2,1)S(1)} collective-permute-done((bf16[4,16,2048]{2,1,0:T(8,128)(2,1)S(1)}, bf16[4,16,2048]{2,1,0:T(8,128)(2,1)S(1)}, u32[]{:S(2)}, u32[]{:S(2)}) %collective-permute-start.14) | collective-permute-done | bytes 262176 | tf_op jit(solution)/shard_map/ppermute | solution.py:17
  76.7 1.1 pad_maximum_fusion.5
  77.8 0.9 collective-permute-start.16
  78.6 3.1 %maximum_bitcast_fusion = (bf16[1,4,4,16,4096]{4,3,2,1,0:T(8,128)(2,1)}, bf16[4,4,16,4096]{3,2,1,0:T(8,128)(2,1)}, bf16[1,4,4,16,4096]{4,3,2,1,0:T(8,128)(2,1)}) fusion(bf16[1,4,16,4096]{3,2,1,0:T(8,128)(2,1)S(1)} %bitcast.106, bf16[1,4,16,4096]{3,2,1,0:T(8,128)(2,1)S(1)} %maximum_bitcast_fusion.7, bf16[1,4,16,4096]{3,2,1,0:T(8,128)(2,1)S(1)} %bitcast.105, ...), kind=kLoop, calls=%fused_computation.6 | loop fusion | flops 9437184 | bytes 10485760 | tf_op jit(solution)/shard_map/stack | solution.py:78
  86.7 1.3 %fusion.34 = (bf16[1,4,16,4096]{3,2,1,0:T(8,128)(2,1)S(1)}, bf16[1,4,16,4096]{3,2,1,0:T(8,128)(2,1)S(1)}) fusion(bf16[2,4,16,4096]{3,2,1,0:T(8,128)(2,1)} %collective-permute-done.16), kind=kLoop, calls=%fused_computation.97 | loop fusion | bytes 2097152 | tf_op jit(solution)/shard_map/slice | solution.py:76
  88.0 1.7 %fusion.32 = (bf16[1,4,16,4096]{3,2,1,0:T(8,128)(2,1)S(1)}, bf16[1,4,16,4096]{3,2,1,0:T(8,128)(2,1)S(1)}, bf16[1,4,16,4096]{3,2,1,0:T(8,128)(2,1)S(1)}, bf16[1,4,16,4096]{3,2,1,0:T(8,128)(2,1)S(1)}) fusion(bf16[4,4,16,4096]{3,2,1,0:T(8,128)(2,1)} %collective-permute-done.13), kind=kLoop, calls=%fused_computation.95 | loop fusion | bytes 4194304 | tf_op jit(solution)/shard_map/slice | solution.py:76
  90.2 1.0 copy-done
  91.8 1.1 pad_maximum_fusion
  92.9 11.3 %convert_bitcast_fusion = bf16[2,4096,512]{2,1,0:T(8,128)(2,1)} fusion(bf16[1024,4096,1]{1,0,2:T(8,128)(2,1)S(1)} %bitcast.87, bf16[1024,1,512]{2,0,1:T(8,128)(2,1)S(1)} %maximum_bitcast_fusion.6, bf16[1024,1,512]{2,0,1:T(8,128)(2,1)S(1)} %maximum_bitcast_fusion.5), kind=kOutput, calls=%fused_computation.1 | convolution fusion | flops 8598323200 | bytes 18874368 | tf_op jit(solution)/shard_map/dot_general | solution.py:110
  104.3 11.3 %convert_bitcast_fusion.1 = bf16[2,4096,512]{2,1,0:T(8,128)(2,1)} fusion(bf16[1024,4096,1]{1,0,2:T(8,128)(2,1)S(1)} %bitcast.88, bf16[1024,1,512]{2,0,1:T(8,128)(2,1)S(1)} %maximum_bitcast_fusion.4, bf16[1024,1,512]{2,0,1:T(8,128)(2,1)S(1)} %maximum_bitcast_fusion.3), kind=kOutput, calls=%fused_computation.2 | convolution fusion | flops 8598323200 | bytes 18874368 | tf_op jit(solution)/shard_map/dot_general | solution.py:109
  (101 shorter events, 11.2 us)
Async XLA Ops:
  0.6 16.7 %copy-start.10 = (bf16[16,4096]{1,0:T(8,128)(2,1)S(1)}, bf16[16,4096]{1,0:T(8,128)(2,1)}, u32[]{:S(2)}) copy-start(bf16[16,4096]{1,0:T(8,128)(2,1)} %param.7) | copy-start | bytes 393220
  0.6 15.0 %copy-start.11 = (bf16[16,4096]{1,0:T(8,128)(2,1)S(1)}, bf16[16,4096]{1,0:T(8,128)(2,1)}, u32[]{:S(2)}) copy-start(bf16[16,4096]{1,0:T(8,128)(2,1)} %param.8) | copy-start | bytes 393220
  0.7 15.0 %copy-start.15 = (s32[16]{0:T(128)S(1)}, s32[16]{0:T(128)}, u32[]{:S(2)}) copy-start(s32[16]{0:T(128)} %param.9) | copy-start | bytes 196
  0.7 15.0 %collective-permute-start = (bf16[16,4096]{1,0:T(8,128)(2,1)}, bf16[16,4096]{1,0:T(8,128)(2,1)S(1)}, u32[]{:S(2)}, u32[]{:S(2)}) collective-permute-start(bf16[16,4096]{1,0:T(8,128)(2,1)} %param.7), channel_id=1, source_target_pairs={{0,24},{8,0},{16,8},{24,16},{1,25},{9,1},{17,9},{25,17},{2,26},{10... | collective-permute-start | bytes 393224 | tf_op jit(solution)/shard_map/ppermute | solution.py:17
  4.0 13.3 %collective-permute-start.2 = (bf16[16,4096]{1,0:T(8,128)(2,1)}, bf16[16,4096]{1,0:T(8,128)(2,1)S(1)}, u32[]{:S(2)}, u32[]{:S(2)}) collective-permute-start(bf16[16,4096]{1,0:T(8,128)(2,1)} %param.7), channel_id=1, source_target_pairs={{0,8},{8,16},{16,24},{24,0},{1,9},{9,17},{17,25},{25,1},{2,10},{10... | collective-permute-start | bytes 393224 | tf_op jit(solution)/shard_map/ppermute | solution.py:17
  4.0 13.3 %collective-permute-start.1 = (bf16[16,4096]{1,0:T(8,128)(2,1)}, bf16[16,4096]{1,0:T(8,128)(2,1)S(1)}, u32[]{:S(2)}, u32[]{:S(2)}) collective-permute-start(bf16[16,4096]{1,0:T(8,128)(2,1)} %param.7), channel_id=1, source_target_pairs={{0,16},{8,24},{16,0},{24,8},{1,17},{9,25},{17,1},{25,9},{2,18},{10... | collective-permute-start | bytes 393224 | tf_op jit(solution)/shard_map/ppermute | solution.py:17
  5.8 13.5 %collective-permute-start.7 = (bf16[16,4096]{1,0:T(8,128)(2,1)}, bf16[16,4096]{1,0:T(8,128)(2,1)S(1)}, u32[]{:S(2)}, u32[]{:S(2)}) collective-permute-start(bf16[16,4096]{1,0:T(8,128)(2,1)} %param.8), channel_id=1, source_target_pairs={{0,6},{2,0},{4,2},{6,4},{1,7},{3,1},{5,3},{7,5},{8,14},{10,8},{12,... | collective-permute-start | bytes 393224 | tf_op jit(solution)/shard_map/ppermute | solution.py:17
  8.5 10.7 %collective-permute-start.9 = (bf16[16,4096]{1,0:T(8,128)(2,1)}, bf16[16,4096]{1,0:T(8,128)(2,1)S(1)}, u32[]{:S(2)}, u32[]{:S(2)}) collective-permute-start(bf16[16,4096]{1,0:T(8,128)(2,1)} %param.8), channel_id=1, source_target_pairs={{0,2},{2,4},{4,6},{6,0},{1,3},{3,5},{5,7},{7,1},{8,10},{10,12},{12... | collective-permute-start | bytes 393224 | tf_op jit(solution)/shard_map/ppermute | solution.py:17
  10.6 30.5 %all-to-all-start = ((bf16[4,2,16,4096]{3,2,1,0:T(8,128)(2,1)}), bf16[4,2,16,4096]{3,2,1,0:T(8,128)(2,1)S(1)}, u32[]{:S(2)}, u32[]{:S(2)}) async-start(bf16[4,2,16,4096]{3,2,1,0:T(8,128)(2,1)} %broadcast_in_dim.28), calls=%async_computation | async-start | bytes 2097152 | tf_op jit(solution)/shard_map/all_to_all | solution.py:53
  15.6 5.4 %collective-permute-start.8 = (bf16[16,4096]{1,0:T(8,128)(2,1)S(1)}, bf16[16,4096]{1,0:T(8,128)(2,1)S(1)}, u32[]{:S(2)}, u32[]{:S(2)}) collective-permute-start(bf16[16,4096]{1,0:T(8,128)(2,1)S(1)} %copy-done.11), channel_id=1, source_target_pairs={{0,4},{2,6},{4,0},{6,2},{1,5},{3,7},{5,1},{7,3},{8,12},{10,14},{12... | collective-permute-start | bytes 393224 | tf_op jit(solution)/shard_map/ppermute | solution.py:17
  17.5 10.2 %copy-start.16 = (s32[16]{0:T(128)S(1)}, s32[16]{0:T(128)}, u32[]{:S(2)}) copy-start(s32[16]{0:T(128)} %param.10) | copy-start | bytes 196
  17.5 14.2 %collective-permute-start.3 = (bf16[4,16,4096]{2,1,0:T(8,128)(2,1)S(1)}, bf16[4,16,4096]{2,1,0:T(8,128)(2,1)S(1)}, u32[]{:S(2)}, u32[]{:S(2)}) collective-permute-start(bf16[4,16,4096]{2,1,0:T(8,128)(2,1)S(1)} %get-tuple-element.34), channel_id=1, source_target_pairs={{0,6},{2,0},{4,2},{6,4},{1,7},{3,1},{5,3},{7,5},{8,14},{10,8},{12,... | collective-permute-start | bytes 1572872 | tf_op jit(solution)/shard_map/ppermute | solution.py:17
  18.6 18.0 %collective-permute-start.4 = (bf16[4,16,4096]{2,1,0:T(8,128)(2,1)S(1)}, bf16[4,16,4096]{2,1,0:T(8,128)(2,1)S(1)}, u32[]{:S(2)}, u32[]{:S(2)}) collective-permute-start(bf16[4,16,4096]{2,1,0:T(8,128)(2,1)S(1)} %get-tuple-element.34), channel_id=1, source_target_pairs={{0,2},{2,4},{4,6},{6,0},{1,3},{3,5},{5,7},{7,1},{8,10},{10,12},{12... | collective-permute-start | bytes 1572872 | tf_op jit(solution)/shard_map/ppermute | solution.py:17
  21.0 17.1 %copy-start.12 = (f32[2]{0:T(128)S(1)}, f32[2]{0:T(128)}, u32[]{:S(2)}) copy-start(f32[2]{0:T(128)} %param.13) | copy-start | bytes 28
  23.0 34.5 %collective-permute-start.10 = (bf16[2,4,16,4096]{3,2,1,0:T(8,128)(2,1)}, bf16[2,4,16,4096]{3,2,1,0:T(8,128)(2,1)}, u32[]{:S(2)}, u32[]{:S(2)}) collective-permute-start(bf16[2,4,16,4096]{3,2,1,0:T(8,128)(2,1)} %pad_maximum_fusion.4), channel_id=1, source_target_pairs={{0,1},{1,0},{2,3},{3,2},{4,5},{5,4},{6,7},{7,6},{8,9},{9,8},{10,11... | collective-permute-start | bytes 3145736 | tf_op jit(solution)/shard_map/ppermute | solution.py:58
  33.2 20.3 %collective-permute-start.6 = (bf16[4,16,2048]{2,1,0:T(8,128)(2,1)}, bf16[4,16,2048]{2,1,0:T(8,128)(2,1)}, u32[]{:S(2)}, u32[]{:S(2)}) collective-permute-start(bf16[4,16,2048]{2,1,0:T(8,128)(2,1)} %slice.85), channel_id=1, source_target_pairs={{0,6},{2,0},{4,2},{6,4},{1,7},{3,1},{5,3},{7,5},{8,14},{10,8},{12,... | collective-permute-start | bytes 786440 | tf_op jit(solution)/shard_map/ppermute | solution.py:17
  38.1 15.3 %collective-permute-start.5 = (bf16[4,16,2048]{2,1,0:T(8,128)(2,1)}, bf16[4,16,2048]{2,1,0:T(8,128)(2,1)}, u32[]{:S(2)}, u32[]{:S(2)}) collective-permute-start(bf16[4,16,2048]{2,1,0:T(8,128)(2,1)} %slice.84), channel_id=1, source_target_pairs={{0,2},{2,4},{4,6},{6,0},{1,3},{3,5},{5,7},{7,1},{8,10},{10,12},{12... | collective-permute-start | bytes 786440 | tf_op jit(solution)/shard_map/ppermute | solution.py:17
  41.5 13.0 %collective-permute-start.12 = (bf16[4,16,4096]{2,1,0:T(8,128)(2,1)}, bf16[4,16,4096]{2,1,0:T(8,128)(2,1)S(1)}, u32[]{:S(2)}, u32[]{:S(2)}) collective-permute-start(bf16[4,16,4096]{2,1,0:T(8,128)(2,1)} %get-tuple-element.4), channel_id=1, source_target_pairs={{0,8},{8,16},{16,24},{24,0},{1,9},{9,17},{17,25},{25,1},{2,10},{10... | collective-permute-start | bytes 1572872 | tf_op jit(solution)/shard_map/ppermute | solution.py:17
  43.1 13.0 %collective-permute-start.11 = (bf16[4,16,4096]{2,1,0:T(8,128)(2,1)}, bf16[4,16,4096]{2,1,0:T(8,128)(2,1)S(1)}, u32[]{:S(2)}, u32[]{:S(2)}) collective-permute-start(bf16[4,16,4096]{2,1,0:T(8,128)(2,1)} %get-tuple-element.4), channel_id=1, source_target_pairs={{0,24},{8,0},{16,8},{24,16},{1,25},{9,1},{17,9},{25,17},{2,26},{10... | collective-permute-start | bytes 1572872 | tf_op jit(solution)/shard_map/ppermute | solution.py:17
  45.9 35.8 %all-to-all-start.1 = ((bf16[32,2,16,640]{3,2,1,0:T(8,128)(2,1)}), bf16[32,2,16,640]{3,2,1,0:T(8,128)(2,1)S(1)}, u32[]{:S(2)}, u32[]{:S(2)}) async-start(bf16[32,2,16,640]{3,2,1,0:T(8,128)(2,1)} %pad_maximum_fusion.3), calls=%async_computation.1 | async-start | bytes 2621440 | tf_op jit(solution)/shard_map/all_to_all | solution.py:64
  54.6 2.9 %copy-start.6 = (bf16[4,16,4096]{2,1,0:T(8,128)(2,1)}, bf16[4,16,4096]{2,1,0:T(8,128)(2,1)S(1)}, u32[]{:S(2)}) copy-start(bf16[4,16,4096]{2,1,0:T(8,128)(2,1)S(1)} %collective-permute-done.12) | copy-start | bytes 1572868
  54.6 22.0 %collective-permute-start.14 = (bf16[4,16,2048]{2,1,0:T(8,128)(2,1)S(1)}, bf16[4,16,2048]{2,1,0:T(8,128)(2,1)S(1)}, u32[]{:S(2)}, u32[]{:S(2)}) collective-permute-start(bf16[4,16,2048]{2,1,0:T(8,128)(2,1)S(1)} %slice.88), channel_id=1, source_target_pairs={{0,8},{8,16},{16,24},{24,0},{1,9},{9,17},{17,25},{25,1},{2,10},{10... | collective-permute-start | bytes 786440 | tf_op jit(solution)/shard_map/ppermute | solution.py:17
  56.1 1.4 %copy-start.8 = (bf16[4,16,4096]{2,1,0:T(8,128)(2,1)}, bf16[4,16,4096]{2,1,0:T(8,128)(2,1)S(1)}, u32[]{:S(2)}) copy-start(bf16[4,16,4096]{2,1,0:T(8,128)(2,1)S(1)} %collective-permute-done.11) | copy-start | bytes 1572868
  56.1 20.5 %collective-permute-start.15 = (bf16[4,16,2048]{2,1,0:T(8,128)(2,1)S(1)}, bf16[4,16,2048]{2,1,0:T(8,128)(2,1)S(1)}, u32[]{:S(2)}, u32[]{:S(2)}) collective-permute-start(bf16[4,16,2048]{2,1,0:T(8,128)(2,1)S(1)} %slice.89), channel_id=1, source_target_pairs={{0,24},{8,0},{16,8},{24,16},{1,25},{9,1},{17,9},{25,17},{2,26},{10... | collective-permute-start | bytes 786440 | tf_op jit(solution)/shard_map/ppermute | solution.py:17
  58.7 19.9 %copy-start.3 = (bf16[4,16,4096]{2,1,0:T(8,128)(2,1)S(1)}, bf16[4,16,4096]{2,1,0:T(8,128)(2,1)}, u32[]{:S(2)}) copy-start(bf16[4,16,4096]{2,1,0:T(8,128)(2,1)} %copy-done.2) | copy-start | bytes 1572868
  58.7 19.9 %copy-start.5 = (bf16[4,16,4096]{2,1,0:T(8,128)(2,1)S(1)}, bf16[4,16,4096]{2,1,0:T(8,128)(2,1)}, u32[]{:S(2)}) copy-start(bf16[4,16,4096]{2,1,0:T(8,128)(2,1)} %copy-done.4) | copy-start | bytes 1572868
  58.8 19.9 %copy-start.7 = (bf16[4,16,4096]{2,1,0:T(8,128)(2,1)S(1)}, bf16[4,16,4096]{2,1,0:T(8,128)(2,1)}, u32[]{:S(2)}) copy-start(bf16[4,16,4096]{2,1,0:T(8,128)(2,1)} %copy-done.6) | copy-start | bytes 1572868
  58.8 19.9 %copy-start.9 = (bf16[4,16,4096]{2,1,0:T(8,128)(2,1)S(1)}, bf16[4,16,4096]{2,1,0:T(8,128)(2,1)}, u32[]{:S(2)}) copy-start(bf16[4,16,4096]{2,1,0:T(8,128)(2,1)} %copy-done.8) | copy-start | bytes 1572868
  77.8 8.9 %collective-permute-start.16 = (bf16[2,4,16,4096]{3,2,1,0:T(8,128)(2,1)}, bf16[2,4,16,4096]{3,2,1,0:T(8,128)(2,1)}, u32[]{:S(2)}, u32[]{:S(2)}) collective-permute-start(bf16[2,4,16,4096]{3,2,1,0:T(8,128)(2,1)} %pad_maximum_fusion.5), channel_id=1, source_target_pairs={{0,1},{1,0},{2,3},{3,2},{4,5},{5,4},{6,7},{7,6},{8,9},{9,8},{10,11... | collective-permute-start | bytes 3145736 | tf_op jit(solution)/shard_map/ppermute | solution.py:71
  81.7 6.2 %collective-permute-start.13 = (bf16[4,4,16,4096]{3,2,1,0:T(8,128)(2,1)}, bf16[4,4,16,4096]{3,2,1,0:T(8,128)(2,1)}, u32[]{:S(2)}, u32[]{:S(2)}) collective-permute-start(bf16[4,4,16,4096]{3,2,1,0:T(8,128)(2,1)} %get-tuple-element.19), channel_id=1, source_target_pairs={{0,1},{1,0},{2,3},{3,2},{4,5},{5,4},{6,7},{7,6},{8,9},{9,8},{10,11... | collective-permute-start | bytes 6291464 | tf_op jit(solution)/shard_map/ppermute | solution.py:69
  89.6 1.6 %copy-start = (bf16[1,4,4,16,4096]{4,3,2,1,0:T(8,128)(2,1)S(1)}, bf16[1,4,4,16,4096]{4,3,2,1,0:T(8,128)(2,1)}, u32[]{:S(2)}) copy-start(bf16[1,4,4,16,4096]{4,3,2,1,0:T(8,128)(2,1)} %get-tuple-element.18) | copy-start | bytes 6291460
  89.6 2.2 %copy-start.1 = (bf16[1,4,4,16,4096]{4,3,2,1,0:T(8,128)(2,1)S(1)}, bf16[1,4,4,16,4096]{4,3,2,1,0:T(8,128)(2,1)}, u32[]{:S(2)}) copy-start(bf16[1,4,4,16,4096]{4,3,2,1,0:T(8,128)(2,1)} %get-tuple-element.20) | copy-start | bytes 6291460
  (4 other events, 3.0 us)

commit v19 on v15

--- a/solution.py
+++ b/solution.py
@@ -66,8 +66,9 @@
     real_plus, real_far, real_minus = ring_gather(row_real, "y")
     imag_plus, imag_far, imag_minus = ring_gather(col_imag, "x")
     near = jnp.stack([real_plus, real_minus, imag_plus, imag_minus])
+    far = jnp.stack([real_far, imag_far])
+    near, far = lax.optimization_barrier((near, far))
     near_other = lax.ppermute(near, "core", CORE_PAIRS)
-    far = jnp.stack([real_far, imag_far])
     far_other = lax.ppermute(far, "core", CORE_PAIRS)
     parts = []
     for part in range(2):

time: 108 us -> 111 us (1.028)
  local copies, waits for them, and re-layouts: 11.5 us -> 15.6 us
  waiting for transfers between devices: 16.8 us -> 14.3 us
  other arithmetic: 14.9 us -> 16.8 us
    ppermute x14, waiting for transfers between devices: 16.8 us -> 14.3 us  [shift(): lax.ppermute(value, axis, [(i, (i + step) % size) for i in range(size)])]
    another operation x0 -> x1, other arithmetic: none -> 1.78 us  [on_device(): near = jnp.stack([real_plus, real_minus, imag_plus, imag_minus])]
    slice x1 -> x2, local copies, waits for them, and re-layouts: 1.65 us -> 3.23 us  [on_device(): src_near[2 * part]]
    slice x1, local copies, waits for them, and re-layouts: 0.17 us -> 1.71 us  [on_device(): scaled_real = (weight[:, None] * wide[0]).astype(jnp.bfloat16)]
    convert_element_type x1, other arithmetic: 0.27 us -> 1.62 us  [on_device(): wide = column[:, :, :width].astype(jnp.float32)]
    another operation x3 -> x4, other arithmetic: 6.02 us -> 4.81 us  [on_device(): left = jnp.stack(parts).reshape(2 * pairs, local_g)]
  transfers between devices with their start and end apart: 19 -> 19, of which waited for: 3 -> 2; matrix products, arithmetic and copies ran while one was open for 20% -> 25% of each run, Pallas kernels for 0% -> 0%
where the time goes in v19:
time: 111 us; the launch traced here: 110 us
  starting transfers between devices  37.4 us (34%)
  matrix products  22.6 us (20%)
  other arithmetic  16.8 us (15%)
  local copies, waits for them, and re-layouts  15.6 us (14%)
  waiting for transfers between devices  14.3 us (13%)
  between operations  3.79 us (3%)
    ppermute x14, starting transfers between devices, shift(): lax.ppermute(value, axis, [(i, (i + step) % size) for i in range(size)])  21 us
    ppermute x14, waiting for transfers between devices, shift(): lax.ppermute(value, axis, [(i, (i + step) % size) for i in range(size)])  14.3 us
    dot_general x1, matrix products, on_device(): lax.dot_general(left, jnp.stack(right_imag, axis=1), dims, preferred_elem...  11.3 us
    dot_general x1, matrix products, on_device(): lax.dot_general(left, jnp.stack(right_real, axis=1), dims, preferred_elem...  11.3 us
    all_to_all x1, starting transfers between devices, on_device(): lax.all_to_all(payload, cols, split_axis=0, concat_axis=0, tiled=True)  7.42 us
    all_to_all x1, starting transfers between devices, on_device(): spread = lax.all_to_all(copies, 'row', 0, 0, tiled=True)  5.03 us
    another operation x4, other arithmetic, on_device(): left = jnp.stack(parts).reshape(2 * pairs, local_g)  4.81 us
    ppermute x1, starting transfers between devices, on_device(): first_other = lax.ppermute(first, 'core', CORE_PAIRS)  3.3 us
  transfers between devices with their start and end apart: 19, of which 2 were waited for; matrix products, arithmetic and copies ran while one was open for 25% of the time, Pallas kernels for 0%

profile of v19, /device:TPU:1, one launch (start us, length us, event | category | flops | bytes accessed | tf_op | source)
XLA Modules:
  0.0 110.5 jit_solution(2030939389621685350)
XLA Ops:
  0.7 3.4 %collective-permute-start = (bf16[16,4096]{1,0:T(8,128)(2,1)}, bf16[16,4096]{1,0:T(8,128)(2,1)S(1)}, u32[]{:S(2)}, u32[]{:S(2)}) collective-permute-start(bf16[16,4096]{1,0:T(8,128)(2,1)} %param.7), channel_id=1, source_target_pairs={{0,24},{8,0},{16,8},{24,16},{1,25},{9,1},{17,9},{25,17},{2,26},{10... | collective-permute-start | bytes 393224 | tf_op jit(solution)/shard_map/ppermute | solution.py:17
  4.1 2.7 %collective-permute-start.3 = (bf16[16,4096]{1,0:T(8,128)(2,1)}, bf16[16,4096]{1,0:T(8,128)(2,1)S(1)}, u32[]{:S(2)}, u32[]{:S(2)}) collective-permute-start(bf16[16,4096]{1,0:T(8,128)(2,1)} %param.8), channel_id=1, source_target_pairs={{0,6},{2,0},{4,2},{6,4},{1,7},{3,1},{5,3},{7,5},{8,14},{10,8},{12,... | collective-permute-start | bytes 393224 | tf_op jit(solution)/shard_map/ppermute | solution.py:17
  6.8 1.6 %collective-permute-start.4 = (bf16[16,4096]{1,0:T(8,128)(2,1)}, bf16[16,4096]{1,0:T(8,128)(2,1)S(1)}, u32[]{:S(2)}, u32[]{:S(2)}) collective-permute-start(bf16[16,4096]{1,0:T(8,128)(2,1)} %param.8), channel_id=1, source_target_pairs={{0,4},{2,6},{4,0},{6,2},{1,5},{3,7},{5,1},{7,3},{8,12},{10,14},{12... | collective-permute-start | bytes 393224 | tf_op jit(solution)/shard_map/ppermute | solution.py:17
  9.4 1.1 broadcast_in_dim.28
  10.5 5.0 %all-to-all-start = ((bf16[4,2,16,4096]{3,2,1,0:T(8,128)(2,1)}), bf16[4,2,16,4096]{3,2,1,0:T(8,128)(2,1)S(1)}, u32[]{:S(2)}, u32[]{:S(2)}) async-start(bf16[4,2,16,4096]{3,2,1,0:T(8,128)(2,1)} %broadcast_in_dim.28), calls=%async_computation | async-start | bytes 2097152 | tf_op jit(solution)/shard_map/all_to_all | solution.py:53
  18.9 1.8 %collective-permute-start.1 = (bf16[16,4096]{1,0:T(8,128)(2,1)S(1)}, bf16[16,4096]{1,0:T(8,128)(2,1)S(1)}, u32[]{:S(2)}, u32[]{:S(2)}) collective-permute-start(bf16[16,4096]{1,0:T(8,128)(2,1)S(1)} %copy-done.7), channel_id=1, source_target_pairs={{0,16},{8,24},{16,0},{24,8},{1,17},{9,25},{17,1},{25,9},{2,18},{10... | collective-permute-start | bytes 393224 | tf_op jit(solution)/shard_map/ppermute | solution.py:17
  21.6 2.7 %collective-permute-done.1 = bf16[16,4096]{1,0:T(8,128)(2,1)S(1)} collective-permute-done((bf16[16,4096]{1,0:T(8,128)(2,1)S(1)}, bf16[16,4096]{1,0:T(8,128)(2,1)S(1)}, u32[]{:S(2)}, u32[]{:S(2)}) %collective-permute-start.1) | collective-permute-done | bytes 131104 | tf_op jit(solution)/shard_map/ppermute | solution.py:17
  25.3 3.3 %collective-permute-start.14 = (bf16[2,4,16,4096]{3,2,1,0:T(8,128)(2,1)S(1)}, bf16[2,4,16,4096]{3,2,1,0:T(8,128)(2,1)}, u32[]{:S(2)}, u32[]{:S(2)}) collective-permute-start(bf16[2,4,16,4096]{3,2,1,0:T(8,128)(2,1)S(1)} %pad_maximum_fusion.3), channel_id=1, source_target_pairs={{0,1},{1,0},{2,3},{3,2},{4,5},{5,4},{6,7},{7,6},{8,9},{9,8},{10,11... | collective-permute-start | bytes 3145736 | tf_op jit(solution)/shard_map/ppermute | solution.py:58
  29.0 1.7 %collective-permute-start.7 = (bf16[4,16,4096]{2,1,0:T(8,128)(2,1)}, bf16[4,16,4096]{2,1,0:T(8,128)(2,1)S(1)}, u32[]{:S(2)}, u32[]{:S(2)}) collective-permute-start(bf16[4,16,4096]{2,1,0:T(8,128)(2,1)} %get-tuple-element.9), channel_id=1, source_target_pairs={{0,2},{2,4},{4,6},{6,0},{1,3},{3,5},{5,7},{7,1},{8,10},{10,12},{12... | collective-permute-start | bytes 1572872 | tf_op jit(solution)/shard_map/ppermute | solution.py:17
  30.7 1.1 collective-permute-start.6
  32.2 2.5 %collective-permute-start.8 = (bf16[4,16,4096]{2,1,0:T(8,128)(2,1)}, bf16[4,16,4096]{2,1,0:T(8,128)(2,1)}, u32[]{:S(2)}, u32[]{:S(2)}) collective-permute-start(bf16[4,16,4096]{2,1,0:T(8,128)(2,1)} %get-tuple-element.10), channel_id=1, source_target_pairs={{0,24},{8,0},{16,8},{24,16},{1,25},{9,1},{17,9},{25,17},{2,26},{10... | collective-permute-start | bytes 1572872 | tf_op jit(solution)/shard_map/ppermute | solution.py:17
  35.1 1.2 %pad_maximum_fusion.2 = bf16[32,2,16,640]{3,2,1,0:T(8,128)(2,1)} fusion(bf16[32,2,16,128]{3,2,1,0:T(8,128)(2,1)S(1)} %broadcast_in_dim.29, bf16[32,2,16,512]{3,2,1,0:T(8,128)(2,1)S(1)} %bitcast.94), kind=kLoop, calls=%fused_computation.14 | loop fusion | flops 2621440 | bytes 2621440 | tf_op jit(solution)/shard_map/concatenate | solution.py:63
  36.3 7.4 %all-to-all-start.1 = ((bf16[32,2,16,640]{3,2,1,0:T(8,128)(2,1)}), bf16[32,2,16,640]{3,2,1,0:T(8,128)(2,1)S(1)}, u32[]{:S(2)}, u32[]{:S(2)}) async-start(bf16[32,2,16,640]{3,2,1,0:T(8,128)(2,1)} %pad_maximum_fusion.2), calls=%async_computation.1 | async-start | bytes 2621440 | tf_op jit(solution)/shard_map/all_to_all | solution.py:64
  43.9 2.2 %fusion.35 = (bf16[1,4,16,4096]{3,2,1,0:T(8,128)(2,1)}, bf16[1,4,16,4096]{3,2,1,0:T(8,128)(2,1)}) fusion(bf16[2,4,16,4096]{3,2,1,0:T(8,128)(2,1)} %collective-permute-done.14), kind=kLoop, calls=%fused_computation.98 | loop fusion | bytes 2097152 | tf_op jit(solution)/shard_map/slice | solution.py:77
  46.1 1.5 %collective-permute-start.10 = (bf16[4,16,2048]{2,1,0:T(8,128)(2,1)S(1)}, bf16[4,16,2048]{2,1,0:T(8,128)(2,1)S(1)}, u32[]{:S(2)}, u32[]{:S(2)}) collective-permute-start(bf16[4,16,2048]{2,1,0:T(8,128)(2,1)S(1)} %slice.116), channel_id=1, source_target_pairs={{0,2},{2,4},{4,6},{6,0},{1,3},{3,5},{5,7},{7,1},{8,10},{10,12},{12... | collective-permute-start | bytes 786440 | tf_op jit(solution)/shard_map/ppermute | solution.py:17
  47.6 1.4 %collective-permute-start.11 = (bf16[4,16,2048]{2,1,0:T(8,128)(2,1)S(1)}, bf16[4,16,2048]{2,1,0:T(8,128)(2,1)S(1)}, u32[]{:S(2)}, u32[]{:S(2)}) collective-permute-start(bf16[4,16,2048]{2,1,0:T(8,128)(2,1)S(1)} %slice.117), channel_id=1, source_target_pairs={{0,6},{2,0},{4,2},{6,4},{1,7},{3,1},{5,3},{7,5},{8,14},{10,8},{12,... | collective-permute-start | bytes 786440 | tf_op jit(solution)/shard_map/ppermute | solution.py:17
  50.0 1.5 %collective-permute-start.12 = (bf16[4,16,2048]{2,1,0:T(8,128)(2,1)S(1)}, bf16[4,16,2048]{2,1,0:T(8,128)(2,1)S(1)}, u32[]{:S(2)}, u32[]{:S(2)}) collective-permute-start(bf16[4,16,2048]{2,1,0:T(8,128)(2,1)S(1)} %slice.118), channel_id=1, source_target_pairs={{0,8},{8,16},{16,24},{24,0},{1,9},{9,17},{17,25},{25,1},{2,10},{10... | collective-permute-start | bytes 786440 | tf_op jit(solution)/shard_map/ppermute | solution.py:17
  52.4 1.4 %collective-permute-start.13 = (bf16[4,16,2048]{2,1,0:T(8,128)(2,1)S(1)}, bf16[4,16,2048]{2,1,0:T(8,128)(2,1)S(1)}, u32[]{:S(2)}, u32[]{:S(2)}) collective-permute-start(bf16[4,16,2048]{2,1,0:T(8,128)(2,1)S(1)} %slice.119), channel_id=1, source_target_pairs={{0,24},{8,0},{16,8},{24,16},{1,25},{9,1},{17,9},{25,17},{2,26},{10... | collective-permute-start | bytes 786440 | tf_op jit(solution)/shard_map/ppermute | solution.py:17
  53.9 1.8 %pad_maximum_fusion.1 = bf16[4,4,16,4096]{3,2,1,0:T(8,128)(2,1)S(1)} fusion(bf16[1,4,16,4096]{3,2,1,0:T(8,128)(2,1)} %bitcast.13, bf16[1,4,16,4096]{3,2,1,0:T(8,128)(2,1)} %bitcast.12, bf16[1,4,16,4096]{3,2,1,0:T(8,128)(2,1)} %bitcast.105, bf16[1,4,16,4096]{3,2,1,0:T(8,128)(2,1)} %bitcast.106), kind=kLoop, calls=%fused_computation.3 | loop fusion | flops 3145728 | bytes 4194304 | tf_op jit(solution)/shard_map/stack | solution.py:68
  55.6 11.6 %collective-permute-done.10 = bf16[4,16,2048]{2,1,0:T(8,128)(2,1)S(1)} collective-permute-done((bf16[4,16,2048]{2,1,0:T(8,128)(2,1)S(1)}, bf16[4,16,2048]{2,1,0:T(8,128)(2,1)S(1)}, u32[]{:S(2)}, u32[]{:S(2)}) %collective-permute-start.10) | collective-permute-done | bytes 262176 | tf_op jit(solution)/shard_map/ppermute | solution.py:17
  67.3 1.1 %pad_maximum_fusion.4 = bf16[2,4,16,4096]{3,2,1,0:T(8,128)(2,1)} fusion(bf16[1,4,16,4096]{3,2,1,0:T(8,128)(2,1)S(1)} %maximum_bitcast_fusion.9, bf16[1,4,16,4096]{3,2,1,0:T(8,128)(2,1)S(1)} %maximum_bitcast_fusion.8), kind=kLoop, calls=%fused_computation.17 | loop fusion | flops 524288 | bytes 2097152 | tf_op jit(solution)/shard_map/stack | solution.py:69
  69.1 1.5 %fusion.31 = (bf16[1,4,16,4096]{3,2,1,0:T(8,128)(2,1)S(1)}, bf16[1,4,16,4096]{3,2,1,0:T(8,128)(2,1)S(1)}, bf16[1,4,16,4096]{3,2,1,0:T(8,128)(2,1)S(1)}, bf16[1,4...) fusion(bf16[4,4,16,4096]{3,2,1,0:T(8,128)(2,1)S(1)} %pad_maximum_fusion.1, ...), kind=kLoop, calls=%fused_computation.94 | loop fusion | bytes 6291456 | tf_op jit(solution)/shard_map/slice | solution.py:77
  70.6 1.6 %maximum_bitcast_fusion = bf16[1,4,4,16,4096]{4,3,2,1,0:T(8,128)(2,1)} fusion(bf16[1,4,16,4096]{3,2,1,0:T(8,128)(2,1)S(1)} %get-tuple-element.21, bf16[1,4,16,4096]{3,2,1,0:T(8,128)(2,1)S(1)} %get-tuple-element.57, bf16[1,4,16,4096]{3,2,1,0:T(8,128)(2,1)S(1)} %get-tuple-element.18, bf16[1,4,16,4096]{3,2,1,0:T(8,128)(2,1)S(1)} %get-tuple-element.30), kind=kLoop, calls=%fused_computation.4 | loop fusion | flops 3145728 | bytes 4194304 | tf_op jit(solution)/shard_map/stack | solution.py:79
  72.2 1.6 %maximum_bitcast_fusion.2 = bf16[1,4,4,16,4096]{4,3,2,1,0:T(8,128)(2,1)} fusion(bf16[1,4,16,4096]{3,2,1,0:T(8,128)(2,1)S(1)} %get-tuple-element.19, bf16[1,4,16,4096]{3,2,1,0:T(8,128)(2,1)S(1)} %get-tuple-element.56, bf16[1,4,16,4096]{3,2,1,0:T(8,128)(2,1)S(1)} %get-tuple-element.20, bf16[1,4,16,4096]{3,2,1,0:T(8,128)(2,1)S(1)} %get-tuple-element.31), kind=kLoop, calls=%fused_computation.6 | loop fusion | flops 3145728 | bytes 4194304 | tf_op jit(solution)/shard_map/stack | solution.py:79
  73.9 1.6 %slice_convert_fusion = f32[2,512,512]{2,1,0:T(8,128)} fusion(bf16[2,512,640]{2,1,0:T(8,128)(2,1)S(1)} %bitcast.90), kind=kLoop, calls=%fused_computation.15 | loop fusion | flops 524288 | bytes 3145728 | tf_op jit(solution)/shard_map/convert_element_type | solution.py:83
  76.2 1.7 %fusion.30 = (f32[1,512,512]{2,1,0:T(8,128)S(1)}, f32[1,512,512]{2,1,0:T(8,128)S(1)}) fusion(f32[2,512,512]{2,1,0:T(8,128)} %slice_convert_fusion), kind=kLoop, calls=%fused_computation.93 | loop fusion | bytes 4194304 | tf_op jit(solution)/shard_map/slice | solution.py:101
  81.4 1.3 %fusion.36 = (bf16[1,4,16,4096]{3,2,1,0:T(8,128)(2,1)S(1)}, bf16[1,4,16,4096]{3,2,1,0:T(8,128)(2,1)S(1)}) fusion(bf16[2,4,16,4096]{3,2,1,0:T(8,128)(2,1)} %collective-permute-done.16), kind=kLoop, calls=%fused_computation.99 | loop fusion | bytes 2097152 | tf_op jit(solution)/shard_map/slice | solution.py:77
  82.8 1.7 %fusion.32 = (bf16[1,4,16,4096]{3,2,1,0:T(8,128)(2,1)S(1)}, bf16[1,4,16,4096]{3,2,1,0:T(8,128)(2,1)S(1)}, bf16[1,4,16,4096]{3,2,1,0:T(8,128)(2,1)S(1)}, bf16[1,4,16,4096]{3,2,1,0:T(8,128)(2,1)S(1)}) fusion(bf16[4,4,16,4096]{3,2,1,0:T(8,128)(2,1)} %collective-permute-done.15), kind=kLoop, calls=%fused_computation.95 | loop fusion | bytes 4194304 | tf_op jit(solution)/shard_map/slice | solution.py:77
  85.1 1.0 copy-done
  86.8 1.1 pad_maximum_fusion
  87.9 11.3 %convert_bitcast_fusion = bf16[2,4096,512]{2,1,0:T(8,128)(2,1)} fusion(bf16[1024,4096,1]{1,0,2:T(8,128)(2,1)S(1)} %bitcast.87, bf16[1024,1,512]{2,0,1:T(8,128)(2,1)S(1)} %maximum_bitcast_fusion.7, bf16[1024,1,512]{2,0,1:T(8,128)(2,1)S(1)} %maximum_bitcast_fusion.6), kind=kOutput, calls=%fused_computation.1 | convolution fusion | flops 8598323200 | bytes 18874368 | tf_op jit(solution)/shard_map/dot_general | solution.py:111
  99.2 11.3 %convert_bitcast_fusion.1 = bf16[2,4096,512]{2,1,0:T(8,128)(2,1)} fusion(bf16[1024,4096,1]{1,0,2:T(8,128)(2,1)S(1)} %bitcast.88, bf16[1024,1,512]{2,0,1:T(8,128)(2,1)S(1)} %maximum_bitcast_fusion.5, bf16[1024,1,512]{2,0,1:T(8,128)(2,1)S(1)} %maximum_bitcast_fusion.4), kind=kOutput, calls=%fused_computation.2 | convolution fusion | flops 8598323200 | bytes 18874368 | tf_op jit(solution)/shard_map/dot_general | solution.py:110
  (97 shorter events, 13.0 us)
Async XLA Ops:
  0.6 18.3 %copy-start.7 = (bf16[16,4096]{1,0:T(8,128)(2,1)S(1)}, bf16[16,4096]{1,0:T(8,128)(2,1)}, u32[]{:S(2)}) copy-start(bf16[16,4096]{1,0:T(8,128)(2,1)} %param.7) | copy-start | bytes 393220
  0.6 20.1 %copy-start.6 = (bf16[16,4096]{1,0:T(8,128)(2,1)S(1)}, bf16[16,4096]{1,0:T(8,128)(2,1)}, u32[]{:S(2)}) copy-start(bf16[16,4096]{1,0:T(8,128)(2,1)} %param.8) | copy-start | bytes 393220
  0.7 14.9 %copy-start.11 = (s32[16]{0:T(128)S(1)}, s32[16]{0:T(128)}, u32[]{:S(2)}) copy-start(s32[16]{0:T(128)} %param.9) | copy-start | bytes 196
  0.7 14.9 %copy-start.12 = (s32[16]{0:T(128)S(1)}, s32[16]{0:T(128)}, u32[]{:S(2)}) copy-start(s32[16]{0:T(128)} %param.10) | copy-start | bytes 196
  0.7 14.9 %copy-start.8 = (f32[2]{0:T(128)S(1)}, f32[2]{0:T(128)}, u32[]{:S(2)}) copy-start(f32[2]{0:T(128)} %param.13) | copy-start | bytes 28
  0.7 20.9 %collective-permute-start = (bf16[16,4096]{1,0:T(8,128)(2,1)}, bf16[16,4096]{1,0:T(8,128)(2,1)S(1)}, u32[]{:S(2)}, u32[]{:S(2)}) collective-permute-start(bf16[16,4096]{1,0:T(8,128)(2,1)} %param.7), channel_id=1, source_target_pairs={{0,24},{8,0},{16,8},{24,16},{1,25},{9,1},{17,9},{25,17},{2,26},{10... | collective-permute-start | bytes 393224 | tf_op jit(solution)/shard_map/ppermute | solution.py:17
  4.1 17.6 %collective-permute-start.2 = (bf16[16,4096]{1,0:T(8,128)(2,1)}, bf16[16,4096]{1,0:T(8,128)(2,1)S(1)}, u32[]{:S(2)}, u32[]{:S(2)}) collective-permute-start(bf16[16,4096]{1,0:T(8,128)(2,1)} %param.7), channel_id=1, source_target_pairs={{0,8},{8,16},{16,24},{24,0},{1,9},{9,17},{17,25},{25,1},{2,10},{10... | collective-permute-start | bytes 393224 | tf_op jit(solution)/shard_map/ppermute | solution.py:17
  4.1 14.8 %collective-permute-start.3 = (bf16[16,4096]{1,0:T(8,128)(2,1)}, bf16[16,4096]{1,0:T(8,128)(2,1)S(1)}, u32[]{:S(2)}, u32[]{:S(2)}) collective-permute-start(bf16[16,4096]{1,0:T(8,128)(2,1)} %param.8), channel_id=1, source_target_pairs={{0,6},{2,0},{4,2},{6,4},{1,7},{3,1},{5,3},{7,5},{8,14},{10,8},{12,... | collective-permute-start | bytes 393224 | tf_op jit(solution)/shard_map/ppermute | solution.py:17
  6.8 13.9 %collective-permute-start.5 = (bf16[16,4096]{1,0:T(8,128)(2,1)}, bf16[16,4096]{1,0:T(8,128)(2,1)S(1)}, u32[]{:S(2)}, u32[]{:S(2)}) collective-permute-start(bf16[16,4096]{1,0:T(8,128)(2,1)} %param.8), channel_id=1, source_target_pairs={{0,2},{2,4},{4,6},{6,0},{1,3},{3,5},{5,7},{7,1},{8,10},{10,12},{12... | collective-permute-start | bytes 393224 | tf_op jit(solution)/shard_map/ppermute | solution.py:17
  6.8 13.9 %collective-permute-start.4 = (bf16[16,4096]{1,0:T(8,128)(2,1)}, bf16[16,4096]{1,0:T(8,128)(2,1)S(1)}, u32[]{:S(2)}, u32[]{:S(2)}) collective-permute-start(bf16[16,4096]{1,0:T(8,128)(2,1)} %param.8), channel_id=1, source_target_pairs={{0,4},{2,6},{4,0},{6,2},{1,5},{3,7},{5,1},{7,3},{8,12},{10,14},{12... | collective-permute-start | bytes 393224 | tf_op jit(solution)/shard_map/ppermute | solution.py:17
  10.5 18.1 %all-to-all-start = ((bf16[4,2,16,4096]{3,2,1,0:T(8,128)(2,1)}), bf16[4,2,16,4096]{3,2,1,0:T(8,128)(2,1)S(1)}, u32[]{:S(2)}, u32[]{:S(2)}) async-start(bf16[4,2,16,4096]{3,2,1,0:T(8,128)(2,1)} %broadcast_in_dim.28), calls=%async_computation | async-start | bytes 2097152 | tf_op jit(solution)/shard_map/all_to_all | solution.py:53
  18.9 5.4 %collective-permute-start.1 = (bf16[16,4096]{1,0:T(8,128)(2,1)S(1)}, bf16[16,4096]{1,0:T(8,128)(2,1)S(1)}, u32[]{:S(2)}, u32[]{:S(2)}) collective-permute-start(bf16[16,4096]{1,0:T(8,128)(2,1)S(1)} %copy-done.7), channel_id=1, source_target_pairs={{0,16},{8,24},{16,0},{24,8},{1,17},{9,25},{17,1},{25,9},{2,18},{10... | collective-permute-start | bytes 393224 | tf_op jit(solution)/shard_map/ppermute | solution.py:17
  25.3 18.6 %collective-permute-start.14 = (bf16[2,4,16,4096]{3,2,1,0:T(8,128)(2,1)S(1)}, bf16[2,4,16,4096]{3,2,1,0:T(8,128)(2,1)}, u32[]{:S(2)}, u32[]{:S(2)}) collective-permute-start(bf16[2,4,16,4096]{3,2,1,0:T(8,128)(2,1)S(1)} %pad_maximum_fusion.3), channel_id=1, source_target_pairs={{0,1},{1,0},{2,3},{3,2},{4,5},{5,4},{6,7},{7,6},{8,9},{9,8},{10,11... | collective-permute-start | bytes 3145736 | tf_op jit(solution)/shard_map/ppermute | solution.py:58
  29.0 17.1 %collective-permute-start.7 = (bf16[4,16,4096]{2,1,0:T(8,128)(2,1)}, bf16[4,16,4096]{2,1,0:T(8,128)(2,1)S(1)}, u32[]{:S(2)}, u32[]{:S(2)}) collective-permute-start(bf16[4,16,4096]{2,1,0:T(8,128)(2,1)} %get-tuple-element.9), channel_id=1, source_target_pairs={{0,2},{2,4},{4,6},{6,0},{1,3},{3,5},{5,7},{7,1},{8,10},{10,12},{12... | collective-permute-start | bytes 1572872 | tf_op jit(solution)/shard_map/ppermute | solution.py:17
  30.7 16.9 %collective-permute-start.6 = (bf16[4,16,4096]{2,1,0:T(8,128)(2,1)}, bf16[4,16,4096]{2,1,0:T(8,128)(2,1)S(1)}, u32[]{:S(2)}, u32[]{:S(2)}) collective-permute-start(bf16[4,16,4096]{2,1,0:T(8,128)(2,1)} %get-tuple-element.9), channel_id=1, source_target_pairs={{0,6},{2,0},{4,2},{6,4},{1,7},{3,1},{5,3},{7,5},{8,14},{10,8},{12,... | collective-permute-start | bytes 1572872 | tf_op jit(solution)/shard_map/ppermute | solution.py:17
  31.8 17.2 %collective-permute-start.9 = (bf16[4,16,4096]{2,1,0:T(8,128)(2,1)}, bf16[4,16,4096]{2,1,0:T(8,128)(2,1)}, u32[]{:S(2)}, u32[]{:S(2)}) collective-permute-start(bf16[4,16,4096]{2,1,0:T(8,128)(2,1)} %get-tuple-element.10), channel_id=1, source_target_pairs={{0,8},{8,16},{16,24},{24,0},{1,9},{9,17},{17,25},{25,1},{2,10},{10... | collective-permute-start | bytes 1572872 | tf_op jit(solution)/shard_map/ppermute | solution.py:17
  32.2 19.2 %collective-permute-start.8 = (bf16[4,16,4096]{2,1,0:T(8,128)(2,1)}, bf16[4,16,4096]{2,1,0:T(8,128)(2,1)}, u32[]{:S(2)}, u32[]{:S(2)}) collective-permute-start(bf16[4,16,4096]{2,1,0:T(8,128)(2,1)} %get-tuple-element.10), channel_id=1, source_target_pairs={{0,24},{8,0},{16,8},{24,16},{1,25},{9,1},{17,9},{25,17},{2,26},{10... | collective-permute-start | bytes 1572872 | tf_op jit(solution)/shard_map/ppermute | solution.py:17
  36.3 37.4 %all-to-all-start.1 = ((bf16[32,2,16,640]{3,2,1,0:T(8,128)(2,1)}), bf16[32,2,16,640]{3,2,1,0:T(8,128)(2,1)S(1)}, u32[]{:S(2)}, u32[]{:S(2)}) async-start(bf16[32,2,16,640]{3,2,1,0:T(8,128)(2,1)} %pad_maximum_fusion.2), calls=%async_computation.1 | async-start | bytes 2621440 | tf_op jit(solution)/shard_map/all_to_all | solution.py:64
  46.1 7.7 %copy-start.4 = (bf16[4,16,4096]{2,1,0:T(8,128)(2,1)}, bf16[4,16,4096]{2,1,0:T(8,128)(2,1)S(1)}, u32[]{:S(2)}) copy-start(bf16[4,16,4096]{2,1,0:T(8,128)(2,1)S(1)} %collective-permute-done.7) | copy-start | bytes 1572868
  46.1 21.1 %collective-permute-start.10 = (bf16[4,16,2048]{2,1,0:T(8,128)(2,1)S(1)}, bf16[4,16,2048]{2,1,0:T(8,128)(2,1)S(1)}, u32[]{:S(2)}, u32[]{:S(2)}) collective-permute-start(bf16[4,16,2048]{2,1,0:T(8,128)(2,1)S(1)} %slice.116), channel_id=1, source_target_pairs={{0,2},{2,4},{4,6},{6,0},{1,3},{3,5},{5,7},{7,1},{8,10},{10,12},{12... | collective-permute-start | bytes 786440 | tf_op jit(solution)/shard_map/ppermute | solution.py:17
  47.6 6.2 %copy-start.5 = (bf16[4,16,4096]{2,1,0:T(8,128)(2,1)}, bf16[4,16,4096]{2,1,0:T(8,128)(2,1)S(1)}, u32[]{:S(2)}) copy-start(bf16[4,16,4096]{2,1,0:T(8,128)(2,1)S(1)} %collective-permute-done.6) | copy-start | bytes 1572868
  47.6 19.6 %collective-permute-start.11 = (bf16[4,16,2048]{2,1,0:T(8,128)(2,1)S(1)}, bf16[4,16,2048]{2,1,0:T(8,128)(2,1)S(1)}, u32[]{:S(2)}, u32[]{:S(2)}) collective-permute-start(bf16[4,16,2048]{2,1,0:T(8,128)(2,1)S(1)} %slice.117), channel_id=1, source_target_pairs={{0,6},{2,0},{4,2},{6,4},{1,7},{3,1},{5,3},{7,5},{8,14},{10,8},{12,... | collective-permute-start | bytes 786440 | tf_op jit(solution)/shard_map/ppermute | solution.py:17
  50.0 17.3 %collective-permute-start.12 = (bf16[4,16,2048]{2,1,0:T(8,128)(2,1)S(1)}, bf16[4,16,2048]{2,1,0:T(8,128)(2,1)S(1)}, u32[]{:S(2)}, u32[]{:S(2)}) collective-permute-start(bf16[4,16,2048]{2,1,0:T(8,128)(2,1)S(1)} %slice.118), channel_id=1, source_target_pairs={{0,8},{8,16},{16,24},{24,0},{1,9},{9,17},{17,25},{25,1},{2,10},{10... | collective-permute-start | bytes 786440 | tf_op jit(solution)/shard_map/ppermute | solution.py:17
  52.4 14.8 %collective-permute-start.13 = (bf16[4,16,2048]{2,1,0:T(8,128)(2,1)S(1)}, bf16[4,16,2048]{2,1,0:T(8,128)(2,1)S(1)}, u32[]{:S(2)}, u32[]{:S(2)}) collective-permute-start(bf16[4,16,2048]{2,1,0:T(8,128)(2,1)S(1)} %slice.119), channel_id=1, source_target_pairs={{0,24},{8,0},{16,8},{24,16},{1,25},{9,1},{17,9},{25,17},{2,26},{10... | collective-permute-start | bytes 786440 | tf_op jit(solution)/shard_map/ppermute | solution.py:17
  68.4 13.0 %collective-permute-start.16 = (bf16[2,4,16,4096]{3,2,1,0:T(8,128)(2,1)}, bf16[2,4,16,4096]{3,2,1,0:T(8,128)(2,1)}, u32[]{:S(2)}, u32[]{:S(2)}) collective-permute-start(bf16[2,4,16,4096]{3,2,1,0:T(8,128)(2,1)} %pad_maximum_fusion.4), channel_id=1, source_target_pairs={{0,1},{1,0},{2,3},{3,2},{4,5},{5,4},{6,7},{7,6},{8,9},{9,8},{10,11... | collective-permute-start | bytes 3145736 | tf_op jit(solution)/shard_map/ppermute | solution.py:72
  69.1 13.7 %collective-permute-start.15 = (bf16[4,4,16,4096]{3,2,1,0:T(8,128)(2,1)S(1)}, bf16[4,4,16,4096]{3,2,1,0:T(8,128)(2,1)}, u32[]{:S(2)}, u32[]{:S(2)}) collective-permute-start(bf16[4,4,16,4096]{3,2,1,0:T(8,128)(2,1)S(1)} %pad_maximum_fusion.1), channel_id=1, source_target_pairs={{0,1},{1,0},{2,3},{3,2},{4,5},{5,4},{6,7},{7,6},{8,9},{9,8},{10,11... | collective-permute-start | bytes 6291464 | tf_op jit(solution)/shard_map/ppermute | solution.py:71
  73.9 1.9 %copy-start.9 = (f32[16]{0:T(128)S(1)}, f32[16]{0:T(128)}, u32[]{:S(2)}) copy-start(f32[16]{0:T(128)} %param.11) | copy-start | bytes 196
  73.9 2.0 %copy-start.10 = (f32[32]{0:T(128)S(1)}, f32[32]{0:T(128)}, u32[]{:S(2)}) copy-start(f32[32]{0:T(128)} %param.12) | copy-start | bytes 388
  82.7 1.8 %copy-start.2 = (bf16[1,4,16,4096]{3,2,1,0:T(8,128)(2,1)S(1)}, bf16[1,4,16,4096]{3,2,1,0:T(8,128)(2,1)}, u32[]{:S(2)}) copy-start(bf16[1,4,16,4096]{3,2,1,0:T(8,128)(2,1)} %get-tuple-element.34) | copy-start | bytes 1572868
  82.7 1.8 %copy-start.3 = (bf16[1,4,16,4096]{3,2,1,0:T(8,128)(2,1)S(1)}, bf16[1,4,16,4096]{3,2,1,0:T(8,128)(2,1)}, u32[]{:S(2)}) copy-start(bf16[1,4,16,4096]{3,2,1,0:T(8,128)(2,1)} %get-tuple-element.35) | copy-start | bytes 1572868
  84.6 1.6 %copy-start = (bf16[1,4,4,16,4096]{4,3,2,1,0:T(8,128)(2,1)S(1)}, bf16[1,4,4,16,4096]{4,3,2,1,0:T(8,128)(2,1)}, u32[]{:S(2)}) copy-start(bf16[1,4,4,16,4096]{4,3,2,1,0:T(8,128)(2,1)} %maximum_bitcast_fusion) | copy-start | bytes 6291460
  84.6 2.2 %copy-start.1 = (bf16[1,4,4,16,4096]{4,3,2,1,0:T(8,128)(2,1)S(1)}, bf16[1,4,4,16,4096]{4,3,2,1,0:T(8,128)(2,1)}, u32[]{:S(2)}) copy-start(bf16[1,4,4,16,4096]{4,3,2,1,0:T(8,128)(2,1)} %maximum_bitcast_fusion.2) | copy-start | bytes 6291460

commit v20 on v15

--- a/solution.py
+++ b/solution.py
@@ -23,8 +23,7 @@
     from_plus = shift(block, axis, -1)
     far_first = shift(from_minus[..., :half], axis, 1)
     far_second = shift(from_plus[..., half:], axis, -1)
-    far = jnp.concatenate([far_first, far_second], axis=-1)
-    return from_plus, far, from_minus
+    return from_plus, (far_first, far_second), from_minus
 
 
 def ring_direct(block, axis):
@@ -67,8 +66,12 @@
     imag_plus, imag_far, imag_minus = ring_gather(col_imag, "x")
     near = jnp.stack([real_plus, real_minus, imag_plus, imag_minus])
     near_other = lax.ppermute(near, "core", CORE_PAIRS)
-    far = jnp.stack([real_far, imag_far])
-    far_other = lax.ppermute(far, "core", CORE_PAIRS)
+    far_a = jnp.stack([real_far[0], imag_far[0]])
+    far_a_other = lax.ppermute(far_a, "core", CORE_PAIRS)
+    far_b = jnp.stack([real_far[1], imag_far[1]])
+    far_b_other = lax.ppermute(far_b, "core", CORE_PAIRS)
+    far = jnp.concatenate([far_a, far_b], axis=-1)
+    far_other = jnp.concatenate([far_a_other, far_b_other], axis=-1)
     parts = []
     for part in range(2):
         for src_first, src_near, src_far in ((first, near, far), (first_other, near_other, far_other)):

time: 108 us -> 111 us (1.028)
  starting transfers between devices: 37.6 us -> 39.6 us
    all_to_all x1, starting transfers between devices: 7.42 us -> 8.61 us  [on_device(): lax.all_to_all(payload, cols, split_axis=0, concat_axis=0, tiled=True)]
    slice x1 -> x2, local copies, waits for them, and re-layouts: 1.27 us -> 0.14 us  [on_device(): src_far[part]]
    unnamed x27 -> x28, local copies, waits for them, and re-layouts: 2.16 us -> 3.24 us
  transfers between devices with their start and end apart: 19 -> 20, of which waited for: 3 -> 5; matrix products, arithmetic and copies ran while one was open for 20% -> 21% of each run, Pallas kernels for 0% -> 0%
where the time goes in v20:
time: 111 us
  starting transfers between devices  39.6 us (36%)
  matrix products  22.6 us (20%)
  waiting for transfers between devices  16.7 us (15%)
  other arithmetic  15.5 us (14%)
  local copies, waits for them, and re-layouts  12.5 us (11%)
  between operations  3.75 us (3%)
    ppermute x14, starting transfers between devices, shift(): lax.ppermute(value, axis, [(i, (i + step) % size) for i in range(size)])  20.7 us
    ppermute x14, waiting for transfers between devices, shift(): lax.ppermute(value, axis, [(i, (i + step) % size) for i in range(size)])  16.5 us
    dot_general x1, matrix products, on_device(): lax.dot_general(left, jnp.stack(right_imag, axis=1), dims, preferred_elem...  11.3 us
    dot_general x1, matrix products, on_device(): lax.dot_general(left, jnp.stack(right_real, axis=1), dims, preferred_elem...  11.3 us
    all_to_all x1, starting transfers between devices, on_device(): lax.all_to_all(payload, cols, split_axis=0, concat_axis=0, tiled=True)  8.61 us
    another operation x3, other arithmetic, on_device(): left = jnp.stack(parts).reshape(2 * pairs, local_g)  6.02 us
    all_to_all x1, starting transfers between devices, on_device(): spread = lax.all_to_all(copies, 'row', 0, 0, tiled=True)  5.03 us
    ppermute x1, starting transfers between devices, on_device(): first_other = lax.ppermute(first, 'core', CORE_PAIRS)  3.3 us
  transfers between devices with their start and end apart: 20, of which 5 were waited for; matrix products, arithmetic and copies ran while one was open for 21% of the time, Pallas kernels for 0%

profile of v20, /device:TPU:1, one launch (start us, length us, event | category | flops | bytes accessed | tf_op | source)
XLA Modules:
  0.0 110.6 jit_solution(1183163913598232963)
XLA Ops:
  0.7 3.4 %collective-permute-start = (bf16[16,4096]{1,0:T(8,128)(2,1)}, bf16[16,4096]{1,0:T(8,128)(2,1)S(1)}, u32[]{:S(2)}, u32[]{:S(2)}) collective-permute-start(bf16[16,4096]{1,0:T(8,128)(2,1)} %param.7), channel_id=1, source_target_pairs={{0,24},{8,0},{16,8},{24,16},{1,25},{9,1},{17,9},{25,17},{2,26},{10... | collective-permute-start | bytes 393224 | tf_op jit(solution)/shard_map/ppermute | solution.py:17
  4.1 2.7 %collective-permute-start.3 = (bf16[16,4096]{1,0:T(8,128)(2,1)}, bf16[16,4096]{1,0:T(8,128)(2,1)S(1)}, u32[]{:S(2)}, u32[]{:S(2)}) collective-permute-start(bf16[16,4096]{1,0:T(8,128)(2,1)} %param.8), channel_id=1, source_target_pairs={{0,6},{2,0},{4,2},{6,4},{1,7},{3,1},{5,3},{7,5},{8,14},{10,8},{12,... | collective-permute-start | bytes 393224 | tf_op jit(solution)/shard_map/ppermute | solution.py:17
  6.8 1.6 %collective-permute-start.4 = (bf16[16,4096]{1,0:T(8,128)(2,1)}, bf16[16,4096]{1,0:T(8,128)(2,1)S(1)}, u32[]{:S(2)}, u32[]{:S(2)}) collective-permute-start(bf16[16,4096]{1,0:T(8,128)(2,1)} %param.8), channel_id=1, source_target_pairs={{0,4},{2,6},{4,0},{6,2},{1,5},{3,7},{5,1},{7,3},{8,12},{10,14},{12... | collective-permute-start | bytes 393224 | tf_op jit(solution)/shard_map/ppermute | solution.py:17
  8.4 1.0 pad_maximum_fusion.9
  9.4 1.1 broadcast_in_dim.28
  10.5 5.0 %all-to-all-start = ((bf16[4,2,16,4096]{3,2,1,0:T(8,128)(2,1)}), bf16[4,2,16,4096]{3,2,1,0:T(8,128)(2,1)S(1)}, u32[]{:S(2)}, u32[]{:S(2)}) async-start(bf16[4,2,16,4096]{3,2,1,0:T(8,128)(2,1)} %broadcast_in_dim.28), calls=%async_computation | async-start | bytes 2097152 | tf_op jit(solution)/shard_map/all_to_all | solution.py:52
  18.8 1.8 %collective-permute-start.1 = (bf16[16,4096]{1,0:T(8,128)(2,1)S(1)}, bf16[16,4096]{1,0:T(8,128)(2,1)S(1)}, u32[]{:S(2)}, u32[]{:S(2)}) collective-permute-start(bf16[16,4096]{1,0:T(8,128)(2,1)S(1)} %copy-done.7), channel_id=1, source_target_pairs={{0,16},{8,24},{16,0},{24,8},{1,17},{9,25},{17,1},{25,9},{2,18},{10... | collective-permute-start | bytes 393224 | tf_op jit(solution)/shard_map/ppermute | solution.py:17
  20.6 0.9 fusion.29
  21.5 2.7 %collective-permute-done.1 = bf16[16,4096]{1,0:T(8,128)(2,1)S(1)} collective-permute-done((bf16[16,4096]{1,0:T(8,128)(2,1)S(1)}, bf16[16,4096]{1,0:T(8,128)(2,1)S(1)}, u32[]{:S(2)}, u32[]{:S(2)}) %collective-permute-start.1) | collective-permute-done | bytes 131104 | tf_op jit(solution)/shard_map/ppermute | solution.py:17
  24.2 0.9 fusion.30
  25.1 3.3 %collective-permute-start.14 = (bf16[2,4,16,4096]{3,2,1,0:T(8,128)(2,1)S(1)}, bf16[2,4,16,4096]{3,2,1,0:T(8,128)(2,1)}, u32[]{:S(2)}, u32[]{:S(2)}) collective-permute-start(bf16[2,4,16,4096]{3,2,1,0:T(8,128)(2,1)S(1)} %pad_maximum_fusion.4), channel_id=1, source_target_pairs={{0,1},{1,0},{2,3},{3,2},{4,5},{5,4},{6,7},{7,6},{8,9},{9,8},{10,11... | collective-permute-start | bytes 3145736 | tf_op jit(solution)/shard_map/ppermute | solution.py:57
  29.0 1.7 %collective-permute-start.7 = (bf16[4,16,4096]{2,1,0:T(8,128)(2,1)}, bf16[4,16,4096]{2,1,0:T(8,128)(2,1)S(1)}, u32[]{:S(2)}, u32[]{:S(2)}) collective-permute-start(bf16[4,16,4096]{2,1,0:T(8,128)(2,1)} %get-tuple-element.7), channel_id=1, source_target_pairs={{0,2},{2,4},{4,6},{6,0},{1,3},{3,5},{5,7},{7,1},{8,10},{10,12},{12... | collective-permute-start | bytes 1572872 | tf_op jit(solution)/shard_map/ppermute | solution.py:17
  30.7 1.1 collective-permute-start.6
  31.7 2.8 %collective-permute-start.12 = (bf16[4,16,4096]{2,1,0:T(8,128)(2,1)}, bf16[4,16,4096]{2,1,0:T(8,128)(2,1)}, u32[]{:S(2)}, u32[]{:S(2)}) collective-permute-start(bf16[4,16,4096]{2,1,0:T(8,128)(2,1)} %get-tuple-element.8), channel_id=1, source_target_pairs={{0,24},{8,0},{16,8},{24,16},{1,25},{9,1},{17,9},{25,17},{2,26},{10... | collective-permute-start | bytes 1572872 | tf_op jit(solution)/shard_map/ppermute | solution.py:17
  35.0 1.2 %pad_maximum_fusion.3 = bf16[32,2,16,640]{3,2,1,0:T(8,128)(2,1)} fusion(bf16[32,2,16,128]{3,2,1,0:T(8,128)(2,1)S(1)} %broadcast_in_dim.29, bf16[32,2,16,512]{3,2,1,0:T(8,128)(2,1)S(1)} %bitcast.94), kind=kLoop, calls=%fused_computation.15 | loop fusion | flops 2621440 | bytes 2621440 | tf_op jit(solution)/shard_map/concatenate | solution.py:62
  36.2 8.6 %all-to-all-start.1 = ((bf16[32,2,16,640]{3,2,1,0:T(8,128)(2,1)}), bf16[32,2,16,640]{3,2,1,0:T(8,128)(2,1)S(1)}, u32[]{:S(2)}, u32[]{:S(2)}) async-start(bf16[32,2,16,640]{3,2,1,0:T(8,128)(2,1)} %pad_maximum_fusion.3), calls=%async_computation.1 | async-start | bytes 2621440 | tf_op jit(solution)/shard_map/all_to_all | solution.py:63
  45.0 1.5 %collective-permute-start.8 = (bf16[4,16,2048]{2,1,0:T(8,128)(2,1)S(1)}, bf16[4,16,2048]{2,1,0:T(8,128)(2,1)S(1)}, u32[]{:S(2)}, u32[]{:S(2)}) collective-permute-start(bf16[4,16,2048]{2,1,0:T(8,128)(2,1)S(1)} %slice.100), channel_id=1, source_target_pairs={{0,2},{2,4},{4,6},{6,0},{1,3},{3,5},{5,7},{7,1},{8,10},{10,12},{12... | collective-permute-start | bytes 786440 | tf_op jit(solution)/shard_map/ppermute | solution.py:17
  46.5 1.4 %collective-permute-start.11 = (bf16[4,16,2048]{2,1,0:T(8,128)(2,1)S(1)}, bf16[4,16,2048]{2,1,0:T(8,128)(2,1)S(1)}, u32[]{:S(2)}, u32[]{:S(2)}) collective-permute-start(bf16[4,16,2048]{2,1,0:T(8,128)(2,1)S(1)} %slice.102), channel_id=1, source_target_pairs={{0,6},{2,0},{4,2},{6,4},{1,7},{3,1},{5,3},{7,5},{8,14},{10,8},{12,... | collective-permute-start | bytes 786440 | tf_op jit(solution)/shard_map/ppermute | solution.py:17
  47.8 1.0 slice.103
  48.8 2.7 %collective-permute-start.13 = (bf16[4,16,2048]{2,1,0:T(8,128)(2,1)S(1)}, bf16[4,16,2048]{2,1,0:T(8,128)(2,1)S(1)}, u32[]{:S(2)}, u32[]{:S(2)}) collective-permute-start(bf16[4,16,2048]{2,1,0:T(8,128)(2,1)S(1)} %slice.103), channel_id=1, source_target_pairs={{0,24},{8,0},{16,8},{24,16},{1,25},{9,1},{17,9},{25,17},{2,26},{10... | collective-permute-start | bytes 786440 | tf_op jit(solution)/shard_map/ppermute | solution.py:17
  51.5 1.0 slice.101
  52.6 1.3 %fusion.35 = (bf16[1,4,16,4096]{3,2,1,0:T(8,128)(2,1)S(1)}, bf16[1,4,16,4096]{3,2,1,0:T(8,128)(2,1)S(1)}) fusion(bf16[2,4,16,4096]{3,2,1,0:T(8,128)(2,1)} %collective-permute-done.14), kind=kLoop, calls=%fused_computation.100 | loop fusion | bytes 2097152 | tf_op jit(solution)/shard_map/slice | solution.py:79
  53.9 12.8 %collective-permute-done.11 = bf16[4,16,2048]{2,1,0:T(8,128)(2,1)S(1)} collective-permute-done((bf16[4,16,2048]{2,1,0:T(8,128)(2,1)S(1)}, bf16[4,16,2048]{2,1,0:T(8,128)(2,1)S(1)}, u32[]{:S(2)}, u32[]{:S(2)}) %collective-permute-start.11) | collective-permute-done | bytes 262176 | tf_op jit(solution)/shard_map/ppermute | solution.py:17
  69.5 1.4 %collective-permute-start.17 = (bf16[2,4,16,2048]{3,2,1,0:T(8,128)(2,1)}, bf16[2,4,16,2048]{3,2,1,0:T(8,128)(2,1)}, u32[]{:S(2)}, u32[]{:S(2)}) collective-permute-start(bf16[2,4,16,2048]{3,2,1,0:T(8,128)(2,1)} %pad_maximum_fusion.8), channel_id=1, source_target_pairs={{0,1},{1,0},{2,3},{3,2},{4,5},{5,4},{6,7},{7,6},{8,9},{9,8},{10,11... | collective-permute-start | bytes 1572872 | tf_op jit(solution)/shard_map/ppermute | solution.py:72
  71.0 4.4 %maximum_bitcast_fusion = (bf16[1,4,4,16,4096]{4,3,2,1,0:T(8,128)(2,1)}, bf16[4,4,16,4096]{3,2,1,0:T(8,128)(2,1)}, bf16[1,4,4,16,4096]{4,3,2,1,0:T(8,128)(2,1)}) fusion(bf16[1,4,16,4096]{3,2,1,0:T(8,128)(2,1)S(1)} %bitcast.105, bf16[1,4,16,4096]{3,2,1,0:T(8,128)(2,1)S(1)} %get-tuple-element.27, bf16[1,4,16,4096]{3,2,1,0:T(8,128)(2,1)S(1)} %bitcast.106, ...), kind=kLoop, calls=%fused_computation.6 | loop fusion | flops 9437184 | bytes 10485760 | tf_op jit(solution)/shard_map/stack | solution.py:81
  80.8 1.1 constant_dynamic-update-slice_fusion.1
  81.9 1.1 constant_dynamic-update-slice_fusion
  83.0 1.7 %fusion.32 = (bf16[1,4,16,4096]{3,2,1,0:T(8,128)(2,1)S(1)}, bf16[1,4,16,4096]{3,2,1,0:T(8,128)(2,1)S(1)}, bf16[1,4,16,4096]{3,2,1,0:T(8,128)(2,1)S(1)}, bf16[1,4,16,4096]{3,2,1,0:T(8,128)(2,1)S(1)}) fusion(bf16[4,4,16,4096]{3,2,1,0:T(8,128)(2,1)} %collective-permute-done.15), kind=kLoop, calls=%fused_computation.97 | loop fusion | bytes 4194304 | tf_op jit(solution)/shard_map/slice | solution.py:79
  85.3 1.0 copy-done
  86.9 1.1 pad_maximum_fusion
  88.0 11.3 %convert_bitcast_fusion = bf16[2,4096,512]{2,1,0:T(8,128)(2,1)} fusion(bf16[1024,4096,1]{1,0,2:T(8,128)(2,1)S(1)} %bitcast.87, bf16[1024,1,512]{2,0,1:T(8,128)(2,1)S(1)} %maximum_bitcast_fusion.6, bf16[1024,1,512]{2,0,1:T(8,128)(2,1)S(1)} %maximum_bitcast_fusion.5), kind=kOutput, calls=%fused_computation.1 | convolution fusion | flops 8598323200 | bytes 18874368 | tf_op jit(solution)/shard_map/dot_general | solution.py:113
  99.3 11.3 %convert_bitcast_fusion.1 = bf16[2,4096,512]{2,1,0:T(8,128)(2,1)} fusion(bf16[1024,4096,1]{1,0,2:T(8,128)(2,1)S(1)} %bitcast.88, bf16[1024,1,512]{2,0,1:T(8,128)(2,1)S(1)} %maximum_bitcast_fusion.4, bf16[1024,1,512]{2,0,1:T(8,128)(2,1)S(1)} %maximum_bitcast_fusion.3), kind=kOutput, calls=%fused_computation.2 | convolution fusion | flops 8598323200 | bytes 18874368 | tf_op jit(solution)/shard_map/dot_general | solution.py:112
  (99 shorter events, 11.2 us)
Async XLA Ops:
  0.6 18.1 %copy-start.7 = (bf16[16,4096]{1,0:T(8,128)(2,1)S(1)}, bf16[16,4096]{1,0:T(8,128)(2,1)}, u32[]{:S(2)}) copy-start(bf16[16,4096]{1,0:T(8,128)(2,1)} %param.7) | copy-start | bytes 393220
  0.6 19.9 %copy-start.6 = (bf16[16,4096]{1,0:T(8,128)(2,1)S(1)}, bf16[16,4096]{1,0:T(8,128)(2,1)}, u32[]{:S(2)}) copy-start(bf16[16,4096]{1,0:T(8,128)(2,1)} %param.8) | copy-start | bytes 393220
  0.7 14.9 %copy-start.11 = (s32[16]{0:T(128)S(1)}, s32[16]{0:T(128)}, u32[]{:S(2)}) copy-start(s32[16]{0:T(128)} %param.9) | copy-start | bytes 196
  0.7 14.9 %copy-start.12 = (s32[16]{0:T(128)S(1)}, s32[16]{0:T(128)}, u32[]{:S(2)}) copy-start(s32[16]{0:T(128)} %param.10) | copy-start | bytes 196
  0.7 14.9 %copy-start.8 = (f32[2]{0:T(128)S(1)}, f32[2]{0:T(128)}, u32[]{:S(2)}) copy-start(f32[2]{0:T(128)} %param.13) | copy-start | bytes 28
  0.7 20.8 %collective-permute-start = (bf16[16,4096]{1,0:T(8,128)(2,1)}, bf16[16,4096]{1,0:T(8,128)(2,1)S(1)}, u32[]{:S(2)}, u32[]{:S(2)}) collective-permute-start(bf16[16,4096]{1,0:T(8,128)(2,1)} %param.7), channel_id=1, source_target_pairs={{0,24},{8,0},{16,8},{24,16},{1,25},{9,1},{17,9},{25,17},{2,26},{10... | collective-permute-start | bytes 393224 | tf_op jit(solution)/shard_map/ppermute | solution.py:17
  4.1 17.4 %collective-permute-start.2 = (bf16[16,4096]{1,0:T(8,128)(2,1)}, bf16[16,4096]{1,0:T(8,128)(2,1)S(1)}, u32[]{:S(2)}, u32[]{:S(2)}) collective-permute-start(bf16[16,4096]{1,0:T(8,128)(2,1)} %param.7), channel_id=1, source_target_pairs={{0,8},{8,16},{16,24},{24,0},{1,9},{9,17},{17,25},{25,1},{2,10},{10... | collective-permute-start | bytes 393224 | tf_op jit(solution)/shard_map/ppermute | solution.py:17
  4.1 14.7 %collective-permute-start.3 = (bf16[16,4096]{1,0:T(8,128)(2,1)}, bf16[16,4096]{1,0:T(8,128)(2,1)S(1)}, u32[]{:S(2)}, u32[]{:S(2)}) collective-permute-start(bf16[16,4096]{1,0:T(8,128)(2,1)} %param.8), channel_id=1, source_target_pairs={{0,6},{2,0},{4,2},{6,4},{1,7},{3,1},{5,3},{7,5},{8,14},{10,8},{12,... | collective-permute-start | bytes 393224 | tf_op jit(solution)/shard_map/ppermute | solution.py:17
  6.8 13.8 %collective-permute-start.5 = (bf16[16,4096]{1,0:T(8,128)(2,1)}, bf16[16,4096]{1,0:T(8,128)(2,1)S(1)}, u32[]{:S(2)}, u32[]{:S(2)}) collective-permute-start(bf16[16,4096]{1,0:T(8,128)(2,1)} %param.8), channel_id=1, source_target_pairs={{0,2},{2,4},{4,6},{6,0},{1,3},{3,5},{5,7},{7,1},{8,10},{10,12},{12... | collective-permute-start | bytes 393224 | tf_op jit(solution)/shard_map/ppermute | solution.py:17
  6.8 13.8 %collective-permute-start.4 = (bf16[16,4096]{1,0:T(8,128)(2,1)}, bf16[16,4096]{1,0:T(8,128)(2,1)S(1)}, u32[]{:S(2)}, u32[]{:S(2)}) collective-permute-start(bf16[16,4096]{1,0:T(8,128)(2,1)} %param.8), channel_id=1, source_target_pairs={{0,4},{2,6},{4,0},{6,2},{1,5},{3,7},{5,1},{7,3},{8,12},{10,14},{12... | collective-permute-start | bytes 393224 | tf_op jit(solution)/shard_map/ppermute | solution.py:17
  10.5 18.1 %all-to-all-start = ((bf16[4,2,16,4096]{3,2,1,0:T(8,128)(2,1)}), bf16[4,2,16,4096]{3,2,1,0:T(8,128)(2,1)S(1)}, u32[]{:S(2)}, u32[]{:S(2)}) async-start(bf16[4,2,16,4096]{3,2,1,0:T(8,128)(2,1)} %broadcast_in_dim.28), calls=%async_computation | async-start | bytes 2097152 | tf_op jit(solution)/shard_map/all_to_all | solution.py:52
  18.8 5.4 %collective-permute-start.1 = (bf16[16,4096]{1,0:T(8,128)(2,1)S(1)}, bf16[16,4096]{1,0:T(8,128)(2,1)S(1)}, u32[]{:S(2)}, u32[]{:S(2)}) collective-permute-start(bf16[16,4096]{1,0:T(8,128)(2,1)S(1)} %copy-done.7), channel_id=1, source_target_pairs={{0,16},{8,24},{16,0},{24,8},{1,17},{9,25},{17,1},{25,9},{2,18},{10... | collective-permute-start | bytes 393224 | tf_op jit(solution)/shard_map/ppermute | solution.py:17
  25.1 27.4 %collective-permute-start.14 = (bf16[2,4,16,4096]{3,2,1,0:T(8,128)(2,1)S(1)}, bf16[2,4,16,4096]{3,2,1,0:T(8,128)(2,1)}, u32[]{:S(2)}, u32[]{:S(2)}) collective-permute-start(bf16[2,4,16,4096]{3,2,1,0:T(8,128)(2,1)S(1)} %pad_maximum_fusion.4), channel_id=1, source_target_pairs={{0,1},{1,0},{2,3},{3,2},{4,5},{5,4},{6,7},{7,6},{8,9},{9,8},{10,11... | collective-permute-start | bytes 3145736 | tf_op jit(solution)/shard_map/ppermute | solution.py:57
  29.0 15.9 %collective-permute-start.7 = (bf16[4,16,4096]{2,1,0:T(8,128)(2,1)}, bf16[4,16,4096]{2,1,0:T(8,128)(2,1)S(1)}, u32[]{:S(2)}, u32[]{:S(2)}) collective-permute-start(bf16[4,16,4096]{2,1,0:T(8,128)(2,1)} %get-tuple-element.7), channel_id=1, source_target_pairs={{0,2},{2,4},{4,6},{6,0},{1,3},{3,5},{5,7},{7,1},{8,10},{10,12},{12... | collective-permute-start | bytes 1572872 | tf_op jit(solution)/shard_map/ppermute | solution.py:17
  30.7 15.8 %collective-permute-start.6 = (bf16[4,16,4096]{2,1,0:T(8,128)(2,1)}, bf16[4,16,4096]{2,1,0:T(8,128)(2,1)S(1)}, u32[]{:S(2)}, u32[]{:S(2)}) collective-permute-start(bf16[4,16,4096]{2,1,0:T(8,128)(2,1)} %get-tuple-element.7), channel_id=1, source_target_pairs={{0,6},{2,0},{4,2},{6,4},{1,7},{3,1},{5,3},{7,5},{8,14},{10,8},{12,... | collective-permute-start | bytes 1572872 | tf_op jit(solution)/shard_map/ppermute | solution.py:17
  31.7 16.1 %collective-permute-start.12 = (bf16[4,16,4096]{2,1,0:T(8,128)(2,1)}, bf16[4,16,4096]{2,1,0:T(8,128)(2,1)}, u32[]{:S(2)}, u32[]{:S(2)}) collective-permute-start(bf16[4,16,4096]{2,1,0:T(8,128)(2,1)} %get-tuple-element.8), channel_id=1, source_target_pairs={{0,24},{8,0},{16,8},{24,16},{1,25},{9,1},{17,9},{25,17},{2,26},{10... | collective-permute-start | bytes 1572872 | tf_op jit(solution)/shard_map/ppermute | solution.py:17
  34.5 17.0 %collective-permute-start.9 = (bf16[4,16,4096]{2,1,0:T(8,128)(2,1)}, bf16[4,16,4096]{2,1,0:T(8,128)(2,1)}, u32[]{:S(2)}, u32[]{:S(2)}) collective-permute-start(bf16[4,16,4096]{2,1,0:T(8,128)(2,1)} %get-tuple-element.8), channel_id=1, source_target_pairs={{0,8},{8,16},{16,24},{24,0},{1,9},{9,17},{17,25},{25,1},{2,10},{10... | collective-permute-start | bytes 1572872 | tf_op jit(solution)/shard_map/ppermute | solution.py:17
  36.2 39.7 %all-to-all-start.1 = ((bf16[32,2,16,640]{3,2,1,0:T(8,128)(2,1)}), bf16[32,2,16,640]{3,2,1,0:T(8,128)(2,1)S(1)}, u32[]{:S(2)}, u32[]{:S(2)}) async-start(bf16[32,2,16,640]{3,2,1,0:T(8,128)(2,1)} %pad_maximum_fusion.3), calls=%async_computation.1 | async-start | bytes 2621440 | tf_op jit(solution)/shard_map/all_to_all | solution.py:63
  44.9 7.6 %copy-start.2 = (bf16[4,16,4096]{2,1,0:T(8,128)(2,1)}, bf16[4,16,4096]{2,1,0:T(8,128)(2,1)S(1)}, u32[]{:S(2)}) copy-start(bf16[4,16,4096]{2,1,0:T(8,128)(2,1)S(1)} %collective-permute-done.7) | copy-start | bytes 1572868
  45.0 23.0 %collective-permute-start.8 = (bf16[4,16,2048]{2,1,0:T(8,128)(2,1)S(1)}, bf16[4,16,2048]{2,1,0:T(8,128)(2,1)S(1)}, u32[]{:S(2)}, u32[]{:S(2)}) collective-permute-start(bf16[4,16,2048]{2,1,0:T(8,128)(2,1)S(1)} %slice.100), channel_id=1, source_target_pairs={{0,2},{2,4},{4,6},{6,0},{1,3},{3,5},{5,7},{7,1},{8,10},{10,12},{12... | collective-permute-start | bytes 786440 | tf_op jit(solution)/shard_map/ppermute | solution.py:17
  46.4 6.1 %copy-start.4 = (bf16[4,16,4096]{2,1,0:T(8,128)(2,1)}, bf16[4,16,4096]{2,1,0:T(8,128)(2,1)S(1)}, u32[]{:S(2)}) copy-start(bf16[4,16,4096]{2,1,0:T(8,128)(2,1)S(1)} %collective-permute-done.6) | copy-start | bytes 1572868
  46.5 20.3 %collective-permute-start.11 = (bf16[4,16,2048]{2,1,0:T(8,128)(2,1)S(1)}, bf16[4,16,2048]{2,1,0:T(8,128)(2,1)S(1)}, u32[]{:S(2)}, u32[]{:S(2)}) collective-permute-start(bf16[4,16,2048]{2,1,0:T(8,128)(2,1)S(1)} %slice.102), channel_id=1, source_target_pairs={{0,6},{2,0},{4,2},{6,4},{1,7},{3,1},{5,3},{7,5},{8,14},{10,8},{12,... | collective-permute-start | bytes 786440 | tf_op jit(solution)/shard_map/ppermute | solution.py:17
  48.8 17.9 %collective-permute-start.13 = (bf16[4,16,2048]{2,1,0:T(8,128)(2,1)S(1)}, bf16[4,16,2048]{2,1,0:T(8,128)(2,1)S(1)}, u32[]{:S(2)}, u32[]{:S(2)}) collective-permute-start(bf16[4,16,2048]{2,1,0:T(8,128)(2,1)S(1)} %slice.103), channel_id=1, source_target_pairs={{0,24},{8,0},{16,8},{24,16},{1,25},{9,1},{17,9},{25,17},{2,26},{10... | collective-permute-start | bytes 786440 | tf_op jit(solution)/shard_map/ppermute | solution.py:17
  52.5 16.1 %collective-permute-start.10 = (bf16[4,16,2048]{2,1,0:T(8,128)(2,1)S(1)}, bf16[4,16,2048]{2,1,0:T(8,128)(2,1)S(1)}, u32[]{:S(2)}, u32[]{:S(2)}) collective-permute-start(bf16[4,16,2048]{2,1,0:T(8,128)(2,1)S(1)} %slice.101), channel_id=1, source_target_pairs={{0,8},{8,16},{16,24},{24,0},{1,9},{9,17},{17,25},{25,1},{2,10},{10... | collective-permute-start | bytes 786440 | tf_op jit(solution)/shard_map/ppermute | solution.py:17
  68.6 2.4 %copy-start.3 = (bf16[4,16,4096]{2,1,0:T(8,128)(2,1)S(1)}, bf16[4,16,4096]{2,1,0:T(8,128)(2,1)}, u32[]{:S(2)}) copy-start(bf16[4,16,4096]{2,1,0:T(8,128)(2,1)} %copy-done.2) | copy-start | bytes 1572868
  68.6 2.4 %copy-start.5 = (bf16[4,16,4096]{2,1,0:T(8,128)(2,1)S(1)}, bf16[4,16,4096]{2,1,0:T(8,128)(2,1)}, u32[]{:S(2)}) copy-start(bf16[4,16,4096]{2,1,0:T(8,128)(2,1)} %copy-done.4) | copy-start | bytes 1572868
  69.5 12.4 %collective-permute-start.17 = (bf16[2,4,16,2048]{3,2,1,0:T(8,128)(2,1)}, bf16[2,4,16,2048]{3,2,1,0:T(8,128)(2,1)}, u32[]{:S(2)}, u32[]{:S(2)}) collective-permute-start(bf16[2,4,16,2048]{3,2,1,0:T(8,128)(2,1)} %pad_maximum_fusion.8), channel_id=1, source_target_pairs={{0,1},{1,0},{2,3},{3,2},{4,5},{5,4},{6,7},{7,6},{8,9},{9,8},{10,11... | collective-permute-start | bytes 1572872 | tf_op jit(solution)/shard_map/ppermute | solution.py:72
  70.9 9.9 %collective-permute-start.16 = (bf16[2,4,16,2048]{3,2,1,0:T(8,128)(2,1)}, bf16[2,4,16,2048]{3,2,1,0:T(8,128)(2,1)}, u32[]{:S(2)}, u32[]{:S(2)}) collective-permute-start(bf16[2,4,16,2048]{3,2,1,0:T(8,128)(2,1)} %pad_maximum_fusion.7), channel_id=1, source_target_pairs={{0,1},{1,0},{2,3},{3,2},{4,5},{5,4},{6,7},{7,6},{8,9},{9,8},{10,11... | collective-permute-start | bytes 1572872 | tf_op jit(solution)/shard_map/ppermute | solution.py:70
  75.4 7.7 %collective-permute-start.15 = (bf16[4,4,16,4096]{3,2,1,0:T(8,128)(2,1)}, bf16[4,4,16,4096]{3,2,1,0:T(8,128)(2,1)}, u32[]{:S(2)}, u32[]{:S(2)}) collective-permute-start(bf16[4,4,16,4096]{3,2,1,0:T(8,128)(2,1)} %get-tuple-element.23), channel_id=1, source_target_pairs={{0,1},{1,0},{2,3},{3,2},{4,5},{5,4},{6,7},{7,6},{8,9},{9,8},{10,11... | collective-permute-start | bytes 6291464 | tf_op jit(solution)/shard_map/ppermute | solution.py:68
  76.0 0.7 copy-start.10
  84.7 1.6 %copy-start = (bf16[1,4,4,16,4096]{4,3,2,1,0:T(8,128)(2,1)S(1)}, bf16[1,4,4,16,4096]{4,3,2,1,0:T(8,128)(2,1)}, u32[]{:S(2)}) copy-start(bf16[1,4,4,16,4096]{4,3,2,1,0:T(8,128)(2,1)} %get-tuple-element.22) | copy-start | bytes 6291460
  84.7 2.2 %copy-start.1 = (bf16[1,4,4,16,4096]{4,3,2,1,0:T(8,128)(2,1)S(1)}, bf16[1,4,4,16,4096]{4,3,2,1,0:T(8,128)(2,1)}, u32[]{:S(2)}) copy-start(bf16[1,4,4,16,4096]{4,3,2,1,0:T(8,128)(2,1)} %get-tuple-element.24) | copy-start | bytes 6291460
  (1 other events, 0.7 us)
